TPU v7x, 512 devices: a whole 4x8x8 slice. The times are simulated.
512 devices in a mesh: dp: 32 (over z, x), fsdp: 16 (over y, core).
Axes of the slice: x: 4, y: 8, z: 8, core: 2. Of those that a mesh axis runs over, the one named last changes fastest.
Arguments:
- projected: bfloat16 [65536, 2304], P(('dp', 'fsdp')), may hold values from -7.03125 to 7.03125
- out_weight: bfloat16 [768, 1536], P('fsdp'), may hold values from -0.21875 to 0.21875
- kernel: float32 [31, 1536], replicated, may hold values from -2 to 2
- cotangent: bfloat16 [65536, 1536], P(('dp', 'fsdp')), may hold values from -6 to 6
- send_rows: int32 [65536], P(('dp', 'fsdp')), may hold values from -1 to 127, as said below
- compute_src: int32 [65536], P(('dp', 'fsdp')), may hold values from -1 to 127, as said below
- segment: int32 [65536], P(('dp', 'fsdp')), may hold values from -1 to 3, as said below
Outputs:
- block_out: bfloat16 [65536, 1536], P(('dp', 'fsdp'))
- projected_grad: bfloat16 [65536, 2304], P(('dp', 'fsdp'))
- out_weight_grad: float32 [768, 1536], P('fsdp')
- kernel_grad: float32 [31, 1536], replicated
Inputs may be any that keep to these rules, and one draw needn't show every extreme that they name: `send_rows`: A device's 128 entries are 32 blocks of 4, block t for index t of dp at the same fsdp index; each lists rows of the device's own block of projected, each row at most once, filled entries first in a block and -1 after them. In every draw some device of each fsdp index fills all its entries. `compute_src`: on device (t, f), a row holds s * 4 + k when it receives entry t * 4 + k of device (s, f); every filled entry of send_rows is received by exactly one row, and a row holds -1 when it receives nothing. Filled rows come first. In every draw some device of each fsdp index receives a full block from every device. On each device, rows with compute_src = -1 hold -1, the others hold segment numbers from 0 that never fall along the rows.
All inputs are finite; a program needn't handle non-finite values.
Results may differ from a plain program's by a relative error of at most 0.018.
Values may be sent and summed in bfloat16 or wider, within the bound.
No kernel may reach another device: no remote copies, remote signals or barrier semaphores. Data moves between devices by JAX's collectives and lax.ppermute only.
A program may use at most 128 MiB of HBM per device.

v0:
```python
import jax
import jax.numpy as jnp
from jax import lax
from jax.sharding import PartitionSpec as P

HEADS = 8
HEAD_DIM = 96


def split_heads(frames):
    length = frames.shape[0]
    inner_width = HEADS * HEAD_DIM
    query_part = frames[:, :inner_width].reshape(length, HEADS, HEAD_DIM)
    key_part = frames[:, inner_width : 2 * inner_width].reshape(length, HEADS, HEAD_DIM)
    value_part = frames[:, 2 * inner_width :].reshape(length, HEADS, HEAD_DIM)
    return (query_part, key_part, value_part)


def attend(frames, segment):
    query_part, key_part, value_part = split_heads(frames)
    scores = jnp.einsum(
        "qhd,khd->hqk", query_part, key_part, preferred_element_type=jnp.float32
    ) * HEAD_DIM ** (-0.5)
    inside = segment[:, None] == segment[None, :]
    scores = jnp.where(inside[None], scores, -1e30)
    highest = jnp.max(scores, axis=2, keepdims=True)
    weights = jnp.exp(scores - highest)
    soft_probs = weights / jnp.sum(weights, axis=2, keepdims=True)
    rounded = soft_probs.astype(jnp.bfloat16)
    context = jnp.einsum("hqk,khd->qhd", rounded, value_part, preferred_element_type=jnp.float32)
    return (
        context.reshape(frames.shape[0], HEADS * HEAD_DIM).astype(jnp.bfloat16),
        soft_probs,
        rounded,
    )


def attend_back(frames, soft_probs, rounded, context_grad):
    query_part, key_part, value_part = split_heads(frames)
    length = frames.shape[0]
    inner_width = HEADS * HEAD_DIM
    upstream = context_grad.reshape(length, HEADS, HEAD_DIM)
    value_grad = jnp.einsum("hqk,qhd->khd", rounded, upstream, preferred_element_type=jnp.float32)
    prob_grad = jnp.einsum("qhd,khd->hqk", upstream, value_part, preferred_element_type=jnp.float32)
    score_grad = soft_probs * (prob_grad - jnp.sum(prob_grad * soft_probs, axis=2, keepdims=True))
    score_grad = (score_grad * HEAD_DIM ** (-0.5)).astype(jnp.bfloat16)
    query_grad = jnp.einsum(
        "hqk,khd->qhd", score_grad, key_part, preferred_element_type=jnp.float32
    )
    key_grad = jnp.einsum(
        "hqk,qhd->khd", score_grad, query_part, preferred_element_type=jnp.float32
    )
    return jnp.concatenate(
        [
            query_grad.reshape(length, inner_width).astype(jnp.bfloat16),
            key_grad.reshape(length, inner_width).astype(jnp.bfloat16),
            value_grad.reshape(length, inner_width).astype(jnp.bfloat16),
        ],
        axis=1,
    )


def finish(mixed, kernel, segment):
    length = mixed.shape[0]
    tap_count = kernel.shape[0]
    half_span = (tap_count - 1) // 2
    signal = mixed.astype(jnp.float32)
    padded = jnp.pad(signal, ((half_span, half_span), (0, 0)))
    neighbours = jnp.pad(segment, (half_span, half_span), constant_values=-2)
    convolved = jnp.zeros_like(signal)
    for offset in range(tap_count):
        matching = (neighbours[offset : offset + length] == segment).astype(jnp.float32)
        convolved = (
            convolved + kernel[offset] * padded[offset : offset + length] * matching[:, None]
        )
    return signal + jax.nn.silu(convolved)


def body(projected, out_weight, kernel, cotangent, send_rows, compute_src, segment):
    row_count = projected.shape[0]
    present = send_rows >= 0
    outgoing = jnp.take(projected, jnp.maximum(send_rows, 0), axis=0)
    outgoing = jnp.where(present[:, None], outgoing, jnp.zeros_like(outgoing))
    incoming = lax.all_to_all(outgoing, "dp", split_axis=0, concat_axis=0, tiled=True)
    filled = compute_src >= 0
    frames = jnp.take(incoming, jnp.maximum(compute_src, 0), axis=0)
    frames = jnp.where(filled[:, None], frames, jnp.zeros_like(frames))
    context, soft_probs, rounded = attend(frames, segment)
    columns = context
    mixed_sums = jnp.dot(
        columns,
        lax.all_gather(out_weight, "fsdp", axis=0, tiled=True),
        preferred_element_type=jnp.float32,
    )
    mixed = mixed_sums.astype(jnp.bfloat16)
    result, pullback = jax.vjp(
        lambda signal, kernel_taps: finish(signal, kernel_taps, segment), mixed, kernel
    )
    mixed_grad, kernel_part = pullback(cotangent.astype(jnp.float32))
    columns = context
    weight_share = lax.psum_scatter(
        jnp.einsum("rc,rd->cd", columns, mixed_grad, preferred_element_type=jnp.float32).astype(
            jnp.bfloat16
        ),
        "fsdp",
        scatter_dimension=0,
        tiled=True,
    ).astype(jnp.float32)
    context_grad = jnp.einsum(
        "rd,cd->rc",
        mixed_grad,
        lax.all_gather(out_weight, "fsdp", axis=0, tiled=True),
        preferred_element_type=jnp.float32,
    ).astype(jnp.bfloat16)
    frame_grad = attend_back(frames, soft_probs, rounded, context_grad)
    slot_total = incoming.shape[0]
    back_index = jnp.where(filled, compute_src, slot_total)
    returning = jnp.zeros_like(incoming).at[back_index].set(frame_grad, mode="drop")
    arrived = lax.all_to_all(returning, "dp", split_axis=0, concat_axis=0, tiled=True)
    source_index = jnp.where(present, send_rows, row_count)
    projected_grad = jnp.zeros_like(projected).at[source_index].set(arrived, mode="drop")
    scale_factor = (row_count * lax.axis_size("dp") * lax.axis_size("fsdp")) ** (-0.5)
    weight_total = lax.psum(weight_share, "dp")
    kernel_total = lax.psum(kernel_part, ("dp", "fsdp"))
    return (
        result.astype(jnp.bfloat16),
        projected_grad,
        weight_total * scale_factor,
        kernel_total * scale_factor,
    )


def solution(mesh):
    placed = (
        P(("dp", "fsdp"), None),
        P("fsdp", None),
        P(),
        P(("dp", "fsdp"), None),
        P(("dp", "fsdp")),
        P(("dp", "fsdp")),
        P(("dp", "fsdp")),
    )
    return jax.shard_map(
        body,
        mesh=mesh,
        in_specs=placed,
        out_specs=(P(("dp", "fsdp"), None), P(("dp", "fsdp"), None), P("fsdp", None), P()),
        check_vma=False,
    )
```

profile of v0, /device:TPU:8, one launch (start us, length us, event | category | flops | bytes accessed | tf_op | source)
XLA Modules:
  0.0 566.0 jit_solution(5995998765189666826)
XLA Ops:
  7.2 0.0 copy-start
  7.2 0.0 all-gather.2.cloned.1.call-start
  7.2 0.7 all-gather.2.cloned.1.call-update
  7.9 1.1 compare_select_fusion.1
  9.1 0.0 copy-start.88
  9.1 1.0 gather_fusion
  10.1 0.0 copy-start.15
  10.1 0.2 select_select_fusion.1
  10.3 1.0 all_to_all.16
  11.2 13.2 %all-to-all-start = ((bf16[32,4,2304]{2,1,0:T(4,128)(2,1)}), bf16[32,4,2304]{2,1,0:T(4,128)(2,1)S(1)}, u32[]{:S(2)}, u32[]{:S(2)}) async-start(bf16[32,4,2304]{2,1,0:T(4,128)(2,1)} %all_to_all.16), calls=%async_computation | async-start | bytes 1179648 | tf_op jit(solution)/shard_map/all_to_all | solution.py:84
  24.4 0.0 all-reduce.67.cloned.1.call-start
  24.5 0.2 slice_reduce_fusion.29
  24.7 0.0 copy-start.22
  24.8 0.5 compare_select_fusion
  25.3 0.3 slice_reduce_fusion.30
  25.7 0.7 compare_convert_fusion.28
  26.4 0.6 compare_convert_fusion.29
  27.1 0.1 broadcast_compare_fusion
  27.2 16.2 %all-to-all-done = bf16[32,4,2304]{2,1,0:T(4,128)(2,1)S(1)} async-done(((bf16[32,4,2304]{2,1,0:T(4,128)(2,1)}), bf16[32,4,2304]{2,1,0:T(4,128)(2,1)S(1)}, u32[]{:S(2)}, u32[]{:S(2)}) %all-to-all-start) | async-done | bytes 589856 | tf_op jit(solution)/shard_map/all_to_all | solution.py:84
  43.4 0.1 all_to_all.18
  43.5 1.0 gather_fusion.1
  44.5 0.2 select_select_fusion
  44.7 0.2 copy.25
  44.9 0.2 copy.24
  45.1 0.0 copy-start.13
  45.1 0.2 copy.23
  45.2 1.7 fusion.39
  47.0 1.2 convolution_convert_fusion.6
  48.2 8.4 %all-gather.2.cloned.1.call-done = bf16[768,1536]{1,0:T(8,128)(2,1)} async-done(((bf16[48,1536]{1,0:T(8,128)(2,1)}), bf16[768,1536]{1,0:T(8,128)(2,1)}) %all-gather.2.cloned.1.call-update) | async-done | bytes 2359312 | tf_op jit(solution)/shard_map/all_gather | solution.py:92
  56.6 2.2 fusion.2
  59.0 8.0 %multiply_reduce_fusion.31 = (f32[1536]{0:T(1024)S(1)}, f32[1536]{0:T(1024)S(1)}, f32[1536]{0:T(1024)S(1)}, f32[1536]{0:T(1024)S(1)}, f32[1536]{0:T(1024)S(1)}, ...) fusion(f32[128,1536]{1,0:T(8,128)S(1)} %fusion.2, ...), kind=kLoop, calls=%fused_computation.99 | loop fusion | flops 25152000 | bytes 3013632 | tf_op jit(solution)/shard_map/transpose(jvp())/reduce_sum | solution.py:74
  67.2 1.8 multiply_reduce_fusion.22
  69.0 3.1 multiply_reduce_fusion.16
  72.3 2.5 multiply_multiply_fusion.27
  75.1 3.4 multiply_multiply_fusion.29
  78.7 4.1 multiply_multiply_fusion.28
  83.3 4.0 multiply_reduce_fusion.4
  87.3 1.0 pad_add_fusion.7
  88.3 0.0 all-reduce.67.cloned.1.call-update
  88.4 0.0 reduce-scatter.2.cloned.1.call-start
  88.5 7.4 %pad_add_fusion = f32[158,1536]{1,0:T(8,128)S(1)} fusion(f32[128,1536]{1,0:T(8,128)} %get-tuple-element.76, f32[128,1536]{1,0:T(8,128)S(1)} %get-tuple-element.78, f32[128,1536]{1,0:T(8,128)S(1)} %get-tuple-element.79, f32[128,1536]{1,0:T(8,128)} %get-tuple-element.80, f32[128,1536]{1,0:T(8,128)} %get-tuple-element.81, f32[128,1536]{1,0:T(8,128)} %get-tuple-element.82, ...), kind=kLoop, calls=%fused_computation.59 | loop fusion | flops 5824512 | bytes 20631552 | tf_op jit(solution)/shard_map/transpose(jvp())/add_any | solution.py:74
  95.9 0.7 fusion.16
  96.6 2.1 convolution_convert_fusion
  98.7 0.0 reduce-scatter.2.cloned.1.call-update
  98.8 0.9 convolution_convert_fusion.5
  99.7 0.0 copy-start.14
  99.7 0.2 copy.27
  99.8 1.6 convolution_convert_fusion.2
  101.5 0.1 copy.33
  101.6 0.3 fusion.40
  101.9 1.6 convolution_convert_fusion.3
  103.5 0.1 copy.32
  103.6 1.6 convolution_convert_fusion.4
  105.2 0.1 copy.31
  105.3 1.8 scatter_custom_fusion
  107.1 1.0 all_to_all.19
  108.1 10.2 %all-to-all-start.1 = ((bf16[32,4,2304]{2,1,0:T(4,128)(2,1)}), bf16[32,4,2304]{2,1,0:T(4,128)(2,1)S(1)}, u32[]{:S(2)}, u32[]{:S(2)}) async-start(bf16[32,4,2304]{2,1,0:T(4,128)(2,1)} %all_to_all.19), calls=%async_computation.1 | async-start | bytes 1179648 | tf_op jit(solution)/shard_map/all_to_all | solution.py:119
  118.2 236.3 %all-reduce.67.cloned.1.call-done = f32[31,1536]{1,0:T(8,128)} async-done(((f32[31,1536]{1,0:T(8,128)}), f32[31,1536]{1,0:T(8,128)}) %all-reduce.67.cloned.1.call-update) | async-done | bytes 190480 | tf_op jit(solution)/shard_map/psum | solution.py:124
  354.6 1.6 broadcast_multiply_fusion.2
  356.2 0.1 reshape.320
  356.4 2.4 scatter_custom_fusion.1
  358.7 52.8 %reduce-scatter.2.cloned.1.call-done = bf16[48,1536]{1,0:T(8,128)(2,1)} async-done(((bf16[768,1536]{1,0:T(8,128)(2,1)}), bf16[48,1536]{1,0:T(8,128)(2,1)}) %reduce-scatter.2.cloned.1.call-update) | async-done | bytes 147472 | tf_op jit(solution)/shard_map/reduce_scatter | solution.py:101
  411.5 147.2 %all-reduce.68 = f32[48,1536]{1,0:T(8,128)S(1)} all-reduce(bf16[48,1536]{1,0:T(8,128)(2,1)} %reduce-scatter.2.cloned.1.call-done), channel_id=1, replica_groups=mesh['dp'=32,'fsdp'=16] {'dp'}, use_global_device_ids=true, to_apply=%region_6.8 | all-reduce | flops 73728 | bytes 442368 | tf_op jit(solution)/shard_map/psum | solution.py:123
  558.7 0.7 broadcast_multiply_fusion.1
  (211 shorter events, 0.6 us)
Async XLA Ops:
  7.2 49.4 %all-gather.2.cloned.1.call-start = ((), (), s32[]{:S(2)}) async-start(), calls=%async_computation.3 | async-start | bytes 2506752 | tf_op jit(solution)/shard_map/all_gather | solution.py:92
  10.1 14.4 %copy-start.15 = (f32[31,1536]{1,0:T(8,128)S(1)}, f32[31,1536]{1,0:T(8,128)}, u32[]{:S(2)}) copy-start(f32[31,1536]{1,0:T(8,128)} %param.11) | copy-start | bytes 571396
  10.1 14.6 %copy-start.89 = (s32[128]{0:T(128)S(1)}, s32[128]{0:T(128)}, u32[]{:S(2)}) copy-start(s32[128]{0:T(128)} %param.14) | copy-start | bytes 1540
  10.1 15.7 %copy-start.87 = (s32[128]{0:T(128)S(1)}, s32[128]{0:T(128)}, u32[]{:S(2)}) copy-start(s32[128]{0:T(128)} %param.15) | copy-start | bytes 1540
  11.2 32.2 %all-to-all-start = ((bf16[32,4,2304]{2,1,0:T(4,128)(2,1)}), bf16[32,4,2304]{2,1,0:T(4,128)(2,1)S(1)}, u32[]{:S(2)}, u32[]{:S(2)}) async-start(bf16[32,4,2304]{2,1,0:T(4,128)(2,1)} %all_to_all.16), calls=%async_computation | async-start | bytes 1179648 | tf_op jit(solution)/shard_map/all_to_all | solution.py:84
  24.4 330.2 %all-reduce.67.cloned.1.call-start = ((), (), s32[]{:S(2)}) async-start(), calls=%async_computation.5 | async-start | bytes 393216 | tf_op jit(solution)/shard_map/psum | solution.py:124
  24.7 34.1 %copy-start.16 = (f32[1536]{0:T(1024)}, f32[1536]{0:T(1024)S(1)}, u32[]{:S(2)}) copy-start(f32[1536]{0:T(1024)S(1)} %get-tuple-element.60) | copy-start | bytes 18436
  24.7 34.1 %copy-start.18 = (f32[1536]{0:T(1024)}, f32[1536]{0:T(1024)S(1)}, u32[]{:S(2)}) copy-start(f32[1536]{0:T(1024)S(1)} %get-tuple-element.61) | copy-start | bytes 18436
  24.7 34.1 %copy-start.20 = (f32[1536]{0:T(1024)}, f32[1536]{0:T(1024)S(1)}, u32[]{:S(2)}) copy-start(f32[1536]{0:T(1024)S(1)} %get-tuple-element.63) | copy-start | bytes 18436
  24.7 34.1 %copy-start.22 = (f32[1536]{0:T(1024)}, f32[1536]{0:T(1024)S(1)}, u32[]{:S(2)}) copy-start(f32[1536]{0:T(1024)S(1)} %get-tuple-element.64) | copy-start | bytes 18436
  24.7 34.1 %copy-start.48 = (f32[1536]{0:T(1024)}, f32[1536]{0:T(1024)S(1)}, u32[]{:S(2)}) copy-start(f32[1536]{0:T(1024)S(1)} %get-tuple-element.66) | copy-start | bytes 18436
  24.7 34.1 %copy-start.50 = (f32[1536]{0:T(1024)}, f32[1536]{0:T(1024)S(1)}, u32[]{:S(2)}) copy-start(f32[1536]{0:T(1024)S(1)} %get-tuple-element.56) | copy-start | bytes 18436
  24.7 34.1 %copy-start.52 = (f32[1536]{0:T(1024)}, f32[1536]{0:T(1024)S(1)}, u32[]{:S(2)}) copy-start(f32[1536]{0:T(1024)S(1)} %get-tuple-element.57) | copy-start | bytes 18436
  24.7 34.1 %copy-start.54 = (f32[1536]{0:T(1024)}, f32[1536]{0:T(1024)S(1)}, u32[]{:S(2)}) copy-start(f32[1536]{0:T(1024)S(1)} %get-tuple-element.58) | copy-start | bytes 18436
  24.7 34.1 %copy-start.56 = (f32[1536]{0:T(1024)}, f32[1536]{0:T(1024)S(1)}, u32[]{:S(2)}) copy-start(f32[1536]{0:T(1024)S(1)} %get-tuple-element.59) | copy-start | bytes 18436
  24.8 34.1 %copy-start.58 = (f32[1536]{0:T(1024)}, f32[1536]{0:T(1024)S(1)}, u32[]{:S(2)}) copy-start(f32[1536]{0:T(1024)S(1)} %get-tuple-element.65) | copy-start | bytes 18436
  25.6 33.3 %copy-start.24 = (f32[1536]{0:T(1024)}, f32[1536]{0:T(1024)S(1)}, u32[]{:S(2)}) copy-start(f32[1536]{0:T(1024)S(1)} %get-tuple-element.43) | copy-start | bytes 18436
  25.6 33.3 %copy-start.26 = (f32[1536]{0:T(1024)}, f32[1536]{0:T(1024)S(1)}, u32[]{:S(2)}) copy-start(f32[1536]{0:T(1024)S(1)} %get-tuple-element.44) | copy-start | bytes 18436
  25.6 33.3 %copy-start.28 = (f32[1536]{0:T(1024)}, f32[1536]{0:T(1024)S(1)}, u32[]{:S(2)}) copy-start(f32[1536]{0:T(1024)S(1)} %get-tuple-element.45) | copy-start | bytes 18436
  25.6 33.3 %copy-start.30 = (f32[1536]{0:T(1024)}, f32[1536]{0:T(1024)S(1)}, u32[]{:S(2)}) copy-start(f32[1536]{0:T(1024)S(1)} %get-tuple-element.46) | copy-start | bytes 18436
  25.6 33.3 %copy-start.32 = (f32[1536]{0:T(1024)}, f32[1536]{0:T(1024)S(1)}, u32[]{:S(2)}) copy-start(f32[1536]{0:T(1024)S(1)} %get-tuple-element.47) | copy-start | bytes 18436
  25.7 33.3 %copy-start.34 = (f32[1536]{0:T(1024)}, f32[1536]{0:T(1024)S(1)}, u32[]{:S(2)}) copy-start(f32[1536]{0:T(1024)S(1)} %get-tuple-element.48) | copy-start | bytes 18436
  25.7 33.3 %copy-start.36 = (f32[1536]{0:T(1024)}, f32[1536]{0:T(1024)S(1)}, u32[]{:S(2)}) copy-start(f32[1536]{0:T(1024)S(1)} %get-tuple-element.49) | copy-start | bytes 18436
  25.7 33.3 %copy-start.38 = (f32[1536]{0:T(1024)}, f32[1536]{0:T(1024)S(1)}, u32[]{:S(2)}) copy-start(f32[1536]{0:T(1024)S(1)} %get-tuple-element.50) | copy-start | bytes 18436
  25.7 33.3 %copy-start.40 = (f32[1536]{0:T(1024)}, f32[1536]{0:T(1024)S(1)}, u32[]{:S(2)}) copy-start(f32[1536]{0:T(1024)S(1)} %get-tuple-element.51) | copy-start | bytes 18436
  25.7 33.3 %copy-start.42 = (f32[1536]{0:T(1024)}, f32[1536]{0:T(1024)S(1)}, u32[]{:S(2)}) copy-start(f32[1536]{0:T(1024)S(1)} %get-tuple-element.52) | copy-start | bytes 18436
  25.7 33.3 %copy-start.44 = (f32[1536]{0:T(1024)}, f32[1536]{0:T(1024)S(1)}, u32[]{:S(2)}) copy-start(f32[1536]{0:T(1024)S(1)} %get-tuple-element.53) | copy-start | bytes 18436
  25.7 33.3 %copy-start.46 = (f32[1536]{0:T(1024)}, f32[1536]{0:T(1024)S(1)}, u32[]{:S(2)}) copy-start(f32[1536]{0:T(1024)S(1)} %get-tuple-element.54) | copy-start | bytes 18436
  26.4 42.6 %copy-start.85 = (f32[128]{0:T(128)}, f32[128]{0:T(128)S(1)}, u32[]{:S(2)}) copy-start(f32[128]{0:T(128)S(1)} %get-tuple-element.129) | copy-start | bytes 1540
  27.1 40.0 %copy-start.61 = (f32[128]{0:T(128)}, f32[128]{0:T(128)S(1)}, u32[]{:S(2)}) copy-start(f32[128]{0:T(128)S(1)} %get-tuple-element.114) | copy-start | bytes 1540
  27.1 40.0 %copy-start.63 = (f32[128]{0:T(128)}, f32[128]{0:T(128)S(1)}, u32[]{:S(2)}) copy-start(f32[128]{0:T(128)S(1)} %get-tuple-element.115) | copy-start | bytes 1540
  27.1 40.0 %copy-start.65 = (f32[128]{0:T(128)}, f32[128]{0:T(128)S(1)}, u32[]{:S(2)}) copy-start(f32[128]{0:T(128)S(1)} %get-tuple-element.116) | copy-start | bytes 1540
  27.1 40.1 %copy-start.67 = (f32[128]{0:T(128)}, f32[128]{0:T(128)S(1)}, u32[]{:S(2)}) copy-start(f32[128]{0:T(128)S(1)} %get-tuple-element.117) | copy-start | bytes 1540
  27.1 40.1 %copy-start.69 = (f32[128]{0:T(128)}, f32[128]{0:T(128)S(1)}, u32[]{:S(2)}) copy-start(f32[128]{0:T(128)S(1)} %get-tuple-element.118) | copy-start | bytes 1540
  27.1 40.1 %copy-start.71 = (f32[128]{0:T(128)}, f32[128]{0:T(128)S(1)}, u32[]{:S(2)}) copy-start(f32[128]{0:T(128)S(1)} %get-tuple-element.119) | copy-start | bytes 1540
  27.1 40.1 %copy-start.73 = (f32[128]{0:T(128)}, f32[128]{0:T(128)S(1)}, u32[]{:S(2)}) copy-start(f32[128]{0:T(128)S(1)} %get-tuple-element.120) | copy-start | bytes 1540
  27.1 40.1 %copy-start.75 = (f32[128]{0:T(128)}, f32[128]{0:T(128)S(1)}, u32[]{:S(2)}) copy-start(f32[128]{0:T(128)S(1)} %get-tuple-element.121) | copy-start | bytes 1540
  27.1 40.1 %copy-start.77 = (f32[128]{0:T(128)}, f32[128]{0:T(128)S(1)}, u32[]{:S(2)}) copy-start(f32[128]{0:T(128)S(1)} %get-tuple-element.122) | copy-start | bytes 1540
  27.1 41.9 %copy-start.79 = (f32[128]{0:T(128)}, f32[128]{0:T(128)S(1)}, u32[]{:S(2)}) copy-start(f32[128]{0:T(128)S(1)} %get-tuple-element.123) | copy-start | bytes 1540
  27.1 41.9 %copy-start.81 = (f32[128]{0:T(128)}, f32[128]{0:T(128)S(1)}, u32[]{:S(2)}) copy-start(f32[128]{0:T(128)S(1)} %get-tuple-element.124) | copy-start | bytes 1540
  27.1 41.9 %copy-start.83 = (f32[128]{0:T(128)}, f32[128]{0:T(128)S(1)}, u32[]{:S(2)}) copy-start(f32[128]{0:T(128)S(1)} %get-tuple-element.125) | copy-start | bytes 1540
  27.2 19.8 %copy-start.60 = (pred[128,128]{0,1:T(8,128)(4,1)}, pred[128,128]{0,1:T(8,128)(4,1)S(1)}, u32[]{:S(2)}) copy-start(pred[128,128]{0,1:T(8,128)(4,1)S(1)} %broadcast_compare_fusion) | copy-start | bytes 49156
  45.1 13.7 %copy-start.13 = (bf16[128,768]{0,1:T(8,128)(2,1)}, bf16[128,768]{0,1:T(8,128)(2,1)S(1)}, u32[]{:S(2)}) copy-start(bf16[128,768]{0,1:T(8,128)(2,1)S(1)} %copy.24) | copy-start | bytes 589828
  45.2 13.6 %copy-start.9 = (bf16[128,768]{0,1:T(8,128)(2,1)}, bf16[128,768]{0,1:T(8,128)(2,1)S(1)}, u32[]{:S(2)}) copy-start(bf16[128,768]{0,1:T(8,128)(2,1)S(1)} %copy.23) | copy-start | bytes 589828
  48.2 10.8 %copy-start.8 = (bf16[128,1536]{1,0:T(8,128)(2,1)S(1)}, bf16[128,1536]{1,0:T(8,128)(2,1)}, u32[]{:S(2)}) copy-start(bf16[128,1536]{1,0:T(8,128)(2,1)} %param.12) | copy-start | bytes 1179652
  75.0 3.6 copy-start.25
  75.0 3.6 copy-start.27
  75.0 3.6 copy-start.29
  75.0 3.5 copy-start.31
  75.0 3.5 copy-start.33
  75.0 3.5 copy-start.35
  78.7 4.6 copy-start.17
  78.7 4.6 copy-start.19
  78.7 4.6 copy-start.21
  78.7 4.6 copy-start.23
  78.7 4.6 copy-start.86
  88.4 323.2 %reduce-scatter.2.cloned.1.call-start = ((), (), s32[]{:S(2)}) async-start(), calls=%async_computation.4 | async-start | bytes 2506752 | tf_op jit(solution)/shard_map/reduce_scatter | solution.py:101
  88.4 7.5 %copy-start.2 = (f32[128,1536]{1,0:T(8,128)S(1)}, f32[128,1536]{1,0:T(8,128)}, u32[]{:S(2)}) copy-start(f32[128,1536]{1,0:T(8,128)} %get-tuple-element.70) | copy-start | bytes 2359300
  88.4 7.5 %copy-start.3 = (f32[128,1536]{1,0:T(8,128)S(1)}, f32[128,1536]{1,0:T(8,128)}, u32[]{:S(2)}) copy-start(f32[128,1536]{1,0:T(8,128)} %get-tuple-element.71) | copy-start | bytes 2359300
  88.4 7.5 %copy-start.4 = (f32[128,1536]{1,0:T(8,128)S(1)}, f32[128,1536]{1,0:T(8,128)}, u32[]{:S(2)}) copy-start(f32[128,1536]{1,0:T(8,128)} %get-tuple-element.72) | copy-start | bytes 2359300
  88.4 7.5 %copy-start.5 = (f32[128,1536]{1,0:T(8,128)S(1)}, f32[128,1536]{1,0:T(8,128)}, u32[]{:S(2)}) copy-start(f32[128,1536]{1,0:T(8,128)} %get-tuple-element.73) | copy-start | bytes 2359300
  88.4 7.5 %copy-start.6 = (f32[128,1536]{1,0:T(8,128)S(1)}, f32[128,1536]{1,0:T(8,128)}, u32[]{:S(2)}) copy-start(f32[128,1536]{1,0:T(8,128)} %get-tuple-element.75) | copy-start | bytes 2359300
  88.5 7.5 %copy-start.7 = (f32[128,1536]{1,0:T(8,128)S(1)}, f32[128,1536]{1,0:T(8,128)}, u32[]{:S(2)}) copy-start(f32[128,1536]{1,0:T(8,128)} %get-tuple-element.69) | copy-start | bytes 2359300
  108.1 248.2 %all-to-all-start.1 = ((bf16[32,4,2304]{2,1,0:T(4,128)(2,1)}), bf16[32,4,2304]{2,1,0:T(4,128)(2,1)S(1)}, u32[]{:S(2)}, u32[]{:S(2)}) async-start(bf16[32,4,2304]{2,1,0:T(4,128)(2,1)} %all_to_all.19), calls=%async_computation.1 | async-start | bytes 1179648 | tf_op jit(solution)/shard_map/all_to_all | solution.py:119
  (31 other events, 86.8 us)
Sparse Core Ops, SparseCore 0:
  10.1 46.4 all-gather.1
  88.5 266.0 all-reduce.66
  357.7 53.8 reduce-scatter.1
where the time goes:
time: 567 us; the launch traced here: 566 us
  waiting for transfers between devices  314 us (55%)
  blocking collectives  147 us (26%)
  other arithmetic  43.6 us (8%)
  starting transfers between devices  23.5 us (4%)
  between operations  15.5 us (3%)
  matrix products  13.1 us (2%)
  local copies, waits for them, and re-layouts  8.7 us (2%)
    psum x1, waiting for transfers between devices, body(): kernel_total = lax.psum(kernel_part, ('dp', 'fsdp'))  236 us
    psum x1, blocking collectives, body(): weight_total = lax.psum(weight_share, 'dp')  147 us
    reduce_scatter x1, waiting for transfers between devices, body(): lax.psum_scatter(jnp.einsum('rc,rd->cd', columns, mixed_grad, preferred_e...  52.8 us
    reduce_sum x4, other arithmetic, finish(): kernel[offset] * padded[offset:offset + length] * matching[:, None]  17 us
    all_to_all x1, waiting for transfers between devices, body(): lax.all_to_all(outgoing, 'dp', split_axis=0, concat_axis=0, tiled=True)  16.2 us
    all_to_all x1, starting transfers between devices, body(): lax.all_to_all(outgoing, 'dp', split_axis=0, concat_axis=0, tiled=True)  13.2 us
  transfers between devices with their start and end apart: 5, of which 4 were waited for; matrix products, arithmetic and copies ran while one was open for 6% of the time, Pallas kernels for 0%

commit v1 on v0

--- a/solution.py
+++ b/solution.py
@@ -120,14 +120,39 @@
     source_index = jnp.where(present, send_rows, row_count)
     projected_grad = jnp.zeros_like(projected).at[source_index].set(arrived, mode="drop")
     scale_factor = (row_count * lax.axis_size("dp") * lax.axis_size("fsdp")) ** (-0.5)
-    weight_total = lax.psum(weight_share, "dp")
-    kernel_total = lax.psum(kernel_part, ("dp", "fsdp"))
+    kernel_f = lax.psum(kernel_part, "fsdp")
+    both = dp_allreduce_a2a(jnp.concatenate([weight_share, kernel_f, jnp.zeros((17, 1536), jnp.float32)], axis=0))
+    weight_total, kernel_total = both[:48], both[48:79]
     return (
         result.astype(jnp.bfloat16),
         projected_grad,
         weight_total * scale_factor,
         kernel_total * scale_factor,
     )
+
+
+def dp_allreduce_rs_ag(x):
+    n = lax.axis_size("dp")
+    flat = x.reshape(n, -1)
+    part = lax.psum_scatter(flat, "dp", scatter_dimension=0, tiled=True)
+    return lax.all_gather(part, "dp", axis=0, tiled=True).reshape(x.shape)
+
+
+def dp_allreduce_a2a(x):
+    n = lax.axis_size("dp")
+    flat = x.reshape(n, -1)
+    got = lax.all_to_all(flat, "dp", split_axis=0, concat_axis=0, tiled=True)
+    part = jnp.sum(got, axis=0, keepdims=True)
+    return lax.all_gather(part, "dp", axis=0, tiled=True).reshape(x.shape)
+
+
+def dp_allreduce_a2a2(x):
+    n = lax.axis_size("dp")
+    flat = x.reshape(n, -1)
+    got = lax.all_to_all(flat, "dp", split_axis=0, concat_axis=0, tiled=True)
+    part = jnp.sum(got, axis=0, keepdims=True)
+    back = lax.all_to_all(jnp.broadcast_to(part, flat.shape), "dp", split_axis=0, concat_axis=0, tiled=True)
+    return back.reshape(x.shape)
 
 
 def solution(mesh):

time: 567 us -> 342 us (0.60)
  the two profiles are of different devices: /device:TPU:8 before, /device:TPU:24 now
where the time goes in v1:
time: 342 us
  waiting for transfers between devices  184 us (54%)
  blocking collectives  48.8 us (14%)
  starting transfers between devices  33.8 us (10%)
  other arithmetic  28.4 us (8%)
  local copies, waits for them, and re-layouts  17.9 us (5%)
  between operations  14.9 us (4%)
  matrix products  14 us (4%)
    psum x1, waiting for transfers between devices, body(): kernel_f = lax.psum(kernel_part, 'fsdp')  113 us
    all_gather x1, blocking collectives, dp_allreduce_a2a(): return lax.all_gather(part, 'dp', axis=0, tiled=True).reshape(x.shape)  48.8 us
    reduce_scatter x1, waiting for transfers between devices, body(): lax.psum_scatter(jnp.einsum('rc,rd->cd', columns, mixed_grad, preferred_e...  26.3 us
    all_to_all x1, waiting for transfers between devices, body(): lax.all_to_all(outgoing, 'dp', split_axis=0, concat_axis=0, tiled=True)  17.5 us
    all_to_all x1, waiting for transfers between devices, dp_allreduce_a2a(): got = lax.all_to_all(flat, 'dp', split_axis=0, concat_axis=0, tiled=True)  17 us
    reduce_sum x4, other arithmetic, finish(): kernel[offset] * padded[offset:offset + length] * matching[:, None]  14.9 us
    all_to_all x1, starting transfers between devices, body(): lax.all_to_all(outgoing, 'dp', split_axis=0, concat_axis=0, tiled=True)  13.2 us
    all_to_all x1, starting transfers between devices, body(): lax.all_to_all(returning, 'dp', split_axis=0, concat_axis=0, tiled=True)  10.3 us
  transfers between devices with their start and end apart: 6, of which 5 were waited for; matrix products, arithmetic and copies ran while one was open for 9% of the time, Pallas kernels for 0%

profile of v1, /device:TPU:24, one launch (start us, length us, event | category | flops | bytes accessed | tf_op | source)
XLA Modules:
  0.0 341.6 jit_solution(10079741374050329405)
XLA Ops:
  7.2 0.7 all-gather.4.cloned.1.call-update
  7.9 1.2 compare_select_fusion.1
  9.1 1.0 gather_fusion
  10.2 0.2 select_select_fusion.1
  10.3 1.0 all_to_all.22
  11.3 13.2 %all-to-all-start = ((bf16[32,4,2304]{2,1,0:T(4,128)(2,1)}), bf16[32,4,2304]{2,1,0:T(4,128)(2,1)S(1)}, u32[]{:S(2)}, u32[]{:S(2)}) async-start(bf16[32,4,2304]{2,1,0:T(4,128)(2,1)} %all_to_all.22), calls=%async_computation | async-start | bytes 1179648 | tf_op jit(solution)/shard_map/all_to_all | solution.py:84
  24.5 0.2 slice_reduce_fusion.29
  24.7 0.5 compare_select_fusion
  25.3 0.3 slice_reduce_fusion.30
  26.0 17.5 %all-to-all-done = bf16[32,4,2304]{2,1,0:T(4,128)(2,1)S(1)} async-done(((bf16[32,4,2304]{2,1,0:T(4,128)(2,1)}), bf16[32,4,2304]{2,1,0:T(4,128)(2,1)S(1)}, u32[]{:S(2)}, u32[]{:S(2)}) %all-to-all-start) | async-done | bytes 589856 | tf_op jit(solution)/shard_map/all_to_all | solution.py:84
  43.6 1.0 gather_fusion.1
  44.6 0.2 select_select_fusion
  44.8 0.2 copy.36
  44.9 0.2 copy.35
  45.1 0.2 copy.34
  45.3 1.2 fusion.40
  46.4 0.5 convolution_convert_fusion.6
  47.0 9.4 %all-gather.4.cloned.1.call-done = bf16[768,1536]{1,0:T(8,128)(2,1)} async-done(((bf16[48,1536]{1,0:T(8,128)(2,1)}), bf16[768,1536]{1,0:T(8,128)(2,1)}) %all-gather.4.cloned.1.call-update) | async-done | bytes 2359312 | tf_op jit(solution)/shard_map/all_gather | solution.py:92
  56.4 2.2 fusion.2
  58.6 7.6 %multiply_reduce_fusion.31 = (f32[1536]{0:T(1024)}, f32[1536]{0:T(1024)}, f32[1536]{0:T(1024)}, f32[1536]{0:T(1024)}, f32[1536]{0:T(1024)}, /*index=5*/f32[1536]...) fusion(f32[128,1536]{1,0:T(8,128)S(1)} %fusion.2, ...), kind=kLoop, calls=%fused_computation.99 | loop fusion | flops 25152000 | bytes 3013632 | tf_op jit(solution)/shard_map/transpose(jvp())/reduce_sum | solution.py:74
  66.2 2.3 multiply_reduce_fusion.16
  68.4 0.5 multiply_multiply_fusion.27
  69.0 0.7 multiply_multiply_fusion.29
  69.8 0.7 multiply_multiply_fusion.28
  70.5 2.6 multiply_reduce_fusion.4
  73.1 2.8 pad_add_fusion
  75.9 0.7 fusion.16
  76.7 2.1 convolution_convert_fusion
  78.8 0.6 reshape.271
  79.4 0.6 reshape.272
  80.0 0.6 reshape.273
  80.6 0.6 reshape.274
  81.2 0.6 reshape.275
  81.8 0.6 reshape.276
  82.4 0.6 reshape.277
  83.0 0.6 reshape.278
  83.6 0.6 reshape.279
  84.2 2.5 convolution_convert_fusion.5
  86.8 0.2 copy.38
  87.0 1.3 convolution_convert_fusion.2
  88.3 0.1 copy.44
  88.4 0.3 fusion.41
  88.7 1.7 convolution_convert_fusion.3
  90.4 0.1 copy.43
  90.6 2.3 convolution_convert_fusion.4
  92.8 1.1 copy.42
  93.9 1.8 scatter_custom_fusion
  95.8 1.0 all_to_all.25
  96.8 10.3 %all-to-all-start.1 = ((bf16[32,4,2304]{2,1,0:T(4,128)(2,1)}), bf16[32,4,2304]{2,1,0:T(4,128)(2,1)S(1)}, u32[]{:S(2)}, u32[]{:S(2)}) async-start(bf16[32,4,2304]{2,1,0:T(4,128)(2,1)} %all_to_all.25), calls=%async_computation.1 | async-start | bytes 1179648 | tf_op jit(solution)/shard_map/all_to_all | solution.py:119
  107.2 2.4 multiply_reduce_fusion.22
  110.1 1.0 pad_add_fusion.7
  111.2 26.3 %reduce-scatter.2.cloned.1.call-done = bf16[48,1536]{1,0:T(8,128)(2,1)} async-done(((bf16[768,1536]{1,0:T(8,128)(2,1)}), bf16[48,1536]{1,0:T(8,128)(2,1)}) %reduce-scatter.2.cloned.1.call-update) | async-done | bytes 147472 | tf_op jit(solution)/shard_map/reduce_scatter | solution.py:101
  137.5 0.9 convert_element_type.212
  138.4 112.9 %all-reduce.66.cloned.1.call-done = f32[31,1536]{1,0:T(8,128)} async-done(((f32[31,1536]{1,0:T(8,128)}), f32[31,1536]{1,0:T(8,128)}) %all-reduce.66.cloned.1.call-update) | async-done | bytes 190480 | tf_op jit(solution)/shard_map/psum | solution.py:123
  251.3 1.0 maximum_maximum_fusion
  252.3 1.5 all_to_all.30
  253.8 10.2 %all-to-all-start.2 = ((f32[32,1,4608]{2,1,0:T(1,128)}), f32[32,1,4608]{2,1,0:T(1,128)S(1)}, u32[]{:S(2)}, u32[]{:S(2)}) async-start(f32[32,1,4608]{2,1,0:T(1,128)} %all_to_all.30), calls=%async_computation.3 | async-start | bytes 1179648 | tf_op jit(solution)/shard_map/all_to_all | solution.py:144
  264.2 2.4 scatter_custom_fusion.1
  266.6 17.0 %all-to-all-done.2 = f32[32,1,4608]{2,1,0:T(1,128)S(1)} async-done(((f32[32,1,4608]{2,1,0:T(1,128)}), f32[32,1,4608]{2,1,0:T(1,128)S(1)}, u32[]{:S(2)}, u32[]{:S(2)}) %all-to-all-start.2) | async-done | bytes 589856 | tf_op jit(solution)/shard_map/all_to_all | solution.py:144
  283.6 0.3 reduce_sum.356
  283.9 48.8 %all-gather.1 = f32[32,1,4608]{2,1,0:T(1,128)S(1)} all-gather(f32[1,1,4608]{2,1,0:T(1,128)S(1)} %reshape.348), channel_id=2, replica_groups=mesh['dp'=32,'fsdp'=16] {'dp'}, dimensions={0}, use_global_device_ids=true | all-gather | bytes 608256 | tf_op jit(solution)/shard_map/all_gather | solution.py:146
  332.7 0.8 fusion.23
  333.6 0.7 reshape.346
  334.3 0.8 mul.1323
  (144 shorter events, 1.2 us)
Async XLA Ops:
  7.2 2.0 copy-start
  7.2 49.2 %all-gather.4.cloned.1.call-start = ((), (), s32[]{:S(2)}) async-start(), calls=%async_computation.4 | async-start | bytes 2506752 | tf_op jit(solution)/shard_map/all_gather | solution.py:92
  9.1 1.0 copy-start.47
  10.1 14.4 %copy-start.6 = (f32[31,1536]{1,0:T(8,128)S(1)}, f32[31,1536]{1,0:T(8,128)}, u32[]{:S(2)}) copy-start(f32[31,1536]{1,0:T(8,128)} %param.11) | copy-start | bytes 571396
  10.1 14.6 %copy-start.48 = (s32[128]{0:T(128)S(1)}, s32[128]{0:T(128)}, u32[]{:S(2)}) copy-start(s32[128]{0:T(128)} %param.14) | copy-start | bytes 1540
  10.1 15.5 %copy-start.46 = (s32[128]{0:T(128)S(1)}, s32[128]{0:T(128)}, u32[]{:S(2)}) copy-start(s32[128]{0:T(128)} %param.15) | copy-start | bytes 1540
  11.3 32.2 %all-to-all-start = ((bf16[32,4,2304]{2,1,0:T(4,128)(2,1)}), bf16[32,4,2304]{2,1,0:T(4,128)(2,1)S(1)}, u32[]{:S(2)}, u32[]{:S(2)}) async-start(bf16[32,4,2304]{2,1,0:T(4,128)(2,1)} %all_to_all.22), calls=%async_computation | async-start | bytes 1179648 | tf_op jit(solution)/shard_map/all_to_all | solution.py:84
  24.4 113.0 %reduce-scatter.2.cloned.1.call-start = ((), (), s32[]{:S(2)}) async-start(), calls=%async_computation.5 | async-start | bytes 2506752 | tf_op jit(solution)/shard_map/reduce_scatter | solution.py:101
  25.8 43.2 %copy-start.43 = (f32[128]{0:T(128)}, f32[128]{0:T(128)S(1)}, u32[]{:S(2)}) copy-start(f32[128]{0:T(128)S(1)} %get-tuple-element.120) | copy-start | bytes 1540
  25.8 43.2 %copy-start.44 = (f32[128]{0:T(128)}, f32[128]{0:T(128)S(1)}, u32[]{:S(2)}) copy-start(f32[128]{0:T(128)S(1)} %get-tuple-element.121) | copy-start | bytes 1540
  25.8 43.2 %copy-start.45 = (f32[128]{0:T(128)}, f32[128]{0:T(128)S(1)}, u32[]{:S(2)}) copy-start(f32[128]{0:T(128)S(1)} %get-tuple-element.122) | copy-start | bytes 1540
  25.8 43.9 %copy-start.37 = (f32[128]{0:T(128)}, f32[128]{0:T(128)S(1)}, u32[]{:S(2)}) copy-start(f32[128]{0:T(128)S(1)} %get-tuple-element.114) | copy-start | bytes 1540
  25.8 43.9 %copy-start.38 = (f32[128]{0:T(128)}, f32[128]{0:T(128)S(1)}, u32[]{:S(2)}) copy-start(f32[128]{0:T(128)S(1)} %get-tuple-element.115) | copy-start | bytes 1540
  25.8 43.9 %copy-start.39 = (f32[128]{0:T(128)}, f32[128]{0:T(128)S(1)}, u32[]{:S(2)}) copy-start(f32[128]{0:T(128)S(1)} %get-tuple-element.116) | copy-start | bytes 1540
  25.9 43.9 %copy-start.40 = (f32[128]{0:T(128)}, f32[128]{0:T(128)S(1)}, u32[]{:S(2)}) copy-start(f32[128]{0:T(128)S(1)} %get-tuple-element.117) | copy-start | bytes 1540
  25.9 43.9 %copy-start.41 = (f32[128]{0:T(128)}, f32[128]{0:T(128)S(1)}, u32[]{:S(2)}) copy-start(f32[128]{0:T(128)S(1)} %get-tuple-element.118) | copy-start | bytes 1540
  25.9 43.9 %copy-start.42 = (f32[128]{0:T(128)}, f32[128]{0:T(128)S(1)}, u32[]{:S(2)}) copy-start(f32[128]{0:T(128)S(1)} %get-tuple-element.119) | copy-start | bytes 1540
  26.0 20.5 %copy-start.36 = (pred[128,128]{0,1:T(8,128)(4,1)}, pred[128,128]{0,1:T(8,128)(4,1)S(1)}, u32[]{:S(2)}) copy-start(pred[128,128]{0,1:T(8,128)(4,1)S(1)} %broadcast_compare_fusion) | copy-start | bytes 49156
  44.9 42.0 %copy-start.2 = (bf16[128,768]{0,1:T(8,128)(2,1)}, bf16[128,768]{0,1:T(8,128)(2,1)S(1)}, u32[]{:S(2)}) copy-start(bf16[128,768]{0,1:T(8,128)(2,1)S(1)} %copy.36) | copy-start | bytes 589828
  45.1 11.3 %copy-start.4 = (bf16[128,768]{0,1:T(8,128)(2,1)}, bf16[128,768]{0,1:T(8,128)(2,1)S(1)}, u32[]{:S(2)}) copy-start(bf16[128,768]{0,1:T(8,128)(2,1)S(1)} %copy.35) | copy-start | bytes 589828
  46.4 9.9 %copy-start.49 = (f32[8,128]{1,0:T(8,128)}, f32[8,128]{1,0:T(8,128)S(1)}, u32[]{:S(2)}) copy-start(f32[8,128]{1,0:T(8,128)S(1)} %get-tuple-element.142) | copy-start | bytes 12292
  47.0 11.6 %copy-start.1 = (bf16[128,1536]{1,0:T(8,128)(2,1)S(1)}, bf16[128,1536]{1,0:T(8,128)(2,1)}, u32[]{:S(2)}) copy-start(bf16[128,1536]{1,0:T(8,128)(2,1)} %param.12) | copy-start | bytes 1179652
  76.6 2.3 copy-start.26
  76.6 2.9 copy-start.25
  76.6 3.4 %copy-start.24 = (f32[1536]{0:T(1024)S(1)}, f32[1536]{0:T(1024)}, u32[]{:S(2)}) copy-start(f32[1536]{0:T(1024)} %get-tuple-element.7) | copy-start | bytes 18436
  76.6 4.0 %copy-start.23 = (f32[1536]{0:T(1024)S(1)}, f32[1536]{0:T(1024)}, u32[]{:S(2)}) copy-start(f32[1536]{0:T(1024)} %get-tuple-element.8) | copy-start | bytes 18436
  76.6 4.6 %copy-start.22 = (f32[1536]{0:T(1024)S(1)}, f32[1536]{0:T(1024)}, u32[]{:S(2)}) copy-start(f32[1536]{0:T(1024)} %get-tuple-element.9) | copy-start | bytes 18436
  76.6 5.2 %copy-start.21 = (f32[1536]{0:T(1024)S(1)}, f32[1536]{0:T(1024)}, u32[]{:S(2)}) copy-start(f32[1536]{0:T(1024)} %get-tuple-element.10) | copy-start | bytes 18436
  76.6 5.8 %copy-start.20 = (f32[1536]{0:T(1024)S(1)}, f32[1536]{0:T(1024)}, u32[]{:S(2)}) copy-start(f32[1536]{0:T(1024)} %get-tuple-element.11) | copy-start | bytes 18436
  76.6 6.4 %copy-start.19 = (f32[1536]{0:T(1024)S(1)}, f32[1536]{0:T(1024)}, u32[]{:S(2)}) copy-start(f32[1536]{0:T(1024)} %get-tuple-element.12) | copy-start | bytes 18436
  76.6 7.0 %copy-start.18 = (f32[1536]{0:T(1024)S(1)}, f32[1536]{0:T(1024)}, u32[]{:S(2)}) copy-start(f32[1536]{0:T(1024)} %get-tuple-element.13) | copy-start | bytes 18436
  78.8 8.2 %copy-start.5 = (bf16[128,768]{0,1:T(8,128)(2,1)S(1)}, bf16[128,768]{0,1:T(8,128)(2,1)}, u32[]{:S(2)}) copy-start(bf16[128,768]{0,1:T(8,128)(2,1)} %copy-done.4) | copy-start | bytes 589828
  88.3 2.3 copy-start.3
  88.3 2.3 copy-start.50
  95.7 14.0 %copy-start.13 = (f32[1536]{0:T(1024)S(1)}, f32[1536]{0:T(1024)}, u32[]{:S(2)}) copy-start(f32[1536]{0:T(1024)} %get-tuple-element.23) | copy-start | bytes 18436
  95.7 14.0 %copy-start.12 = (f32[1536]{0:T(1024)S(1)}, f32[1536]{0:T(1024)}, u32[]{:S(2)}) copy-start(f32[1536]{0:T(1024)} %get-tuple-element.24) | copy-start | bytes 18436
  95.7 14.0 %copy-start.11 = (f32[1536]{0:T(1024)S(1)}, f32[1536]{0:T(1024)}, u32[]{:S(2)}) copy-start(f32[1536]{0:T(1024)} %get-tuple-element.25) | copy-start | bytes 18436
  95.7 14.1 %copy-start.10 = (f32[1536]{0:T(1024)S(1)}, f32[1536]{0:T(1024)}, u32[]{:S(2)}) copy-start(f32[1536]{0:T(1024)} %get-tuple-element.26) | copy-start | bytes 18436
  95.7 14.1 %copy-start.9 = (f32[1536]{0:T(1024)S(1)}, f32[1536]{0:T(1024)}, u32[]{:S(2)}) copy-start(f32[1536]{0:T(1024)} %get-tuple-element.27) | copy-start | bytes 18436
  95.7 14.1 %copy-start.8 = (f32[1536]{0:T(1024)S(1)}, f32[1536]{0:T(1024)}, u32[]{:S(2)}) copy-start(f32[1536]{0:T(1024)} %get-tuple-element.28) | copy-start | bytes 18436
  95.7 14.1 %copy-start.7 = (f32[1536]{0:T(1024)S(1)}, f32[1536]{0:T(1024)}, u32[]{:S(2)}) copy-start(f32[1536]{0:T(1024)} %get-tuple-element.29) | copy-start | bytes 18436
  95.7 14.1 %copy-start.17 = (f32[1536]{0:T(1024)S(1)}, f32[1536]{0:T(1024)}, u32[]{:S(2)}) copy-start(f32[1536]{0:T(1024)} %get-tuple-element.32) | copy-start | bytes 18436
  95.7 14.2 %copy-start.16 = (f32[1536]{0:T(1024)S(1)}, f32[1536]{0:T(1024)}, u32[]{:S(2)}) copy-start(f32[1536]{0:T(1024)} %get-tuple-element.33) | copy-start | bytes 18436
  95.8 14.2 %copy-start.15 = (f32[1536]{0:T(1024)S(1)}, f32[1536]{0:T(1024)}, u32[]{:S(2)}) copy-start(f32[1536]{0:T(1024)} %get-tuple-element.34) | copy-start | bytes 18436
  95.8 14.2 %copy-start.14 = (f32[1536]{0:T(1024)S(1)}, f32[1536]{0:T(1024)}, u32[]{:S(2)}) copy-start(f32[1536]{0:T(1024)} %get-tuple-element.35) | copy-start | bytes 18436
  95.8 14.2 %copy-start.27 = (f32[1,1536]{1,0:T(1,128)S(1)}, f32[1,1536]{1,0:T(1,128)}, u32[]{:S(2)}) copy-start(f32[1,1536]{1,0:T(1,128)} %reshape.271) | copy-start | bytes 18436
  95.8 14.2 %copy-start.28 = (f32[1,1536]{1,0:T(1,128)S(1)}, f32[1,1536]{1,0:T(1,128)}, u32[]{:S(2)}) copy-start(f32[1,1536]{1,0:T(1,128)} %reshape.272) | copy-start | bytes 18436
  95.8 14.2 %copy-start.29 = (f32[1,1536]{1,0:T(1,128)S(1)}, f32[1,1536]{1,0:T(1,128)}, u32[]{:S(2)}) copy-start(f32[1,1536]{1,0:T(1,128)} %reshape.273) | copy-start | bytes 18436
  95.8 14.2 %copy-start.30 = (f32[1,1536]{1,0:T(1,128)S(1)}, f32[1,1536]{1,0:T(1,128)}, u32[]{:S(2)}) copy-start(f32[1,1536]{1,0:T(1,128)} %reshape.274) | copy-start | bytes 18436
  96.8 13.2 %copy-start.31 = (f32[1,1536]{1,0:T(1,128)S(1)}, f32[1,1536]{1,0:T(1,128)}, u32[]{:S(2)}) copy-start(f32[1,1536]{1,0:T(1,128)} %reshape.275) | copy-start | bytes 18436
  96.8 13.2 %copy-start.32 = (f32[1,1536]{1,0:T(1,128)S(1)}, f32[1,1536]{1,0:T(1,128)}, u32[]{:S(2)}) copy-start(f32[1,1536]{1,0:T(1,128)} %reshape.276) | copy-start | bytes 18436
  96.8 13.3 %copy-start.33 = (f32[1,1536]{1,0:T(1,128)S(1)}, f32[1,1536]{1,0:T(1,128)}, u32[]{:S(2)}) copy-start(f32[1,1536]{1,0:T(1,128)} %reshape.277) | copy-start | bytes 18436
  96.8 13.3 %copy-start.34 = (f32[1,1536]{1,0:T(1,128)S(1)}, f32[1,1536]{1,0:T(1,128)}, u32[]{:S(2)}) copy-start(f32[1,1536]{1,0:T(1,128)} %reshape.278) | copy-start | bytes 18436
  96.8 13.3 %copy-start.35 = (f32[1,1536]{1,0:T(1,128)S(1)}, f32[1,1536]{1,0:T(1,128)}, u32[]{:S(2)}) copy-start(f32[1,1536]{1,0:T(1,128)} %reshape.279) | copy-start | bytes 18436
  96.8 157.1 %all-to-all-start.1 = ((bf16[32,4,2304]{2,1,0:T(4,128)(2,1)}), bf16[32,4,2304]{2,1,0:T(4,128)(2,1)S(1)}, u32[]{:S(2)}, u32[]{:S(2)}) async-start(bf16[32,4,2304]{2,1,0:T(4,128)(2,1)} %all_to_all.25), calls=%async_computation.1 | async-start | bytes 1179648 | tf_op jit(solution)/shard_map/all_to_all | solution.py:119
  107.1 144.2 %all-reduce.66.cloned.1.call-start = ((), (), s32[]{:S(2)}) async-start(), calls=%async_computation.6 | async-start | bytes 393216 | tf_op jit(solution)/shard_map/psum | solution.py:123
  253.8 29.7 %all-to-all-start.2 = ((f32[32,1,4608]{2,1,0:T(1,128)}), f32[32,1,4608]{2,1,0:T(1,128)S(1)}, u32[]{:S(2)}, u32[]{:S(2)}) async-start(f32[32,1,4608]{2,1,0:T(1,128)} %all_to_all.30), calls=%async_computation.3 | async-start | bytes 1179648 | tf_op jit(solution)/shard_map/all_to_all | solution.py:144
Sparse Core Ops, SparseCore 0:
  10.1 46.2 all-gather.3
  78.9 58.4 reduce-scatter.1
  140.4 110.8 all-reduce.65

commit v2 on v0

--- a/solution.py
+++ b/solution.py
@@ -120,8 +120,11 @@
     source_index = jnp.where(present, send_rows, row_count)
     projected_grad = jnp.zeros_like(projected).at[source_index].set(arrived, mode="drop")
     scale_factor = (row_count * lax.axis_size("dp") * lax.axis_size("fsdp")) ** (-0.5)
-    weight_total = lax.psum(weight_share, "dp")
-    kernel_total = lax.psum(kernel_part, ("dp", "fsdp"))
+    kernel_piece = fsdp_sum_rows(kernel_part)
+    owned_rows = weight_share.shape[0]
+    both = dp_allreduce_a2a(jnp.concatenate([weight_share, kernel_piece], axis=0))
+    weight_total = both[:owned_rows]
+    kernel_total = lax.all_gather(both[owned_rows:], "fsdp", axis=0, tiled=True)[: kernel.shape[0]]
     return (
         result.astype(jnp.bfloat16),
         projected_grad,
@@ -129,6 +132,23 @@
         kernel_total * scale_factor,
     )
 
+
+def fsdp_sum_rows(x):
+    n = lax.axis_size("fsdp")
+    per = -(-x.shape[0] // n)
+    padded = jnp.pad(x, ((0, n * per - x.shape[0]), (0, 0)))
+    got = lax.all_to_all(padded.reshape(n, per, x.shape[1]), "fsdp", split_axis=0, concat_axis=0, tiled=True)
+    return jnp.sum(got, axis=0)
+
+
+def dp_allreduce_a2a(x):
+    n = lax.axis_size("dp")
+    per = -(-x.shape[0] // n)
+    padded = jnp.pad(x, ((0, n * per - x.shape[0]), (0, 0))).reshape(n, per, x.shape[1])
+    got = lax.all_to_all(padded, "dp", split_axis=0, concat_axis=0, tiled=True)
+    part = jnp.sum(got, axis=0, keepdims=True)
+    whole = lax.all_gather(part, "dp", axis=0, tiled=True)
+    return whole.reshape(n * per, x.shape[1])[: x.shape[0]]
 
 def solution(mesh):
     placed = (

time: 567 us -> 244 us (0.43)
  the two profiles are of different devices: /device:TPU:8 before, /device:TPU:1 now
where the time goes in v2:
time: 244 us; the launch traced here: 243 us
  blocking collectives  70.5 us (29%)
  waiting for transfers between devices  67.4 us (28%)
  starting transfers between devices  38.1 us (16%)
  other arithmetic  25.8 us (11%)
  between operations  15.7 us (6%)
  matrix products  13.3 us (5%)
  local copies, waits for them, and re-layouts  12.5 us (5%)
    all_gather x1, blocking collectives, dp_allreduce_a2a(): whole = lax.all_gather(part, 'dp', axis=0, tiled=True)  35.8 us
    all_gather x1, blocking collectives, body(): lax.all_gather(both[owned_rows:], 'fsdp', axis=0, tiled=True)  34.8 us
    reduce_scatter x1, waiting for transfers between devices, body(): lax.psum_scatter(jnp.einsum('rc,rd->cd', columns, mixed_grad, preferred_e...  30.3 us
    all_to_all x1, waiting for transfers between devices, body(): lax.all_to_all(outgoing, 'dp', split_axis=0, concat_axis=0, tiled=True)  14.8 us
    reduce_sum x4, other arithmetic, finish(): kernel[offset] * padded[offset:offset + length] * matching[:, None]  14.8 us
    all_to_all x1, starting transfers between devices, body(): lax.all_to_all(outgoing, 'dp', split_axis=0, concat_axis=0, tiled=True)  13.7 us
    all_gather x1, waiting for transfers between devices, body(): lax.all_gather(out_weight, 'fsdp', axis=0, tiled=True)  12.5 us
    all_to_all x1, starting transfers between devices, body(): lax.all_to_all(returning, 'dp', split_axis=0, concat_axis=0, tiled=True)  10.2 us
  transfers between devices with their start and end apart: 6, of which 4 were waited for; matrix products, arithmetic and copies ran while one was open for 10% of the time, Pallas kernels for 0%

profile of v2, /device:TPU:1, one launch (start us, length us, event | category | flops | bytes accessed | tf_op | source)
XLA Modules:
  0.0 243.4 jit_solution(6522760111335242949)
XLA Ops:
  7.2 0.0 all-gather.7.cloned.1.call-start
  7.2 0.7 all-gather.7.cloned.1.call-update
  7.9 0.7 compare_select_fusion.1
  8.6 1.0 gather_fusion
  9.6 0.2 select_select_fusion.1
  9.8 1.0 all_to_all.22
  10.7 13.7 %all-to-all-start = ((bf16[32,4,2304]{2,1,0:T(4,128)(2,1)}), bf16[32,4,2304]{2,1,0:T(4,128)(2,1)S(1)}, u32[]{:S(2)}, u32[]{:S(2)}) async-start(bf16[32,4,2304]{2,1,0:T(4,128)(2,1)} %all_to_all.22), calls=%async_computation | async-start | bytes 1179648 | tf_op jit(solution)/shard_map/all_to_all | solution.py:84
  24.5 0.0 reduce-scatter.2.cloned.1.call-start
  24.5 0.8 slice_reduce_fusion.29
  25.3 0.9 slice_reduce_fusion.30
  26.2 0.1 compare_convert_fusion.28
  26.3 0.7 compare_convert_fusion.29
  27.0 0.1 broadcast_compare_fusion
  27.1 14.8 %all-to-all-done = bf16[32,4,2304]{2,1,0:T(4,128)(2,1)S(1)} async-done(((bf16[32,4,2304]{2,1,0:T(4,128)(2,1)}), bf16[32,4,2304]{2,1,0:T(4,128)(2,1)S(1)}, u32[]{:S(2)}, u32[]{:S(2)}) %all-to-all-start) | async-done | bytes 589856 | tf_op jit(solution)/shard_map/all_to_all | solution.py:84
  42.0 0.1 all_to_all.24
  42.1 1.0 gather_fusion.1
  43.1 0.2 select_select_fusion
  43.3 0.2 copy.58
  43.4 0.2 copy.57
  43.6 0.2 copy.56
  43.8 1.2 fusion.40
  45.0 0.5 convolution_convert_fusion.6
  45.7 12.5 %all-gather.7.cloned.1.call-done = bf16[768,1536]{1,0:T(8,128)(2,1)} async-done(((bf16[48,1536]{1,0:T(8,128)(2,1)}), bf16[768,1536]{1,0:T(8,128)(2,1)}) %all-gather.7.cloned.1.call-update) | async-done | bytes 2359312 | tf_op jit(solution)/shard_map/all_gather | solution.py:92
  58.4 2.2 fusion.2
  60.9 7.8 %multiply_reduce_fusion.31 = (f32[1536]{0:T(1024)}, f32[1536]{0:T(1024)}, f32[1536]{0:T(1024)}, f32[1536]{0:T(1024)}, f32[1536]{0:T(1024)}, /*index=5*/f32[1536]...) fusion(f32[128,1536]{1,0:T(8,128)S(1)} %fusion.2, ...), kind=kLoop, calls=%fused_computation.99 | loop fusion | flops 25152000 | bytes 3013632 | tf_op jit(solution)/shard_map/transpose(jvp())/reduce_sum | solution.py:74
  68.7 2.4 multiply_reduce_fusion.16
  71.1 0.5 multiply_multiply_fusion.27
  71.6 0.7 multiply_multiply_fusion.29
  72.3 0.7 multiply_multiply_fusion.28
  73.0 2.6 %multiply_reduce_fusion.4 = (f32[1536]{0:T(1024)}, f32[1536]{0:T(1024)}, f32[1536]{0:T(1024)}, f32[1536]{0:T(1024)S(1)}, f32[128,1536]{1,0:T(8,128)S(1)}, /*inde...) fusion(f32[128,1536]{1,0:T(8,128)S(1)} %get-tuple-element.67, ...), kind=kLoop, calls=%fused_computation.72 | loop fusion | flops 5105664 | bytes 7535616 | tf_op jit(solution)/shard_map/transpose(jvp())/reduce_sum | solution.py:74
  75.7 2.6 %pad_add_fusion = f32[158,1536]{1,0:T(8,128)S(1)} fusion(f32[128,1536]{1,0:T(8,128)S(1)} %get-tuple-element.76, f32[128,1536]{1,0:T(8,128)S(1)} %get-tuple-element.78, f32[128,1536]{1,0:T(8,128)S(1)} %get-tuple-element.79, f32[128,1536]{1,0:T(8,128)S(1)} %get-tuple-element.80, f32[128,1536]{1,0:T(8,128)S(1)} %get-tuple-element.81, ...), kind=kLoop, calls=%fused_computation.59 | loop fusion | flops 5824512 | bytes 20631552 | tf_op jit(solution)/shard_map/transpose(jvp())/add_any | solution.py:74
  78.3 0.7 fusion.16
  79.1 2.1 convolution_convert_fusion
  81.7 2.0 multiply_reduce_fusion.22
  84.2 0.3 pad_add_fusion.7
  84.5 0.8 reshape.304
  85.3 4.6 %all-to-all-start.2 = ((f32[16,2,1536]{2,1,0:T(2,128)}), f32[16,2,1536]{2,1,0:T(2,128)S(1)}, u32[]{:S(2)}, u32[]{:S(2)}) async-start(f32[16,2,1536]{2,1,0:T(2,128)} %reshape.304), calls=%async_computation.3 | async-start | bytes 393216 | tf_op jit(solution)/shard_map/all_to_all | solution.py:140
  89.9 2.5 %convolution_convert_fusion.5 = bf16[128,768]{1,0:T(8,128)(2,1)S(1)} fusion(bf16[128,1536]{1,0:T(8,128)(2,1)S(1)} %fusion.16, bf16[768,1536]{1,0:T(8,128)(2,1)} %all-gather.7.cloned.1.call-done), kind=kOutput, calls=%fused_computation.54 | convolution fusion | flops 302088192 | bytes 2949120 | tf_op jit(solution)/shard_map/rd,cd->rc/dot_general | solution.py:109
  92.4 0.2 copy.60
  92.6 1.3 convolution_convert_fusion.2
  93.9 0.1 copy.66
  94.0 0.3 fusion.41
  94.3 1.6 convolution_convert_fusion.3
  95.9 0.1 copy.65
  96.1 1.6 convolution_convert_fusion.4
  97.7 0.1 copy.64
  97.8 1.6 scatter_custom_fusion
  99.5 1.0 all_to_all.25
  100.4 10.2 %all-to-all-start.1 = ((bf16[32,4,2304]{2,1,0:T(4,128)(2,1)}), bf16[32,4,2304]{2,1,0:T(4,128)(2,1)S(1)}, u32[]{:S(2)}, u32[]{:S(2)}) async-start(bf16[32,4,2304]{2,1,0:T(4,128)(2,1)} %all_to_all.25), calls=%async_computation.1 | async-start | bytes 1179648 | tf_op jit(solution)/shard_map/all_to_all | solution.py:119
  110.7 0.1 reduce_sum.364
  110.8 30.3 %reduce-scatter.2.cloned.1.call-done = bf16[48,1536]{1,0:T(8,128)(2,1)} async-done(((bf16[768,1536]{1,0:T(8,128)(2,1)}), bf16[48,1536]{1,0:T(8,128)(2,1)}) %reduce-scatter.2.cloned.1.call-update) | async-done | bytes 147472 | tf_op jit(solution)/shard_map/reduce_scatter | solution.py:101
  141.1 0.9 convert_element_type.216
  142.0 1.0 reshape.305
  143.0 9.5 %all-to-all-start.3 = ((f32[32,2,1536]{2,1,0:T(2,128)}), f32[32,2,1536]{2,1,0:T(2,128)S(1)}, u32[]{:S(2)}, u32[]{:S(2)}) async-start(f32[32,2,1536]{2,1,0:T(2,128)} %reshape.305), calls=%async_computation.4 | async-start | bytes 786432 | tf_op jit(solution)/shard_map/all_to_all | solution.py:148
  152.5 0.1 reshape.334
  152.7 2.3 scatter_custom_fusion.1
  154.9 9.1 %all-to-all-done.3 = f32[32,2,1536]{2,1,0:T(2,128)S(1)} async-done(((f32[32,2,1536]{2,1,0:T(2,128)}), f32[32,2,1536]{2,1,0:T(2,128)S(1)}, u32[]{:S(2)}, u32[]{:S(2)}) %all-to-all-start.3) | async-done | bytes 393248 | tf_op jit(solution)/shard_map/all_to_all | solution.py:148
  164.0 0.1 reduce_sum.365
  164.1 35.8 %all-gather.3 = f32[32,2,1536]{2,1,0:T(2,128)S(1)} all-gather(f32[1,2,1536]{2,1,0:T(2,128)S(1)} %bitcast.56), channel_id=2, replica_groups=mesh['dp'=32,'fsdp'=16] {'dp'}, dimensions={0}, use_global_device_ids=true | all-gather | bytes 405504 | tf_op jit(solution)/shard_map/all_gather | solution.py:150
  199.9 0.1 slice_multiply_fusion
  200.0 0.9 reshape.362
  201.0 34.8 %all-gather.4 = f32[16,2,1536]{2,1,0:T(2,128)S(1)} all-gather(f32[1,2,1536]{2,1,0:T(2,128)S(1)} %slice.416), channel_id=4, replica_groups=mesh['dp'=32,'fsdp'=16] {'fsdp'}, dimensions={0}, use_global_device_ids=true | all-gather | bytes 208896 | tf_op jit(solution)/shard_map/all_gather | solution.py:127
  235.7 0.1 reshape.347
  235.9 0.7 fusion.28
  (203 shorter events, 0.7 us)
Async XLA Ops:
  7.2 51.1 %all-gather.7.cloned.1.call-start = ((), (), s32[]{:S(2)}) async-start(), calls=%async_computation.5 | async-start | bytes 2506752 | tf_op jit(solution)/shard_map/all_gather | solution.py:92
  9.6 14.9 %copy-start.4 = (f32[31,1536]{1,0:T(8,128)S(1)}, f32[31,1536]{1,0:T(8,128)}, u32[]{:S(2)}) copy-start(f32[31,1536]{1,0:T(8,128)} %param.11) | copy-start | bytes 571396
  9.6 15.7 %copy-start.77 = (s32[128]{0:T(128)S(1)}, s32[128]{0:T(128)}, u32[]{:S(2)}) copy-start(s32[128]{0:T(128)} %param.14) | copy-start | bytes 1540
  9.6 16.6 %copy-start.75 = (s32[128]{0:T(128)S(1)}, s32[128]{0:T(128)}, u32[]{:S(2)}) copy-start(s32[128]{0:T(128)} %param.15) | copy-start | bytes 1540
  10.7 31.2 %all-to-all-start = ((bf16[32,4,2304]{2,1,0:T(4,128)(2,1)}), bf16[32,4,2304]{2,1,0:T(4,128)(2,1)S(1)}, u32[]{:S(2)}, u32[]{:S(2)}) async-start(bf16[32,4,2304]{2,1,0:T(4,128)(2,1)} %all_to_all.22), calls=%async_computation | async-start | bytes 1179648 | tf_op jit(solution)/shard_map/all_to_all | solution.py:84
  24.5 116.6 %reduce-scatter.2.cloned.1.call-start = ((), (), s32[]{:S(2)}) async-start(), calls=%async_computation.6 | async-start | bytes 2506752 | tf_op jit(solution)/shard_map/reduce_scatter | solution.py:101
  27.1 17.8 %copy-start.55 = (pred[128,128]{0,1:T(8,128)(4,1)}, pred[128,128]{0,1:T(8,128)(4,1)S(1)}, u32[]{:S(2)}) copy-start(pred[128,128]{0,1:T(8,128)(4,1)S(1)} %broadcast_compare_fusion) | copy-start | bytes 49156
  43.6 14.6 %copy-start.2 = (bf16[128,768]{0,1:T(8,128)(2,1)}, bf16[128,768]{0,1:T(8,128)(2,1)S(1)}, u32[]{:S(2)}) copy-start(bf16[128,768]{0,1:T(8,128)(2,1)S(1)} %copy.57) | copy-start | bytes 589828
  45.0 15.6 %copy-start.78 = (f32[8,128]{1,0:T(8,128)}, f32[8,128]{1,0:T(8,128)S(1)}, u32[]{:S(2)}) copy-start(f32[8,128]{1,0:T(8,128)S(1)} %get-tuple-element.142) | copy-start | bytes 12292
  45.5 15.1 %copy-start.1 = (bf16[128,1536]{1,0:T(8,128)(2,1)S(1)}, bf16[128,1536]{1,0:T(8,128)(2,1)}, u32[]{:S(2)}) copy-start(bf16[128,1536]{1,0:T(8,128)(2,1)} %param.12) | copy-start | bytes 1179652
  45.5 15.1 %copy-start.5 = (f32[1536]{0:T(1024)S(1)}, f32[1536]{0:T(1024)}, u32[]{:S(2)}) copy-start(f32[1536]{0:T(1024)} %get-tuple-element.38) | copy-start | bytes 18436
  45.5 15.1 %copy-start.6 = (f32[1536]{0:T(1024)S(1)}, f32[1536]{0:T(1024)}, u32[]{:S(2)}) copy-start(f32[1536]{0:T(1024)} %get-tuple-element.39) | copy-start | bytes 18436
  45.5 15.1 %copy-start.7 = (f32[1536]{0:T(1024)S(1)}, f32[1536]{0:T(1024)}, u32[]{:S(2)}) copy-start(f32[1536]{0:T(1024)} %get-tuple-element.40) | copy-start | bytes 18436
  45.5 15.1 %copy-start.8 = (f32[1536]{0:T(1024)S(1)}, f32[1536]{0:T(1024)}, u32[]{:S(2)}) copy-start(f32[1536]{0:T(1024)} %get-tuple-element.41) | copy-start | bytes 18436
  45.5 15.1 %copy-start.9 = (f32[1536]{0:T(1024)S(1)}, f32[1536]{0:T(1024)}, u32[]{:S(2)}) copy-start(f32[1536]{0:T(1024)} %get-tuple-element.42) | copy-start | bytes 18436
  45.5 15.1 %copy-start.10 = (f32[1536]{0:T(1024)S(1)}, f32[1536]{0:T(1024)}, u32[]{:S(2)}) copy-start(f32[1536]{0:T(1024)} %get-tuple-element.55) | copy-start | bytes 18436
  45.6 15.1 %copy-start.11 = (f32[1536]{0:T(1024)S(1)}, f32[1536]{0:T(1024)}, u32[]{:S(2)}) copy-start(f32[1536]{0:T(1024)} %get-tuple-element.60) | copy-start | bytes 18436
  45.6 15.1 %copy-start.12 = (f32[1536]{0:T(1024)S(1)}, f32[1536]{0:T(1024)}, u32[]{:S(2)}) copy-start(f32[1536]{0:T(1024)} %get-tuple-element.61) | copy-start | bytes 18436
  45.6 15.1 %copy-start.13 = (f32[1536]{0:T(1024)S(1)}, f32[1536]{0:T(1024)}, u32[]{:S(2)}) copy-start(f32[1536]{0:T(1024)} %get-tuple-element.63) | copy-start | bytes 18436
  45.6 15.1 %copy-start.14 = (f32[1536]{0:T(1024)S(1)}, f32[1536]{0:T(1024)}, u32[]{:S(2)}) copy-start(f32[1536]{0:T(1024)} %get-tuple-element.64) | copy-start | bytes 18436
  45.6 15.1 %copy-start.15 = (f32[1536]{0:T(1024)S(1)}, f32[1536]{0:T(1024)}, u32[]{:S(2)}) copy-start(f32[1536]{0:T(1024)} %get-tuple-element.62) | copy-start | bytes 18436
  45.6 15.1 %copy-start.16 = (f32[1536]{0:T(1024)S(1)}, f32[1536]{0:T(1024)}, u32[]{:S(2)}) copy-start(f32[1536]{0:T(1024)} %get-tuple-element.43) | copy-start | bytes 18436
  45.6 15.1 %copy-start.17 = (f32[1536]{0:T(1024)S(1)}, f32[1536]{0:T(1024)}, u32[]{:S(2)}) copy-start(f32[1536]{0:T(1024)} %get-tuple-element.44) | copy-start | bytes 18436
  45.6 15.1 %copy-start.18 = (f32[1536]{0:T(1024)S(1)}, f32[1536]{0:T(1024)}, u32[]{:S(2)}) copy-start(f32[1536]{0:T(1024)} %get-tuple-element.45) | copy-start | bytes 18436
  45.6 15.1 %copy-start.19 = (f32[1536]{0:T(1024)S(1)}, f32[1536]{0:T(1024)}, u32[]{:S(2)}) copy-start(f32[1536]{0:T(1024)} %get-tuple-element.46) | copy-start | bytes 18436
  45.6 15.1 %copy-start.20 = (f32[1536]{0:T(1024)S(1)}, f32[1536]{0:T(1024)}, u32[]{:S(2)}) copy-start(f32[1536]{0:T(1024)} %get-tuple-element.47) | copy-start | bytes 18436
  45.7 15.1 %copy-start.21 = (f32[1536]{0:T(1024)S(1)}, f32[1536]{0:T(1024)}, u32[]{:S(2)}) copy-start(f32[1536]{0:T(1024)} %get-tuple-element.48) | copy-start | bytes 18436
  45.7 15.1 %copy-start.22 = (f32[1536]{0:T(1024)S(1)}, f32[1536]{0:T(1024)}, u32[]{:S(2)}) copy-start(f32[1536]{0:T(1024)} %get-tuple-element.49) | copy-start | bytes 18436
  45.7 15.1 %copy-start.23 = (f32[1536]{0:T(1024)S(1)}, f32[1536]{0:T(1024)}, u32[]{:S(2)}) copy-start(f32[1536]{0:T(1024)} %get-tuple-element.50) | copy-start | bytes 18436
  45.7 15.1 %copy-start.24 = (f32[1536]{0:T(1024)S(1)}, f32[1536]{0:T(1024)}, u32[]{:S(2)}) copy-start(f32[1536]{0:T(1024)} %get-tuple-element.51) | copy-start | bytes 18436
  45.7 15.1 %copy-start.25 = (f32[1536]{0:T(1024)S(1)}, f32[1536]{0:T(1024)}, u32[]{:S(2)}) copy-start(f32[1536]{0:T(1024)} %get-tuple-element.52) | copy-start | bytes 18436
  45.7 15.1 %copy-start.26 = (f32[1536]{0:T(1024)S(1)}, f32[1536]{0:T(1024)}, u32[]{:S(2)}) copy-start(f32[1536]{0:T(1024)} %get-tuple-element.53) | copy-start | bytes 18436
  45.7 15.1 %copy-start.27 = (f32[1536]{0:T(1024)S(1)}, f32[1536]{0:T(1024)}, u32[]{:S(2)}) copy-start(f32[1536]{0:T(1024)} %get-tuple-element.54) | copy-start | bytes 18436
  45.7 15.1 %copy-start.28 = (f32[1536]{0:T(1024)S(1)}, f32[1536]{0:T(1024)}, u32[]{:S(2)}) copy-start(f32[1536]{0:T(1024)} %get-tuple-element.66) | copy-start | bytes 18436
  58.3 2.6 %copy-start.32 = (f32[1536]{0:T(1024)S(1)}, f32[1536]{0:T(1024)}, u32[]{:S(2)}) copy-start(f32[1536]{0:T(1024)} %get-tuple-element.59) | copy-start | bytes 18436
  58.3 2.6 %copy-start.33 = (f32[1536]{0:T(1024)S(1)}, f32[1536]{0:T(1024)}, u32[]{:S(2)}) copy-start(f32[1536]{0:T(1024)} %get-tuple-element.65) | copy-start | bytes 18436
  58.3 2.6 %copy-start.56 = (f32[128]{0:T(128)S(1)}, f32[128]{0:T(128)}, u32[]{:S(2)}) copy-start(f32[128]{0:T(128)} %get-tuple-element.114) | copy-start | bytes 1540
  58.3 2.6 %copy-start.58 = (f32[128]{0:T(128)S(1)}, f32[128]{0:T(128)}, u32[]{:S(2)}) copy-start(f32[128]{0:T(128)} %get-tuple-element.115) | copy-start | bytes 1540
  58.3 2.6 %copy-start.60 = (f32[128]{0:T(128)S(1)}, f32[128]{0:T(128)}, u32[]{:S(2)}) copy-start(f32[128]{0:T(128)} %get-tuple-element.116) | copy-start | bytes 1540
  58.3 2.6 %copy-start.62 = (f32[128]{0:T(128)S(1)}, f32[128]{0:T(128)}, u32[]{:S(2)}) copy-start(f32[128]{0:T(128)} %get-tuple-element.117) | copy-start | bytes 1540
  58.3 2.6 %copy-start.64 = (f32[128]{0:T(128)S(1)}, f32[128]{0:T(128)}, u32[]{:S(2)}) copy-start(f32[128]{0:T(128)} %get-tuple-element.118) | copy-start | bytes 1540
  58.3 2.6 %copy-start.66 = (f32[128]{0:T(128)S(1)}, f32[128]{0:T(128)}, u32[]{:S(2)}) copy-start(f32[128]{0:T(128)} %get-tuple-element.119) | copy-start | bytes 1540
  58.3 2.6 %copy-start.68 = (f32[128]{0:T(128)S(1)}, f32[128]{0:T(128)}, u32[]{:S(2)}) copy-start(f32[128]{0:T(128)} %get-tuple-element.120) | copy-start | bytes 1540
  58.3 2.6 %copy-start.70 = (f32[128]{0:T(128)S(1)}, f32[128]{0:T(128)}, u32[]{:S(2)}) copy-start(f32[128]{0:T(128)} %get-tuple-element.121) | copy-start | bytes 1540
  58.4 2.6 %copy-start.72 = (f32[128]{0:T(128)S(1)}, f32[128]{0:T(128)}, u32[]{:S(2)}) copy-start(f32[128]{0:T(128)} %get-tuple-element.122) | copy-start | bytes 1540
  58.4 2.6 %copy-start.74 = (f32[128]{0:T(128)S(1)}, f32[128]{0:T(128)}, u32[]{:S(2)}) copy-start(f32[128]{0:T(128)} %get-tuple-element.123) | copy-start | bytes 1540
  79.0 2.6 %copy-start.57 = (f32[128]{0:T(128)S(1)}, f32[128]{0:T(128)}, u32[]{:S(2)}) copy-start(f32[128]{0:T(128)} %get-tuple-element.114) | copy-start | bytes 1540
  79.1 2.6 %copy-start.59 = (f32[128]{0:T(128)S(1)}, f32[128]{0:T(128)}, u32[]{:S(2)}) copy-start(f32[128]{0:T(128)} %get-tuple-element.115) | copy-start | bytes 1540
  81.3 2.6 %copy-start.41 = (f32[1536]{0:T(1024)S(1)}, f32[1536]{0:T(1024)}, u32[]{:S(2)}) copy-start(f32[1536]{0:T(1024)} %get-tuple-element.24) | copy-start | bytes 18436
  81.3 2.6 %copy-start.40 = (f32[1536]{0:T(1024)S(1)}, f32[1536]{0:T(1024)}, u32[]{:S(2)}) copy-start(f32[1536]{0:T(1024)} %get-tuple-element.25) | copy-start | bytes 18436
  81.3 2.6 %copy-start.39 = (f32[1536]{0:T(1024)S(1)}, f32[1536]{0:T(1024)}, u32[]{:S(2)}) copy-start(f32[1536]{0:T(1024)} %get-tuple-element.26) | copy-start | bytes 18436
  81.3 2.6 %copy-start.38 = (f32[1536]{0:T(1024)S(1)}, f32[1536]{0:T(1024)}, u32[]{:S(2)}) copy-start(f32[1536]{0:T(1024)} %get-tuple-element.27) | copy-start | bytes 18436
  81.3 2.7 %copy-start.37 = (f32[1536]{0:T(1024)S(1)}, f32[1536]{0:T(1024)}, u32[]{:S(2)}) copy-start(f32[1536]{0:T(1024)} %get-tuple-element.28) | copy-start | bytes 18436
  81.3 2.7 %copy-start.36 = (f32[1536]{0:T(1024)S(1)}, f32[1536]{0:T(1024)}, u32[]{:S(2)}) copy-start(f32[1536]{0:T(1024)} %get-tuple-element.29) | copy-start | bytes 18436
  81.3 2.7 %copy-start.35 = (f32[1536]{0:T(1024)S(1)}, f32[1536]{0:T(1024)}, u32[]{:S(2)}) copy-start(f32[1536]{0:T(1024)} %get-tuple-element.30) | copy-start | bytes 18436
  81.3 2.7 %copy-start.34 = (f32[1536]{0:T(1024)S(1)}, f32[1536]{0:T(1024)}, u32[]{:S(2)}) copy-start(f32[1536]{0:T(1024)} %get-tuple-element.31) | copy-start | bytes 18436
  81.3 2.7 %copy-start.54 = (f32[1536]{0:T(1024)S(1)}, f32[1536]{0:T(1024)}, u32[]{:S(2)}) copy-start(f32[1536]{0:T(1024)} %get-tuple-element.32) | copy-start | bytes 18436
  81.3 2.7 %copy-start.53 = (f32[1536]{0:T(1024)S(1)}, f32[1536]{0:T(1024)}, u32[]{:S(2)}) copy-start(f32[1536]{0:T(1024)} %get-tuple-element.33) | copy-start | bytes 18436
  81.4 2.7 %copy-start.52 = (f32[1536]{0:T(1024)S(1)}, f32[1536]{0:T(1024)}, u32[]{:S(2)}) copy-start(f32[1536]{0:T(1024)} %get-tuple-element.34) | copy-start | bytes 18436
  84.1 8.4 %copy-start.3 = (bf16[128,768]{0,1:T(8,128)(2,1)S(1)}, bf16[128,768]{0,1:T(8,128)(2,1)}, u32[]{:S(2)}) copy-start(bf16[128,768]{0,1:T(8,128)(2,1)} %copy-done.2) | copy-start | bytes 589828
  84.2 8.4 %copy-start.79 = (f32[8,128]{1,0:T(8,128)S(1)}, f32[8,128]{1,0:T(8,128)}, u32[]{:S(2)}) copy-start(f32[8,128]{1,0:T(8,128)} %copy-done.78) | copy-start | bytes 12292
  85.3 15.2 %all-to-all-start.2 = ((f32[16,2,1536]{2,1,0:T(2,128)}), f32[16,2,1536]{2,1,0:T(2,128)S(1)}, u32[]{:S(2)}, u32[]{:S(2)}) async-start(f32[16,2,1536]{2,1,0:T(2,128)} %reshape.304), calls=%async_computation.3 | async-start | bytes 393216 | tf_op jit(solution)/shard_map/all_to_all | solution.py:140
  100.4 42.6 %all-to-all-start.1 = ((bf16[32,4,2304]{2,1,0:T(4,128)(2,1)}), bf16[32,4,2304]{2,1,0:T(4,128)(2,1)S(1)}, u32[]{:S(2)}, u32[]{:S(2)}) async-start(bf16[32,4,2304]{2,1,0:T(4,128)(2,1)} %all_to_all.25), calls=%async_computation.1 | async-start | bytes 1179648 | tf_op jit(solution)/shard_map/all_to_all | solution.py:119
  143.0 21.0 %all-to-all-start.3 = ((f32[32,2,1536]{2,1,0:T(2,128)}), f32[32,2,1536]{2,1,0:T(2,128)S(1)}, u32[]{:S(2)}, u32[]{:S(2)}) async-start(f32[32,2,1536]{2,1,0:T(2,128)} %reshape.305), calls=%async_computation.4 | async-start | bytes 786432 | tf_op jit(solution)/shard_map/all_to_all | solution.py:148
  (22 other events, 53.1 us)
Sparse Core Ops, SparseCore 0:
  10.1 48.0 all-gather.6
  81.5 59.5 reduce-scatter.1

commit v3 on v0

--- a/solution.py
+++ b/solution.py
@@ -120,14 +120,26 @@
     source_index = jnp.where(present, send_rows, row_count)
     projected_grad = jnp.zeros_like(projected).at[source_index].set(arrived, mode="drop")
     scale_factor = (row_count * lax.axis_size("dp") * lax.axis_size("fsdp")) ** (-0.5)
-    weight_total = lax.psum(weight_share, "dp")
-    kernel_total = lax.psum(kernel_part, ("dp", "fsdp"))
+    weight_total = exchange_sum(weight_share, "dp")
+    kernel_total = exchange_sum(exchange_sum(kernel_part, "fsdp"), "dp")
+
     return (
         result.astype(jnp.bfloat16),
         projected_grad,
         weight_total * scale_factor,
         kernel_total * scale_factor,
     )
+
+
+def exchange_sum(x, axis):
+    count = lax.axis_size(axis)
+    assert count & (count - 1) == 0
+    distance = 1
+    while distance < count:
+        pairs = [(index, index ^ distance) for index in range(count)]
+        x = x + lax.ppermute(x, axis, pairs)
+        distance *= 2
+    return x
 
 
 def solution(mesh):

time: 567 us -> 273 us (0.48)
  the two profiles are of different devices: /device:TPU:8 before, /device:TPU:28 now
where the time goes in v3:
time: 273 us; the launch traced here: 272 us
  waiting for transfers between devices  118 us (43%)
  starting transfers between devices  90.7 us (33%)
  other arithmetic  27.6 us (10%)
  between operations  15.7 us (6%)
  matrix products  11.6 us (4%)
  local copies, waits for them, and re-layouts  8.6 us (3%)
    ppermute x14, starting transfers between devices, exchange_sum(): x = x + lax.ppermute(x, axis, pairs)  66.7 us
    ppermute x14, waiting for transfers between devices, exchange_sum(): x = x + lax.ppermute(x, axis, pairs)  52.2 us
    reduce_scatter x1, waiting for transfers between devices, body(): lax.psum_scatter(jnp.einsum('rc,rd->cd', columns, mixed_grad, preferred_e...  38.4 us
    all_to_all x1, waiting for transfers between devices, body(): lax.all_to_all(outgoing, 'dp', split_axis=0, concat_axis=0, tiled=True)  16.7 us
    reduce_sum x4, other arithmetic, finish(): kernel[offset] * padded[offset:offset + length] * matching[:, None]  14.6 us
    all_to_all x1, starting transfers between devices, body(): lax.all_to_all(outgoing, 'dp', split_axis=0, concat_axis=0, tiled=True)  13.4 us
    all_to_all x1, starting transfers between devices, body(): lax.all_to_all(returning, 'dp', split_axis=0, concat_axis=0, tiled=True)  10.5 us
    all_gather x1, waiting for transfers between devices, body(): lax.all_gather(out_weight, 'fsdp', axis=0, tiled=True)  9.83 us
  transfers between devices with their start and end apart: 18, of which 10 were waited for; matrix products, arithmetic and copies ran while one was open for 8% of the time, Pallas kernels for 0%

profile of v3, /device:TPU:28, one launch (start us, length us, event | category | flops | bytes accessed | tf_op | source)
XLA Modules:
  0.0 272.0 jit_solution(6253662994135388980)
XLA Ops:
  7.2 0.7 all-gather.2.cloned.1.call-update
  7.9 1.2 compare_select_fusion.1
  9.2 1.0 gather_fusion
  10.4 1.0 all_to_all.16
  11.3 13.4 %all-to-all-start = ((bf16[32,4,2304]{2,1,0:T(4,128)(2,1)}), bf16[32,4,2304]{2,1,0:T(4,128)(2,1)S(1)}, u32[]{:S(2)}, u32[]{:S(2)}) async-start(bf16[32,4,2304]{2,1,0:T(4,128)(2,1)} %all_to_all.16), calls=%async_computation | async-start | bytes 1179648 | tf_op jit(solution)/shard_map/all_to_all | solution.py:84
  24.8 0.2 slice_reduce_fusion.29
  25.0 0.5 compare_select_fusion
  25.6 0.3 slice_reduce_fusion.30
  26.3 16.7 %all-to-all-done = bf16[32,4,2304]{2,1,0:T(4,128)(2,1)S(1)} async-done(((bf16[32,4,2304]{2,1,0:T(4,128)(2,1)}), bf16[32,4,2304]{2,1,0:T(4,128)(2,1)S(1)}, u32[]{:S(2)}, u32[]{:S(2)}) %all-to-all-start) | async-done | bytes 589856 | tf_op jit(solution)/shard_map/all_to_all | solution.py:84
  43.1 1.0 gather_fusion.1
  44.3 0.2 copy.25
  44.5 0.2 copy.24
  44.8 1.2 fusion.39
  46.0 0.5 convolution_convert_fusion.6
  46.5 9.8 %all-gather.2.cloned.1.call-done = bf16[768,1536]{1,0:T(8,128)(2,1)} async-done(((bf16[48,1536]{1,0:T(8,128)(2,1)}), bf16[768,1536]{1,0:T(8,128)(2,1)}) %all-gather.2.cloned.1.call-update) | async-done | bytes 2359312 | tf_op jit(solution)/shard_map/all_gather | solution.py:92
  56.3 2.2 fusion.2
  58.5 7.8 %multiply_reduce_fusion.31 = (f32[1536]{0:T(1024)S(1)}, f32[1536]{0:T(1024)}, f32[1536]{0:T(1024)}, f32[1536]{0:T(1024)}, f32[1536]{0:T(1024)}, /*index=5*/f32[1...) fusion(f32[128,1536]{1,0:T(8,128)S(1)} %fusion.2, ...), kind=kLoop, calls=%fused_computation.99 | loop fusion | flops 25152000 | bytes 3013632 | tf_op jit(solution)/shard_map/transpose(jvp())/reduce_sum | solution.py:74
  66.3 2.3 multiply_reduce_fusion.16
  68.6 0.5 multiply_multiply_fusion.27
  69.1 0.7 multiply_multiply_fusion.29
  69.9 0.7 multiply_multiply_fusion.28
  70.6 2.6 multiply_reduce_fusion.4
  73.3 2.6 pad_add_fusion
  75.9 0.7 fusion.16
  76.7 2.1 convolution_convert_fusion
  79.4 2.0 multiply_reduce_fusion.22
  81.8 0.3 pad_add_fusion.7
  82.1 2.3 collective-permute-start.5
  84.4 0.9 convolution_convert_fusion.5
  85.3 0.2 copy.27
  85.4 0.3 fusion.40
  85.8 0.3 fusion.59
  86.2 2.1 collective-permute-start.6
  88.3 1.3 convolution_convert_fusion.2
  89.5 6.5 %collective-permute-done.6 = f32[31,1536]{1,0:T(8,128)S(1)} collective-permute-done((f32[31,1536]{1,0:T(8,128)S(1)}, f32[31,1536]{1,0:T(8,128)S(1)}, u32[]{:S(2)}, u32[]{:S(2)}) %collective-permute-start.6) | collective-permute-done | bytes 190496 | tf_op jit(solution)/shard_map/ppermute | solution.py:140
  96.1 0.3 fusion.60
  96.5 2.5 collective-permute-start.7
  99.0 38.4 %reduce-scatter.2.cloned.1.call-done = bf16[48,1536]{1,0:T(8,128)(2,1)} async-done(((bf16[768,1536]{1,0:T(8,128)(2,1)}), bf16[48,1536]{1,0:T(8,128)(2,1)}) %reduce-scatter.2.cloned.1.call-update) | async-done | bytes 147472 | tf_op jit(solution)/shard_map/reduce_scatter | solution.py:101
  137.3 0.9 convert_element_type.212
  138.2 3.2 %collective-permute-start = (f32[48,1536]{1,0:T(8,128)S(1)}, f32[48,1536]{1,0:T(8,128)S(1)}, u32[]{:S(2)}, u32[]{:S(2)}) collective-permute-start(f32[48,1536]{1,0:T(8,128)S(1)} %convert_element_type.212), channel_id=1, source_target_pairs={{0,16},{16,0},{32,48},{48,32},{64,80},{80,64},{96,112},{112,96},{1... | collective-permute-start | bytes 884744 | tf_op jit(solution)/shard_map/ppermute | solution.py:140
  141.4 1.6 convolution_convert_fusion.3
  143.4 4.7 %collective-permute-start.8 = (f32[31,1536]{1,0:T(8,128)S(1)}, f32[31,1536]{1,0:T(8,128)S(1)}, u32[]{:S(2)}, u32[]{:S(2)}) collective-permute-start(f32[31,1536]{1,0:T(8,128)S(1)} %add.322), channel_id=1, source_target_pairs={{0,8},{1,9},{2,10},{3,11},{4,12},{5,13},{6,14},{7,15},{8,0},{9,1},... | collective-permute-start | bytes 571400 | tf_op jit(solution)/shard_map/ppermute | solution.py:140
  148.1 1.6 convolution_convert_fusion.4
  149.9 1.8 scatter_custom_fusion
  151.7 1.0 all_to_all.19
  152.6 10.5 %all-to-all-start.1 = ((bf16[32,4,2304]{2,1,0:T(4,128)(2,1)}), bf16[32,4,2304]{2,1,0:T(4,128)(2,1)S(1)}, u32[]{:S(2)}, u32[]{:S(2)}) async-start(bf16[32,4,2304]{2,1,0:T(4,128)(2,1)} %all_to_all.19), calls=%async_computation.1 | async-start | bytes 1179648 | tf_op jit(solution)/shard_map/all_to_all | solution.py:119
  163.1 3.1 %collective-permute-start.9 = (f32[31,1536]{1,0:T(8,128)S(1)}, f32[31,1536]{1,0:T(8,128)S(1)}, u32[]{:S(2)}, u32[]{:S(2)}) collective-permute-start(f32[31,1536]{1,0:T(8,128)S(1)} %add.323), channel_id=1, source_target_pairs={{0,16},{16,0},{32,48},{48,32},{64,80},{80,64},{96,112},{112,96},{1... | collective-permute-start | bytes 571400 | tf_op jit(solution)/shard_map/ppermute | solution.py:140
  166.3 2.8 %collective-permute-start.1 = (f32[48,1536]{1,0:T(8,128)S(1)}, f32[48,1536]{1,0:T(8,128)S(1)}, u32[]{:S(2)}, u32[]{:S(2)}) collective-permute-start(f32[48,1536]{1,0:T(8,128)S(1)} %convert_add_fusion.1), channel_id=1, source_target_pairs={{0,32},{16,48},{32,0},{48,16},{64,96},{80,112},{96,64},{112,80},{1... | collective-permute-start | bytes 884744 | tf_op jit(solution)/shard_map/ppermute | solution.py:140
  169.0 7.8 %collective-permute-done.9 = f32[31,1536]{1,0:T(8,128)S(1)} collective-permute-done((f32[31,1536]{1,0:T(8,128)S(1)}, f32[31,1536]{1,0:T(8,128)S(1)}, u32[]{:S(2)}, u32[]{:S(2)}) %collective-permute-start.9) | collective-permute-done | bytes 190496 | tf_op jit(solution)/shard_map/ppermute | solution.py:140
  176.9 1.9 collective-permute-start.10
  178.8 5.1 %collective-permute-done.1 = f32[48,1536]{1,0:T(8,128)S(1)} collective-permute-done((f32[48,1536]{1,0:T(8,128)S(1)}, f32[48,1536]{1,0:T(8,128)S(1)}, u32[]{:S(2)}, u32[]{:S(2)}) %collective-permute-start.1) | collective-permute-done | bytes 294944 | tf_op jit(solution)/shard_map/ppermute | solution.py:140
  184.0 3.0 %collective-permute-start.2 = (f32[48,1536]{1,0:T(8,128)S(1)}, f32[48,1536]{1,0:T(8,128)S(1)}, u32[]{:S(2)}, u32[]{:S(2)}) collective-permute-start(f32[48,1536]{1,0:T(8,128)S(1)} %add.316), channel_id=1, source_target_pairs={{0,64},{16,80},{32,96},{48,112},{64,0},{80,16},{96,32},{112,48},{1... | collective-permute-start | bytes 884744 | tf_op jit(solution)/shard_map/ppermute | solution.py:140
  187.0 0.5 collective-permute-done.10
  187.5 3.1 %collective-permute-start.11 = (f32[31,1536]{1,0:T(8,128)S(1)}, f32[31,1536]{1,0:T(8,128)S(1)}, u32[]{:S(2)}, u32[]{:S(2)}) collective-permute-start(f32[31,1536]{1,0:T(8,128)S(1)} %add.325), channel_id=1, source_target_pairs={{0,64},{16,80},{32,96},{48,112},{64,0},{80,16},{96,32},{112,48},{1... | collective-permute-start | bytes 571400 | tf_op jit(solution)/shard_map/ppermute | solution.py:140
  190.6 7.2 %collective-permute-done.11 = f32[31,1536]{1,0:T(8,128)S(1)} collective-permute-done((f32[31,1536]{1,0:T(8,128)S(1)}, f32[31,1536]{1,0:T(8,128)S(1)}, u32[]{:S(2)}, u32[]{:S(2)}) %collective-permute-start.11) | collective-permute-done | bytes 190496 | tf_op jit(solution)/shard_map/ppermute | solution.py:140
  197.8 3.8 %collective-permute-start.12 = (f32[31,1536]{1,0:T(8,128)S(1)}, f32[31,1536]{1,0:T(8,128)S(1)}, u32[]{:S(2)}, u32[]{:S(2)}) collective-permute-start(f32[31,1536]{1,0:T(8,128)S(1)} %add.326), channel_id=1, source_target_pairs={{0,128},{16,144},{32,160},{48,176},{64,192},{80,208},{96,224},{112... | collective-permute-start | bytes 571400 | tf_op jit(solution)/shard_map/ppermute | solution.py:140
  201.6 2.9 %collective-permute-start.3 = (f32[48,1536]{1,0:T(8,128)S(1)}, f32[48,1536]{1,0:T(8,128)S(1)}, u32[]{:S(2)}, u32[]{:S(2)}) collective-permute-start(f32[48,1536]{1,0:T(8,128)S(1)} %add.317), channel_id=1, source_target_pairs={{0,128},{16,144},{32,160},{48,176},{64,192},{80,208},{96,224},{112... | collective-permute-start | bytes 884744 | tf_op jit(solution)/shard_map/ppermute | solution.py:140
  204.6 12.4 %collective-permute-done.12 = f32[31,1536]{1,0:T(8,128)S(1)} collective-permute-done((f32[31,1536]{1,0:T(8,128)S(1)}, f32[31,1536]{1,0:T(8,128)S(1)}, u32[]{:S(2)}, u32[]{:S(2)}) %collective-permute-start.12) | collective-permute-done | bytes 190496 | tf_op jit(solution)/shard_map/ppermute | solution.py:140
  217.0 6.4 %collective-permute-start.13 = (f32[31,1536]{1,0:T(8,128)S(1)}, f32[31,1536]{1,0:T(8,128)S(1)}, u32[]{:S(2)}, u32[]{:S(2)}) collective-permute-start(f32[31,1536]{1,0:T(8,128)S(1)} %add.327), channel_id=1, source_target_pairs={{0,256},{16,272},{32,288},{48,304},{64,320},{80,336},{96,352},{112... | collective-permute-start | bytes 571400 | tf_op jit(solution)/shard_map/ppermute | solution.py:140
  223.6 2.4 scatter_custom_fusion.1
  226.0 24.9 %collective-permute-start.4 = (f32[48,1536]{1,0:T(8,128)S(1)}, f32[48,1536]{1,0:T(8,128)S(1)}, u32[]{:S(2)}, u32[]{:S(2)}) collective-permute-start(f32[48,1536]{1,0:T(8,128)S(1)} %add.318), channel_id=1, source_target_pairs={{0,256},{16,272},{32,288},{48,304},{64,320},{80,336},{96,352},{112... | collective-permute-start | bytes 884744 | tf_op jit(solution)/shard_map/ppermute | solution.py:140
  250.9 0.7 add_multiply_fusion.1
  251.6 12.8 %collective-permute-done.4 = f32[48,1536]{1,0:T(8,128)S(1)} collective-permute-done((f32[48,1536]{1,0:T(8,128)S(1)}, f32[48,1536]{1,0:T(8,128)S(1)}, u32[]{:S(2)}, u32[]{:S(2)}) %collective-permute-start.4) | collective-permute-done | bytes 294944 | tf_op jit(solution)/shard_map/ppermute | solution.py:140
  264.4 0.8 add_multiply_fusion
  (196 shorter events, 2.4 us)
Async XLA Ops:
  7.2 49.2 %all-gather.2.cloned.1.call-start = ((), (), s32[]{:S(2)}) async-start(), calls=%async_computation.3 | async-start | bytes 2506752 | tf_op jit(solution)/shard_map/all_gather | solution.py:92
  10.1 14.7 %copy-start.6 = (f32[31,1536]{1,0:T(8,128)S(1)}, f32[31,1536]{1,0:T(8,128)}, u32[]{:S(2)}) copy-start(f32[31,1536]{1,0:T(8,128)} %param.11) | copy-start | bytes 571396
  10.2 14.9 %copy-start.63 = (s32[128]{0:T(128)S(1)}, s32[128]{0:T(128)}, u32[]{:S(2)}) copy-start(s32[128]{0:T(128)} %param.14) | copy-start | bytes 1540
  10.2 15.7 %copy-start.61 = (s32[128]{0:T(128)S(1)}, s32[128]{0:T(128)}, u32[]{:S(2)}) copy-start(s32[128]{0:T(128)} %param.15) | copy-start | bytes 1540
  11.3 31.7 %all-to-all-start = ((bf16[32,4,2304]{2,1,0:T(4,128)(2,1)}), bf16[32,4,2304]{2,1,0:T(4,128)(2,1)S(1)}, u32[]{:S(2)}, u32[]{:S(2)}) async-start(bf16[32,4,2304]{2,1,0:T(4,128)(2,1)} %all_to_all.16), calls=%async_computation | async-start | bytes 1179648 | tf_op jit(solution)/shard_map/all_to_all | solution.py:84
  24.7 112.6 %reduce-scatter.2.cloned.1.call-start = ((), (), s32[]{:S(2)}) async-start(), calls=%async_computation.4 | async-start | bytes 2506752 | tf_op jit(solution)/shard_map/reduce_scatter | solution.py:101
  26.1 43.0 %copy-start.55 = (f32[128]{0:T(128)}, f32[128]{0:T(128)S(1)}, u32[]{:S(2)}) copy-start(f32[128]{0:T(128)S(1)} %get-tuple-element.120) | copy-start | bytes 1540
  26.1 43.0 %copy-start.57 = (f32[128]{0:T(128)}, f32[128]{0:T(128)S(1)}, u32[]{:S(2)}) copy-start(f32[128]{0:T(128)S(1)} %get-tuple-element.121) | copy-start | bytes 1540
  26.1 43.0 %copy-start.59 = (f32[128]{0:T(128)}, f32[128]{0:T(128)S(1)}, u32[]{:S(2)}) copy-start(f32[128]{0:T(128)S(1)} %get-tuple-element.122) | copy-start | bytes 1540
  26.1 43.7 %copy-start.43 = (f32[128]{0:T(128)}, f32[128]{0:T(128)S(1)}, u32[]{:S(2)}) copy-start(f32[128]{0:T(128)S(1)} %get-tuple-element.114) | copy-start | bytes 1540
  26.1 43.7 %copy-start.45 = (f32[128]{0:T(128)}, f32[128]{0:T(128)S(1)}, u32[]{:S(2)}) copy-start(f32[128]{0:T(128)S(1)} %get-tuple-element.115) | copy-start | bytes 1540
  26.1 43.7 %copy-start.47 = (f32[128]{0:T(128)}, f32[128]{0:T(128)S(1)}, u32[]{:S(2)}) copy-start(f32[128]{0:T(128)S(1)} %get-tuple-element.116) | copy-start | bytes 1540
  26.2 43.7 %copy-start.49 = (f32[128]{0:T(128)}, f32[128]{0:T(128)S(1)}, u32[]{:S(2)}) copy-start(f32[128]{0:T(128)S(1)} %get-tuple-element.117) | copy-start | bytes 1540
  26.2 43.7 %copy-start.51 = (f32[128]{0:T(128)}, f32[128]{0:T(128)S(1)}, u32[]{:S(2)}) copy-start(f32[128]{0:T(128)S(1)} %get-tuple-element.118) | copy-start | bytes 1540
  26.2 43.7 %copy-start.53 = (f32[128]{0:T(128)}, f32[128]{0:T(128)S(1)}, u32[]{:S(2)}) copy-start(f32[128]{0:T(128)S(1)} %get-tuple-element.119) | copy-start | bytes 1540
  26.3 19.7 %copy-start.42 = (pred[128,128]{0,1:T(8,128)(4,1)}, pred[128,128]{0,1:T(8,128)(4,1)S(1)}, u32[]{:S(2)}) copy-start(pred[128,128]{0,1:T(8,128)(4,1)S(1)} %broadcast_compare_fusion) | copy-start | bytes 49156
  44.6 11.7 %copy-start.4 = (bf16[128,768]{0,1:T(8,128)(2,1)}, bf16[128,768]{0,1:T(8,128)(2,1)S(1)}, u32[]{:S(2)}) copy-start(bf16[128,768]{0,1:T(8,128)(2,1)S(1)} %copy.24) | copy-start | bytes 589828
  46.5 12.0 %copy-start.2 = (bf16[128,1536]{1,0:T(8,128)(2,1)S(1)}, bf16[128,1536]{1,0:T(8,128)(2,1)}, u32[]{:S(2)}) copy-start(bf16[128,1536]{1,0:T(8,128)(2,1)} %param.12) | copy-start | bytes 1179652
  76.6 2.6 copy-start.44
  76.6 2.6 copy-start.46
  76.6 2.6 copy-start.48
  78.9 2.6 copy-start.27
  78.9 2.7 copy-start.26
  78.9 2.7 copy-start.25
  78.9 2.7 copy-start.24
  78.9 2.7 copy-start.23
  78.9 2.7 %copy-start.22 = (f32[1536]{0:T(1024)S(1)}, f32[1536]{0:T(1024)}, u32[]{:S(2)}) copy-start(f32[1536]{0:T(1024)} %get-tuple-element.30) | copy-start | bytes 18436
  78.9 2.7 %copy-start.21 = (f32[1536]{0:T(1024)S(1)}, f32[1536]{0:T(1024)}, u32[]{:S(2)}) copy-start(f32[1536]{0:T(1024)} %get-tuple-element.31) | copy-start | bytes 18436
  78.9 2.8 %copy-start.41 = (f32[1536]{0:T(1024)S(1)}, f32[1536]{0:T(1024)}, u32[]{:S(2)}) copy-start(f32[1536]{0:T(1024)} %get-tuple-element.32) | copy-start | bytes 18436
  78.9 2.8 %copy-start.40 = (f32[1536]{0:T(1024)S(1)}, f32[1536]{0:T(1024)}, u32[]{:S(2)}) copy-start(f32[1536]{0:T(1024)} %get-tuple-element.33) | copy-start | bytes 18436
  78.9 2.8 %copy-start.39 = (f32[1536]{0:T(1024)S(1)}, f32[1536]{0:T(1024)}, u32[]{:S(2)}) copy-start(f32[1536]{0:T(1024)} %get-tuple-element.34) | copy-start | bytes 18436
  78.9 2.8 %copy-start.38 = (f32[1536]{0:T(1024)S(1)}, f32[1536]{0:T(1024)}, u32[]{:S(2)}) copy-start(f32[1536]{0:T(1024)} %get-tuple-element.35) | copy-start | bytes 18436
  79.0 5.4 %copy-start.1 = (bf16[768,1536]{1,0:T(8,128)(2,1)S(1)}, bf16[768,1536]{1,0:T(8,128)(2,1)}, u32[]{:S(2)}) copy-start(bf16[768,1536]{1,0:T(8,128)(2,1)} %all-gather.2.cloned.1.call-done) | copy-start | bytes 7077892
  79.0 6.7 %copy-start.7 = (f32[1,1536]{1,0:T(1,128)}, f32[1,1536]{1,0:T(1,128)S(1)}, u32[]{:S(2)}) copy-start(f32[1,1536]{1,0:T(1,128)S(1)} %reshape.263) | copy-start | bytes 18436
  79.1 6.6 %copy-start.9 = (f32[1,1536]{1,0:T(1,128)}, f32[1,1536]{1,0:T(1,128)S(1)}, u32[]{:S(2)}) copy-start(f32[1,1536]{1,0:T(1,128)S(1)} %reshape.264) | copy-start | bytes 18436
  79.1 6.6 %copy-start.11 = (f32[1,1536]{1,0:T(1,128)}, f32[1,1536]{1,0:T(1,128)S(1)}, u32[]{:S(2)}) copy-start(f32[1,1536]{1,0:T(1,128)S(1)} %reshape.265) | copy-start | bytes 18436
  79.2 6.6 %copy-start.13 = (f32[1,1536]{1,0:T(1,128)}, f32[1,1536]{1,0:T(1,128)S(1)}, u32[]{:S(2)}) copy-start(f32[1,1536]{1,0:T(1,128)S(1)} %reshape.266) | copy-start | bytes 18436
  79.2 6.6 %copy-start.15 = (f32[1,1536]{1,0:T(1,128)}, f32[1,1536]{1,0:T(1,128)S(1)}, u32[]{:S(2)}) copy-start(f32[1,1536]{1,0:T(1,128)S(1)} %reshape.267) | copy-start | bytes 18436
  79.2 6.6 %copy-start.17 = (f32[1,1536]{1,0:T(1,128)}, f32[1,1536]{1,0:T(1,128)S(1)}, u32[]{:S(2)}) copy-start(f32[1,1536]{1,0:T(1,128)S(1)} %reshape.268) | copy-start | bytes 18436
  79.3 6.4 %copy-start.19 = (f32[1,1536]{1,0:T(1,128)}, f32[1,1536]{1,0:T(1,128)S(1)}, u32[]{:S(2)}) copy-start(f32[1,1536]{1,0:T(1,128)S(1)} %reshape.269) | copy-start | bytes 18436
  82.1 6.2 %copy-start.5 = (bf16[128,768]{0,1:T(8,128)(2,1)S(1)}, bf16[128,768]{0,1:T(8,128)(2,1)}, u32[]{:S(2)}) copy-start(bf16[128,768]{0,1:T(8,128)(2,1)} %copy-done.4) | copy-start | bytes 589828
  82.1 3.6 %collective-permute-start.5 = (f32[31,1536]{1,0:T(8,128)S(1)}, f32[31,1536]{1,0:T(8,128)S(1)}, u32[]{:S(2)}, u32[]{:S(2)}) collective-permute-start(f32[31,1536]{1,0:T(8,128)S(1)} %pad_add_fusion.7), channel_id=1, source_target_pairs={{0,1},{1,0},{2,3},{3,2},{4,5},{5,4},{6,7},{7,6},{8,9},{9,8},{10,11... | collective-permute-start | bytes 571400 | tf_op jit(solution)/shard_map/ppermute | solution.py:140
  86.1 10.0 %copy-start.8 = (f32[1,1536]{1,0:T(1,128)S(1)}, f32[1,1536]{1,0:T(1,128)}, u32[]{:S(2)}) copy-start(f32[1,1536]{1,0:T(1,128)} %copy-done.7) | copy-start | bytes 18436
  86.1 10.0 %copy-start.10 = (f32[1,1536]{1,0:T(1,128)S(1)}, f32[1,1536]{1,0:T(1,128)}, u32[]{:S(2)}) copy-start(f32[1,1536]{1,0:T(1,128)} %copy-done.9) | copy-start | bytes 18436
  86.1 10.0 %copy-start.12 = (f32[1,1536]{1,0:T(1,128)S(1)}, f32[1,1536]{1,0:T(1,128)}, u32[]{:S(2)}) copy-start(f32[1,1536]{1,0:T(1,128)} %copy-done.11) | copy-start | bytes 18436
  86.1 9.9 %copy-start.14 = (f32[1,1536]{1,0:T(1,128)S(1)}, f32[1,1536]{1,0:T(1,128)}, u32[]{:S(2)}) copy-start(f32[1,1536]{1,0:T(1,128)} %copy-done.13) | copy-start | bytes 18436
  86.2 9.9 %copy-start.16 = (f32[1,1536]{1,0:T(1,128)S(1)}, f32[1,1536]{1,0:T(1,128)}, u32[]{:S(2)}) copy-start(f32[1,1536]{1,0:T(1,128)} %copy-done.15) | copy-start | bytes 18436
  86.2 9.9 %copy-start.18 = (f32[1,1536]{1,0:T(1,128)S(1)}, f32[1,1536]{1,0:T(1,128)}, u32[]{:S(2)}) copy-start(f32[1,1536]{1,0:T(1,128)} %copy-done.17) | copy-start | bytes 18436
  86.2 9.9 %copy-start.20 = (f32[1,1536]{1,0:T(1,128)S(1)}, f32[1,1536]{1,0:T(1,128)}, u32[]{:S(2)}) copy-start(f32[1,1536]{1,0:T(1,128)} %copy-done.19) | copy-start | bytes 18436
  86.2 9.9 %collective-permute-start.6 = (f32[31,1536]{1,0:T(8,128)S(1)}, f32[31,1536]{1,0:T(8,128)S(1)}, u32[]{:S(2)}, u32[]{:S(2)}) collective-permute-start(f32[31,1536]{1,0:T(8,128)S(1)} %fusion.59), channel_id=1, source_target_pairs={{0,2},{1,3},{2,0},{3,1},{4,6},{5,7},{6,4},{7,5},{8,10},{9,11},{10,... | collective-permute-start | bytes 571400 | tf_op jit(solution)/shard_map/ppermute | solution.py:140
  96.5 46.9 %collective-permute-start.7 = (f32[31,1536]{1,0:T(8,128)S(1)}, f32[31,1536]{1,0:T(8,128)S(1)}, u32[]{:S(2)}, u32[]{:S(2)}) collective-permute-start(f32[31,1536]{1,0:T(8,128)S(1)} %fusion.60), channel_id=1, source_target_pairs={{0,4},{1,5},{2,6},{3,7},{4,0},{5,1},{6,2},{7,3},{8,12},{9,13},{10,... | collective-permute-start | bytes 571400 | tf_op jit(solution)/shard_map/ppermute | solution.py:140
  138.2 28.0 %collective-permute-start = (f32[48,1536]{1,0:T(8,128)S(1)}, f32[48,1536]{1,0:T(8,128)S(1)}, u32[]{:S(2)}, u32[]{:S(2)}) collective-permute-start(f32[48,1536]{1,0:T(8,128)S(1)} %convert_element_type.212), channel_id=1, source_target_pairs={{0,16},{16,0},{32,48},{48,32},{64,80},{80,64},{96,112},{112,96},{1... | collective-permute-start | bytes 884744 | tf_op jit(solution)/shard_map/ppermute | solution.py:140
  143.4 19.7 %collective-permute-start.8 = (f32[31,1536]{1,0:T(8,128)S(1)}, f32[31,1536]{1,0:T(8,128)S(1)}, u32[]{:S(2)}, u32[]{:S(2)}) collective-permute-start(f32[31,1536]{1,0:T(8,128)S(1)} %add.322), channel_id=1, source_target_pairs={{0,8},{1,9},{2,10},{3,11},{4,12},{5,13},{6,14},{7,15},{8,0},{9,1},... | collective-permute-start | bytes 571400 | tf_op jit(solution)/shard_map/ppermute | solution.py:140
  149.7 16.5 %copy-start.3 = (bf16[48,1536]{1,0:T(8,128)(2,1)S(1)}, bf16[48,1536]{1,0:T(8,128)(2,1)}, u32[]{:S(2)}) copy-start(bf16[48,1536]{1,0:T(8,128)(2,1)} %reduce-scatter.2.cloned.1.call-done) | copy-start | bytes 442372
  152.6 70.8 %all-to-all-start.1 = ((bf16[32,4,2304]{2,1,0:T(4,128)(2,1)}), bf16[32,4,2304]{2,1,0:T(4,128)(2,1)S(1)}, u32[]{:S(2)}, u32[]{:S(2)}) async-start(bf16[32,4,2304]{2,1,0:T(4,128)(2,1)} %all_to_all.19), calls=%async_computation.1 | async-start | bytes 1179648 | tf_op jit(solution)/shard_map/all_to_all | solution.py:119
  163.1 13.7 %collective-permute-start.9 = (f32[31,1536]{1,0:T(8,128)S(1)}, f32[31,1536]{1,0:T(8,128)S(1)}, u32[]{:S(2)}, u32[]{:S(2)}) collective-permute-start(f32[31,1536]{1,0:T(8,128)S(1)} %add.323), channel_id=1, source_target_pairs={{0,16},{16,0},{32,48},{48,32},{64,80},{80,64},{96,112},{112,96},{1... | collective-permute-start | bytes 571400 | tf_op jit(solution)/shard_map/ppermute | solution.py:140
  166.3 17.6 %collective-permute-start.1 = (f32[48,1536]{1,0:T(8,128)S(1)}, f32[48,1536]{1,0:T(8,128)S(1)}, u32[]{:S(2)}, u32[]{:S(2)}) collective-permute-start(f32[48,1536]{1,0:T(8,128)S(1)} %convert_add_fusion.1), channel_id=1, source_target_pairs={{0,32},{16,48},{32,0},{48,16},{64,96},{80,112},{96,64},{112,80},{1... | collective-permute-start | bytes 884744 | tf_op jit(solution)/shard_map/ppermute | solution.py:140
  176.9 10.6 %collective-permute-start.10 = (f32[31,1536]{1,0:T(8,128)S(1)}, f32[31,1536]{1,0:T(8,128)S(1)}, u32[]{:S(2)}, u32[]{:S(2)}) collective-permute-start(f32[31,1536]{1,0:T(8,128)S(1)} %add.324), channel_id=1, source_target_pairs={{0,32},{16,48},{32,0},{48,16},{64,96},{80,112},{96,64},{112,80},{1... | collective-permute-start | bytes 571400 | tf_op jit(solution)/shard_map/ppermute | solution.py:140
  184.0 17.6 %collective-permute-start.2 = (f32[48,1536]{1,0:T(8,128)S(1)}, f32[48,1536]{1,0:T(8,128)S(1)}, u32[]{:S(2)}, u32[]{:S(2)}) collective-permute-start(f32[48,1536]{1,0:T(8,128)S(1)} %add.316), channel_id=1, source_target_pairs={{0,64},{16,80},{32,96},{48,112},{64,0},{80,16},{96,32},{112,48},{1... | collective-permute-start | bytes 884744 | tf_op jit(solution)/shard_map/ppermute | solution.py:140
  187.5 10.3 %collective-permute-start.11 = (f32[31,1536]{1,0:T(8,128)S(1)}, f32[31,1536]{1,0:T(8,128)S(1)}, u32[]{:S(2)}, u32[]{:S(2)}) collective-permute-start(f32[31,1536]{1,0:T(8,128)S(1)} %add.325), channel_id=1, source_target_pairs={{0,64},{16,80},{32,96},{48,112},{64,0},{80,16},{96,32},{112,48},{1... | collective-permute-start | bytes 571400 | tf_op jit(solution)/shard_map/ppermute | solution.py:140
  197.8 19.2 %collective-permute-start.12 = (f32[31,1536]{1,0:T(8,128)S(1)}, f32[31,1536]{1,0:T(8,128)S(1)}, u32[]{:S(2)}, u32[]{:S(2)}) collective-permute-start(f32[31,1536]{1,0:T(8,128)S(1)} %add.326), channel_id=1, source_target_pairs={{0,128},{16,144},{32,160},{48,176},{64,192},{80,208},{96,224},{112... | collective-permute-start | bytes 571400 | tf_op jit(solution)/shard_map/ppermute | solution.py:140
  201.6 24.3 %collective-permute-start.3 = (f32[48,1536]{1,0:T(8,128)S(1)}, f32[48,1536]{1,0:T(8,128)S(1)}, u32[]{:S(2)}, u32[]{:S(2)}) collective-permute-start(f32[48,1536]{1,0:T(8,128)S(1)} %add.317), channel_id=1, source_target_pairs={{0,128},{16,144},{32,160},{48,176},{64,192},{80,208},{96,224},{112... | collective-permute-start | bytes 884744 | tf_op jit(solution)/shard_map/ppermute | solution.py:140
  217.0 33.9 %collective-permute-start.13 = (f32[31,1536]{1,0:T(8,128)S(1)}, f32[31,1536]{1,0:T(8,128)S(1)}, u32[]{:S(2)}, u32[]{:S(2)}) collective-permute-start(f32[31,1536]{1,0:T(8,128)S(1)} %add.327), channel_id=1, source_target_pairs={{0,256},{16,272},{32,288},{48,304},{64,320},{80,336},{96,352},{112... | collective-permute-start | bytes 571400 | tf_op jit(solution)/shard_map/ppermute | solution.py:140
  226.0 38.4 %collective-permute-start.4 = (f32[48,1536]{1,0:T(8,128)S(1)}, f32[48,1536]{1,0:T(8,128)S(1)}, u32[]{:S(2)}, u32[]{:S(2)}) collective-permute-start(f32[48,1536]{1,0:T(8,128)S(1)} %add.318), channel_id=1, source_target_pairs={{0,256},{16,272},{32,288},{48,304},{64,320},{80,336},{96,352},{112... | collective-permute-start | bytes 884744 | tf_op jit(solution)/shard_map/ppermute | solution.py:140
  (18 other events, 44.4 us)
Sparse Core Ops, SparseCore 0:
  10.1 46.1 all-gather.1
  79.1 58.1 reduce-scatter.1

commit v4 on v2

--- a/solution.py
+++ b/solution.py
@@ -147,8 +147,25 @@
     padded = jnp.pad(x, ((0, n * per - x.shape[0]), (0, 0))).reshape(n, per, x.shape[1])
     got = lax.all_to_all(padded, "dp", split_axis=0, concat_axis=0, tiled=True)
     part = jnp.sum(got, axis=0, keepdims=True)
-    whole = lax.all_gather(part, "dp", axis=0, tiled=True)
+    whole = exchange_gather(part[0], "dp")
     return whole.reshape(n * per, x.shape[1])[: x.shape[0]]
+
+
+def exchange_gather(piece, axis):
+    count = lax.axis_size(axis)
+    assert count & (count - 1) == 0
+    index = lax.axis_index(axis)
+    blocks = piece[None]
+    distance = 1
+    while distance < count:
+        pairs = [(source, source ^ distance) for source in range(count)]
+        other = lax.ppermute(blocks, axis, pairs)
+        upper = (index // distance) % 2 == 1
+        blocks = jnp.where(
+            upper, jnp.concatenate([other, blocks], axis=0), jnp.concatenate([blocks, other], axis=0)
+        )
+        distance *= 2
+    return blocks
 
 def solution(mesh):
     placed = (

time: 244 us -> 249 us (1.020)
  blocking collectives: 70.5 us -> 30.8 us
  waiting for transfers between devices: 67.4 us -> 92.3 us
  starting transfers between devices: 38.1 us -> 54.2 us
  other arithmetic: 25.8 us -> 28.5 us
    all_gather x1 -> x0, blocking collectives: 35.8 us -> none  [dp_allreduce_a2a(): whole = lax.all_gather(part, 'dp', axis=0, tiled=True)]
    ppermute x0 -> x5, starting transfers between devices: none -> 21.5 us  [exchange_gather(): other = lax.ppermute(blocks, axis, pairs)]
    all_to_all x1, waiting for transfers between devices: 0.01 us -> 10.3 us  [fsdp_sum_rows(): lax.all_to_all(padded.reshape(n, per, x.shape[1]), 'fsdp', split_axis=0,...]
    reduce_scatter x1, waiting for transfers between devices: 30.3 us -> 40.5 us  [body(): lax.psum_scatter(jnp.einsum('rc,rd->cd', columns, mixed_grad, preferred_e...]
    ppermute x0 -> x5, waiting for transfers between devices: none -> 9.56 us  [exchange_gather(): other = lax.ppermute(blocks, axis, pairs)]
    all_to_all x1, starting transfers between devices: 10.2 us -> 4.8 us  [body(): lax.all_to_all(returning, 'dp', split_axis=0, concat_axis=0, tiled=True)]
    all_gather x1, blocking collectives: 34.8 us -> 30.8 us  [body(): lax.all_gather(both[owned_rows:], 'fsdp', axis=0, tiled=True)]
    all_to_all x1, waiting for transfers between devices: 9.08 us -> 5.65 us  [dp_allreduce_a2a(): got = lax.all_to_all(padded, 'dp', split_axis=0, concat_axis=0, tiled=True)]
  transfers between devices with their start and end apart: 6 -> 11, of which waited for: 4 -> 9; matrix products, arithmetic and copies ran while one was open for 10% -> 10% of each run, Pallas kernels for 0% -> 0%
where the time goes in v4:
time: 249 us
  waiting for transfers between devices  92.3 us (37%)
  starting transfers between devices  54.2 us (22%)
  blocking collectives  30.8 us (12%)
  other arithmetic  28.5 us (11%)
  between operations  16.1 us (6%)
  local copies, waits for them, and re-layouts  13.6 us (5%)
  matrix products  13.1 us (5%)
    reduce_scatter x1, waiting for transfers between devices, body(): lax.psum_scatter(jnp.einsum('rc,rd->cd', columns, mixed_grad, preferred_e...  40.5 us
    all_gather x1, blocking collectives, body(): lax.all_gather(both[owned_rows:], 'fsdp', axis=0, tiled=True)  30.8 us
    ppermute x5, starting transfers between devices, exchange_gather(): other = lax.ppermute(blocks, axis, pairs)  21.5 us
    reduce_sum x4, other arithmetic, finish(): kernel[offset] * padded[offset:offset + length] * matching[:, None]  16.1 us
    all_to_all x1, starting transfers between devices, body(): lax.all_to_all(outgoing, 'dp', split_axis=0, concat_axis=0, tiled=True)  13.7 us
    all_to_all x1, waiting for transfers between devices, body(): lax.all_to_all(outgoing, 'dp', split_axis=0, concat_axis=0, tiled=True)  13.7 us
    all_gather x1, waiting for transfers between devices, body(): lax.all_gather(out_weight, 'fsdp', axis=0, tiled=True)  12 us
    all_to_all x1, waiting for transfers between devices, fsdp_sum_rows(): lax.all_to_all(padded.reshape(n, per, x.shape[1]), 'fsdp', split_axis=0,...  10.3 us
  transfers between devices with their start and end apart: 11, of which 9 were waited for; matrix products, arithmetic and copies ran while one was open for 10% of the time, Pallas kernels for 0%

profile of v4, /device:TPU:1, one launch (start us, length us, event | category | flops | bytes accessed | tf_op | source)
XLA Modules:
  0.0 248.5 jit_solution(4668880804918637035)
XLA Ops:
  7.2 0.7 all-gather.3.cloned.1.call-update
  7.9 1.2 compare_select_fusion.1
  9.1 1.0 gather_fusion
  10.2 0.2 select_select_fusion.1
  10.3 1.0 all_to_all.22
  11.3 13.7 %all-to-all-start = ((bf16[32,4,2304]{2,1,0:T(4,128)(2,1)}), bf16[32,4,2304]{2,1,0:T(4,128)(2,1)S(1)}, u32[]{:S(2)}, u32[]{:S(2)}) async-start(bf16[32,4,2304]{2,1,0:T(4,128)(2,1)} %all_to_all.22), calls=%async_computation | async-start | bytes 1179648 | tf_op jit(solution)/shard_map/all_to_all | solution.py:84
  25.1 0.8 slice_reduce_fusion.29
  25.8 0.5 compare_select_fusion
  26.4 0.9 slice_reduce_fusion.30
  27.3 0.7 compare_convert_fusion.28
  28.0 0.7 compare_convert_fusion.29
  28.8 13.7 %all-to-all-done = bf16[32,4,2304]{2,1,0:T(4,128)(2,1)S(1)} async-done(((bf16[32,4,2304]{2,1,0:T(4,128)(2,1)}), bf16[32,4,2304]{2,1,0:T(4,128)(2,1)S(1)}, u32[]{:S(2)}, u32[]{:S(2)}) %all-to-all-start) | async-done | bytes 589856 | tf_op jit(solution)/shard_map/all_to_all | solution.py:84
  42.6 1.0 gather_fusion.1
  43.6 0.2 select_select_fusion
  43.8 0.2 copy.71
  44.0 0.2 copy.70
  44.1 0.2 copy.69
  44.3 1.2 fusion.39
  45.5 0.5 convolution_convert_fusion.6
  46.3 12.0 %all-gather.3.cloned.1.call-done = bf16[768,1536]{1,0:T(8,128)(2,1)} async-done(((bf16[48,1536]{1,0:T(8,128)(2,1)}), bf16[768,1536]{1,0:T(8,128)(2,1)}) %all-gather.3.cloned.1.call-update) | async-done | bytes 2359312 | tf_op jit(solution)/shard_map/all_gather | solution.py:92
  58.4 2.2 fusion.2
  60.9 8.5 %multiply_reduce_fusion.31 = (f32[1536]{0:T(1024)}, f32[1536]{0:T(1024)}, f32[1536]{0:T(1024)}, f32[1536]{0:T(1024)}, f32[1536]{0:T(1024)}, /*index=5*/f32[1536]...) fusion(f32[128,1536]{1,0:T(8,128)S(1)} %fusion.2, ...), kind=kLoop, calls=%fused_computation.99 | loop fusion | flops 25152000 | bytes 3013632 | tf_op jit(solution)/shard_map/transpose(jvp())/reduce_sum | solution.py:74
  69.5 3.0 %multiply_reduce_fusion.16 = (f32[1536]{0:T(1024)}, f32[1536]{0:T(1024)}, f32[1536]{0:T(1024)}, f32[1536]{0:T(1024)}, f32[1536]{0:T(1024)}, /*index=5*/f32[1536]...) fusion(f32[128,1536]{1,0:T(8,128)S(1)} %get-tuple-element.67, ...), kind=kLoop, calls=%fused_computation.84 | loop fusion | flops 5294592 | bytes 2424832 | tf_op jit(solution)/shard_map/transpose(jvp())/reduce_sum | solution.py:74
  72.5 0.5 multiply_multiply_fusion.27
  73.2 0.7 multiply_multiply_fusion.29
  73.9 0.7 multiply_multiply_fusion.28
  74.7 2.6 %multiply_reduce_fusion.4 = (f32[1536]{0:T(1024)}, f32[1536]{0:T(1024)}, f32[1536]{0:T(1024)}, f32[1536]{0:T(1024)S(1)}, f32[128,1536]{1,0:T(8,128)S(1)}, /*inde...) fusion(f32[128,1536]{1,0:T(8,128)S(1)} %get-tuple-element.67, ...), kind=kLoop, calls=%fused_computation.72 | loop fusion | flops 5105664 | bytes 7535616 | tf_op jit(solution)/shard_map/transpose(jvp())/reduce_sum | solution.py:74
  77.3 2.6 %pad_add_fusion = f32[158,1536]{1,0:T(8,128)S(1)} fusion(f32[128,1536]{1,0:T(8,128)S(1)} %get-tuple-element.76, f32[128,1536]{1,0:T(8,128)S(1)} %get-tuple-element.78, f32[128,1536]{1,0:T(8,128)S(1)} %get-tuple-element.79, f32[128,1536]{1,0:T(8,128)S(1)} %get-tuple-element.80, f32[128,1536]{1,0:T(8,128)S(1)} %get-tuple-element.81, ...), kind=kLoop, calls=%fused_computation.59 | loop fusion | flops 5824512 | bytes 20631552 | tf_op jit(solution)/shard_map/transpose(jvp())/add_any | solution.py:74
  79.9 0.7 fusion.16
  80.8 2.2 convolution_convert_fusion
  83.4 2.0 multiply_reduce_fusion.22
  85.8 0.3 pad_add_fusion.7
  86.1 0.8 reshape.304
  86.9 4.9 %all-to-all-start.2 = ((f32[16,2,1536]{2,1,0:T(2,128)}), f32[16,2,1536]{2,1,0:T(2,128)S(1)}, u32[]{:S(2)}, u32[]{:S(2)}) async-start(f32[16,2,1536]{2,1,0:T(2,128)} %reshape.304), calls=%async_computation.3 | async-start | bytes 393216 | tf_op jit(solution)/shard_map/all_to_all | solution.py:140
  91.8 10.3 %all-to-all-done.2 = f32[16,2,1536]{2,1,0:T(2,128)S(1)} async-done(((f32[16,2,1536]{2,1,0:T(2,128)}), f32[16,2,1536]{2,1,0:T(2,128)S(1)}, u32[]{:S(2)}, u32[]{:S(2)}) %all-to-all-start.2) | async-done | bytes 196640 | tf_op jit(solution)/shard_map/all_to_all | solution.py:140
  102.1 40.5 %reduce-scatter.2.cloned.1.call-done = bf16[48,1536]{1,0:T(8,128)(2,1)} async-done(((bf16[768,1536]{1,0:T(8,128)(2,1)}), bf16[48,1536]{1,0:T(8,128)(2,1)}) %reduce-scatter.2.cloned.1.call-update) | async-done | bytes 147472 | tf_op jit(solution)/shard_map/reduce_scatter | solution.py:101
  142.6 0.9 convert_element_type.216
  143.6 1.0 reshape.305
  144.5 9.2 %all-to-all-start.3 = ((f32[32,2,1536]{2,1,0:T(2,128)}), f32[32,2,1536]{2,1,0:T(2,128)S(1)}, u32[]{:S(2)}, u32[]{:S(2)}) async-start(f32[32,2,1536]{2,1,0:T(2,128)} %reshape.305), calls=%async_computation.4 | async-start | bytes 786432 | tf_op jit(solution)/shard_map/all_to_all | solution.py:148
  153.8 2.5 %convolution_convert_fusion.5 = bf16[128,768]{1,0:T(8,128)(2,1)S(1)} fusion(bf16[128,1536]{1,0:T(8,128)(2,1)S(1)} %fusion.16, bf16[768,1536]{1,0:T(8,128)(2,1)} %all-gather.3.cloned.1.call-done), kind=kOutput, calls=%fused_computation.54 | convolution fusion | flops 302088192 | bytes 2949120 | tf_op jit(solution)/shard_map/rd,cd->rc/dot_general | solution.py:109
  156.3 0.2 copy.73
  156.5 0.3 fusion.40
  156.8 1.5 convolution_convert_fusion.4
  158.3 1.3 convolution_convert_fusion.2
  159.6 5.6 %all-to-all-done.3 = f32[32,2,1536]{2,1,0:T(2,128)S(1)} async-done(((f32[32,2,1536]{2,1,0:T(2,128)}), f32[32,2,1536]{2,1,0:T(2,128)S(1)}, u32[]{:S(2)}, u32[]{:S(2)}) %all-to-all-start.3) | async-done | bytes 393248 | tf_op jit(solution)/shard_map/all_to_all | solution.py:148
  165.4 2.2 collective-permute-start
  167.6 1.5 convolution_convert_fusion.3
  169.6 1.8 scatter_custom_fusion
  171.4 1.0 all_to_all.25
  172.3 4.8 %all-to-all-start.1 = ((bf16[32,4,2304]{2,1,0:T(4,128)(2,1)}), bf16[32,4,2304]{2,1,0:T(4,128)(2,1)S(1)}, u32[]{:S(2)}, u32[]{:S(2)}) async-start(bf16[32,4,2304]{2,1,0:T(4,128)(2,1)} %all_to_all.25), calls=%async_computation.1 | async-start | bytes 1179648 | tf_op jit(solution)/shard_map/all_to_all | solution.py:119
  177.2 4.6 %collective-permute-start.1 = (f32[2,2,1536]{2,0,1:T(2,128)S(1)}, f32[2,2,1536]{2,0,1:T(2,128)S(1)}, u32[]{:S(2)}, u32[]{:S(2)}) collective-permute-start(f32[2,2,1536]{2,0,1:T(2,128)S(1)} %maximum_select_fusion.4), channel_id=1, source_target_pairs={{0,32},{16,48},{32,0},{48,16},{64,96},{80,112},{96,64},{112,80},{1... | collective-permute-start | bytes 73736 | tf_op jit(solution)/shard_map/ppermute | solution.py:162
  181.9 1.4 collective-permute-done.1
  183.3 3.9 %collective-permute-start.2 = (f32[4,2,1536]{2,0,1:T(4,128)S(1)}, f32[4,2,1536]{2,0,1:T(4,128)S(1)}, u32[]{:S(2)}, u32[]{:S(2)}) collective-permute-start(f32[4,2,1536]{2,0,1:T(4,128)S(1)} %maximum_select_fusion.3), channel_id=1, source_target_pairs={{0,64},{16,80},{32,96},{48,112},{64,0},{80,16},{96,32},{112,48},{1... | collective-permute-start | bytes 147464 | tf_op jit(solution)/shard_map/ppermute | solution.py:162
  187.3 3.6 %collective-permute-done.2 = f32[4,2,1536]{2,0,1:T(4,128)S(1)} collective-permute-done((f32[4,2,1536]{2,0,1:T(4,128)S(1)}, f32[4,2,1536]{2,0,1:T(4,128)S(1)}, u32[]{:S(2)}, u32[]{:S(2)}) %collective-permute-start.2) | collective-permute-done | bytes 49184 | tf_op jit(solution)/shard_map/ppermute | solution.py:162
  190.9 3.7 %collective-permute-start.3 = (f32[8,2,1536]{2,0,1:T(8,128)S(1)}, f32[8,2,1536]{2,0,1:T(8,128)S(1)}, u32[]{:S(2)}, u32[]{:S(2)}) collective-permute-start(f32[8,2,1536]{2,0,1:T(8,128)S(1)} %maximum_select_fusion.2), channel_id=1, source_target_pairs={{0,128},{16,144},{32,160},{48,176},{64,192},{80,208},{96,224},{112... | collective-permute-start | bytes 294920 | tf_op jit(solution)/shard_map/ppermute | solution.py:162
  194.6 3.8 %collective-permute-done.3 = f32[8,2,1536]{2,0,1:T(8,128)S(1)} collective-permute-done((f32[8,2,1536]{2,0,1:T(8,128)S(1)}, f32[8,2,1536]{2,0,1:T(8,128)S(1)}, u32[]{:S(2)}, u32[]{:S(2)}) %collective-permute-start.3) | collective-permute-done | bytes 98336 | tf_op jit(solution)/shard_map/ppermute | solution.py:162
  198.4 7.1 %collective-permute-start.4 = (f32[16,2,1536]{2,0,1:T(8,128)S(1)}, f32[16,2,1536]{2,0,1:T(8,128)S(1)}, u32[]{:S(2)}, u32[]{:S(2)}) collective-permute-start(f32[16,2,1536]{2,0,1:T(8,128)S(1)} %maximum_select_fusion.1), channel_id=1, source_target_pairs={{0,256},{16,272},{32,288},{48,304},{64,320},{80,336},{96,352},{112... | collective-permute-start | bytes 589832 | tf_op jit(solution)/shard_map/ppermute | solution.py:162
  205.6 2.4 scatter_custom_fusion.1
  208.0 0.8 collective-permute-done.4
  208.9 0.2 copy.81
  209.1 0.9 mul.1323
  210.1 30.8 %all-gather = f32[1,32,1536]{2,0,1:T(1,128)S(1)} all-gather(f32[1,2,1536]{2,0,1:T(1,128)S(1)} %slice.412), channel_id=2, replica_groups=mesh['dp'=32,'fsdp'=16] {'fsdp'}, dimensions={1}, use_global_device_ids=true | all-gather | bytes 208896 | tf_op jit(solution)/shard_map/all_gather | solution.py:127
  240.8 0.2 slice_multiply_fusion.1
  241.0 0.7 copy.89
  (249 shorter events, 2.1 us)
Async XLA Ops:
  7.2 51.1 %all-gather.3.cloned.1.call-start = ((), (), s32[]{:S(2)}) async-start(), calls=%async_computation.5 | async-start | bytes 2506752 | tf_op jit(solution)/shard_map/all_gather | solution.py:92
  10.1 14.9 %copy-start.4 = (f32[31,1536]{1,0:T(8,128)S(1)}, f32[31,1536]{1,0:T(8,128)}, u32[]{:S(2)}) copy-start(f32[31,1536]{1,0:T(8,128)} %param.11) | copy-start | bytes 571396
  10.1 15.7 %copy-start.92 = (s32[128]{0:T(128)S(1)}, s32[128]{0:T(128)}, u32[]{:S(2)}) copy-start(s32[128]{0:T(128)} %param.14) | copy-start | bytes 1540
  10.1 17.2 %copy-start.77 = (s32[128]{0:T(128)S(1)}, s32[128]{0:T(128)}, u32[]{:S(2)}) copy-start(s32[128]{0:T(128)} %param.15) | copy-start | bytes 1540
  11.3 31.2 %all-to-all-start = ((bf16[32,4,2304]{2,1,0:T(4,128)(2,1)}), bf16[32,4,2304]{2,1,0:T(4,128)(2,1)S(1)}, u32[]{:S(2)}, u32[]{:S(2)}) async-start(bf16[32,4,2304]{2,1,0:T(4,128)(2,1)} %all_to_all.22), calls=%async_computation | async-start | bytes 1179648 | tf_op jit(solution)/shard_map/all_to_all | solution.py:84
  25.0 117.6 %reduce-scatter.2.cloned.1.call-start = ((), (), s32[]{:S(2)}) async-start(), calls=%async_computation.6 | async-start | bytes 2506752 | tf_op jit(solution)/shard_map/reduce_scatter | solution.py:101
  28.8 16.7 %copy-start.55 = (pred[128,128]{0,1:T(8,128)(4,1)}, pred[128,128]{0,1:T(8,128)(4,1)S(1)}, u32[]{:S(2)}) copy-start(pred[128,128]{0,1:T(8,128)(4,1)S(1)} %broadcast_compare_fusion) | copy-start | bytes 49156
  45.5 12.8 %copy-start.93 = (f32[8,128]{1,0:T(8,128)}, f32[8,128]{1,0:T(8,128)S(1)}, u32[]{:S(2)}) copy-start(f32[8,128]{1,0:T(8,128)S(1)} %get-tuple-element.142) | copy-start | bytes 12292
  46.0 14.5 %copy-start.1 = (bf16[128,1536]{1,0:T(8,128)(2,1)S(1)}, bf16[128,1536]{1,0:T(8,128)(2,1)}, u32[]{:S(2)}) copy-start(bf16[128,1536]{1,0:T(8,128)(2,1)} %param.12) | copy-start | bytes 1179652
  46.0 14.5 %copy-start.5 = (f32[1536]{0:T(1024)S(1)}, f32[1536]{0:T(1024)}, u32[]{:S(2)}) copy-start(f32[1536]{0:T(1024)} %get-tuple-element.38) | copy-start | bytes 18436
  46.0 14.5 %copy-start.6 = (f32[1536]{0:T(1024)S(1)}, f32[1536]{0:T(1024)}, u32[]{:S(2)}) copy-start(f32[1536]{0:T(1024)} %get-tuple-element.39) | copy-start | bytes 18436
  46.0 14.5 %copy-start.7 = (f32[1536]{0:T(1024)S(1)}, f32[1536]{0:T(1024)}, u32[]{:S(2)}) copy-start(f32[1536]{0:T(1024)} %get-tuple-element.40) | copy-start | bytes 18436
  46.1 14.5 %copy-start.8 = (f32[1536]{0:T(1024)S(1)}, f32[1536]{0:T(1024)}, u32[]{:S(2)}) copy-start(f32[1536]{0:T(1024)} %get-tuple-element.41) | copy-start | bytes 18436
  46.1 14.5 %copy-start.9 = (f32[1536]{0:T(1024)S(1)}, f32[1536]{0:T(1024)}, u32[]{:S(2)}) copy-start(f32[1536]{0:T(1024)} %get-tuple-element.42) | copy-start | bytes 18436
  46.1 14.5 %copy-start.10 = (f32[1536]{0:T(1024)S(1)}, f32[1536]{0:T(1024)}, u32[]{:S(2)}) copy-start(f32[1536]{0:T(1024)} %get-tuple-element.55) | copy-start | bytes 18436
  46.1 14.5 %copy-start.11 = (f32[1536]{0:T(1024)S(1)}, f32[1536]{0:T(1024)}, u32[]{:S(2)}) copy-start(f32[1536]{0:T(1024)} %get-tuple-element.60) | copy-start | bytes 18436
  46.1 14.5 %copy-start.12 = (f32[1536]{0:T(1024)S(1)}, f32[1536]{0:T(1024)}, u32[]{:S(2)}) copy-start(f32[1536]{0:T(1024)} %get-tuple-element.61) | copy-start | bytes 18436
  46.1 14.5 %copy-start.13 = (f32[1536]{0:T(1024)S(1)}, f32[1536]{0:T(1024)}, u32[]{:S(2)}) copy-start(f32[1536]{0:T(1024)} %get-tuple-element.63) | copy-start | bytes 18436
  46.1 14.5 %copy-start.14 = (f32[1536]{0:T(1024)S(1)}, f32[1536]{0:T(1024)}, u32[]{:S(2)}) copy-start(f32[1536]{0:T(1024)} %get-tuple-element.64) | copy-start | bytes 18436
  46.1 14.5 %copy-start.15 = (f32[1536]{0:T(1024)S(1)}, f32[1536]{0:T(1024)}, u32[]{:S(2)}) copy-start(f32[1536]{0:T(1024)} %get-tuple-element.62) | copy-start | bytes 18436
  46.1 14.5 %copy-start.16 = (f32[1536]{0:T(1024)S(1)}, f32[1536]{0:T(1024)}, u32[]{:S(2)}) copy-start(f32[1536]{0:T(1024)} %get-tuple-element.43) | copy-start | bytes 18436
  46.1 14.5 %copy-start.17 = (f32[1536]{0:T(1024)S(1)}, f32[1536]{0:T(1024)}, u32[]{:S(2)}) copy-start(f32[1536]{0:T(1024)} %get-tuple-element.44) | copy-start | bytes 18436
  46.2 14.5 %copy-start.18 = (f32[1536]{0:T(1024)S(1)}, f32[1536]{0:T(1024)}, u32[]{:S(2)}) copy-start(f32[1536]{0:T(1024)} %get-tuple-element.45) | copy-start | bytes 18436
  46.2 14.5 %copy-start.19 = (f32[1536]{0:T(1024)S(1)}, f32[1536]{0:T(1024)}, u32[]{:S(2)}) copy-start(f32[1536]{0:T(1024)} %get-tuple-element.46) | copy-start | bytes 18436
  46.2 14.5 %copy-start.20 = (f32[1536]{0:T(1024)S(1)}, f32[1536]{0:T(1024)}, u32[]{:S(2)}) copy-start(f32[1536]{0:T(1024)} %get-tuple-element.47) | copy-start | bytes 18436
  46.2 14.5 %copy-start.21 = (f32[1536]{0:T(1024)S(1)}, f32[1536]{0:T(1024)}, u32[]{:S(2)}) copy-start(f32[1536]{0:T(1024)} %get-tuple-element.48) | copy-start | bytes 18436
  46.2 14.5 %copy-start.22 = (f32[1536]{0:T(1024)S(1)}, f32[1536]{0:T(1024)}, u32[]{:S(2)}) copy-start(f32[1536]{0:T(1024)} %get-tuple-element.49) | copy-start | bytes 18436
  46.2 14.5 %copy-start.23 = (f32[1536]{0:T(1024)S(1)}, f32[1536]{0:T(1024)}, u32[]{:S(2)}) copy-start(f32[1536]{0:T(1024)} %get-tuple-element.50) | copy-start | bytes 18436
  46.2 14.5 %copy-start.24 = (f32[1536]{0:T(1024)S(1)}, f32[1536]{0:T(1024)}, u32[]{:S(2)}) copy-start(f32[1536]{0:T(1024)} %get-tuple-element.51) | copy-start | bytes 18436
  46.2 14.5 %copy-start.25 = (f32[1536]{0:T(1024)S(1)}, f32[1536]{0:T(1024)}, u32[]{:S(2)}) copy-start(f32[1536]{0:T(1024)} %get-tuple-element.52) | copy-start | bytes 18436
  46.2 14.5 %copy-start.26 = (f32[1536]{0:T(1024)S(1)}, f32[1536]{0:T(1024)}, u32[]{:S(2)}) copy-start(f32[1536]{0:T(1024)} %get-tuple-element.53) | copy-start | bytes 18436
  46.2 14.5 %copy-start.27 = (f32[1536]{0:T(1024)S(1)}, f32[1536]{0:T(1024)}, u32[]{:S(2)}) copy-start(f32[1536]{0:T(1024)} %get-tuple-element.54) | copy-start | bytes 18436
  46.3 14.5 %copy-start.28 = (f32[1536]{0:T(1024)S(1)}, f32[1536]{0:T(1024)}, u32[]{:S(2)}) copy-start(f32[1536]{0:T(1024)} %get-tuple-element.66) | copy-start | bytes 18436
  69.5 3.0 %copy-start.80 = (f32[128]{0:T(128)S(1)}, f32[128]{0:T(128)}, u32[]{:S(2)}) copy-start(f32[128]{0:T(128)} %get-tuple-element.109) | copy-start | bytes 1540
  69.5 3.0 %copy-start.81 = (f32[128]{0:T(128)S(1)}, f32[128]{0:T(128)}, u32[]{:S(2)}) copy-start(f32[128]{0:T(128)} %get-tuple-element.110) | copy-start | bytes 1540
  69.5 3.0 %copy-start.82 = (f32[128]{0:T(128)S(1)}, f32[128]{0:T(128)}, u32[]{:S(2)}) copy-start(f32[128]{0:T(128)} %get-tuple-element.111) | copy-start | bytes 1540
  69.5 3.0 %copy-start.83 = (f32[128]{0:T(128)S(1)}, f32[128]{0:T(128)}, u32[]{:S(2)}) copy-start(f32[128]{0:T(128)} %get-tuple-element.112) | copy-start | bytes 1540
  69.5 3.0 %copy-start.89 = (f32[128]{0:T(128)S(1)}, f32[128]{0:T(128)}, u32[]{:S(2)}) copy-start(f32[128]{0:T(128)} %get-tuple-element.134) | copy-start | bytes 1540
  69.5 3.0 %copy-start.90 = (f32[128]{0:T(128)S(1)}, f32[128]{0:T(128)}, u32[]{:S(2)}) copy-start(f32[128]{0:T(128)} %get-tuple-element.135) | copy-start | bytes 1540
  80.7 2.6 %copy-start.57 = (f32[128]{0:T(128)S(1)}, f32[128]{0:T(128)}, u32[]{:S(2)}) copy-start(f32[128]{0:T(128)} %get-tuple-element.114) | copy-start | bytes 1540
  80.7 2.6 %copy-start.59 = (f32[128]{0:T(128)S(1)}, f32[128]{0:T(128)}, u32[]{:S(2)}) copy-start(f32[128]{0:T(128)} %get-tuple-element.115) | copy-start | bytes 1540
  80.7 2.6 %copy-start.61 = (f32[128]{0:T(128)S(1)}, f32[128]{0:T(128)}, u32[]{:S(2)}) copy-start(f32[128]{0:T(128)} %get-tuple-element.116) | copy-start | bytes 1540
  80.7 2.6 %copy-start.63 = (f32[128]{0:T(128)S(1)}, f32[128]{0:T(128)}, u32[]{:S(2)}) copy-start(f32[128]{0:T(128)} %get-tuple-element.117) | copy-start | bytes 1540
  82.9 2.6 %copy-start.41 = (f32[1536]{0:T(1024)S(1)}, f32[1536]{0:T(1024)}, u32[]{:S(2)}) copy-start(f32[1536]{0:T(1024)} %get-tuple-element.24) | copy-start | bytes 18436
  82.9 2.6 %copy-start.40 = (f32[1536]{0:T(1024)S(1)}, f32[1536]{0:T(1024)}, u32[]{:S(2)}) copy-start(f32[1536]{0:T(1024)} %get-tuple-element.25) | copy-start | bytes 18436
  82.9 2.6 %copy-start.39 = (f32[1536]{0:T(1024)S(1)}, f32[1536]{0:T(1024)}, u32[]{:S(2)}) copy-start(f32[1536]{0:T(1024)} %get-tuple-element.26) | copy-start | bytes 18436
  83.0 2.6 %copy-start.38 = (f32[1536]{0:T(1024)S(1)}, f32[1536]{0:T(1024)}, u32[]{:S(2)}) copy-start(f32[1536]{0:T(1024)} %get-tuple-element.27) | copy-start | bytes 18436
  83.0 2.7 %copy-start.37 = (f32[1536]{0:T(1024)S(1)}, f32[1536]{0:T(1024)}, u32[]{:S(2)}) copy-start(f32[1536]{0:T(1024)} %get-tuple-element.28) | copy-start | bytes 18436
  83.0 2.7 %copy-start.36 = (f32[1536]{0:T(1024)S(1)}, f32[1536]{0:T(1024)}, u32[]{:S(2)}) copy-start(f32[1536]{0:T(1024)} %get-tuple-element.29) | copy-start | bytes 18436
  83.0 2.7 %copy-start.35 = (f32[1536]{0:T(1024)S(1)}, f32[1536]{0:T(1024)}, u32[]{:S(2)}) copy-start(f32[1536]{0:T(1024)} %get-tuple-element.30) | copy-start | bytes 18436
  83.0 2.7 %copy-start.34 = (f32[1536]{0:T(1024)S(1)}, f32[1536]{0:T(1024)}, u32[]{:S(2)}) copy-start(f32[1536]{0:T(1024)} %get-tuple-element.31) | copy-start | bytes 18436
  83.0 2.7 %copy-start.54 = (f32[1536]{0:T(1024)S(1)}, f32[1536]{0:T(1024)}, u32[]{:S(2)}) copy-start(f32[1536]{0:T(1024)} %get-tuple-element.32) | copy-start | bytes 18436
  83.0 2.7 %copy-start.53 = (f32[1536]{0:T(1024)S(1)}, f32[1536]{0:T(1024)}, u32[]{:S(2)}) copy-start(f32[1536]{0:T(1024)} %get-tuple-element.33) | copy-start | bytes 18436
  83.0 2.7 %copy-start.52 = (f32[1536]{0:T(1024)S(1)}, f32[1536]{0:T(1024)}, u32[]{:S(2)}) copy-start(f32[1536]{0:T(1024)} %get-tuple-element.34) | copy-start | bytes 18436
  86.9 15.1 %all-to-all-start.2 = ((f32[16,2,1536]{2,1,0:T(2,128)}), f32[16,2,1536]{2,1,0:T(2,128)S(1)}, u32[]{:S(2)}, u32[]{:S(2)}) async-start(f32[16,2,1536]{2,1,0:T(2,128)} %reshape.304), calls=%async_computation.3 | async-start | bytes 393216 | tf_op jit(solution)/shard_map/all_to_all | solution.py:140
  144.5 12.3 %copy-start.3 = (bf16[128,768]{0,1:T(8,128)(2,1)S(1)}, bf16[128,768]{0,1:T(8,128)(2,1)}, u32[]{:S(2)}) copy-start(bf16[128,768]{0,1:T(8,128)(2,1)} %copy-done.2) | copy-start | bytes 589828
  144.5 12.3 %copy-start.94 = (f32[8,128]{1,0:T(8,128)S(1)}, f32[8,128]{1,0:T(8,128)}, u32[]{:S(2)}) copy-start(f32[8,128]{1,0:T(8,128)} %copy-done.93) | copy-start | bytes 12292
  144.5 20.7 %all-to-all-start.3 = ((f32[32,2,1536]{2,1,0:T(2,128)}), f32[32,2,1536]{2,1,0:T(2,128)S(1)}, u32[]{:S(2)}, u32[]{:S(2)}) async-start(f32[32,2,1536]{2,1,0:T(2,128)} %reshape.305), calls=%async_computation.4 | async-start | bytes 786432 | tf_op jit(solution)/shard_map/all_to_all | solution.py:148
  165.4 11.7 %collective-permute-start = (f32[1,2,1536]{2,0,1:T(1,128)S(1)}, f32[1,2,1536]{2,0,1:T(1,128)S(1)}, u32[]{:S(2)}, u32[]{:S(2)}) collective-permute-start(f32[1,2,1536]{2,0,1:T(1,128)S(1)} %broadcast_in_dim.51), channel_id=1, source_target_pairs={{0,16},{16,0},{32,48},{48,32},{64,80},{80,64},{96,112},{112,96},{1... | collective-permute-start | bytes 36872 | tf_op jit(solution)/shard_map/ppermute | solution.py:162
  172.3 33.2 %all-to-all-start.1 = ((bf16[32,4,2304]{2,1,0:T(4,128)(2,1)}), bf16[32,4,2304]{2,1,0:T(4,128)(2,1)S(1)}, u32[]{:S(2)}, u32[]{:S(2)}) async-start(bf16[32,4,2304]{2,1,0:T(4,128)(2,1)} %all_to_all.25), calls=%async_computation.1 | async-start | bytes 1179648 | tf_op jit(solution)/shard_map/all_to_all | solution.py:119
  177.2 6.1 %collective-permute-start.1 = (f32[2,2,1536]{2,0,1:T(2,128)S(1)}, f32[2,2,1536]{2,0,1:T(2,128)S(1)}, u32[]{:S(2)}, u32[]{:S(2)}) collective-permute-start(f32[2,2,1536]{2,0,1:T(2,128)S(1)} %maximum_select_fusion.4), channel_id=1, source_target_pairs={{0,32},{16,48},{32,0},{48,16},{64,96},{80,112},{96,64},{112,80},{1... | collective-permute-start | bytes 73736 | tf_op jit(solution)/shard_map/ppermute | solution.py:162
  183.3 7.5 %collective-permute-start.2 = (f32[4,2,1536]{2,0,1:T(4,128)S(1)}, f32[4,2,1536]{2,0,1:T(4,128)S(1)}, u32[]{:S(2)}, u32[]{:S(2)}) collective-permute-start(f32[4,2,1536]{2,0,1:T(4,128)S(1)} %maximum_select_fusion.3), channel_id=1, source_target_pairs={{0,64},{16,80},{32,96},{48,112},{64,0},{80,16},{96,32},{112,48},{1... | collective-permute-start | bytes 147464 | tf_op jit(solution)/shard_map/ppermute | solution.py:162
  190.9 7.5 %collective-permute-start.3 = (f32[8,2,1536]{2,0,1:T(8,128)S(1)}, f32[8,2,1536]{2,0,1:T(8,128)S(1)}, u32[]{:S(2)}, u32[]{:S(2)}) collective-permute-start(f32[8,2,1536]{2,0,1:T(8,128)S(1)} %maximum_select_fusion.2), channel_id=1, source_target_pairs={{0,128},{16,144},{32,160},{48,176},{64,192},{80,208},{96,224},{112... | collective-permute-start | bytes 294920 | tf_op jit(solution)/shard_map/ppermute | solution.py:162
  198.4 10.4 %collective-permute-start.4 = (f32[16,2,1536]{2,0,1:T(8,128)S(1)}, f32[16,2,1536]{2,0,1:T(8,128)S(1)}, u32[]{:S(2)}, u32[]{:S(2)}) collective-permute-start(f32[16,2,1536]{2,0,1:T(8,128)S(1)} %maximum_select_fusion.1), channel_id=1, source_target_pairs={{0,256},{16,272},{32,288},{48,304},{64,320},{80,336},{96,352},{112... | collective-permute-start | bytes 589832 | tf_op jit(solution)/shard_map/ppermute | solution.py:162
  (42 other events, 87.9 us)
Sparse Core Ops, SparseCore 0:
  10.1 48.0 all-gather.2
  83.2 59.3 reduce-scatter.1

commit v5 on v0

--- a/solution.py
+++ b/solution.py
@@ -1,7 +1,10 @@
 import jax
 import jax.numpy as jnp
 from jax import lax
-from jax.sharding import PartitionSpec as P
+from jax.sharding import Mesh, PartitionSpec as P
+
+DP = ("dz", "dx")
+FSDP = ("fy", "fc")
 
 HEADS = 8
 HEAD_DIM = 96
@@ -81,7 +84,7 @@
     present = send_rows >= 0
     outgoing = jnp.take(projected, jnp.maximum(send_rows, 0), axis=0)
     outgoing = jnp.where(present[:, None], outgoing, jnp.zeros_like(outgoing))
-    incoming = lax.all_to_all(outgoing, "dp", split_axis=0, concat_axis=0, tiled=True)
+    incoming = lax.all_to_all(outgoing, DP, split_axis=0, concat_axis=0, tiled=True)
     filled = compute_src >= 0
     frames = jnp.take(incoming, jnp.maximum(compute_src, 0), axis=0)
     frames = jnp.where(filled[:, None], frames, jnp.zeros_like(frames))
@@ -89,7 +92,7 @@
     columns = context
     mixed_sums = jnp.dot(
         columns,
-        lax.all_gather(out_weight, "fsdp", axis=0, tiled=True),
+        lax.all_gather(out_weight, FSDP, axis=0, tiled=True),
         preferred_element_type=jnp.float32,
     )
     mixed = mixed_sums.astype(jnp.bfloat16)
@@ -102,26 +105,34 @@
         jnp.einsum("rc,rd->cd", columns, mixed_grad, preferred_element_type=jnp.float32).astype(
             jnp.bfloat16
         ),
-        "fsdp",
+        FSDP,
         scatter_dimension=0,
         tiled=True,
     ).astype(jnp.float32)
     context_grad = jnp.einsum(
         "rd,cd->rc",
         mixed_grad,
-        lax.all_gather(out_weight, "fsdp", axis=0, tiled=True),
+        lax.all_gather(out_weight, FSDP, axis=0, tiled=True),
         preferred_element_type=jnp.float32,
     ).astype(jnp.bfloat16)
     frame_grad = attend_back(frames, soft_probs, rounded, context_grad)
     slot_total = incoming.shape[0]
     back_index = jnp.where(filled, compute_src, slot_total)
     returning = jnp.zeros_like(incoming).at[back_index].set(frame_grad, mode="drop")
-    arrived = lax.all_to_all(returning, "dp", split_axis=0, concat_axis=0, tiled=True)
+    arrived = lax.all_to_all(returning, DP, split_axis=0, concat_axis=0, tiled=True)
     source_index = jnp.where(present, send_rows, row_count)
     projected_grad = jnp.zeros_like(projected).at[source_index].set(arrived, mode="drop")
-    scale_factor = (row_count * lax.axis_size("dp") * lax.axis_size("fsdp")) ** (-0.5)
-    weight_total = lax.psum(weight_share, "dp")
-    kernel_total = lax.psum(kernel_part, ("dp", "fsdp"))
+    scale_factor = (row_count * lax.axis_size(DP) * lax.axis_size(FSDP)) ** (-0.5)
+    kernel_piece = sum_rows(kernel_part, FSDP)
+    owned_rows = weight_share.shape[0]
+    both = jnp.concatenate([weight_share, kernel_piece], axis=0)
+    inner = sum_rows(both, "dx")
+    inner_rows = inner.shape[0]
+    inner = gather_rows(sum_rows(inner, "dz"), "dz")[:inner_rows]
+    both = gather_rows(inner, "dx")[: both.shape[0]]
+    weight_total = both[:owned_rows]
+    kernel_total = gather_rows(gather_rows(both[owned_rows:], "fc"), "fy")[: kernel.shape[0]]
+
     return (
         result.astype(jnp.bfloat16),
         projected_grad,
@@ -130,20 +141,35 @@
     )
 
 
+def sum_rows(x, axis):
+    count = lax.axis_size(axis)
+    per = -(-x.shape[0] // count)
+    padded = jnp.pad(x, ((0, count * per - x.shape[0]), (0, 0)))
+    got = lax.all_to_all(padded.reshape(count, per, x.shape[1]), axis, split_axis=0, concat_axis=0, tiled=True)
+    return jnp.sum(got, axis=0)
+
+
+def gather_rows(piece, axis):
+    return lax.all_gather(piece, axis, axis=0, tiled=True)
+
 def solution(mesh):
+    dp_count, fsdp_count = mesh.devices.shape
+    fine = Mesh(
+        mesh.devices.reshape(dp_count // 4, 4, fsdp_count // 2, 2), ("dz", "dx", "fy", "fc")
+    )
     placed = (
-        P(("dp", "fsdp"), None),
-        P("fsdp", None),
+        P((*DP, *FSDP), None),
+        P(FSDP, None),
         P(),
-        P(("dp", "fsdp"), None),
-        P(("dp", "fsdp")),
-        P(("dp", "fsdp")),
-        P(("dp", "fsdp")),
+        P((*DP, *FSDP), None),
+        P((*DP, *FSDP)),
+        P((*DP, *FSDP)),
+        P((*DP, *FSDP)),
     )
     return jax.shard_map(
         body,
-        mesh=mesh,
+        mesh=fine,
         in_specs=placed,
-        out_specs=(P(("dp", "fsdp"), None), P(("dp", "fsdp"), None), P("fsdp", None), P()),
+        out_specs=(P((*DP, *FSDP), None), P((*DP, *FSDP), None), P(FSDP, None), P()),
         check_vma=False,
     )

time: 567 us -> 266 us (0.47)
  the two profiles are of different devices: /device:TPU:8 before, /device:TPU:24 now
where the time goes in v5:
time: 266 us
  waiting for transfers between devices  98.8 us (37%)
  blocking collectives  63.6 us (24%)
  starting transfers between devices  36.2 us (14%)
  other arithmetic  26.7 us (10%)
  between operations  15.3 us (6%)
  matrix products  13.3 us (5%)
  local copies, waits for them, and re-layouts  11.6 us (4%)
    all_gather x4, blocking collectives, gather_rows(): return lax.all_gather(piece, axis, axis=0, tiled=True)  63.6 us
    reduce_scatter x1, waiting for transfers between devices, body(): lax.psum_scatter(jnp.einsum('rc,rd->cd', columns, mixed_grad, preferred_e...  41.8 us
    all_to_all x1, waiting for transfers between devices, body(): lax.all_to_all(returning, DP, split_axis=0, concat_axis=0, tiled=True)  18 us
    all_to_all x1, waiting for transfers between devices, body(): lax.all_to_all(outgoing, DP, split_axis=0, concat_axis=0, tiled=True)  17.5 us
    reduce_sum x4, other arithmetic, finish(): kernel[offset] * padded[offset:offset + length] * matching[:, None]  14.6 us
    all_to_all x3, starting transfers between devices, sum_rows(): lax.all_to_all(padded.reshape(count, per, x.shape[1]), axis, split_axis=0...  13.4 us
    all_to_all x1, starting transfers between devices, body(): lax.all_to_all(outgoing, DP, split_axis=0, concat_axis=0, tiled=True)  13.2 us
    all_to_all x3, waiting for transfers between devices, sum_rows(): lax.all_to_all(padded.reshape(count, per, x.shape[1]), axis, split_axis=0...  12 us
  transfers between devices with their start and end apart: 7, of which 7 were waited for; matrix products, arithmetic and copies ran while one was open for 9% of the time, Pallas kernels for 0%

profile of v5, /device:TPU:24, one launch (start us, length us, event | category | flops | bytes accessed | tf_op | source)
XLA Modules:
  0.0 265.6 jit_solution(12610258095926007026)
XLA Ops:
  7.2 0.7 all-gather.6.cloned.1.call-update
  7.9 1.2 compare_select_fusion.1
  9.2 1.0 gather_fusion
  10.2 0.2 select_select_fusion.1
  10.4 1.0 all_to_all.25
  11.3 13.2 %all-to-all-start = ((bf16[32,4,2304]{2,1,0:T(4,128)(2,1)}), bf16[32,4,2304]{2,1,0:T(4,128)(2,1)S(1)}, u32[]{:S(2)}, u32[]{:S(2)}) async-start(bf16[32,4,2304]{2,1,0:T(4,128)(2,1)} %all_to_all.25), calls=%async_computation | async-start | bytes 1179648 | tf_op jit(solution)/shard_map/all_to_all | solution.py:87
  24.5 0.2 slice_reduce_fusion.29
  24.7 0.5 compare_select_fusion
  25.3 0.3 slice_reduce_fusion.30
  26.0 17.5 %all-to-all-done = bf16[32,4,2304]{2,1,0:T(4,128)(2,1)S(1)} async-done(((bf16[32,4,2304]{2,1,0:T(4,128)(2,1)}), bf16[32,4,2304]{2,1,0:T(4,128)(2,1)S(1)}, u32[]{:S(2)}, u32[]{:S(2)}) %all-to-all-start) | async-done | bytes 589856 | tf_op jit(solution)/shard_map/all_to_all | solution.py:87
  43.5 0.1 all_to_all.27
  43.6 1.0 gather_fusion.1
  44.6 0.2 select_select_fusion
  44.8 0.2 copy.58
  45.0 0.2 copy.57
  45.1 0.2 copy.56
  45.3 1.2 fusion.39
  46.5 0.6 copy-done.47
  47.1 0.5 convolution_convert_fusion.6
  47.6 8.8 %all-gather.6.cloned.1.call-done = bf16[768,1536]{1,0:T(8,128)(2,1)} async-done(((bf16[48,1536]{1,0:T(8,128)(2,1)}), bf16[768,1536]{1,0:T(8,128)(2,1)}) %all-gather.6.cloned.1.call-update) | async-done | bytes 2359312 | tf_op jit(solution)/shard_map/all_gather | solution.py:95
  56.4 2.2 fusion.2
  58.6 7.7 %multiply_reduce_fusion.31 = (f32[1536]{0:T(1024)}, f32[1536]{0:T(1024)}, f32[1536]{0:T(1024)}, f32[1536]{0:T(1024)}, f32[1536]{0:T(1024)}, /*index=5*/f32[1536]...) fusion(f32[128,1536]{1,0:T(8,128)S(1)} %fusion.2, ...), kind=kLoop, calls=%fused_computation.99 | loop fusion | flops 25152000 | bytes 3013632 | tf_op jit(solution)/shard_map/transpose(jvp())/reduce_sum | solution.py:77
  66.3 2.3 multiply_reduce_fusion.16
  68.6 0.5 multiply_multiply_fusion.27
  69.1 0.7 multiply_multiply_fusion.29
  69.9 0.7 multiply_multiply_fusion.28
  70.6 2.6 multiply_reduce_fusion.4
  73.3 2.6 pad_add_fusion
  75.9 0.7 fusion.16
  76.7 2.2 convolution_convert_fusion
  79.3 2.0 multiply_reduce_fusion.22
  81.7 0.3 pad_add_fusion.7
  82.0 0.8 reshape.301
  82.8 5.2 %all-to-all-start.2 = ((f32[16,2,1536]{2,1,0:T(2,128)}), f32[16,2,1536]{2,1,0:T(2,128)S(1)}, u32[]{:S(2)}, u32[]{:S(2)}) async-start(f32[16,2,1536]{2,1,0:T(2,128)} %reshape.301), calls=%async_computation.3 | async-start | bytes 393216 | tf_op jit(solution)/shard_map/all_to_all | solution.py:148
  88.0 2.5 convolution_convert_fusion.5
  90.6 0.2 copy.60
  90.8 1.3 convolution_convert_fusion.2
  92.0 0.3 fusion.40
  92.3 3.7 %all-to-all-done.2 = f32[16,2,1536]{2,1,0:T(2,128)S(1)} async-done(((f32[16,2,1536]{2,1,0:T(2,128)}), f32[16,2,1536]{2,1,0:T(2,128)S(1)}, u32[]{:S(2)}, u32[]{:S(2)}) %all-to-all-start.2) | async-done | bytes 196640 | tf_op jit(solution)/shard_map/all_to_all | solution.py:148
  96.1 41.8 %reduce-scatter.2.cloned.1.call-done = bf16[48,1536]{1,0:T(8,128)(2,1)} async-done(((bf16[768,1536]{1,0:T(8,128)(2,1)}), bf16[48,1536]{1,0:T(8,128)(2,1)}) %reduce-scatter.2.cloned.1.call-update) | async-done | bytes 147472 | tf_op jit(solution)/shard_map/reduce_scatter | solution.py:104
  137.9 0.9 convert_element_type.218
  138.9 0.8 reshape.302
  139.7 4.1 %all-to-all-start.3 = ((f32[4,13,1536]{2,1,0:T(8,128)}), f32[4,13,1536]{2,1,0:T(8,128)S(1)}, u32[]{:S(2)}, u32[]{:S(2)}) async-start(f32[4,13,1536]{2,1,0:T(8,128)} %reshape.302), calls=%async_computation.4 | async-start | bytes 786432 | tf_op jit(solution)/shard_map/all_to_all | solution.py:148
  143.8 1.6 convolution_convert_fusion.3
  145.4 0.1 copy.66
  145.6 0.1 copy.65
  145.7 1.6 convolution_convert_fusion.4
  147.3 0.1 copy.64
  147.5 1.8 scatter_custom_fusion
  149.2 1.0 all_to_all.28
  150.2 1.3 all-to-all-done.3
  151.5 9.5 %all-to-all-start.1 = ((bf16[32,4,2304]{2,1,0:T(4,128)(2,1)}), bf16[32,4,2304]{2,1,0:T(4,128)(2,1)S(1)}, u32[]{:S(2)}, u32[]{:S(2)}) async-start(bf16[32,4,2304]{2,1,0:T(4,128)(2,1)} %all_to_all.28), calls=%async_computation.1 | async-start | bytes 1179648 | tf_op jit(solution)/shard_map/all_to_all | solution.py:122
  161.1 0.7 reshape.303
  161.8 18.0 %all-to-all-done.1 = bf16[32,4,2304]{2,1,0:T(4,128)(2,1)S(1)} async-done(((bf16[32,4,2304]{2,1,0:T(4,128)(2,1)}), bf16[32,4,2304]{2,1,0:T(4,128)(2,1)S(1)}, u32[]{:S(2)}, u32[]{:S(2)}) %all-to-all-start.1) | async-done | bytes 589856 | tf_op jit(solution)/shard_map/all_to_all | solution.py:122
  179.8 4.1 %all-to-all-start.4 = ((f32[8,2,1536]{2,1,0:T(2,128)}), f32[8,2,1536]{2,1,0:T(2,128)S(1)}, u32[]{:S(2)}, u32[]{:S(2)}) async-start(f32[8,2,1536]{2,1,0:T(2,128)} %reshape.303), calls=%async_computation.5 | async-start | bytes 196608 | tf_op jit(solution)/shard_map/all_to_all | solution.py:148
  183.8 0.1 reshape.332
  184.0 2.4 scatter_custom_fusion.1
  186.4 7.0 %all-to-all-done.4 = f32[8,2,1536]{2,1,0:T(2,128)S(1)} async-done(((f32[8,2,1536]{2,1,0:T(2,128)}), f32[8,2,1536]{2,1,0:T(2,128)S(1)}, u32[]{:S(2)}, u32[]{:S(2)}) %all-to-all-start.4) | async-done | bytes 98336 | tf_op jit(solution)/shard_map/all_to_all | solution.py:148
  193.4 24.6 %all-gather = f32[8,2,1536]{2,1,0:T(2,128)S(1)} all-gather(f32[1,2,1536]{2,1,0:T(2,128)S(1)} %bitcast.58), channel_id=1, replica_groups=mesh['dz'=8,'dx'=4,'fy'=8,'fc'=2] {'dz'}, dimensions={0}, use_global_device_ids=true | all-gather | bytes 110592 | tf_op jit(solution)/shard_map/all_gather | solution.py:153
  218.1 12.5 %all-gather.1 = f32[4,13,1536]{2,1,0:T(8,128)S(1)} all-gather(f32[1,13,1536]{2,1,0:T(8,128)S(1)} %slice_bitcast_fusion), channel_id=1, replica_groups=mesh['dz'=8,'dx'=4,'fy'=8,'fc'=2] {'dx'}, dimensions={0}, use_global_device_ids=true | all-gather | bytes 399360 | tf_op jit(solution)/shard_map/all_gather | solution.py:153
  230.7 0.7 slice_multiply_fusion
  231.5 1.8 all-gather.2
  233.3 24.7 %all-gather.3 = f32[8,4,1536]{2,1,0:T(4,128)S(1)} all-gather(f32[1,4,1536]{2,1,0:T(4,128)S(1)} %reshape.346), channel_id=1, replica_groups=mesh['dz'=8,'dx'=4,'fy'=8,'fc'=2] {'fy'}, dimensions={0}, use_global_device_ids=true | all-gather | bytes 221184 | tf_op jit(solution)/shard_map/all_gather | solution.py:153
  258.1 0.7 slice_multiply_fusion.1
  (151 shorter events, 1.3 us)
Async XLA Ops:
  7.2 2.0 copy-start
  7.2 49.2 %all-gather.6.cloned.1.call-start = ((), (), s32[]{:S(2)}) async-start(), calls=%async_computation.6 | async-start | bytes 2506752 | tf_op jit(solution)/shard_map/all_gather | solution.py:95
  9.1 1.0 copy-start.45
  10.1 14.4 %copy-start.4 = (f32[31,1536]{1,0:T(8,128)S(1)}, f32[31,1536]{1,0:T(8,128)}, u32[]{:S(2)}) copy-start(f32[31,1536]{1,0:T(8,128)} %param.11) | copy-start | bytes 571396
  10.2 14.6 %copy-start.46 = (s32[128]{0:T(128)S(1)}, s32[128]{0:T(128)}, u32[]{:S(2)}) copy-start(s32[128]{0:T(128)} %param.14) | copy-start | bytes 1540
  10.2 15.5 %copy-start.44 = (s32[128]{0:T(128)S(1)}, s32[128]{0:T(128)}, u32[]{:S(2)}) copy-start(s32[128]{0:T(128)} %param.15) | copy-start | bytes 1540
  11.3 32.2 %all-to-all-start = ((bf16[32,4,2304]{2,1,0:T(4,128)(2,1)}), bf16[32,4,2304]{2,1,0:T(4,128)(2,1)S(1)}, u32[]{:S(2)}, u32[]{:S(2)}) async-start(bf16[32,4,2304]{2,1,0:T(4,128)(2,1)} %all_to_all.25), calls=%async_computation | async-start | bytes 1179648 | tf_op jit(solution)/shard_map/all_to_all | solution.py:87
  24.5 113.5 %reduce-scatter.2.cloned.1.call-start = ((), (), s32[]{:S(2)}) async-start(), calls=%async_computation.7 | async-start | bytes 2506752 | tf_op jit(solution)/shard_map/reduce_scatter | solution.py:104
  25.8 43.3 %copy-start.38 = (f32[128]{0:T(128)}, f32[128]{0:T(128)S(1)}, u32[]{:S(2)}) copy-start(f32[128]{0:T(128)S(1)} %get-tuple-element.120) | copy-start | bytes 1540
  25.8 43.3 %copy-start.40 = (f32[128]{0:T(128)}, f32[128]{0:T(128)S(1)}, u32[]{:S(2)}) copy-start(f32[128]{0:T(128)S(1)} %get-tuple-element.121) | copy-start | bytes 1540
  25.8 43.3 %copy-start.42 = (f32[128]{0:T(128)}, f32[128]{0:T(128)S(1)}, u32[]{:S(2)}) copy-start(f32[128]{0:T(128)S(1)} %get-tuple-element.122) | copy-start | bytes 1540
  25.9 44.0 %copy-start.26 = (f32[128]{0:T(128)}, f32[128]{0:T(128)S(1)}, u32[]{:S(2)}) copy-start(f32[128]{0:T(128)S(1)} %get-tuple-element.114) | copy-start | bytes 1540
  25.9 44.0 %copy-start.28 = (f32[128]{0:T(128)}, f32[128]{0:T(128)S(1)}, u32[]{:S(2)}) copy-start(f32[128]{0:T(128)S(1)} %get-tuple-element.115) | copy-start | bytes 1540
  25.9 44.0 %copy-start.30 = (f32[128]{0:T(128)}, f32[128]{0:T(128)S(1)}, u32[]{:S(2)}) copy-start(f32[128]{0:T(128)S(1)} %get-tuple-element.116) | copy-start | bytes 1540
  25.9 44.0 %copy-start.32 = (f32[128]{0:T(128)}, f32[128]{0:T(128)S(1)}, u32[]{:S(2)}) copy-start(f32[128]{0:T(128)S(1)} %get-tuple-element.117) | copy-start | bytes 1540
  25.9 44.0 %copy-start.34 = (f32[128]{0:T(128)}, f32[128]{0:T(128)S(1)}, u32[]{:S(2)}) copy-start(f32[128]{0:T(128)S(1)} %get-tuple-element.118) | copy-start | bytes 1540
  25.9 44.0 %copy-start.36 = (f32[128]{0:T(128)}, f32[128]{0:T(128)S(1)}, u32[]{:S(2)}) copy-start(f32[128]{0:T(128)S(1)} %get-tuple-element.119) | copy-start | bytes 1540
  26.0 20.5 %copy-start.25 = (pred[128,128]{0,1:T(8,128)(4,1)}, pred[128,128]{0,1:T(8,128)(4,1)S(1)}, u32[]{:S(2)}) copy-start(pred[128,128]{0,1:T(8,128)(4,1)S(1)} %broadcast_compare_fusion) | copy-start | bytes 49156
  45.1 11.3 %copy-start.2 = (bf16[128,768]{0,1:T(8,128)(2,1)}, bf16[128,768]{0,1:T(8,128)(2,1)S(1)}, u32[]{:S(2)}) copy-start(bf16[128,768]{0,1:T(8,128)(2,1)S(1)} %copy.57) | copy-start | bytes 589828
  46.5 0.6 copy-start.47
  47.6 11.0 %copy-start.1 = (bf16[128,1536]{1,0:T(8,128)(2,1)S(1)}, bf16[128,1536]{1,0:T(8,128)(2,1)}, u32[]{:S(2)}) copy-start(bf16[128,1536]{1,0:T(8,128)(2,1)} %param.12) | copy-start | bytes 1179652
  76.5 2.4 copy-start.20
  76.6 2.5 copy-start.19
  76.6 2.5 copy-start.18
  76.6 2.5 copy-start.17
  76.6 2.5 copy-start.16
  76.6 2.5 copy-start.15
  76.6 2.5 copy-start.14
  76.6 2.5 copy-start.13
  76.6 2.6 copy-start.12
  76.6 2.6 copy-start.27
  76.6 2.6 copy-start.29
  76.7 2.6 copy-start.31
  76.7 2.6 copy-start.33
  76.7 2.6 copy-start.35
  76.7 2.6 copy-start.37
  76.7 2.6 copy-start.39
  76.7 2.6 copy-start.41
  76.7 2.6 copy-start.43
  78.9 2.5 copy-start.11
  78.9 2.5 copy-start.10
  78.9 2.6 copy-start.9
  78.9 2.6 copy-start.8
  78.9 2.6 copy-start.7
  78.9 2.6 copy-start.6
  78.9 2.6 copy-start.5
  78.9 2.7 %copy-start.24 = (f32[1536]{0:T(1024)S(1)}, f32[1536]{0:T(1024)}, u32[]{:S(2)}) copy-start(f32[1536]{0:T(1024)} %get-tuple-element.32) | copy-start | bytes 18436
  78.9 2.7 %copy-start.23 = (f32[1536]{0:T(1024)S(1)}, f32[1536]{0:T(1024)}, u32[]{:S(2)}) copy-start(f32[1536]{0:T(1024)} %get-tuple-element.33) | copy-start | bytes 18436
  78.9 2.7 %copy-start.22 = (f32[1536]{0:T(1024)S(1)}, f32[1536]{0:T(1024)}, u32[]{:S(2)}) copy-start(f32[1536]{0:T(1024)} %get-tuple-element.34) | copy-start | bytes 18436
  79.0 2.7 %copy-start.21 = (f32[1536]{0:T(1024)S(1)}, f32[1536]{0:T(1024)}, u32[]{:S(2)}) copy-start(f32[1536]{0:T(1024)} %get-tuple-element.35) | copy-start | bytes 18436
  81.7 9.1 %copy-start.3 = (bf16[128,768]{0,1:T(8,128)(2,1)S(1)}, bf16[128,768]{0,1:T(8,128)(2,1)}, u32[]{:S(2)}) copy-start(bf16[128,768]{0,1:T(8,128)(2,1)} %copy-done.2) | copy-start | bytes 589828
  81.7 9.0 %copy-start.48 = (f32[8,128]{1,0:T(8,128)S(1)}, f32[8,128]{1,0:T(8,128)}, u32[]{:S(2)}) copy-start(f32[8,128]{1,0:T(8,128)} %copy-done.47) | copy-start | bytes 12292
  82.8 13.2 %all-to-all-start.2 = ((f32[16,2,1536]{2,1,0:T(2,128)}), f32[16,2,1536]{2,1,0:T(2,128)S(1)}, u32[]{:S(2)}, u32[]{:S(2)}) async-start(f32[16,2,1536]{2,1,0:T(2,128)} %reshape.301), calls=%async_computation.3 | async-start | bytes 393216 | tf_op jit(solution)/shard_map/all_to_all | solution.py:148
  139.7 11.8 %all-to-all-start.3 = ((f32[4,13,1536]{2,1,0:T(8,128)}), f32[4,13,1536]{2,1,0:T(8,128)S(1)}, u32[]{:S(2)}, u32[]{:S(2)}) async-start(f32[4,13,1536]{2,1,0:T(8,128)} %reshape.302), calls=%async_computation.4 | async-start | bytes 786432 | tf_op jit(solution)/shard_map/all_to_all | solution.py:148
  151.5 28.3 %all-to-all-start.1 = ((bf16[32,4,2304]{2,1,0:T(4,128)(2,1)}), bf16[32,4,2304]{2,1,0:T(4,128)(2,1)S(1)}, u32[]{:S(2)}, u32[]{:S(2)}) async-start(bf16[32,4,2304]{2,1,0:T(4,128)(2,1)} %all_to_all.28), calls=%async_computation.1 | async-start | bytes 1179648 | tf_op jit(solution)/shard_map/all_to_all | solution.py:122
  179.8 13.6 %all-to-all-start.4 = ((f32[8,2,1536]{2,1,0:T(2,128)}), f32[8,2,1536]{2,1,0:T(2,128)S(1)}, u32[]{:S(2)}, u32[]{:S(2)}) async-start(f32[8,2,1536]{2,1,0:T(2,128)} %reshape.303), calls=%async_computation.5 | async-start | bytes 196608 | tf_op jit(solution)/shard_map/all_to_all | solution.py:148
Sparse Core Ops, SparseCore 0:
  10.1 46.2 all-gather.5
  79.1 58.7 reduce-scatter.1

commit v6 on v5

--- a/solution.py
+++ b/solution.py
@@ -123,6 +123,7 @@
     source_index = jnp.where(present, send_rows, row_count)
     projected_grad = jnp.zeros_like(projected).at[source_index].set(arrived, mode="drop")
     scale_factor = (row_count * lax.axis_size(DP) * lax.axis_size(FSDP)) ** (-0.5)
+    weight_share, arrived = lax.optimization_barrier((weight_share, arrived))
     kernel_piece = sum_rows(kernel_part, FSDP)
     owned_rows = weight_share.shape[0]
     both = jnp.concatenate([weight_share, kernel_piece], axis=0)
@@ -150,7 +151,10 @@
 
 
 def gather_rows(piece, axis):
-    return lax.all_gather(piece, axis, axis=0, tiled=True)
+    count = lax.axis_size(axis)
+    copies = jnp.broadcast_to(piece[None], (count, *piece.shape))
+    got = lax.all_to_all(copies, axis, split_axis=0, concat_axis=0, tiled=True)
+    return got.reshape(count * piece.shape[0], piece.shape[1])
 
 def solution(mesh):
     dp_count, fsdp_count = mesh.devices.shape

time: 266 us -> 221 us (0.83)
  the two profiles are of different devices: /device:TPU:24 before, /device:TPU:1 now
where the time goes in v6:
time: 221 us; the launch traced here: 220 us
  waiting for transfers between devices  71.1 us (32%)
  blocking collectives  45.6 us (21%)
  starting transfers between devices  36.3 us (16%)
  other arithmetic  26.7 us (12%)
  between operations  15.3 us (7%)
  matrix products  13.3 us (6%)
  local copies, waits for them, and re-layouts  11.7 us (5%)
    all_to_all x2, blocking collectives, sum_rows(): lax.all_to_all(padded.reshape(count, per, x.shape[1]), axis, split_axis=0...  23.9 us
    all_to_all x2, blocking collectives, gather_rows(): got = lax.all_to_all(copies, axis, split_axis=0, concat_axis=0, tiled=True)  21.8 us
    all_to_all x1, waiting for transfers between devices, body(): lax.all_to_all(returning, DP, split_axis=0, concat_axis=0, tiled=True)  17.9 us
    all_to_all x1, waiting for transfers between devices, body(): lax.all_to_all(outgoing, DP, split_axis=0, concat_axis=0, tiled=True)  16 us
    reduce_sum x4, other arithmetic, finish(): kernel[offset] * padded[offset:offset + length] * matching[:, None]  14.6 us
    all_to_all x1, starting transfers between devices, body(): lax.all_to_all(outgoing, DP, split_axis=0, concat_axis=0, tiled=True)  13.7 us
    all_to_all x2, waiting for transfers between devices, gather_rows(): got = lax.all_to_all(copies, axis, split_axis=0, concat_axis=0, tiled=True)  12.5 us
    reduce_scatter x1, waiting for transfers between devices, body(): lax.psum_scatter(jnp.einsum('rc,rd->cd', columns, mixed_grad, preferred_e...  12.4 us
  transfers between devices with their start and end apart: 7, of which 6 were waited for; matrix products, arithmetic and copies ran while one was open for 11% of the time, Pallas kernels for 0%

profile of v6, /device:TPU:1, one launch (start us, length us, event | category | flops | bytes accessed | tf_op | source)
XLA Modules:
  0.0 220.1 jit_solution(1403677261969724617)
XLA Ops:
  7.2 0.7 all-gather.2.cloned.1.call-update
  7.9 1.2 compare_select_fusion.1
  9.2 1.0 gather_fusion
  10.2 0.2 select_select_fusion.1
  10.4 1.0 all_to_all.37
  11.3 13.7 %all-to-all-start = ((bf16[32,4,2304]{2,1,0:T(4,128)(2,1)}), bf16[32,4,2304]{2,1,0:T(4,128)(2,1)S(1)}, u32[]{:S(2)}, u32[]{:S(2)}) async-start(bf16[32,4,2304]{2,1,0:T(4,128)(2,1)} %all_to_all.37), calls=%async_computation | async-start | bytes 1179648 | tf_op jit(solution)/shard_map/all_to_all | solution.py:87
  25.1 0.2 slice_reduce_fusion.29
  25.3 0.5 compare_select_fusion
  25.8 0.3 slice_reduce_fusion.30
  26.3 0.1 compare_convert_fusion.29
  26.6 16.0 %all-to-all-done = bf16[32,4,2304]{2,1,0:T(4,128)(2,1)S(1)} async-done(((bf16[32,4,2304]{2,1,0:T(4,128)(2,1)}), bf16[32,4,2304]{2,1,0:T(4,128)(2,1)S(1)}, u32[]{:S(2)}, u32[]{:S(2)}) %all-to-all-start) | async-done | bytes 589856 | tf_op jit(solution)/shard_map/all_to_all | solution.py:87
  42.5 0.1 all_to_all.39
  42.7 1.0 gather_fusion.1
  43.6 0.2 select_select_fusion
  43.8 0.2 copy.47
  44.0 0.2 copy.46
  44.2 0.2 copy.45
  44.3 1.2 fusion.39
  45.5 0.6 copy-done.47
  46.1 0.5 convolution_convert_fusion.6
  46.6 11.6 %all-gather.2.cloned.1.call-done = bf16[768,1536]{1,0:T(8,128)(2,1)} async-done(((bf16[48,1536]{1,0:T(8,128)(2,1)}), bf16[768,1536]{1,0:T(8,128)(2,1)}) %all-gather.2.cloned.1.call-update) | async-done | bytes 2359312 | tf_op jit(solution)/shard_map/all_gather | solution.py:95
  58.2 2.2 fusion.2
  60.4 7.7 %multiply_reduce_fusion.31 = (f32[1536]{0:T(1024)}, f32[1536]{0:T(1024)}, f32[1536]{0:T(1024)}, f32[1536]{0:T(1024)}, f32[1536]{0:T(1024)}, /*index=5*/f32[1536]...) fusion(f32[128,1536]{1,0:T(8,128)S(1)} %fusion.2, ...), kind=kLoop, calls=%fused_computation.99 | loop fusion | flops 25152000 | bytes 3013632 | tf_op jit(solution)/shard_map/transpose(jvp())/reduce_sum | solution.py:77
  68.2 2.3 %multiply_reduce_fusion.16 = (f32[1536]{0:T(1024)}, f32[1536]{0:T(1024)}, f32[1536]{0:T(1024)}, f32[1536]{0:T(1024)}, f32[1536]{0:T(1024)}, /*index=5*/f32[1536]...) fusion(f32[128,1536]{1,0:T(8,128)S(1)} %get-tuple-element.69, ...), kind=kLoop, calls=%fused_computation.84 | loop fusion | flops 5294592 | bytes 2424832 | tf_op jit(solution)/shard_map/transpose(jvp())/reduce_sum | solution.py:77
  70.4 0.5 multiply_multiply_fusion.27
  71.0 0.7 multiply_multiply_fusion.29
  71.8 0.7 multiply_multiply_fusion.28
  72.5 2.6 %multiply_reduce_fusion.4 = (f32[1536]{0:T(1024)}, f32[1536]{0:T(1024)}, f32[1536]{0:T(1024)}, f32[1536]{0:T(1024)}, f32[128,1536]{1,0:T(8,128)S(1)}, /*index=5*...) fusion(f32[128,1536]{1,0:T(8,128)S(1)} %get-tuple-element.69, ...), kind=kLoop, calls=%fused_computation.72 | loop fusion | flops 5105664 | bytes 7535616 | tf_op jit(solution)/shard_map/transpose(jvp())/reduce_sum | solution.py:77
  75.1 2.6 %pad_add_fusion = f32[158,1536]{1,0:T(8,128)S(1)} fusion(f32[128,1536]{1,0:T(8,128)S(1)} %get-tuple-element.78, f32[128,1536]{1,0:T(8,128)S(1)} %get-tuple-element.80, f32[128,1536]{1,0:T(8,128)S(1)} %get-tuple-element.81, f32[128,1536]{1,0:T(8,128)S(1)} %get-tuple-element.82, f32[128,1536]{1,0:T(8,128)S(1)} %get-tuple-element.83, ...), kind=kLoop, calls=%fused_computation.59 | loop fusion | flops 5824512 | bytes 20631552 | tf_op jit(solution)/shard_map/transpose(jvp())/add_any | solution.py:77
  77.7 0.7 fusion.16
  78.6 2.2 convolution_convert_fusion
  81.1 2.0 multiply_reduce_fusion.22
  83.6 0.3 pad_add_fusion.7
  83.9 0.8 reshape.314
  84.7 4.6 %all-to-all-start.2 = ((f32[16,2,1536]{2,1,0:T(2,128)}), f32[16,2,1536]{2,1,0:T(2,128)S(1)}, u32[]{:S(2)}, u32[]{:S(2)}) async-start(f32[16,2,1536]{2,1,0:T(2,128)} %reshape.314), calls=%async_computation.3 | async-start | bytes 393216 | tf_op jit(solution)/shard_map/all_to_all | solution.py:149
  89.3 2.5 %convolution_convert_fusion.5 = bf16[128,768]{1,0:T(8,128)(2,1)S(1)} fusion(bf16[128,1536]{1,0:T(8,128)(2,1)S(1)} %fusion.16, bf16[768,1536]{1,0:T(8,128)(2,1)} %all-gather.2.cloned.1.call-done), kind=kOutput, calls=%fused_computation.54 | convolution fusion | flops 302088192 | bytes 2949120 | tf_op jit(solution)/shard_map/rd,cd->rc/dot_general | solution.py:112
  91.9 0.2 copy.49
  92.0 1.3 convolution_convert_fusion.2
  93.3 0.1 copy.55
  93.5 0.3 fusion.40
  93.8 1.6 convolution_convert_fusion.3
  95.4 0.1 copy.54
  95.5 1.6 convolution_convert_fusion.4
  97.1 0.1 copy.53
  97.3 1.8 scatter_custom_fusion
  99.0 1.0 all_to_all.40
  100.0 10.0 %all-to-all-start.1 = ((bf16[32,4,2304]{2,1,0:T(4,128)(2,1)}), bf16[32,4,2304]{2,1,0:T(4,128)(2,1)S(1)}, u32[]{:S(2)}, u32[]{:S(2)}) async-start(bf16[32,4,2304]{2,1,0:T(4,128)(2,1)} %all_to_all.40), calls=%async_computation.1 | async-start | bytes 1179648 | tf_op jit(solution)/shard_map/all_to_all | solution.py:122
  110.1 17.9 %all-to-all-done.1 = bf16[32,4,2304]{2,1,0:T(4,128)(2,1)S(1)} async-done(((bf16[32,4,2304]{2,1,0:T(4,128)(2,1)}), bf16[32,4,2304]{2,1,0:T(4,128)(2,1)S(1)}, u32[]{:S(2)}, u32[]{:S(2)}) %all-to-all-start.1) | async-done | bytes 589856 | tf_op jit(solution)/shard_map/all_to_all | solution.py:122
  128.1 0.1 reshape.348
  128.2 12.4 %reduce-scatter.2.cloned.1.call-done = bf16[48,1536]{1,0:T(8,128)(2,1)} async-done(((bf16[768,1536]{1,0:T(8,128)(2,1)}), bf16[48,1536]{1,0:T(8,128)(2,1)}) %reduce-scatter.2.cloned.1.call-update) | async-done | bytes 147472 | tf_op jit(solution)/shard_map/reduce_scatter | solution.py:104
  140.6 0.9 convert_element_type.218
  141.6 9.4 %all_to_all.59 = f32[4,13,1536]{2,1,0:T(8,128)S(1)} all-to-all(f32[4,13,1536]{2,1,0:T(8,128)S(1)} %reshape.315), channel_id=1, replica_groups=mesh['dz'=8,'dx'=4,'fy'=8,'fc'=2] {'dx'}, dimensions={0} | all-to-all | bytes 638976 | tf_op jit(solution)/shard_map/all_to_all | solution.py:149
  151.1 14.5 %all_to_all.60 = f32[8,2,1536]{2,1,0:T(2,128)S(1)} all-to-all(f32[8,2,1536]{2,1,0:T(2,128)S(1)} %reshape.316), channel_id=1, replica_groups=mesh['dz'=8,'dx'=4,'fy'=8,'fc'=2] {'dz'}, dimensions={0} | all-to-all | bytes 196608 | tf_op jit(solution)/shard_map/all_to_all | solution.py:149
  165.6 10.0 %all_to_all.61 = f32[8,2,1536]{2,1,0:T(2,128)S(1)} all-to-all(f32[8,2,1536]{2,1,0:T(2,128)S(1)} %broadcast_in_dim.59), channel_id=1, replica_groups=mesh['dz'=8,'dx'=4,'fy'=8,'fc'=2] {'dz'}, dimensions={0} | all-to-all | bytes 196608 | tf_op jit(solution)/shard_map/all_to_all | solution.py:156
  175.7 0.8 broadcast_in_dim.60
  176.4 3.5 %all-to-all-start.6 = ((f32[4,13,1536]{2,1,0:T(8,128)}), f32[4,13,1536]{2,1,0:T(8,128)S(1)}, u32[]{:S(2)}, u32[]{:S(2)}) async-start(f32[4,13,1536]{2,1,0:T(8,128)} %broadcast_in_dim.60), calls=%async_computation.7 | async-start | bytes 786432 | tf_op jit(solution)/shard_map/all_to_all | solution.py:156
  179.9 2.4 %scatter_custom_fusion.1 = bf16[128,2304]{1,0:T(8,128)(2,1)} fusion(s32[128]{0:T(128)} %get-tuple-element.108, bf16[128,2304]{1,0:T(8,128)(2,1)S(1)} %reshape.348, bf16[]{:T(256)} %constant.10.clone.1), kind=kCustom, calls=%fused_computation.145 | custom fusion | bytes 590336 | tf_op jit(solution)/shard_map/scatter | solution.py:124
  182.3 3.8 %all-to-all-done.6 = f32[4,13,1536]{2,1,0:T(8,128)S(1)} async-done(((f32[4,13,1536]{2,1,0:T(8,128)}), f32[4,13,1536]{2,1,0:T(8,128)S(1)}, u32[]{:S(2)}, u32[]{:S(2)}) %all-to-all-start.6) | async-done | bytes 319520 | tf_op jit(solution)/shard_map/all_to_all | solution.py:156
  186.2 11.8 %all_to_all.62 = f32[2,2,1536]{2,1,0:T(2,128)S(1)} all-to-all(f32[2,2,1536]{2,1,0:T(2,128)S(1)} %broadcast_in_dim.61), channel_id=1, replica_groups=mesh['dz'=8,'dx'=4,'fy'=8,'fc'=2] {'fc'}, dimensions={0} | all-to-all | bytes 49152 | tf_op jit(solution)/shard_map/all_to_all | solution.py:156
  198.0 0.7 broadcast_in_dim.63
  198.7 4.3 %all-to-all-start.8 = ((f32[8,4,1536]{2,1,0:T(4,128)}), f32[8,4,1536]{2,1,0:T(4,128)S(1)}, u32[]{:S(2)}, u32[]{:S(2)}) async-start(f32[8,4,1536]{2,1,0:T(4,128)} %broadcast_in_dim.63), calls=%async_computation.9 | async-start | bytes 393216 | tf_op jit(solution)/shard_map/all_to_all | solution.py:156
  203.0 0.7 slice_multiply_fusion
  203.8 8.7 %all-to-all-done.8 = f32[8,4,1536]{2,1,0:T(4,128)S(1)} async-done(((f32[8,4,1536]{2,1,0:T(4,128)}), f32[8,4,1536]{2,1,0:T(4,128)S(1)}, u32[]{:S(2)}, u32[]{:S(2)}) %all-to-all-start.8) | async-done | bytes 196640 | tf_op jit(solution)/shard_map/all_to_all | solution.py:156
  212.6 0.7 slice_multiply_fusion.1
  (154 shorter events, 1.3 us)
Async XLA Ops:
  7.2 2.0 copy-start
  7.2 51.1 %all-gather.2.cloned.1.call-start = ((), (), s32[]{:S(2)}) async-start(), calls=%async_computation.10 | async-start | bytes 2506752 | tf_op jit(solution)/shard_map/all_gather | solution.py:95
  9.1 1.0 copy-start.45
  10.1 14.9 %copy-start.4 = (f32[31,1536]{1,0:T(8,128)S(1)}, f32[31,1536]{1,0:T(8,128)}, u32[]{:S(2)}) copy-start(f32[31,1536]{1,0:T(8,128)} %param.11) | copy-start | bytes 571396
  10.2 15.1 %copy-start.46 = (s32[128]{0:T(128)S(1)}, s32[128]{0:T(128)}, u32[]{:S(2)}) copy-start(s32[128]{0:T(128)} %param.14) | copy-start | bytes 1540
  10.2 16.0 %copy-start.44 = (s32[128]{0:T(128)S(1)}, s32[128]{0:T(128)}, u32[]{:S(2)}) copy-start(s32[128]{0:T(128)} %param.15) | copy-start | bytes 1540
  11.3 31.2 %all-to-all-start = ((bf16[32,4,2304]{2,1,0:T(4,128)(2,1)}), bf16[32,4,2304]{2,1,0:T(4,128)(2,1)S(1)}, u32[]{:S(2)}, u32[]{:S(2)}) async-start(bf16[32,4,2304]{2,1,0:T(4,128)(2,1)} %all_to_all.37), calls=%async_computation | async-start | bytes 1179648 | tf_op jit(solution)/shard_map/all_to_all | solution.py:87
  25.0 115.5 %reduce-scatter.2.cloned.1.call-start = ((), (), s32[]{:S(2)}) async-start(), calls=%async_computation.11 | async-start | bytes 2506752 | tf_op jit(solution)/shard_map/reduce_scatter | solution.py:104
  26.4 44.6 %copy-start.38 = (f32[128]{0:T(128)}, f32[128]{0:T(128)S(1)}, u32[]{:S(2)}) copy-start(f32[128]{0:T(128)S(1)} %get-tuple-element.122) | copy-start | bytes 1540
  26.4 44.6 %copy-start.40 = (f32[128]{0:T(128)}, f32[128]{0:T(128)S(1)}, u32[]{:S(2)}) copy-start(f32[128]{0:T(128)S(1)} %get-tuple-element.123) | copy-start | bytes 1540
  26.4 44.6 %copy-start.42 = (f32[128]{0:T(128)}, f32[128]{0:T(128)S(1)}, u32[]{:S(2)}) copy-start(f32[128]{0:T(128)S(1)} %get-tuple-element.124) | copy-start | bytes 1540
  26.4 45.3 %copy-start.26 = (f32[128]{0:T(128)}, f32[128]{0:T(128)S(1)}, u32[]{:S(2)}) copy-start(f32[128]{0:T(128)S(1)} %get-tuple-element.116) | copy-start | bytes 1540
  26.4 45.3 %copy-start.28 = (f32[128]{0:T(128)}, f32[128]{0:T(128)S(1)}, u32[]{:S(2)}) copy-start(f32[128]{0:T(128)S(1)} %get-tuple-element.117) | copy-start | bytes 1540
  26.4 45.3 %copy-start.30 = (f32[128]{0:T(128)}, f32[128]{0:T(128)S(1)}, u32[]{:S(2)}) copy-start(f32[128]{0:T(128)S(1)} %get-tuple-element.118) | copy-start | bytes 1540
  26.4 45.3 %copy-start.32 = (f32[128]{0:T(128)}, f32[128]{0:T(128)S(1)}, u32[]{:S(2)}) copy-start(f32[128]{0:T(128)S(1)} %get-tuple-element.119) | copy-start | bytes 1540
  26.4 45.3 %copy-start.34 = (f32[128]{0:T(128)}, f32[128]{0:T(128)S(1)}, u32[]{:S(2)}) copy-start(f32[128]{0:T(128)S(1)} %get-tuple-element.120) | copy-start | bytes 1540
  26.5 45.3 %copy-start.36 = (f32[128]{0:T(128)}, f32[128]{0:T(128)S(1)}, u32[]{:S(2)}) copy-start(f32[128]{0:T(128)S(1)} %get-tuple-element.121) | copy-start | bytes 1540
  26.6 19.0 %copy-start.25 = (pred[128,128]{0,1:T(8,128)(4,1)}, pred[128,128]{0,1:T(8,128)(4,1)S(1)}, u32[]{:S(2)}) copy-start(pred[128,128]{0,1:T(8,128)(4,1)S(1)} %broadcast_compare_fusion) | copy-start | bytes 49156
  44.2 14.1 %copy-start.2 = (bf16[128,768]{0,1:T(8,128)(2,1)}, bf16[128,768]{0,1:T(8,128)(2,1)S(1)}, u32[]{:S(2)}) copy-start(bf16[128,768]{0,1:T(8,128)(2,1)S(1)} %copy.46) | copy-start | bytes 589828
  45.5 0.6 copy-start.47
  46.6 13.8 %copy-start.1 = (bf16[128,1536]{1,0:T(8,128)(2,1)S(1)}, bf16[128,1536]{1,0:T(8,128)(2,1)}, u32[]{:S(2)}) copy-start(bf16[128,1536]{1,0:T(8,128)(2,1)} %param.12) | copy-start | bytes 1179652
  78.4 2.4 %copy-start.20 = (f32[1536]{0:T(1024)S(1)}, f32[1536]{0:T(1024)}, u32[]{:S(2)}) copy-start(f32[1536]{0:T(1024)} %get-tuple-element.7) | copy-start | bytes 18436
  78.4 2.5 %copy-start.19 = (f32[1536]{0:T(1024)S(1)}, f32[1536]{0:T(1024)}, u32[]{:S(2)}) copy-start(f32[1536]{0:T(1024)} %get-tuple-element.8) | copy-start | bytes 18436
  78.4 2.5 %copy-start.18 = (f32[1536]{0:T(1024)S(1)}, f32[1536]{0:T(1024)}, u32[]{:S(2)}) copy-start(f32[1536]{0:T(1024)} %get-tuple-element.9) | copy-start | bytes 18436
  78.4 2.5 %copy-start.17 = (f32[1536]{0:T(1024)S(1)}, f32[1536]{0:T(1024)}, u32[]{:S(2)}) copy-start(f32[1536]{0:T(1024)} %get-tuple-element.10) | copy-start | bytes 18436
  78.4 2.5 %copy-start.16 = (f32[1536]{0:T(1024)S(1)}, f32[1536]{0:T(1024)}, u32[]{:S(2)}) copy-start(f32[1536]{0:T(1024)} %get-tuple-element.11) | copy-start | bytes 18436
  78.5 2.5 %copy-start.15 = (f32[1536]{0:T(1024)S(1)}, f32[1536]{0:T(1024)}, u32[]{:S(2)}) copy-start(f32[1536]{0:T(1024)} %get-tuple-element.12) | copy-start | bytes 18436
  78.5 2.5 %copy-start.14 = (f32[1536]{0:T(1024)S(1)}, f32[1536]{0:T(1024)}, u32[]{:S(2)}) copy-start(f32[1536]{0:T(1024)} %get-tuple-element.13) | copy-start | bytes 18436
  78.5 2.5 %copy-start.13 = (f32[1536]{0:T(1024)S(1)}, f32[1536]{0:T(1024)}, u32[]{:S(2)}) copy-start(f32[1536]{0:T(1024)} %get-tuple-element.14) | copy-start | bytes 18436
  78.5 2.6 %copy-start.12 = (f32[1536]{0:T(1024)S(1)}, f32[1536]{0:T(1024)}, u32[]{:S(2)}) copy-start(f32[1536]{0:T(1024)} %get-tuple-element.15) | copy-start | bytes 18436
  78.5 2.6 %copy-start.27 = (f32[128]{0:T(128)S(1)}, f32[128]{0:T(128)}, u32[]{:S(2)}) copy-start(f32[128]{0:T(128)} %copy-done.26) | copy-start | bytes 1540
  78.5 2.6 %copy-start.29 = (f32[128]{0:T(128)S(1)}, f32[128]{0:T(128)}, u32[]{:S(2)}) copy-start(f32[128]{0:T(128)} %copy-done.28) | copy-start | bytes 1540
  78.5 2.6 %copy-start.31 = (f32[128]{0:T(128)S(1)}, f32[128]{0:T(128)}, u32[]{:S(2)}) copy-start(f32[128]{0:T(128)} %copy-done.30) | copy-start | bytes 1540
  78.5 2.6 %copy-start.33 = (f32[128]{0:T(128)S(1)}, f32[128]{0:T(128)}, u32[]{:S(2)}) copy-start(f32[128]{0:T(128)} %copy-done.32) | copy-start | bytes 1540
  78.5 2.6 %copy-start.35 = (f32[128]{0:T(128)S(1)}, f32[128]{0:T(128)}, u32[]{:S(2)}) copy-start(f32[128]{0:T(128)} %copy-done.34) | copy-start | bytes 1540
  78.5 2.6 %copy-start.37 = (f32[128]{0:T(128)S(1)}, f32[128]{0:T(128)}, u32[]{:S(2)}) copy-start(f32[128]{0:T(128)} %copy-done.36) | copy-start | bytes 1540
  78.6 2.6 %copy-start.39 = (f32[128]{0:T(128)S(1)}, f32[128]{0:T(128)}, u32[]{:S(2)}) copy-start(f32[128]{0:T(128)} %copy-done.38) | copy-start | bytes 1540
  78.6 2.6 %copy-start.41 = (f32[128]{0:T(128)S(1)}, f32[128]{0:T(128)}, u32[]{:S(2)}) copy-start(f32[128]{0:T(128)} %copy-done.40) | copy-start | bytes 1540
  78.6 2.6 %copy-start.43 = (f32[128]{0:T(128)S(1)}, f32[128]{0:T(128)}, u32[]{:S(2)}) copy-start(f32[128]{0:T(128)} %copy-done.42) | copy-start | bytes 1540
  80.7 2.5 %copy-start.11 = (f32[1536]{0:T(1024)S(1)}, f32[1536]{0:T(1024)}, u32[]{:S(2)}) copy-start(f32[1536]{0:T(1024)} %get-tuple-element.25) | copy-start | bytes 18436
  80.7 2.5 %copy-start.10 = (f32[1536]{0:T(1024)S(1)}, f32[1536]{0:T(1024)}, u32[]{:S(2)}) copy-start(f32[1536]{0:T(1024)} %get-tuple-element.26) | copy-start | bytes 18436
  80.7 2.6 %copy-start.9 = (f32[1536]{0:T(1024)S(1)}, f32[1536]{0:T(1024)}, u32[]{:S(2)}) copy-start(f32[1536]{0:T(1024)} %get-tuple-element.27) | copy-start | bytes 18436
  80.7 2.6 %copy-start.8 = (f32[1536]{0:T(1024)S(1)}, f32[1536]{0:T(1024)}, u32[]{:S(2)}) copy-start(f32[1536]{0:T(1024)} %get-tuple-element.28) | copy-start | bytes 18436
  80.7 2.6 %copy-start.7 = (f32[1536]{0:T(1024)S(1)}, f32[1536]{0:T(1024)}, u32[]{:S(2)}) copy-start(f32[1536]{0:T(1024)} %get-tuple-element.29) | copy-start | bytes 18436
  80.8 2.6 %copy-start.6 = (f32[1536]{0:T(1024)S(1)}, f32[1536]{0:T(1024)}, u32[]{:S(2)}) copy-start(f32[1536]{0:T(1024)} %get-tuple-element.30) | copy-start | bytes 18436
  80.8 2.6 %copy-start.5 = (f32[1536]{0:T(1024)S(1)}, f32[1536]{0:T(1024)}, u32[]{:S(2)}) copy-start(f32[1536]{0:T(1024)} %get-tuple-element.31) | copy-start | bytes 18436
  80.8 2.7 %copy-start.24 = (f32[1536]{0:T(1024)S(1)}, f32[1536]{0:T(1024)}, u32[]{:S(2)}) copy-start(f32[1536]{0:T(1024)} %get-tuple-element.34) | copy-start | bytes 18436
  80.8 2.7 %copy-start.23 = (f32[1536]{0:T(1024)S(1)}, f32[1536]{0:T(1024)}, u32[]{:S(2)}) copy-start(f32[1536]{0:T(1024)} %get-tuple-element.35) | copy-start | bytes 18436
  80.8 2.7 %copy-start.22 = (f32[1536]{0:T(1024)S(1)}, f32[1536]{0:T(1024)}, u32[]{:S(2)}) copy-start(f32[1536]{0:T(1024)} %get-tuple-element.36) | copy-start | bytes 18436
  80.8 2.7 %copy-start.21 = (f32[1536]{0:T(1024)S(1)}, f32[1536]{0:T(1024)}, u32[]{:S(2)}) copy-start(f32[1536]{0:T(1024)} %get-tuple-element.37) | copy-start | bytes 18436
  83.5 8.5 %copy-start.3 = (bf16[128,768]{0,1:T(8,128)(2,1)S(1)}, bf16[128,768]{0,1:T(8,128)(2,1)}, u32[]{:S(2)}) copy-start(bf16[128,768]{0,1:T(8,128)(2,1)} %copy-done.2) | copy-start | bytes 589828
  83.6 8.5 %copy-start.48 = (f32[8,128]{1,0:T(8,128)S(1)}, f32[8,128]{1,0:T(8,128)}, u32[]{:S(2)}) copy-start(f32[8,128]{1,0:T(8,128)} %copy-done.47) | copy-start | bytes 12292
  84.7 15.3 %all-to-all-start.2 = ((f32[16,2,1536]{2,1,0:T(2,128)}), f32[16,2,1536]{2,1,0:T(2,128)S(1)}, u32[]{:S(2)}, u32[]{:S(2)}) async-start(f32[16,2,1536]{2,1,0:T(2,128)} %reshape.314), calls=%async_computation.3 | async-start | bytes 393216 | tf_op jit(solution)/shard_map/all_to_all | solution.py:149
  100.0 28.1 %all-to-all-start.1 = ((bf16[32,4,2304]{2,1,0:T(4,128)(2,1)}), bf16[32,4,2304]{2,1,0:T(4,128)(2,1)S(1)}, u32[]{:S(2)}, u32[]{:S(2)}) async-start(bf16[32,4,2304]{2,1,0:T(4,128)(2,1)} %all_to_all.40), calls=%async_computation.1 | async-start | bytes 1179648 | tf_op jit(solution)/shard_map/all_to_all | solution.py:122
  176.4 9.7 %all-to-all-start.6 = ((f32[4,13,1536]{2,1,0:T(8,128)}), f32[4,13,1536]{2,1,0:T(8,128)S(1)}, u32[]{:S(2)}, u32[]{:S(2)}) async-start(f32[4,13,1536]{2,1,0:T(8,128)} %broadcast_in_dim.60), calls=%async_computation.7 | async-start | bytes 786432 | tf_op jit(solution)/shard_map/all_to_all | solution.py:156
  198.7 13.8 %all-to-all-start.8 = ((f32[8,4,1536]{2,1,0:T(4,128)}), f32[8,4,1536]{2,1,0:T(4,128)S(1)}, u32[]{:S(2)}, u32[]{:S(2)}) async-start(f32[8,4,1536]{2,1,0:T(4,128)} %broadcast_in_dim.63), calls=%async_computation.9 | async-start | bytes 393216 | tf_op jit(solution)/shard_map/all_to_all | solution.py:156
Sparse Core Ops, SparseCore 0:
  10.1 48.0 all-gather.1
  81.0 59.5 reduce-scatter.1

commit v7 on v6

--- a/solution.py
+++ b/solution.py
@@ -123,16 +123,10 @@
     source_index = jnp.where(present, send_rows, row_count)
     projected_grad = jnp.zeros_like(projected).at[source_index].set(arrived, mode="drop")
     scale_factor = (row_count * lax.axis_size(DP) * lax.axis_size(FSDP)) ** (-0.5)
-    weight_share, arrived = lax.optimization_barrier((weight_share, arrived))
-    kernel_piece = sum_rows(kernel_part, FSDP)
-    owned_rows = weight_share.shape[0]
-    both = jnp.concatenate([weight_share, kernel_piece], axis=0)
-    inner = sum_rows(both, "dx")
-    inner_rows = inner.shape[0]
-    inner = gather_rows(sum_rows(inner, "dz"), "dz")[:inner_rows]
-    both = gather_rows(inner, "dx")[: both.shape[0]]
-    weight_total = both[:owned_rows]
-    kernel_total = gather_rows(gather_rows(both[owned_rows:], "fc"), "fy")[: kernel.shape[0]]
+    kernel_total = reduce_rows(sum_rows(kernel_part, FSDP))
+    kernel_total = gather_rows(gather_rows(kernel_total, "fc"), "fy")[: kernel.shape[0]]
+    weight_share, arrived, kernel_total = lax.optimization_barrier((weight_share, arrived, kernel_total))
+    weight_total = reduce_rows(weight_share)
 
     return (
         result.astype(jnp.bfloat16),
@@ -156,6 +150,13 @@
     got = lax.all_to_all(copies, axis, split_axis=0, concat_axis=0, tiled=True)
     return got.reshape(count * piece.shape[0], piece.shape[1])
 
+
+def reduce_rows(x):
+    inner = sum_rows(x, "dx")
+    inner_rows = inner.shape[0]
+    inner = gather_rows(sum_rows(inner, "dz"), "dz")[:inner_rows]
+    return gather_rows(inner, "dx")[: x.shape[0]]
+
 def solution(mesh):
     dp_count, fsdp_count = mesh.devices.shape
     fine = Mesh(

time: 221 us -> 246 us (1.11)
  the two profiles are of different devices: /device:TPU:1 before, /device:TPU:2 now
where the time goes in v7:
time: 246 us; the launch traced here: 244 us
  waiting for transfers between devices  77.7 us (32%)
  blocking collectives  48.8 us (20%)
  starting transfers between devices  45.9 us (19%)
  other arithmetic  28.5 us (12%)
  local copies, waits for them, and re-layouts  15.4 us (6%)
  between operations  15.4 us (6%)
  matrix products  12.4 us (5%)
    all_to_all x4, blocking collectives, sum_rows(): lax.all_to_all(padded.reshape(count, per, x.shape[1]), axis, split_axis=0...  45 us
    all_to_all x5, waiting for transfers between devices, gather_rows(): got = lax.all_to_all(copies, axis, split_axis=0, concat_axis=0, tiled=True)  26.4 us
    all_to_all x5, starting transfers between devices, gather_rows(): got = lax.all_to_all(copies, axis, split_axis=0, concat_axis=0, tiled=True)  19.8 us
    all_to_all x1, waiting for transfers between devices, body(): lax.all_to_all(returning, DP, split_axis=0, concat_axis=0, tiled=True)  17.8 us
    all_to_all x1, waiting for transfers between devices, body(): lax.all_to_all(outgoing, DP, split_axis=0, concat_axis=0, tiled=True)  16.7 us
    reduce_sum x4, other arithmetic, finish(): kernel[offset] * padded[offset:offset + length] * matching[:, None]  14.6 us
    all_to_all x1, starting transfers between devices, body(): lax.all_to_all(outgoing, DP, split_axis=0, concat_axis=0, tiled=True)  13.5 us
    all_gather x1, waiting for transfers between devices, body(): lax.all_gather(out_weight, FSDP, axis=0, tiled=True)  10.4 us
  transfers between devices with their start and end apart: 10, of which 9 were waited for; matrix products, arithmetic and copies ran while one was open for 12% of the time, Pallas kernels for 0%

profile of v7, /device:TPU:2, one launch (start us, length us, event | category | flops | bytes accessed | tf_op | source)
XLA Modules:
  0.0 244.2 jit_solution(15218485018331283336)
XLA Ops:
  7.2 0.7 all-gather.2.cloned.1.call-update
  7.9 1.2 compare_select_fusion.1
  9.2 1.0 gather_fusion
  10.4 1.0 all_to_all.49
  11.3 13.5 %all-to-all-start = ((bf16[32,4,2304]{2,1,0:T(4,128)(2,1)}), bf16[32,4,2304]{2,1,0:T(4,128)(2,1)S(1)}, u32[]{:S(2)}, u32[]{:S(2)}) async-start(bf16[32,4,2304]{2,1,0:T(4,128)(2,1)} %all_to_all.49), calls=%async_computation | async-start | bytes 1179648 | tf_op jit(solution)/shard_map/all_to_all | solution.py:87
  25.1 0.5 compare_select_fusion
  25.6 0.3 slice_reduce_fusion.31
  26.3 16.7 %all-to-all-done = bf16[32,4,2304]{2,1,0:T(4,128)(2,1)S(1)} async-done(((bf16[32,4,2304]{2,1,0:T(4,128)(2,1)}), bf16[32,4,2304]{2,1,0:T(4,128)(2,1)S(1)}, u32[]{:S(2)}, u32[]{:S(2)}) %all-to-all-start) | async-done | bytes 589856 | tf_op jit(solution)/shard_map/all_to_all | solution.py:87
  43.2 1.0 gather_fusion.1
  44.9 1.2 fusion.39
  46.0 0.5 convolution_convert_fusion.6
  46.6 10.4 %all-gather.2.cloned.1.call-done = bf16[768,1536]{1,0:T(8,128)(2,1)} async-done(((bf16[48,1536]{1,0:T(8,128)(2,1)}), bf16[768,1536]{1,0:T(8,128)(2,1)}) %all-gather.2.cloned.1.call-update) | async-done | bytes 2359312 | tf_op jit(solution)/shard_map/all_gather | solution.py:95
  57.0 2.2 fusion.2
  59.2 7.7 %multiply_reduce_fusion.31 = (f32[1536]{0:T(1024)}, f32[1536]{0:T(1024)}, f32[1536]{0:T(1024)}, f32[1536]{0:T(1024)}, f32[1536]{0:T(1024)}, /*index=5*/f32[1536]...) fusion(f32[128,1536]{1,0:T(8,128)S(1)} %fusion.2, ...), kind=kLoop, calls=%fused_computation.99 | loop fusion | flops 25152000 | bytes 3013632 | tf_op jit(solution)/shard_map/transpose(jvp())/reduce_sum | solution.py:77
  66.9 2.2 multiply_reduce_fusion.16
  69.2 0.5 multiply_multiply_fusion.27
  69.7 0.7 multiply_multiply_fusion.29
  70.5 0.7 multiply_multiply_fusion.28
  71.2 2.6 %multiply_reduce_fusion.4 = (f32[1536]{0:T(1024)}, f32[1536]{0:T(1024)}, f32[1536]{0:T(1024)}, f32[1536]{0:T(1024)}, f32[128,1536]{1,0:T(8,128)S(1)}, /*index=5*...) fusion(f32[128,1536]{1,0:T(8,128)S(1)} %get-tuple-element.71, ...), kind=kLoop, calls=%fused_computation.72 | loop fusion | flops 5105664 | bytes 7535616 | tf_op jit(solution)/shard_map/transpose(jvp())/reduce_sum | solution.py:77
  73.8 2.6 %pad_add_fusion = f32[158,1536]{1,0:T(8,128)S(1)} fusion(f32[128,1536]{1,0:T(8,128)S(1)} %get-tuple-element.80, f32[128,1536]{1,0:T(8,128)S(1)} %get-tuple-element.82, f32[128,1536]{1,0:T(8,128)S(1)} %get-tuple-element.83, f32[128,1536]{1,0:T(8,128)S(1)} %get-tuple-element.84, f32[128,1536]{1,0:T(8,128)S(1)} %get-tuple-element.85, ...), kind=kLoop, calls=%fused_computation.59 | loop fusion | flops 5824512 | bytes 20631552 | tf_op jit(solution)/shard_map/transpose(jvp())/add_any | solution.py:77
  76.4 0.7 fusion.16
  77.3 2.1 convolution_convert_fusion
  79.9 2.0 multiply_reduce_fusion.22
  82.3 0.3 pad_add_fusion.7
  82.6 0.8 reshape.334
  83.4 14.7 %all_to_all.79 = f32[16,2,1536]{2,1,0:T(2,128)} all-to-all(f32[16,2,1536]{2,1,0:T(2,128)} %reshape.334), channel_id=1, replica_groups=mesh['dz'=8,'dx'=4,'fy'=8,'fc'=2] {'fy','fc'}, dimensions={0} | all-to-all | bytes 393216 | tf_op jit(solution)/shard_map/all_to_all | solution.py:143
  98.1 1.0 reduce_sum.393
  99.1 8.7 %all_to_all.80 = f32[4,1,1536]{2,1,0:T(1,128)} all-to-all(f32[4,1,1536]{2,1,0:T(1,128)S(1)} %copy.69), channel_id=1, replica_groups=mesh['dz'=8,'dx'=4,'fy'=8,'fc'=2] {'dx'}, dimensions={0} | all-to-all | bytes 49152 | tf_op jit(solution)/shard_map/all_to_all | solution.py:143
  107.8 0.8 reduce_sum.394
  108.6 0.7 reshape.336
  109.3 7.5 %all-to-all-start.4 = ((f32[8,1,1536]{2,1,0:T(1,128)}), f32[8,1,1536]{2,1,0:T(1,128)}, u32[]{:S(2)}, u32[]{:S(2)}) async-start(f32[8,1,1536]{2,1,0:T(1,128)} %reshape.336), calls=%async_computation.5 | async-start | bytes 98304 | tf_op jit(solution)/shard_map/all_to_all | solution.py:143
  116.8 1.6 convolution_convert_fusion.5
  118.4 1.1 copy.61
  119.5 5.7 %all-to-all-done.4 = f32[8,1,1536]{2,1,0:T(1,128)} async-done(((f32[8,1,1536]{2,1,0:T(1,128)}), f32[8,1,1536]{2,1,0:T(1,128)}, u32[]{:S(2)}, u32[]{:S(2)}) %all-to-all-start.4) | async-done | bytes 49184 | tf_op jit(solution)/shard_map/all_to_all | solution.py:143
  125.1 0.8 reduce_sum.399
  126.0 0.6 broadcast_in_dim.69
  126.6 3.5 %all-to-all-start.5 = ((f32[8,1,1536]{2,1,0:T(1,128)}), f32[8,1,1536]{2,1,0:T(1,128)S(1)}, u32[]{:S(2)}, u32[]{:S(2)}) async-start(f32[8,1,1536]{2,1,0:T(1,128)} %broadcast_in_dim.69), calls=%async_computation.6 | async-start | bytes 98304 | tf_op jit(solution)/shard_map/all_to_all | solution.py:150
  130.4 7.8 %all-to-all-done.5 = f32[8,1,1536]{2,1,0:T(1,128)S(1)} async-done(((f32[8,1,1536]{2,1,0:T(1,128)}), f32[8,1,1536]{2,1,0:T(1,128)S(1)}, u32[]{:S(2)}, u32[]{:S(2)}) %all-to-all-start.5) | async-done | bytes 49184 | tf_op jit(solution)/shard_map/all_to_all | solution.py:150
  138.3 0.6 broadcast_in_dim.71
  138.9 4.7 %all-to-all-start.6 = ((f32[4,1,1536]{2,1,0:T(1,128)}), f32[4,1,1536]{2,1,0:T(1,128)S(1)}, u32[]{:S(2)}, u32[]{:S(2)}) async-start(f32[4,1,1536]{2,1,0:T(1,128)} %broadcast_in_dim.71), calls=%async_computation.7 | async-start | bytes 49152 | tf_op jit(solution)/shard_map/all_to_all | solution.py:150
  143.6 1.6 convolution_convert_fusion.2
  145.2 2.4 all-to-all-done.6
  147.6 3.7 %all_to_all.81 = f32[2,2,1536]{2,1,0:T(2,128)S(1)} all-to-all(f32[2,2,1536]{2,1,0:T(2,128)S(1)} %broadcast_in_dim.73), channel_id=1, replica_groups=mesh['dz'=8,'dx'=4,'fy'=8,'fc'=2] {'fc'}, dimensions={0} | all-to-all | bytes 49152 | tf_op jit(solution)/shard_map/all_to_all | solution.py:150
  151.3 0.7 broadcast_in_dim.75
  152.0 3.4 %all-to-all-start.8 = ((f32[8,4,1536]{2,1,0:T(4,128)}), f32[8,4,1536]{2,1,0:T(4,128)S(1)}, u32[]{:S(2)}, u32[]{:S(2)}) async-start(f32[8,4,1536]{2,1,0:T(4,128)} %broadcast_in_dim.75), calls=%async_computation.9 | async-start | bytes 393216 | tf_op jit(solution)/shard_map/all_to_all | solution.py:150
  155.4 1.5 convolution_convert_fusion.3
  157.3 1.5 convolution_convert_fusion.4
  158.9 1.8 scatter_custom_fusion
  160.7 1.0 all_to_all.52
  161.7 4.8 %all-to-all-done.8 = f32[8,4,1536]{2,1,0:T(4,128)S(1)} async-done(((f32[8,4,1536]{2,1,0:T(4,128)}), f32[8,4,1536]{2,1,0:T(4,128)S(1)}, u32[]{:S(2)}, u32[]{:S(2)}) %all-to-all-start.8) | async-done | bytes 196640 | tf_op jit(solution)/shard_map/all_to_all | solution.py:150
  166.4 5.0 %all-to-all-start.1 = ((bf16[32,4,2304]{2,1,0:T(4,128)(2,1)}), bf16[32,4,2304]{2,1,0:T(4,128)(2,1)S(1)}, u32[]{:S(2)}, u32[]{:S(2)}) async-start(bf16[32,4,2304]{2,1,0:T(4,128)(2,1)} %all_to_all.52), calls=%async_computation.1 | async-start | bytes 1179648 | tf_op jit(solution)/shard_map/all_to_all | solution.py:122
  171.5 17.8 %all-to-all-done.1 = bf16[32,4,2304]{2,1,0:T(4,128)(2,1)S(1)} async-done(((bf16[32,4,2304]{2,1,0:T(4,128)(2,1)}), bf16[32,4,2304]{2,1,0:T(4,128)(2,1)S(1)}, u32[]{:S(2)}, u32[]{:S(2)}) %all-to-all-start.1) | async-done | bytes 589856 | tf_op jit(solution)/shard_map/all_to_all | solution.py:122
  189.5 0.9 convert_element_type.220
  190.4 10.5 %all_to_all.82 = f32[4,12,1536]{2,1,0:T(8,128)S(1)} all-to-all(f32[4,12,1536]{2,1,0:T(8,128)S(1)} %reshape.338), channel_id=1, replica_groups=mesh['dz'=8,'dx'=4,'fy'=8,'fc'=2] {'dx'}, dimensions={0} | all-to-all | bytes 589824 | tf_op jit(solution)/shard_map/all_to_all | solution.py:143
  201.1 11.1 %all_to_all.83 = f32[8,2,1536]{2,1,0:T(2,128)S(1)} all-to-all(f32[8,2,1536]{2,1,0:T(2,128)S(1)} %reshape.339), channel_id=1, replica_groups=mesh['dz'=8,'dx'=4,'fy'=8,'fc'=2] {'dz'}, dimensions={0} | all-to-all | bytes 196608 | tf_op jit(solution)/shard_map/all_to_all | solution.py:143
  212.2 0.7 broadcast_in_dim.76
  212.9 3.4 %all-to-all-start.11 = ((f32[8,2,1536]{2,1,0:T(2,128)}), f32[8,2,1536]{2,1,0:T(2,128)S(1)}, u32[]{:S(2)}, u32[]{:S(2)}) async-start(f32[8,2,1536]{2,1,0:T(2,128)} %broadcast_in_dim.76), calls=%async_computation.12 | async-start | bytes 196608 | tf_op jit(solution)/shard_map/all_to_all | solution.py:150
  216.3 2.4 scatter_custom_fusion.1
  218.6 6.3 %all-to-all-done.11 = f32[8,2,1536]{2,1,0:T(2,128)S(1)} async-done(((f32[8,2,1536]{2,1,0:T(2,128)}), f32[8,2,1536]{2,1,0:T(2,128)S(1)}, u32[]{:S(2)}, u32[]{:S(2)}) %all-to-all-start.11) | async-done | bytes 98336 | tf_op jit(solution)/shard_map/all_to_all | solution.py:150
  225.0 0.8 broadcast_in_dim.78
  225.7 4.9 %all-to-all-start.12 = ((f32[4,12,1536]{2,1,0:T(8,128)}), f32[4,12,1536]{2,1,0:T(8,128)S(1)}, u32[]{:S(2)}, u32[]{:S(2)}) async-start(f32[4,12,1536]{2,1,0:T(8,128)} %broadcast_in_dim.78), calls=%async_computation.13 | async-start | bytes 786432 | tf_op jit(solution)/shard_map/all_to_all | solution.py:150
  230.6 0.7 broadcast_multiply_fusion.2
  231.3 5.2 %all-to-all-done.12 = f32[4,12,1536]{2,1,0:T(8,128)S(1)} async-done(((f32[4,12,1536]{2,1,0:T(8,128)}), f32[4,12,1536]{2,1,0:T(8,128)S(1)}, u32[]{:S(2)}, u32[]{:S(2)}) %all-to-all-start.12) | async-done | bytes 294944 | tf_op jit(solution)/shard_map/all_to_all | solution.py:150
  236.6 0.7 mul.1323
  (184 shorter events, 3.3 us)
Async XLA Ops:
  7.2 2.0 copy-start
  7.2 49.8 %all-gather.2.cloned.1.call-start = ((), (), s32[]{:S(2)}) async-start(), calls=%async_computation.14 | async-start | bytes 2506752 | tf_op jit(solution)/shard_map/all_gather | solution.py:95
  10.1 14.7 %copy-start.10 = (f32[31,1536]{1,0:T(8,128)S(1)}, f32[31,1536]{1,0:T(8,128)}, u32[]{:S(2)}) copy-start(f32[31,1536]{1,0:T(8,128)} %param.11) | copy-start | bytes 571396
  10.2 14.9 %copy-start.52 = (s32[128]{0:T(128)S(1)}, s32[128]{0:T(128)}, u32[]{:S(2)}) copy-start(s32[128]{0:T(128)} %param.14) | copy-start | bytes 1540
  10.2 15.7 %copy-start.50 = (s32[128]{0:T(128)S(1)}, s32[128]{0:T(128)}, u32[]{:S(2)}) copy-start(s32[128]{0:T(128)} %param.15) | copy-start | bytes 1540
  11.3 31.7 %all-to-all-start = ((bf16[32,4,2304]{2,1,0:T(4,128)(2,1)}), bf16[32,4,2304]{2,1,0:T(4,128)(2,1)S(1)}, u32[]{:S(2)}, u32[]{:S(2)}) async-start(bf16[32,4,2304]{2,1,0:T(4,128)(2,1)} %all_to_all.49), calls=%async_computation | async-start | bytes 1179648 | tf_op jit(solution)/shard_map/all_to_all | solution.py:87
  24.8 164.7 %reduce-scatter.2.cloned.1.call-start = ((), (), s32[]{:S(2)}) async-start(), calls=%async_computation.15 | async-start | bytes 2506752 | tf_op jit(solution)/shard_map/reduce_scatter | solution.py:104
  26.1 43.6 %copy-start.44 = (f32[128]{0:T(128)}, f32[128]{0:T(128)S(1)}, u32[]{:S(2)}) copy-start(f32[128]{0:T(128)S(1)} %get-tuple-element.124) | copy-start | bytes 1540
  26.1 43.6 %copy-start.46 = (f32[128]{0:T(128)}, f32[128]{0:T(128)S(1)}, u32[]{:S(2)}) copy-start(f32[128]{0:T(128)S(1)} %get-tuple-element.125) | copy-start | bytes 1540
  26.1 43.6 %copy-start.48 = (f32[128]{0:T(128)}, f32[128]{0:T(128)S(1)}, u32[]{:S(2)}) copy-start(f32[128]{0:T(128)S(1)} %get-tuple-element.126) | copy-start | bytes 1540
  26.1 44.3 %copy-start.32 = (f32[128]{0:T(128)}, f32[128]{0:T(128)S(1)}, u32[]{:S(2)}) copy-start(f32[128]{0:T(128)S(1)} %get-tuple-element.118) | copy-start | bytes 1540
  26.1 44.3 %copy-start.34 = (f32[128]{0:T(128)}, f32[128]{0:T(128)S(1)}, u32[]{:S(2)}) copy-start(f32[128]{0:T(128)S(1)} %get-tuple-element.119) | copy-start | bytes 1540
  26.2 44.3 %copy-start.36 = (f32[128]{0:T(128)}, f32[128]{0:T(128)S(1)}, u32[]{:S(2)}) copy-start(f32[128]{0:T(128)S(1)} %get-tuple-element.120) | copy-start | bytes 1540
  26.2 44.3 %copy-start.38 = (f32[128]{0:T(128)}, f32[128]{0:T(128)S(1)}, u32[]{:S(2)}) copy-start(f32[128]{0:T(128)S(1)} %get-tuple-element.121) | copy-start | bytes 1540
  26.2 44.3 %copy-start.40 = (f32[128]{0:T(128)}, f32[128]{0:T(128)S(1)}, u32[]{:S(2)}) copy-start(f32[128]{0:T(128)S(1)} %get-tuple-element.122) | copy-start | bytes 1540
  26.2 44.3 %copy-start.42 = (f32[128]{0:T(128)}, f32[128]{0:T(128)S(1)}, u32[]{:S(2)}) copy-start(f32[128]{0:T(128)S(1)} %get-tuple-element.123) | copy-start | bytes 1540
  26.3 19.7 %copy-start.31 = (pred[128,128]{0,1:T(8,128)(4,1)}, pred[128,128]{0,1:T(8,128)(4,1)S(1)}, u32[]{:S(2)}) copy-start(pred[128,128]{0,1:T(8,128)(4,1)S(1)} %broadcast_compare_fusion) | copy-start | bytes 49156
  44.5 2.0 copy-start.6
  44.7 12.3 %copy-start.8 = (bf16[128,768]{0,1:T(8,128)(2,1)}, bf16[128,768]{0,1:T(8,128)(2,1)S(1)}, u32[]{:S(2)}) copy-start(bf16[128,768]{0,1:T(8,128)(2,1)S(1)} %copy.58) | copy-start | bytes 589828
  44.8 12.1 %copy-start.4 = (bf16[128,768]{0,1:T(8,128)(2,1)}, bf16[128,768]{0,1:T(8,128)(2,1)S(1)}, u32[]{:S(2)}) copy-start(bf16[128,768]{0,1:T(8,128)(2,1)S(1)} %copy.57) | copy-start | bytes 589828
  46.0 11.0 %copy-start.53 = (f32[8,128]{1,0:T(8,128)}, f32[8,128]{1,0:T(8,128)S(1)}, u32[]{:S(2)}) copy-start(f32[8,128]{1,0:T(8,128)S(1)} %get-tuple-element.146) | copy-start | bytes 12292
  46.6 12.6 %copy-start.2 = (bf16[128,1536]{1,0:T(8,128)(2,1)S(1)}, bf16[128,1536]{1,0:T(8,128)(2,1)}, u32[]{:S(2)}) copy-start(bf16[128,1536]{1,0:T(8,128)(2,1)} %param.12) | copy-start | bytes 1179652
  73.8 2.6 %copy-start.3 = (bf16[128,1536]{1,0:T(8,128)(2,1)S(1)}, bf16[128,1536]{1,0:T(8,128)(2,1)}, u32[]{:S(2)}) copy-start(bf16[128,1536]{1,0:T(8,128)(2,1)} %param.12) | copy-start | bytes 1179652
  77.1 2.4 copy-start.26
  77.1 2.4 %copy-start.25 = (f32[1536]{0:T(1024)S(1)}, f32[1536]{0:T(1024)}, u32[]{:S(2)}) copy-start(f32[1536]{0:T(1024)} %get-tuple-element.10) | copy-start | bytes 18436
  77.1 2.5 %copy-start.24 = (f32[1536]{0:T(1024)S(1)}, f32[1536]{0:T(1024)}, u32[]{:S(2)}) copy-start(f32[1536]{0:T(1024)} %get-tuple-element.11) | copy-start | bytes 18436
  77.1 2.5 %copy-start.23 = (f32[1536]{0:T(1024)S(1)}, f32[1536]{0:T(1024)}, u32[]{:S(2)}) copy-start(f32[1536]{0:T(1024)} %get-tuple-element.12) | copy-start | bytes 18436
  77.2 2.5 %copy-start.22 = (f32[1536]{0:T(1024)S(1)}, f32[1536]{0:T(1024)}, u32[]{:S(2)}) copy-start(f32[1536]{0:T(1024)} %get-tuple-element.13) | copy-start | bytes 18436
  77.2 2.5 %copy-start.21 = (f32[1536]{0:T(1024)S(1)}, f32[1536]{0:T(1024)}, u32[]{:S(2)}) copy-start(f32[1536]{0:T(1024)} %get-tuple-element.14) | copy-start | bytes 18436
  77.2 2.5 %copy-start.20 = (f32[1536]{0:T(1024)S(1)}, f32[1536]{0:T(1024)}, u32[]{:S(2)}) copy-start(f32[1536]{0:T(1024)} %get-tuple-element.15) | copy-start | bytes 18436
  77.2 2.5 %copy-start.19 = (f32[1536]{0:T(1024)S(1)}, f32[1536]{0:T(1024)}, u32[]{:S(2)}) copy-start(f32[1536]{0:T(1024)} %get-tuple-element.16) | copy-start | bytes 18436
  77.2 2.5 %copy-start.18 = (f32[1536]{0:T(1024)S(1)}, f32[1536]{0:T(1024)}, u32[]{:S(2)}) copy-start(f32[1536]{0:T(1024)} %get-tuple-element.17) | copy-start | bytes 18436
  77.2 2.6 %copy-start.33 = (f32[128]{0:T(128)S(1)}, f32[128]{0:T(128)}, u32[]{:S(2)}) copy-start(f32[128]{0:T(128)} %copy-done.32) | copy-start | bytes 1540
  77.2 2.6 %copy-start.35 = (f32[128]{0:T(128)S(1)}, f32[128]{0:T(128)}, u32[]{:S(2)}) copy-start(f32[128]{0:T(128)} %copy-done.34) | copy-start | bytes 1540
  77.2 2.6 %copy-start.37 = (f32[128]{0:T(128)S(1)}, f32[128]{0:T(128)}, u32[]{:S(2)}) copy-start(f32[128]{0:T(128)} %copy-done.36) | copy-start | bytes 1540
  77.2 2.6 %copy-start.39 = (f32[128]{0:T(128)S(1)}, f32[128]{0:T(128)}, u32[]{:S(2)}) copy-start(f32[128]{0:T(128)} %copy-done.38) | copy-start | bytes 1540
  77.2 2.6 %copy-start.41 = (f32[128]{0:T(128)S(1)}, f32[128]{0:T(128)}, u32[]{:S(2)}) copy-start(f32[128]{0:T(128)} %copy-done.40) | copy-start | bytes 1540
  77.3 2.6 %copy-start.43 = (f32[128]{0:T(128)S(1)}, f32[128]{0:T(128)}, u32[]{:S(2)}) copy-start(f32[128]{0:T(128)} %copy-done.42) | copy-start | bytes 1540
  77.3 2.6 %copy-start.45 = (f32[128]{0:T(128)S(1)}, f32[128]{0:T(128)}, u32[]{:S(2)}) copy-start(f32[128]{0:T(128)} %copy-done.44) | copy-start | bytes 1540
  77.3 2.6 %copy-start.47 = (f32[128]{0:T(128)S(1)}, f32[128]{0:T(128)}, u32[]{:S(2)}) copy-start(f32[128]{0:T(128)} %copy-done.46) | copy-start | bytes 1540
  77.3 2.6 %copy-start.49 = (f32[128]{0:T(128)S(1)}, f32[128]{0:T(128)}, u32[]{:S(2)}) copy-start(f32[128]{0:T(128)} %copy-done.48) | copy-start | bytes 1540
  79.4 2.5 %copy-start.17 = (f32[1536]{0:T(1024)S(1)}, f32[1536]{0:T(1024)}, u32[]{:S(2)}) copy-start(f32[1536]{0:T(1024)} %get-tuple-element.27) | copy-start | bytes 18436
  79.4 2.5 %copy-start.16 = (f32[1536]{0:T(1024)S(1)}, f32[1536]{0:T(1024)}, u32[]{:S(2)}) copy-start(f32[1536]{0:T(1024)} %get-tuple-element.28) | copy-start | bytes 18436
  79.4 2.6 %copy-start.15 = (f32[1536]{0:T(1024)S(1)}, f32[1536]{0:T(1024)}, u32[]{:S(2)}) copy-start(f32[1536]{0:T(1024)} %get-tuple-element.29) | copy-start | bytes 18436
  79.4 2.6 %copy-start.14 = (f32[1536]{0:T(1024)S(1)}, f32[1536]{0:T(1024)}, u32[]{:S(2)}) copy-start(f32[1536]{0:T(1024)} %get-tuple-element.30) | copy-start | bytes 18436
  79.5 2.6 %copy-start.13 = (f32[1536]{0:T(1024)S(1)}, f32[1536]{0:T(1024)}, u32[]{:S(2)}) copy-start(f32[1536]{0:T(1024)} %get-tuple-element.31) | copy-start | bytes 18436
  79.5 2.6 %copy-start.12 = (f32[1536]{0:T(1024)S(1)}, f32[1536]{0:T(1024)}, u32[]{:S(2)}) copy-start(f32[1536]{0:T(1024)} %get-tuple-element.32) | copy-start | bytes 18436
  79.5 2.6 %copy-start.11 = (f32[1536]{0:T(1024)S(1)}, f32[1536]{0:T(1024)}, u32[]{:S(2)}) copy-start(f32[1536]{0:T(1024)} %get-tuple-element.33) | copy-start | bytes 18436
  79.5 2.7 %copy-start.30 = (f32[1536]{0:T(1024)S(1)}, f32[1536]{0:T(1024)}, u32[]{:S(2)}) copy-start(f32[1536]{0:T(1024)} %get-tuple-element.36) | copy-start | bytes 18436
  79.5 2.7 %copy-start.29 = (f32[1536]{0:T(1024)S(1)}, f32[1536]{0:T(1024)}, u32[]{:S(2)}) copy-start(f32[1536]{0:T(1024)} %get-tuple-element.37) | copy-start | bytes 18436
  79.5 2.7 %copy-start.28 = (f32[1536]{0:T(1024)S(1)}, f32[1536]{0:T(1024)}, u32[]{:S(2)}) copy-start(f32[1536]{0:T(1024)} %get-tuple-element.38) | copy-start | bytes 18436
  79.5 2.7 %copy-start.27 = (f32[1536]{0:T(1024)S(1)}, f32[1536]{0:T(1024)}, u32[]{:S(2)}) copy-start(f32[1536]{0:T(1024)} %get-tuple-element.39) | copy-start | bytes 18436
  81.8 35.0 %copy-start.1 = (bf16[768,1536]{1,0:T(8,128)(2,1)S(1)}, bf16[768,1536]{1,0:T(8,128)(2,1)}, u32[]{:S(2)}) copy-start(bf16[768,1536]{1,0:T(8,128)(2,1)} %all-gather.2.cloned.1.call-done) | copy-start | bytes 7077892
  83.4 46.7 %copy-start.5 = (bf16[128,768]{0,1:T(8,128)(2,1)S(1)}, bf16[128,768]{0,1:T(8,128)(2,1)}, u32[]{:S(2)}) copy-start(bf16[128,768]{0,1:T(8,128)(2,1)} %copy-done.4) | copy-start | bytes 589828
  109.3 34.3 %copy-start.54 = (f32[8,128]{1,0:T(8,128)S(1)}, f32[8,128]{1,0:T(8,128)}, u32[]{:S(2)}) copy-start(f32[8,128]{1,0:T(8,128)} %copy-done.53) | copy-start | bytes 12292
  109.3 15.9 %all-to-all-start.4 = ((f32[8,1,1536]{2,1,0:T(1,128)}), f32[8,1,1536]{2,1,0:T(1,128)}, u32[]{:S(2)}, u32[]{:S(2)}) async-start(f32[8,1,1536]{2,1,0:T(1,128)} %reshape.336), calls=%async_computation.5 | async-start | bytes 98304 | tf_op jit(solution)/shard_map/all_to_all | solution.py:143
  126.6 28.8 %copy-start.9 = (bf16[128,768]{0,1:T(8,128)(2,1)S(1)}, bf16[128,768]{0,1:T(8,128)(2,1)}, u32[]{:S(2)}) copy-start(bf16[128,768]{0,1:T(8,128)(2,1)} %copy-done.8) | copy-start | bytes 589828
  126.6 11.6 %all-to-all-start.5 = ((f32[8,1,1536]{2,1,0:T(1,128)}), f32[8,1,1536]{2,1,0:T(1,128)S(1)}, u32[]{:S(2)}, u32[]{:S(2)}) async-start(f32[8,1,1536]{2,1,0:T(1,128)} %broadcast_in_dim.69), calls=%async_computation.6 | async-start | bytes 98304 | tf_op jit(solution)/shard_map/all_to_all | solution.py:150
  138.9 8.6 %all-to-all-start.6 = ((f32[4,1,1536]{2,1,0:T(1,128)}), f32[4,1,1536]{2,1,0:T(1,128)S(1)}, u32[]{:S(2)}, u32[]{:S(2)}) async-start(f32[4,1,1536]{2,1,0:T(1,128)} %broadcast_in_dim.71), calls=%async_computation.7 | async-start | bytes 49152 | tf_op jit(solution)/shard_map/all_to_all | solution.py:150
  145.2 12.1 %copy-start.7 = (bf16[128,768]{0,1:T(8,128)(2,1)S(1)}, bf16[128,768]{0,1:T(8,128)(2,1)}, u32[]{:S(2)}) copy-start(bf16[128,768]{0,1:T(8,128)(2,1)} %copy-done.6) | copy-start | bytes 589828
  152.0 14.4 %all-to-all-start.8 = ((f32[8,4,1536]{2,1,0:T(4,128)}), f32[8,4,1536]{2,1,0:T(4,128)S(1)}, u32[]{:S(2)}, u32[]{:S(2)}) async-start(f32[8,4,1536]{2,1,0:T(4,128)} %broadcast_in_dim.75), calls=%async_computation.9 | async-start | bytes 393216 | tf_op jit(solution)/shard_map/all_to_all | solution.py:150
  166.4 22.9 %all-to-all-start.1 = ((bf16[32,4,2304]{2,1,0:T(4,128)(2,1)}), bf16[32,4,2304]{2,1,0:T(4,128)(2,1)S(1)}, u32[]{:S(2)}, u32[]{:S(2)}) async-start(bf16[32,4,2304]{2,1,0:T(4,128)(2,1)} %all_to_all.52), calls=%async_computation.1 | async-start | bytes 1179648 | tf_op jit(solution)/shard_map/all_to_all | solution.py:122
  212.9 12.0 %all-to-all-start.11 = ((f32[8,2,1536]{2,1,0:T(2,128)}), f32[8,2,1536]{2,1,0:T(2,128)S(1)}, u32[]{:S(2)}, u32[]{:S(2)}) async-start(f32[8,2,1536]{2,1,0:T(2,128)} %broadcast_in_dim.76), calls=%async_computation.12 | async-start | bytes 196608 | tf_op jit(solution)/shard_map/all_to_all | solution.py:150
  225.7 10.8 %all-to-all-start.12 = ((f32[4,12,1536]{2,1,0:T(8,128)}), f32[4,12,1536]{2,1,0:T(8,128)S(1)}, u32[]{:S(2)}, u32[]{:S(2)}) async-start(f32[4,12,1536]{2,1,0:T(8,128)} %broadcast_in_dim.78), calls=%async_computation.13 | async-start | bytes 786432 | tf_op jit(solution)/shard_map/all_to_all | solution.py:150
  (1 other events, 1.0 us)
Sparse Core Ops, SparseCore 0:
  10.1 46.7 all-gather.1
  79.7 61.6 reduce-scatter.1

commit v8 on v6

--- a/solution.py
+++ b/solution.py
@@ -127,12 +127,10 @@
     kernel_piece = sum_rows(kernel_part, FSDP)
     owned_rows = weight_share.shape[0]
     both = jnp.concatenate([weight_share, kernel_piece], axis=0)
-    inner = sum_rows(both, "dx")
-    inner_rows = inner.shape[0]
-    inner = gather_rows(sum_rows(inner, "dz"), "dz")[:inner_rows]
-    both = gather_rows(inner, "dx")[: both.shape[0]]
+    piece = sum_rows(both, DP)
+    both = gather_rows(gather_rows(piece, "dx"), "dz")[: both.shape[0]]
     weight_total = both[:owned_rows]
-    kernel_total = gather_rows(gather_rows(both[owned_rows:], "fc"), "fy")[: kernel.shape[0]]
+    kernel_total = gather_rows(both[owned_rows:], FSDP)[: kernel.shape[0]]
 
     return (
         result.astype(jnp.bfloat16),

time: 221 us -> 219 us (level)
  blocking collectives: 45.6 us -> 27.8 us
  starting transfers between devices: 36.3 us -> 46.3 us
  waiting for transfers between devices: 71.1 us -> 76.5 us
    all_to_all x2 -> x1, blocking collectives: 21.8 us -> 7.19 us  [gather_rows(): got = lax.all_to_all(copies, axis, split_axis=0, concat_axis=0, tiled=True)]
    all_to_all x2, starting transfers between devices: 7.78 us -> 17.9 us  [gather_rows(): got = lax.all_to_all(copies, axis, split_axis=0, concat_axis=0, tiled=True)]
    all_to_all x2, waiting for transfers between devices: 12.5 us -> 18 us  [gather_rows(): got = lax.all_to_all(copies, axis, split_axis=0, concat_axis=0, tiled=True)]
    all_to_all x2 -> x1, blocking collectives: 23.9 us -> 20.6 us  [sum_rows(): lax.all_to_all(padded.reshape(count, per, x.shape[1]), axis, split_axis=0...]
where the time goes in v8:
time: 219 us; the launch traced here: 218 us
  waiting for transfers between devices  76.5 us (35%)
  starting transfers between devices  46.3 us (21%)
  blocking collectives  27.8 us (13%)
  other arithmetic  26.8 us (12%)
  between operations  15.3 us (7%)
  matrix products  13.3 us (6%)
  local copies, waits for them, and re-layouts  11.8 us (5%)
    all_to_all x1, blocking collectives, sum_rows(): lax.all_to_all(padded.reshape(count, per, x.shape[1]), axis, split_axis=0...  20.6 us
    all_to_all x2, waiting for transfers between devices, gather_rows(): got = lax.all_to_all(copies, axis, split_axis=0, concat_axis=0, tiled=True)  18 us
    all_to_all x1, waiting for transfers between devices, body(): lax.all_to_all(returning, DP, split_axis=0, concat_axis=0, tiled=True)  17.9 us
    all_to_all x2, starting transfers between devices, gather_rows(): got = lax.all_to_all(copies, axis, split_axis=0, concat_axis=0, tiled=True)  17.9 us
    all_to_all x1, waiting for transfers between devices, body(): lax.all_to_all(outgoing, DP, split_axis=0, concat_axis=0, tiled=True)  16 us
    reduce_sum x4, other arithmetic, finish(): kernel[offset] * padded[offset:offset + length] * matching[:, None]  14.6 us
    all_to_all x1, starting transfers between devices, body(): lax.all_to_all(outgoing, DP, split_axis=0, concat_axis=0, tiled=True)  13.7 us
    reduce_scatter x1, waiting for transfers between devices, body(): lax.psum_scatter(jnp.einsum('rc,rd->cd', columns, mixed_grad, preferred_e...  12.3 us
  transfers between devices with their start and end apart: 7, of which 6 were waited for; matrix products, arithmetic and copies ran while one was open for 11% of the time, Pallas kernels for 0%

profile of v8, /device:TPU:1, one launch (start us, length us, event | category | flops | bytes accessed | tf_op | source)
XLA Modules:
  0.0 217.8 jit_solution(15162383935797481764)
XLA Ops:
  7.2 0.7 all-gather.2.cloned.1.call-update
  7.9 1.2 compare_select_fusion.1
  9.2 1.0 gather_fusion
  10.2 0.2 select_select_fusion.1
  10.4 1.0 all_to_all.31
  11.3 13.7 %all-to-all-start = ((bf16[32,4,2304]{2,1,0:T(4,128)(2,1)}), bf16[32,4,2304]{2,1,0:T(4,128)(2,1)S(1)}, u32[]{:S(2)}, u32[]{:S(2)}) async-start(bf16[32,4,2304]{2,1,0:T(4,128)(2,1)} %all_to_all.31), calls=%async_computation | async-start | bytes 1179648 | tf_op jit(solution)/shard_map/all_to_all | solution.py:87
  25.1 0.2 slice_reduce_fusion.29
  25.3 0.5 compare_select_fusion
  25.8 0.3 slice_reduce_fusion.30
  26.6 16.0 %all-to-all-done = bf16[32,4,2304]{2,1,0:T(4,128)(2,1)S(1)} async-done(((bf16[32,4,2304]{2,1,0:T(4,128)(2,1)}), bf16[32,4,2304]{2,1,0:T(4,128)(2,1)S(1)}, u32[]{:S(2)}, u32[]{:S(2)}) %all-to-all-start) | async-done | bytes 589856 | tf_op jit(solution)/shard_map/all_to_all | solution.py:87
  42.5 0.1 all_to_all.33
  42.7 1.0 gather_fusion.1
  43.6 0.2 select_select_fusion
  43.8 0.2 copy.47
  44.0 0.2 copy.46
  44.2 0.2 copy.45
  44.3 1.2 fusion.40
  45.5 0.6 copy-done.47
  46.1 0.5 convolution_convert_fusion.6
  46.6 11.6 %all-gather.2.cloned.1.call-done = bf16[768,1536]{1,0:T(8,128)(2,1)} async-done(((bf16[48,1536]{1,0:T(8,128)(2,1)}), bf16[768,1536]{1,0:T(8,128)(2,1)}) %all-gather.2.cloned.1.call-update) | async-done | bytes 2359312 | tf_op jit(solution)/shard_map/all_gather | solution.py:95
  58.2 2.2 fusion.2
  60.4 7.7 %multiply_reduce_fusion.31 = (f32[1536]{0:T(1024)}, f32[1536]{0:T(1024)}, f32[1536]{0:T(1024)}, f32[1536]{0:T(1024)}, f32[1536]{0:T(1024)}, /*index=5*/f32[1536]...) fusion(f32[128,1536]{1,0:T(8,128)S(1)} %fusion.2, ...), kind=kLoop, calls=%fused_computation.99 | loop fusion | flops 25152000 | bytes 3013632 | tf_op jit(solution)/shard_map/transpose(jvp())/reduce_sum | solution.py:77
  68.2 2.3 %multiply_reduce_fusion.16 = (f32[1536]{0:T(1024)}, f32[1536]{0:T(1024)}, f32[1536]{0:T(1024)}, f32[1536]{0:T(1024)}, f32[1536]{0:T(1024)}, /*index=5*/f32[1536]...) fusion(f32[128,1536]{1,0:T(8,128)S(1)} %get-tuple-element.69, ...), kind=kLoop, calls=%fused_computation.84 | loop fusion | flops 5294592 | bytes 2424832 | tf_op jit(solution)/shard_map/transpose(jvp())/reduce_sum | solution.py:77
  70.4 0.5 multiply_multiply_fusion.27
  71.0 0.7 multiply_multiply_fusion.29
  71.8 0.7 multiply_multiply_fusion.28
  72.5 2.6 %multiply_reduce_fusion.4 = (f32[1536]{0:T(1024)}, f32[1536]{0:T(1024)}, f32[1536]{0:T(1024)}, f32[1536]{0:T(1024)}, f32[128,1536]{1,0:T(8,128)S(1)}, /*index=5*...) fusion(f32[128,1536]{1,0:T(8,128)S(1)} %get-tuple-element.69, ...), kind=kLoop, calls=%fused_computation.72 | loop fusion | flops 5105664 | bytes 7535616 | tf_op jit(solution)/shard_map/transpose(jvp())/reduce_sum | solution.py:77
  75.1 2.6 %pad_add_fusion = f32[158,1536]{1,0:T(8,128)S(1)} fusion(f32[128,1536]{1,0:T(8,128)S(1)} %get-tuple-element.78, f32[128,1536]{1,0:T(8,128)S(1)} %get-tuple-element.80, f32[128,1536]{1,0:T(8,128)S(1)} %get-tuple-element.81, f32[128,1536]{1,0:T(8,128)S(1)} %get-tuple-element.82, f32[128,1536]{1,0:T(8,128)S(1)} %get-tuple-element.83, ...), kind=kLoop, calls=%fused_computation.59 | loop fusion | flops 5824512 | bytes 20631552 | tf_op jit(solution)/shard_map/transpose(jvp())/add_any | solution.py:77
  77.7 0.7 fusion.16
  78.6 2.2 convolution_convert_fusion
  81.1 2.0 multiply_reduce_fusion.22
  83.6 0.3 pad_add_fusion.7
  83.9 0.8 reshape.310
  84.7 4.6 %all-to-all-start.2 = ((f32[16,2,1536]{2,1,0:T(2,128)}), f32[16,2,1536]{2,1,0:T(2,128)S(1)}, u32[]{:S(2)}, u32[]{:S(2)}) async-start(f32[16,2,1536]{2,1,0:T(2,128)} %reshape.310), calls=%async_computation.3 | async-start | bytes 393216 | tf_op jit(solution)/shard_map/all_to_all | solution.py:147
  89.3 2.5 %convolution_convert_fusion.5 = bf16[128,768]{1,0:T(8,128)(2,1)S(1)} fusion(bf16[128,1536]{1,0:T(8,128)(2,1)S(1)} %fusion.16, bf16[768,1536]{1,0:T(8,128)(2,1)} %all-gather.2.cloned.1.call-done), kind=kOutput, calls=%fused_computation.54 | convolution fusion | flops 302088192 | bytes 2949120 | tf_op jit(solution)/shard_map/rd,cd->rc/dot_general | solution.py:112
  91.9 0.2 copy.49
  92.0 1.3 convolution_convert_fusion.2
  93.3 0.1 copy.55
  93.5 0.3 fusion.41
  93.8 1.6 convolution_convert_fusion.3
  95.4 0.1 copy.54
  95.5 1.6 convolution_convert_fusion.4
  97.1 0.1 copy.53
  97.3 1.8 scatter_custom_fusion
  99.0 1.0 all_to_all.34
  100.0 10.0 %all-to-all-start.1 = ((bf16[32,4,2304]{2,1,0:T(4,128)(2,1)}), bf16[32,4,2304]{2,1,0:T(4,128)(2,1)S(1)}, u32[]{:S(2)}, u32[]{:S(2)}) async-start(bf16[32,4,2304]{2,1,0:T(4,128)(2,1)} %all_to_all.34), calls=%async_computation.1 | async-start | bytes 1179648 | tf_op jit(solution)/shard_map/all_to_all | solution.py:122
  110.1 17.9 %all-to-all-done.1 = bf16[32,4,2304]{2,1,0:T(4,128)(2,1)S(1)} async-done(((bf16[32,4,2304]{2,1,0:T(4,128)(2,1)}), bf16[32,4,2304]{2,1,0:T(4,128)(2,1)S(1)}, u32[]{:S(2)}, u32[]{:S(2)}) %all-to-all-start.1) | async-done | bytes 589856 | tf_op jit(solution)/shard_map/all_to_all | solution.py:122
  128.1 0.1 reshape.342
  128.2 12.3 %reduce-scatter.2.cloned.1.call-done = bf16[48,1536]{1,0:T(8,128)(2,1)} async-done(((bf16[768,1536]{1,0:T(8,128)(2,1)}), bf16[48,1536]{1,0:T(8,128)(2,1)}) %reduce-scatter.2.cloned.1.call-update) | async-done | bytes 147472 | tf_op jit(solution)/shard_map/reduce_scatter | solution.py:104
  140.5 0.9 convert_element_type.216
  141.5 0.2 reshape.311
  141.7 20.6 %all_to_all.49 = f32[32,2,1536]{2,1,0:T(2,128)S(1)} all-to-all(f32[32,2,1536]{2,1,0:T(2,128)S(1)} %reshape.311), channel_id=1, replica_groups=mesh['dz'=8,'dx'=4,'fy'=8,'fc'=2] {'dz','dx'}, dimensions={0} | all-to-all | bytes 786432 | tf_op jit(solution)/shard_map/all_to_all | solution.py:147
  162.3 0.1 reduce_sum.365
  162.5 7.2 %all_to_all.50 = f32[4,2,1536]{2,1,0:T(2,128)S(1)} all-to-all(f32[4,2,1536]{2,1,0:T(2,128)S(1)} %broadcast_in_dim.57), channel_id=1, replica_groups=mesh['dz'=8,'dx'=4,'fy'=8,'fc'=2] {'dx'}, dimensions={0} | all-to-all | bytes 98304 | tf_op jit(solution)/shard_map/all_to_all | solution.py:154
  169.7 0.8 broadcast_in_dim.59
  170.5 3.5 %all-to-all-start.5 = ((f32[8,8,1536]{2,1,0:T(8,128)}), f32[8,8,1536]{2,1,0:T(8,128)S(1)}, u32[]{:S(2)}, u32[]{:S(2)}) async-start(f32[8,8,1536]{2,1,0:T(8,128)} %broadcast_in_dim.59), calls=%async_computation.6 | async-start | bytes 786432 | tf_op jit(solution)/shard_map/all_to_all | solution.py:154
  173.9 2.4 %scatter_custom_fusion.1 = bf16[128,2304]{1,0:T(8,128)(2,1)} fusion(s32[128]{0:T(128)} %get-tuple-element.108, bf16[128,2304]{1,0:T(8,128)(2,1)S(1)} %reshape.342, bf16[]{:T(256)} %constant.10.clone.1), kind=kCustom, calls=%fused_computation.146 | custom fusion | bytes 590336 | tf_op jit(solution)/shard_map/scatter | solution.py:124
  176.3 8.4 %all-to-all-done.5 = f32[8,8,1536]{2,1,0:T(8,128)S(1)} async-done(((f32[8,8,1536]{2,1,0:T(8,128)}), f32[8,8,1536]{2,1,0:T(8,128)S(1)}, u32[]{:S(2)}, u32[]{:S(2)}) %all-to-all-start.5) | async-done | bytes 393248 | tf_op jit(solution)/shard_map/all_to_all | solution.py:154
  184.7 0.7 broadcast_in_dim.60
  185.4 14.4 %all-to-all-start.6 = ((f32[16,2,1536]{2,1,0:T(2,128)}), f32[16,2,1536]{2,1,0:T(2,128)S(1)}, u32[]{:S(2)}, u32[]{:S(2)}) async-start(f32[16,2,1536]{2,1,0:T(2,128)} %broadcast_in_dim.60), calls=%async_computation.7 | async-start | bytes 393216 | tf_op jit(solution)/shard_map/all_to_all | solution.py:154
  199.8 0.7 fusion.23
  200.6 9.6 %all-to-all-done.6 = f32[16,2,1536]{2,1,0:T(2,128)S(1)} async-done(((f32[16,2,1536]{2,1,0:T(2,128)}), f32[16,2,1536]{2,1,0:T(2,128)S(1)}, u32[]{:S(2)}, u32[]{:S(2)}) %all-to-all-start.6) | async-done | bytes 196640 | tf_op jit(solution)/shard_map/all_to_all | solution.py:154
  210.1 0.1 reshape.313
  210.3 0.7 slice_multiply_fusion.1
  (146 shorter events, 1.0 us)
Async XLA Ops:
  7.2 2.0 copy-start
  7.2 51.1 %all-gather.2.cloned.1.call-start = ((), (), s32[]{:S(2)}) async-start(), calls=%async_computation.8 | async-start | bytes 2506752 | tf_op jit(solution)/shard_map/all_gather | solution.py:95
  9.1 1.0 copy-start.45
  10.1 14.9 %copy-start.4 = (f32[31,1536]{1,0:T(8,128)S(1)}, f32[31,1536]{1,0:T(8,128)}, u32[]{:S(2)}) copy-start(f32[31,1536]{1,0:T(8,128)} %param.11) | copy-start | bytes 571396
  10.2 15.1 %copy-start.46 = (s32[128]{0:T(128)S(1)}, s32[128]{0:T(128)}, u32[]{:S(2)}) copy-start(s32[128]{0:T(128)} %param.14) | copy-start | bytes 1540
  10.2 16.0 %copy-start.44 = (s32[128]{0:T(128)S(1)}, s32[128]{0:T(128)}, u32[]{:S(2)}) copy-start(s32[128]{0:T(128)} %param.15) | copy-start | bytes 1540
  11.3 31.2 %all-to-all-start = ((bf16[32,4,2304]{2,1,0:T(4,128)(2,1)}), bf16[32,4,2304]{2,1,0:T(4,128)(2,1)S(1)}, u32[]{:S(2)}, u32[]{:S(2)}) async-start(bf16[32,4,2304]{2,1,0:T(4,128)(2,1)} %all_to_all.31), calls=%async_computation | async-start | bytes 1179648 | tf_op jit(solution)/shard_map/all_to_all | solution.py:87
  25.0 115.5 %reduce-scatter.2.cloned.1.call-start = ((), (), s32[]{:S(2)}) async-start(), calls=%async_computation.9 | async-start | bytes 2506752 | tf_op jit(solution)/shard_map/reduce_scatter | solution.py:104
  26.4 44.6 %copy-start.38 = (f32[128]{0:T(128)}, f32[128]{0:T(128)S(1)}, u32[]{:S(2)}) copy-start(f32[128]{0:T(128)S(1)} %get-tuple-element.122) | copy-start | bytes 1540
  26.4 44.6 %copy-start.40 = (f32[128]{0:T(128)}, f32[128]{0:T(128)S(1)}, u32[]{:S(2)}) copy-start(f32[128]{0:T(128)S(1)} %get-tuple-element.123) | copy-start | bytes 1540
  26.4 44.6 %copy-start.42 = (f32[128]{0:T(128)}, f32[128]{0:T(128)S(1)}, u32[]{:S(2)}) copy-start(f32[128]{0:T(128)S(1)} %get-tuple-element.124) | copy-start | bytes 1540
  26.4 45.3 %copy-start.26 = (f32[128]{0:T(128)}, f32[128]{0:T(128)S(1)}, u32[]{:S(2)}) copy-start(f32[128]{0:T(128)S(1)} %get-tuple-element.116) | copy-start | bytes 1540
  26.4 45.3 %copy-start.28 = (f32[128]{0:T(128)}, f32[128]{0:T(128)S(1)}, u32[]{:S(2)}) copy-start(f32[128]{0:T(128)S(1)} %get-tuple-element.117) | copy-start | bytes 1540
  26.4 45.3 %copy-start.30 = (f32[128]{0:T(128)}, f32[128]{0:T(128)S(1)}, u32[]{:S(2)}) copy-start(f32[128]{0:T(128)S(1)} %get-tuple-element.118) | copy-start | bytes 1540
  26.4 45.3 %copy-start.32 = (f32[128]{0:T(128)}, f32[128]{0:T(128)S(1)}, u32[]{:S(2)}) copy-start(f32[128]{0:T(128)S(1)} %get-tuple-element.119) | copy-start | bytes 1540
  26.4 45.3 %copy-start.34 = (f32[128]{0:T(128)}, f32[128]{0:T(128)S(1)}, u32[]{:S(2)}) copy-start(f32[128]{0:T(128)S(1)} %get-tuple-element.120) | copy-start | bytes 1540
  26.5 45.3 %copy-start.36 = (f32[128]{0:T(128)}, f32[128]{0:T(128)S(1)}, u32[]{:S(2)}) copy-start(f32[128]{0:T(128)S(1)} %get-tuple-element.121) | copy-start | bytes 1540
  26.6 19.0 %copy-start.25 = (pred[128,128]{0,1:T(8,128)(4,1)}, pred[128,128]{0,1:T(8,128)(4,1)S(1)}, u32[]{:S(2)}) copy-start(pred[128,128]{0,1:T(8,128)(4,1)S(1)} %broadcast_compare_fusion) | copy-start | bytes 49156
  44.2 14.1 %copy-start.2 = (bf16[128,768]{0,1:T(8,128)(2,1)}, bf16[128,768]{0,1:T(8,128)(2,1)S(1)}, u32[]{:S(2)}) copy-start(bf16[128,768]{0,1:T(8,128)(2,1)S(1)} %copy.46) | copy-start | bytes 589828
  45.5 0.6 copy-start.47
  46.6 13.8 %copy-start.1 = (bf16[128,1536]{1,0:T(8,128)(2,1)S(1)}, bf16[128,1536]{1,0:T(8,128)(2,1)}, u32[]{:S(2)}) copy-start(bf16[128,1536]{1,0:T(8,128)(2,1)} %param.12) | copy-start | bytes 1179652
  78.4 2.4 %copy-start.20 = (f32[1536]{0:T(1024)S(1)}, f32[1536]{0:T(1024)}, u32[]{:S(2)}) copy-start(f32[1536]{0:T(1024)} %get-tuple-element.7) | copy-start | bytes 18436
  78.4 2.5 %copy-start.19 = (f32[1536]{0:T(1024)S(1)}, f32[1536]{0:T(1024)}, u32[]{:S(2)}) copy-start(f32[1536]{0:T(1024)} %get-tuple-element.8) | copy-start | bytes 18436
  78.4 2.5 %copy-start.18 = (f32[1536]{0:T(1024)S(1)}, f32[1536]{0:T(1024)}, u32[]{:S(2)}) copy-start(f32[1536]{0:T(1024)} %get-tuple-element.9) | copy-start | bytes 18436
  78.4 2.5 %copy-start.17 = (f32[1536]{0:T(1024)S(1)}, f32[1536]{0:T(1024)}, u32[]{:S(2)}) copy-start(f32[1536]{0:T(1024)} %get-tuple-element.10) | copy-start | bytes 18436
  78.4 2.5 %copy-start.16 = (f32[1536]{0:T(1024)S(1)}, f32[1536]{0:T(1024)}, u32[]{:S(2)}) copy-start(f32[1536]{0:T(1024)} %get-tuple-element.11) | copy-start | bytes 18436
  78.5 2.5 %copy-start.15 = (f32[1536]{0:T(1024)S(1)}, f32[1536]{0:T(1024)}, u32[]{:S(2)}) copy-start(f32[1536]{0:T(1024)} %get-tuple-element.12) | copy-start | bytes 18436
  78.5 2.5 %copy-start.14 = (f32[1536]{0:T(1024)S(1)}, f32[1536]{0:T(1024)}, u32[]{:S(2)}) copy-start(f32[1536]{0:T(1024)} %get-tuple-element.13) | copy-start | bytes 18436
  78.5 2.5 %copy-start.13 = (f32[1536]{0:T(1024)S(1)}, f32[1536]{0:T(1024)}, u32[]{:S(2)}) copy-start(f32[1536]{0:T(1024)} %get-tuple-element.14) | copy-start | bytes 18436
  78.5 2.6 %copy-start.12 = (f32[1536]{0:T(1024)S(1)}, f32[1536]{0:T(1024)}, u32[]{:S(2)}) copy-start(f32[1536]{0:T(1024)} %get-tuple-element.15) | copy-start | bytes 18436
  78.5 2.6 %copy-start.27 = (f32[128]{0:T(128)S(1)}, f32[128]{0:T(128)}, u32[]{:S(2)}) copy-start(f32[128]{0:T(128)} %copy-done.26) | copy-start | bytes 1540
  78.5 2.6 %copy-start.29 = (f32[128]{0:T(128)S(1)}, f32[128]{0:T(128)}, u32[]{:S(2)}) copy-start(f32[128]{0:T(128)} %copy-done.28) | copy-start | bytes 1540
  78.5 2.6 %copy-start.31 = (f32[128]{0:T(128)S(1)}, f32[128]{0:T(128)}, u32[]{:S(2)}) copy-start(f32[128]{0:T(128)} %copy-done.30) | copy-start | bytes 1540
  78.5 2.6 %copy-start.33 = (f32[128]{0:T(128)S(1)}, f32[128]{0:T(128)}, u32[]{:S(2)}) copy-start(f32[128]{0:T(128)} %copy-done.32) | copy-start | bytes 1540
  78.5 2.6 %copy-start.35 = (f32[128]{0:T(128)S(1)}, f32[128]{0:T(128)}, u32[]{:S(2)}) copy-start(f32[128]{0:T(128)} %copy-done.34) | copy-start | bytes 1540
  78.5 2.6 %copy-start.37 = (f32[128]{0:T(128)S(1)}, f32[128]{0:T(128)}, u32[]{:S(2)}) copy-start(f32[128]{0:T(128)} %copy-done.36) | copy-start | bytes 1540
  78.6 2.6 %copy-start.39 = (f32[128]{0:T(128)S(1)}, f32[128]{0:T(128)}, u32[]{:S(2)}) copy-start(f32[128]{0:T(128)} %copy-done.38) | copy-start | bytes 1540
  78.6 2.6 %copy-start.41 = (f32[128]{0:T(128)S(1)}, f32[128]{0:T(128)}, u32[]{:S(2)}) copy-start(f32[128]{0:T(128)} %copy-done.40) | copy-start | bytes 1540
  78.6 2.6 %copy-start.43 = (f32[128]{0:T(128)S(1)}, f32[128]{0:T(128)}, u32[]{:S(2)}) copy-start(f32[128]{0:T(128)} %copy-done.42) | copy-start | bytes 1540
  80.7 2.5 %copy-start.11 = (f32[1536]{0:T(1024)S(1)}, f32[1536]{0:T(1024)}, u32[]{:S(2)}) copy-start(f32[1536]{0:T(1024)} %get-tuple-element.25) | copy-start | bytes 18436
  80.7 2.5 %copy-start.10 = (f32[1536]{0:T(1024)S(1)}, f32[1536]{0:T(1024)}, u32[]{:S(2)}) copy-start(f32[1536]{0:T(1024)} %get-tuple-element.26) | copy-start | bytes 18436
  80.7 2.6 %copy-start.9 = (f32[1536]{0:T(1024)S(1)}, f32[1536]{0:T(1024)}, u32[]{:S(2)}) copy-start(f32[1536]{0:T(1024)} %get-tuple-element.27) | copy-start | bytes 18436
  80.7 2.6 %copy-start.8 = (f32[1536]{0:T(1024)S(1)}, f32[1536]{0:T(1024)}, u32[]{:S(2)}) copy-start(f32[1536]{0:T(1024)} %get-tuple-element.28) | copy-start | bytes 18436
  80.7 2.6 %copy-start.7 = (f32[1536]{0:T(1024)S(1)}, f32[1536]{0:T(1024)}, u32[]{:S(2)}) copy-start(f32[1536]{0:T(1024)} %get-tuple-element.29) | copy-start | bytes 18436
  80.8 2.6 %copy-start.6 = (f32[1536]{0:T(1024)S(1)}, f32[1536]{0:T(1024)}, u32[]{:S(2)}) copy-start(f32[1536]{0:T(1024)} %get-tuple-element.30) | copy-start | bytes 18436
  80.8 2.6 %copy-start.5 = (f32[1536]{0:T(1024)S(1)}, f32[1536]{0:T(1024)}, u32[]{:S(2)}) copy-start(f32[1536]{0:T(1024)} %get-tuple-element.31) | copy-start | bytes 18436
  80.8 2.7 %copy-start.24 = (f32[1536]{0:T(1024)S(1)}, f32[1536]{0:T(1024)}, u32[]{:S(2)}) copy-start(f32[1536]{0:T(1024)} %get-tuple-element.34) | copy-start | bytes 18436
  80.8 2.7 %copy-start.23 = (f32[1536]{0:T(1024)S(1)}, f32[1536]{0:T(1024)}, u32[]{:S(2)}) copy-start(f32[1536]{0:T(1024)} %get-tuple-element.35) | copy-start | bytes 18436
  80.8 2.7 %copy-start.22 = (f32[1536]{0:T(1024)S(1)}, f32[1536]{0:T(1024)}, u32[]{:S(2)}) copy-start(f32[1536]{0:T(1024)} %get-tuple-element.36) | copy-start | bytes 18436
  80.8 2.7 %copy-start.21 = (f32[1536]{0:T(1024)S(1)}, f32[1536]{0:T(1024)}, u32[]{:S(2)}) copy-start(f32[1536]{0:T(1024)} %get-tuple-element.37) | copy-start | bytes 18436
  83.5 8.5 %copy-start.3 = (bf16[128,768]{0,1:T(8,128)(2,1)S(1)}, bf16[128,768]{0,1:T(8,128)(2,1)}, u32[]{:S(2)}) copy-start(bf16[128,768]{0,1:T(8,128)(2,1)} %copy-done.2) | copy-start | bytes 589828
  83.6 8.5 %copy-start.48 = (f32[8,128]{1,0:T(8,128)S(1)}, f32[8,128]{1,0:T(8,128)}, u32[]{:S(2)}) copy-start(f32[8,128]{1,0:T(8,128)} %copy-done.47) | copy-start | bytes 12292
  84.7 15.3 %all-to-all-start.2 = ((f32[16,2,1536]{2,1,0:T(2,128)}), f32[16,2,1536]{2,1,0:T(2,128)S(1)}, u32[]{:S(2)}, u32[]{:S(2)}) async-start(f32[16,2,1536]{2,1,0:T(2,128)} %reshape.310), calls=%async_computation.3 | async-start | bytes 393216 | tf_op jit(solution)/shard_map/all_to_all | solution.py:147
  100.0 28.1 %all-to-all-start.1 = ((bf16[32,4,2304]{2,1,0:T(4,128)(2,1)}), bf16[32,4,2304]{2,1,0:T(4,128)(2,1)S(1)}, u32[]{:S(2)}, u32[]{:S(2)}) async-start(bf16[32,4,2304]{2,1,0:T(4,128)(2,1)} %all_to_all.34), calls=%async_computation.1 | async-start | bytes 1179648 | tf_op jit(solution)/shard_map/all_to_all | solution.py:122
  170.5 14.2 %all-to-all-start.5 = ((f32[8,8,1536]{2,1,0:T(8,128)}), f32[8,8,1536]{2,1,0:T(8,128)S(1)}, u32[]{:S(2)}, u32[]{:S(2)}) async-start(f32[8,8,1536]{2,1,0:T(8,128)} %broadcast_in_dim.59), calls=%async_computation.6 | async-start | bytes 786432 | tf_op jit(solution)/shard_map/all_to_all | solution.py:154
  185.4 24.7 %all-to-all-start.6 = ((f32[16,2,1536]{2,1,0:T(2,128)}), f32[16,2,1536]{2,1,0:T(2,128)S(1)}, u32[]{:S(2)}, u32[]{:S(2)}) async-start(f32[16,2,1536]{2,1,0:T(2,128)} %broadcast_in_dim.60), calls=%async_computation.7 | async-start | bytes 393216 | tf_op jit(solution)/shard_map/all_to_all | solution.py:154
Sparse Core Ops, SparseCore 0:
  10.1 48.0 all-gather.1
  81.0 59.5 reduce-scatter.1

commit v9 on v8

--- a/solution.py
+++ b/solution.py
@@ -101,14 +101,8 @@
     )
     mixed_grad, kernel_part = pullback(cotangent.astype(jnp.float32))
     columns = context
-    weight_share = lax.psum_scatter(
-        jnp.einsum("rc,rd->cd", columns, mixed_grad, preferred_element_type=jnp.float32).astype(
-            jnp.bfloat16
-        ),
-        FSDP,
-        scatter_dimension=0,
-        tiled=True,
-    ).astype(jnp.float32)
+    weight_part = jnp.einsum("rc,rd->cd", columns, mixed_grad, preferred_element_type=jnp.float32)
+    weight_share = core_then_chip_sum(weight_part.astype(jnp.bfloat16)).astype(jnp.float32)
     context_grad = jnp.einsum(
         "rd,cd->rc",
         mixed_grad,
@@ -154,6 +148,15 @@
     got = lax.all_to_all(copies, axis, split_axis=0, concat_axis=0, tiled=True)
     return got.reshape(count * piece.shape[0], piece.shape[1])
 
+
+def core_then_chip_sum(x):
+    chips, cores = lax.axis_size("fy"), lax.axis_size("fc")
+    blocks = x.reshape(chips, cores, x.shape[0] // (chips * cores), x.shape[1]).swapaxes(0, 1)
+    got = lax.all_to_all(blocks, "fc", split_axis=0, concat_axis=0, tiled=True)
+    summed = jnp.sum(got.astype(jnp.float32), axis=0).astype(x.dtype)
+    flat = summed.reshape(-1, x.shape[1])
+    return lax.psum_scatter(flat, "fy", scatter_dimension=0, tiled=True)
+
 def solution(mesh):
     dp_count, fsdp_count = mesh.devices.shape
     fine = Mesh(

time: 219 us -> 232 us (1.059)
  other arithmetic: 26.8 us -> 47.3 us
  waiting for transfers between devices: 76.5 us -> 62.2 us
  blocking collectives: 27.8 us -> 34.8 us
    reduce_scatter x1, waiting for transfers between devices: 12.3 us -> 1.34 us  [core_then_chip_sum(): return lax.psum_scatter(flat, 'fy', scatter_dimension=0, tiled=True)]
    mul x3, other arithmetic: 1.94 us -> 10.1 us  [finish(): kernel[offset] * padded[offset:offset + length] * matching[:, None]]
    all_to_all x0 -> x1, blocking collectives: none -> 6.41 us  [core_then_chip_sum(): got = lax.all_to_all(blocks, 'fc', split_axis=0, concat_axis=0, tiled=True)]
    add_any x1, other arithmetic: 2.6 us -> 7.17 us  [finish(): padded[offset:offset + length]]
    reduce_sum x0 -> x1, other arithmetic: none -> 3.61 us  [core_then_chip_sum(): summed = jnp.sum(got.astype(jnp.float32), axis=0).astype(x.dtype)]
where the time goes in v9:
time: 232 us; the launch traced here: 231 us
  waiting for transfers between devices  62.2 us (27%)
  other arithmetic  47.3 us (20%)
  starting transfers between devices  45.5 us (20%)
  blocking collectives  34.8 us (15%)
  between operations  15.8 us (7%)
  local copies, waits for them, and re-layouts  13.2 us (6%)
  matrix products  11.7 us (5%)
    all_to_all x1, blocking collectives, sum_rows(): lax.all_to_all(padded.reshape(count, per, x.shape[1]), axis, split_axis=0...  21.2 us
    all_to_all x2, waiting for transfers between devices, gather_rows(): got = lax.all_to_all(copies, axis, split_axis=0, concat_axis=0, tiled=True)  17.9 us
    reduce_sum x4, other arithmetic, finish(): kernel[offset] * padded[offset:offset + length] * matching[:, None]  16.8 us
    all_to_all x1, waiting for transfers between devices, body(): lax.all_to_all(returning, DP, split_axis=0, concat_axis=0, tiled=True)  16.6 us
    all_to_all x2, starting transfers between devices, gather_rows(): got = lax.all_to_all(copies, axis, split_axis=0, concat_axis=0, tiled=True)  16.6 us
    all_to_all x1, waiting for transfers between devices, body(): lax.all_to_all(outgoing, DP, split_axis=0, concat_axis=0, tiled=True)  14.7 us
    all_to_all x1, starting transfers between devices, body(): lax.all_to_all(outgoing, DP, split_axis=0, concat_axis=0, tiled=True)  13.7 us
    all_gather x1, waiting for transfers between devices, body(): lax.all_gather(out_weight, FSDP, axis=0, tiled=True)  11 us
  transfers between devices with their start and end apart: 7, of which 6 were waited for; matrix products, arithmetic and copies ran while one was open for 11% of the time, Pallas kernels for 0%

profile of v9, /device:TPU:1, one launch (start us, length us, event | category | flops | bytes accessed | tf_op | source)
XLA Modules:
  0.0 230.6 jit_solution(5608514810648205561)
XLA Ops:
  7.2 0.7 all-gather.2.cloned.1.call-update
  7.9 1.1 compare_select_fusion.1
  9.1 1.0 gather_fusion
  10.1 0.2 select_select_fusion.1
  10.3 1.0 all_to_all.34
  11.2 13.7 %all-to-all-start = ((bf16[32,4,2304]{2,1,0:T(4,128)(2,1)}), bf16[32,4,2304]{2,1,0:T(4,128)(2,1)S(1)}, u32[]{:S(2)}, u32[]{:S(2)}) async-start(bf16[32,4,2304]{2,1,0:T(4,128)(2,1)} %all_to_all.34), calls=%async_computation | async-start | bytes 1179648 | tf_op jit(solution)/shard_map/all_to_all | solution.py:87
  24.9 0.2 slice_reduce_fusion.29
  25.3 0.5 compare_select_fusion
  25.8 0.3 slice_reduce_fusion.30
  26.2 0.7 compare_convert_fusion.28
  26.9 0.6 compare_convert_fusion.29
  27.7 14.7 %all-to-all-done = bf16[32,4,2304]{2,1,0:T(4,128)(2,1)S(1)} async-done(((bf16[32,4,2304]{2,1,0:T(4,128)(2,1)}), bf16[32,4,2304]{2,1,0:T(4,128)(2,1)S(1)}, u32[]{:S(2)}, u32[]{:S(2)}) %all-to-all-start) | async-done | bytes 589856 | tf_op jit(solution)/shard_map/all_to_all | solution.py:87
  42.6 1.0 gather_fusion.1
  43.5 0.2 select_select_fusion
  43.8 0.2 copy.60
  43.9 0.2 copy.59
  44.1 0.2 copy.58
  44.3 1.8 fusion.40
  46.0 1.2 convolution_convert_fusion.6
  47.3 11.0 %all-gather.2.cloned.1.call-done = bf16[768,1536]{1,0:T(8,128)(2,1)} async-done(((bf16[48,1536]{1,0:T(8,128)(2,1)}), bf16[768,1536]{1,0:T(8,128)(2,1)}) %all-gather.2.cloned.1.call-update) | async-done | bytes 2359312 | tf_op jit(solution)/shard_map/all_gather | solution.py:95
  58.2 2.2 fusion.2
  60.7 7.9 %multiply_reduce_fusion.31 = (f32[1536]{0:T(1024)S(1)}, f32[1536]{0:T(1024)S(1)}, f32[1536]{0:T(1024)S(1)}, f32[1536]{0:T(1024)S(1)}, f32[1536]{0:T(1024)S(1)}, ...) fusion(f32[128,1536]{1,0:T(8,128)S(1)} %fusion.2, ...), kind=kLoop, calls=%fused_computation.100 | loop fusion | flops 25152000 | bytes 3013632 | tf_op jit(solution)/shard_map/transpose(jvp())/reduce_sum | solution.py:77
  68.6 1.8 multiply_reduce_fusion.22
  70.5 3.1 %multiply_reduce_fusion.16 = (f32[1536]{0:T(1024)S(1)}, f32[1536]{0:T(1024)S(1)}, f32[1536]{0:T(1024)S(1)}, f32[1536]{0:T(1024)S(1)}, f32[1536]{0:T(1024)S(1)}, ...) fusion(f32[128,1536]{1,0:T(8,128)S(1)} %get-tuple-element.69, ...), kind=kLoop, calls=%fused_computation.85 | loop fusion | flops 5294592 | bytes 2424832 | tf_op jit(solution)/shard_map/transpose(jvp())/reduce_sum | solution.py:77
  73.7 2.5 %multiply_multiply_fusion.27 = (f32[128,1536]{1,0:T(8,128)}, f32[128,1536]{1,0:T(8,128)}, f32[128,1536]{1,0:T(8,128)}, f32[128,1536]{1,0:T(8,128)}, f32[128,1536]{1,0:T(8,128)}, /*index=5*/f32[128,1536]{1,0:T(8,128)}) fusion(f32[128,1536]{1,0:T(8,128)S(1)} %get-tuple-element.69, f32[128]{0:T(128)S(1)} %get-tuple-element.137, ...), kind=kLoop, calls=%fused_computation.131 | loop fusion | flops 2359296 | bytes 5544960 | tf_op jit(solution)/shard_map/transpose(jvp())/mul | solution.py:77
  76.6 3.4 %multiply_multiply_fusion.29 = (f32[128,1536]{1,0:T(8,128)S(1)}, f32[128,1536]{1,0:T(8,128)S(1)}, f32[128,1536]{1,0:T(8,128)S(1)}, f32[128,1536]{1,0:T(8,128)}, ...) fusion(f32[128,1536]{1,0:T(8,128)S(1)} %get-tuple-element.69, ...), kind=kLoop, calls=%fused_computation.133 | loop fusion | flops 3538944 | bytes 7924224 | tf_op jit(solution)/shard_map/transpose(jvp())/mul | solution.py:77
  80.2 4.1 %multiply_multiply_fusion.28 = (f32[128,1536]{1,0:T(8,128)}, f32[128,1536]{1,0:T(8,128)}, f32[128,1536]{1,0:T(8,128)}, f32[128,1536]{1,0:T(8,128)}, f32[128,1536...) fusion(f32[128,1536]{1,0:T(8,128)S(1)} %get-tuple-element.69, ...), kind=kLoop, calls=%fused_computation.132 | loop fusion | flops 3342336 | bytes 7923712 | tf_op jit(solution)/shard_map/transpose(jvp())/mul | solution.py:77
  84.7 4.0 %multiply_reduce_fusion.4 = (f32[1536]{0:T(1024)S(1)}, f32[1536]{0:T(1024)S(1)}, f32[1536]{0:T(1024)S(1)}, f32[1536]{0:T(1024)S(1)}, f32[128,1536]{1,0:T(8,128)}...) fusion(f32[128,1536]{1,0:T(8,128)S(1)} %get-tuple-element.69, ...), kind=kLoop, calls=%fused_computation.73 | loop fusion | flops 5105664 | bytes 7535616 | tf_op jit(solution)/shard_map/transpose(jvp())/reduce_sum | solution.py:77
  88.8 0.3 pad_add_fusion.7
  89.1 0.7 pad.272
  89.8 1.7 reshape.318
  91.5 7.2 %pad_add_fusion = f32[158,1536]{1,0:T(8,128)S(1)} fusion(f32[128,1536]{1,0:T(8,128)} %get-tuple-element.78, f32[128,1536]{1,0:T(8,128)S(1)} %get-tuple-element.80, f32[128,1536]{1,0:T(8,128)S(1)} %get-tuple-element.81, f32[128,1536]{1,0:T(8,128)} %get-tuple-element.82, f32[128,1536]{1,0:T(8,128)} %get-tuple-element.83, f32[128,1536]{1,0:T(8,128)} %get-tuple-element.84, ...), kind=kLoop, calls=%fused_computation.60 | loop fusion | flops 5824512 | bytes 20631552 | tf_op jit(solution)/shard_map/transpose(jvp())/add_any | solution.py:77
  98.8 0.7 fusion.16
  99.4 0.8 convolution_convert_fusion
  100.2 0.2 copy.79
  100.4 6.4 %all_to_all.54 = bf16[2,8,48,1536]{3,2,1,0:T(8,128)(2,1)} all-to-all(bf16[2,8,48,1536]{3,2,1,0:T(8,128)(2,1)S(1)} %bitcast.45), channel_id=1, replica_groups=mesh['dz'=8,'dx'=4,'fy'=8,'fc'=2] {'fc'}, dimensions={0} | all-to-all | bytes 4718592 | tf_op jit(solution)/shard_map/all_to_all | solution.py:155
  106.8 4.7 %all-to-all-start.3 = ((f32[16,2,1536]{2,1,0:T(2,128)}), f32[16,2,1536]{2,1,0:T(2,128)}, u32[]{:S(2)}, u32[]{:S(2)}) async-start(f32[16,2,1536]{2,1,0:T(2,128)} %reshape.318), calls=%async_computation.4 | async-start | bytes 393216 | tf_op jit(solution)/shard_map/all_to_all | solution.py:141
  111.6 3.6 %reduce_sum.323 = bf16[8,48,1536]{2,1,0:T(8,128)(2,1)} reduce(bf16[2,8,48,1536]{3,2,1,0:T(8,128)(2,1)} %all_to_all.54, bf16[]{:T(256)} %constant.11.clone.1), dimensions={0}, to_apply=%region_5.7 | reduce | flops 589824 | bytes 3538946 | tf_op jit(solution)/shard_map/reduce_sum | solution.py:156
  115.2 0.9 convolution_convert_fusion.5
  116.1 0.2 copy.62
  116.3 1.6 convolution_convert_fusion.2
  117.9 0.1 copy.68
  118.1 0.3 fusion.41
  118.4 1.6 convolution_convert_fusion.3
  120.1 1.6 convolution_convert_fusion.4
  121.8 1.8 scatter_custom_fusion
  123.6 1.0 all_to_all.37
  124.5 10.4 %all-to-all-start.1 = ((bf16[32,4,2304]{2,1,0:T(4,128)(2,1)}), bf16[32,4,2304]{2,1,0:T(4,128)(2,1)S(1)}, u32[]{:S(2)}, u32[]{:S(2)}) async-start(bf16[32,4,2304]{2,1,0:T(4,128)(2,1)} %all_to_all.37), calls=%async_computation.1 | async-start | bytes 1179648 | tf_op jit(solution)/shard_map/all_to_all | solution.py:116
  134.9 1.0 reduce_sum.379
  135.9 16.6 %all-to-all-done.1 = bf16[32,4,2304]{2,1,0:T(4,128)(2,1)S(1)} async-done(((bf16[32,4,2304]{2,1,0:T(4,128)(2,1)}), bf16[32,4,2304]{2,1,0:T(4,128)(2,1)S(1)}, u32[]{:S(2)}, u32[]{:S(2)}) %all-to-all-start.1) | async-done | bytes 589856 | tf_op jit(solution)/shard_map/all_to_all | solution.py:116
  152.7 1.3 reduce-scatter.2.cloned.1.call-done
  154.1 0.9 convert_element_type.218
  155.0 0.2 reshape.319
  155.3 21.2 %all_to_all.55 = f32[32,2,1536]{2,1,0:T(2,128)S(1)} all-to-all(f32[32,2,1536]{2,1,0:T(2,128)S(1)} %reshape.319), channel_id=1, replica_groups=mesh['dz'=8,'dx'=4,'fy'=8,'fc'=2] {'dz','dx'}, dimensions={0} | all-to-all | bytes 786432 | tf_op jit(solution)/shard_map/all_to_all | solution.py:141
  176.6 7.2 %all_to_all.56 = f32[4,2,1536]{2,1,0:T(2,128)S(1)} all-to-all(f32[4,2,1536]{2,1,0:T(2,128)S(1)} %broadcast_in_dim.57), channel_id=1, replica_groups=mesh['dz'=8,'dx'=4,'fy'=8,'fc'=2] {'dx'}, dimensions={0} | all-to-all | bytes 98304 | tf_op jit(solution)/shard_map/all_to_all | solution.py:148
  183.9 0.8 broadcast_in_dim.59
  184.6 3.5 %all-to-all-start.6 = ((f32[8,8,1536]{2,1,0:T(8,128)}), f32[8,8,1536]{2,1,0:T(8,128)S(1)}, u32[]{:S(2)}, u32[]{:S(2)}) async-start(f32[8,8,1536]{2,1,0:T(8,128)} %broadcast_in_dim.59), calls=%async_computation.7 | async-start | bytes 786432 | tf_op jit(solution)/shard_map/all_to_all | solution.py:148
  188.1 2.4 %scatter_custom_fusion.1 = bf16[128,2304]{1,0:T(8,128)(2,1)} fusion(s32[128]{0:T(128)} %get-tuple-element.108, bf16[128,2304]{1,0:T(8,128)(2,1)S(1)} %reshape.350, bf16[]{:T(256)} %constant.11.clone.1), kind=kCustom, calls=%fused_computation.147 | custom fusion | bytes 590336 | tf_op jit(solution)/shard_map/scatter | solution.py:118
  190.5 8.3 %all-to-all-done.6 = f32[8,8,1536]{2,1,0:T(8,128)S(1)} async-done(((f32[8,8,1536]{2,1,0:T(8,128)}), f32[8,8,1536]{2,1,0:T(8,128)S(1)}, u32[]{:S(2)}, u32[]{:S(2)}) %all-to-all-start.6) | async-done | bytes 393248 | tf_op jit(solution)/shard_map/all_to_all | solution.py:148
  198.8 0.7 broadcast_in_dim.60
  199.5 13.1 %all-to-all-start.7 = ((f32[16,2,1536]{2,1,0:T(2,128)}), f32[16,2,1536]{2,1,0:T(2,128)S(1)}, u32[]{:S(2)}, u32[]{:S(2)}) async-start(f32[16,2,1536]{2,1,0:T(2,128)} %broadcast_in_dim.60), calls=%async_computation.8 | async-start | bytes 393216 | tf_op jit(solution)/shard_map/all_to_all | solution.py:148
  212.6 0.7 fusion.23
  213.4 9.6 %all-to-all-done.7 = f32[16,2,1536]{2,1,0:T(2,128)S(1)} async-done(((f32[16,2,1536]{2,1,0:T(2,128)}), f32[16,2,1536]{2,1,0:T(2,128)S(1)}, u32[]{:S(2)}, u32[]{:S(2)}) %all-to-all-start.7) | async-done | bytes 196640 | tf_op jit(solution)/shard_map/all_to_all | solution.py:148
  223.1 0.7 slice_multiply_fusion.1
  (231 shorter events, 1.8 us)
Async XLA Ops:
  7.2 51.1 %all-gather.2.cloned.1.call-start = ((), (), s32[]{:S(2)}) async-start(), calls=%async_computation.9 | async-start | bytes 2506752 | tf_op jit(solution)/shard_map/all_gather | solution.py:95
  10.1 14.9 %copy-start.15 = (f32[31,1536]{1,0:T(8,128)S(1)}, f32[31,1536]{1,0:T(8,128)}, u32[]{:S(2)}) copy-start(f32[31,1536]{1,0:T(8,128)} %param.11) | copy-start | bytes 571396
  10.1 15.1 %copy-start.89 = (s32[128]{0:T(128)S(1)}, s32[128]{0:T(128)}, u32[]{:S(2)}) copy-start(s32[128]{0:T(128)} %param.14) | copy-start | bytes 1540
  10.1 16.2 %copy-start.87 = (s32[128]{0:T(128)S(1)}, s32[128]{0:T(128)}, u32[]{:S(2)}) copy-start(s32[128]{0:T(128)} %param.15) | copy-start | bytes 1540
  11.2 31.2 %all-to-all-start = ((bf16[32,4,2304]{2,1,0:T(4,128)(2,1)}), bf16[32,4,2304]{2,1,0:T(4,128)(2,1)S(1)}, u32[]{:S(2)}, u32[]{:S(2)}) async-start(bf16[32,4,2304]{2,1,0:T(4,128)(2,1)} %all_to_all.34), calls=%async_computation | async-start | bytes 1179648 | tf_op jit(solution)/shard_map/all_to_all | solution.py:87
  25.2 35.3 %copy-start.16 = (f32[1536]{0:T(1024)}, f32[1536]{0:T(1024)S(1)}, u32[]{:S(2)}) copy-start(f32[1536]{0:T(1024)S(1)} %get-tuple-element.62) | copy-start | bytes 18436
  25.2 35.3 %copy-start.18 = (f32[1536]{0:T(1024)}, f32[1536]{0:T(1024)S(1)}, u32[]{:S(2)}) copy-start(f32[1536]{0:T(1024)S(1)} %get-tuple-element.63) | copy-start | bytes 18436
  25.2 35.3 %copy-start.20 = (f32[1536]{0:T(1024)}, f32[1536]{0:T(1024)S(1)}, u32[]{:S(2)}) copy-start(f32[1536]{0:T(1024)S(1)} %get-tuple-element.65) | copy-start | bytes 18436
  25.2 35.3 %copy-start.22 = (f32[1536]{0:T(1024)}, f32[1536]{0:T(1024)S(1)}, u32[]{:S(2)}) copy-start(f32[1536]{0:T(1024)S(1)} %get-tuple-element.66) | copy-start | bytes 18436
  25.2 35.3 %copy-start.48 = (f32[1536]{0:T(1024)}, f32[1536]{0:T(1024)S(1)}, u32[]{:S(2)}) copy-start(f32[1536]{0:T(1024)S(1)} %get-tuple-element.68) | copy-start | bytes 18436
  25.2 35.3 %copy-start.50 = (f32[1536]{0:T(1024)}, f32[1536]{0:T(1024)S(1)}, u32[]{:S(2)}) copy-start(f32[1536]{0:T(1024)S(1)} %get-tuple-element.58) | copy-start | bytes 18436
  25.2 35.3 %copy-start.52 = (f32[1536]{0:T(1024)}, f32[1536]{0:T(1024)S(1)}, u32[]{:S(2)}) copy-start(f32[1536]{0:T(1024)S(1)} %get-tuple-element.59) | copy-start | bytes 18436
  25.2 35.3 %copy-start.54 = (f32[1536]{0:T(1024)}, f32[1536]{0:T(1024)S(1)}, u32[]{:S(2)}) copy-start(f32[1536]{0:T(1024)S(1)} %get-tuple-element.60) | copy-start | bytes 18436
  25.2 35.3 %copy-start.56 = (f32[1536]{0:T(1024)}, f32[1536]{0:T(1024)S(1)}, u32[]{:S(2)}) copy-start(f32[1536]{0:T(1024)S(1)} %get-tuple-element.61) | copy-start | bytes 18436
  25.3 35.3 %copy-start.58 = (f32[1536]{0:T(1024)}, f32[1536]{0:T(1024)S(1)}, u32[]{:S(2)}) copy-start(f32[1536]{0:T(1024)S(1)} %get-tuple-element.67) | copy-start | bytes 18436
  26.1 34.4 %copy-start.24 = (f32[1536]{0:T(1024)}, f32[1536]{0:T(1024)S(1)}, u32[]{:S(2)}) copy-start(f32[1536]{0:T(1024)S(1)} %get-tuple-element.45) | copy-start | bytes 18436
  26.1 34.4 %copy-start.26 = (f32[1536]{0:T(1024)}, f32[1536]{0:T(1024)S(1)}, u32[]{:S(2)}) copy-start(f32[1536]{0:T(1024)S(1)} %get-tuple-element.46) | copy-start | bytes 18436
  26.1 34.4 %copy-start.28 = (f32[1536]{0:T(1024)}, f32[1536]{0:T(1024)S(1)}, u32[]{:S(2)}) copy-start(f32[1536]{0:T(1024)S(1)} %get-tuple-element.47) | copy-start | bytes 18436
  26.1 34.4 %copy-start.30 = (f32[1536]{0:T(1024)}, f32[1536]{0:T(1024)S(1)}, u32[]{:S(2)}) copy-start(f32[1536]{0:T(1024)S(1)} %get-tuple-element.48) | copy-start | bytes 18436
  26.1 34.4 %copy-start.32 = (f32[1536]{0:T(1024)}, f32[1536]{0:T(1024)S(1)}, u32[]{:S(2)}) copy-start(f32[1536]{0:T(1024)S(1)} %get-tuple-element.49) | copy-start | bytes 18436
  26.2 34.4 %copy-start.34 = (f32[1536]{0:T(1024)}, f32[1536]{0:T(1024)S(1)}, u32[]{:S(2)}) copy-start(f32[1536]{0:T(1024)S(1)} %get-tuple-element.50) | copy-start | bytes 18436
  26.2 34.4 %copy-start.36 = (f32[1536]{0:T(1024)}, f32[1536]{0:T(1024)S(1)}, u32[]{:S(2)}) copy-start(f32[1536]{0:T(1024)S(1)} %get-tuple-element.51) | copy-start | bytes 18436
  26.2 34.4 %copy-start.38 = (f32[1536]{0:T(1024)}, f32[1536]{0:T(1024)S(1)}, u32[]{:S(2)}) copy-start(f32[1536]{0:T(1024)S(1)} %get-tuple-element.52) | copy-start | bytes 18436
  26.2 34.4 %copy-start.40 = (f32[1536]{0:T(1024)}, f32[1536]{0:T(1024)S(1)}, u32[]{:S(2)}) copy-start(f32[1536]{0:T(1024)S(1)} %get-tuple-element.53) | copy-start | bytes 18436
  26.2 34.4 %copy-start.42 = (f32[1536]{0:T(1024)}, f32[1536]{0:T(1024)S(1)}, u32[]{:S(2)}) copy-start(f32[1536]{0:T(1024)S(1)} %get-tuple-element.54) | copy-start | bytes 18436
  26.2 34.4 %copy-start.44 = (f32[1536]{0:T(1024)}, f32[1536]{0:T(1024)S(1)}, u32[]{:S(2)}) copy-start(f32[1536]{0:T(1024)S(1)} %get-tuple-element.55) | copy-start | bytes 18436
  26.2 34.4 %copy-start.46 = (f32[1536]{0:T(1024)}, f32[1536]{0:T(1024)S(1)}, u32[]{:S(2)}) copy-start(f32[1536]{0:T(1024)S(1)} %get-tuple-element.56) | copy-start | bytes 18436
  26.9 43.5 %copy-start.85 = (f32[128]{0:T(128)}, f32[128]{0:T(128)S(1)}, u32[]{:S(2)}) copy-start(f32[128]{0:T(128)S(1)} %get-tuple-element.131) | copy-start | bytes 1540
  27.5 41.0 %copy-start.61 = (f32[128]{0:T(128)}, f32[128]{0:T(128)S(1)}, u32[]{:S(2)}) copy-start(f32[128]{0:T(128)S(1)} %get-tuple-element.116) | copy-start | bytes 1540
  27.6 41.0 %copy-start.63 = (f32[128]{0:T(128)}, f32[128]{0:T(128)S(1)}, u32[]{:S(2)}) copy-start(f32[128]{0:T(128)S(1)} %get-tuple-element.117) | copy-start | bytes 1540
  27.6 41.0 %copy-start.65 = (f32[128]{0:T(128)}, f32[128]{0:T(128)S(1)}, u32[]{:S(2)}) copy-start(f32[128]{0:T(128)S(1)} %get-tuple-element.118) | copy-start | bytes 1540
  27.6 41.0 %copy-start.67 = (f32[128]{0:T(128)}, f32[128]{0:T(128)S(1)}, u32[]{:S(2)}) copy-start(f32[128]{0:T(128)S(1)} %get-tuple-element.119) | copy-start | bytes 1540
  27.6 41.0 %copy-start.69 = (f32[128]{0:T(128)}, f32[128]{0:T(128)S(1)}, u32[]{:S(2)}) copy-start(f32[128]{0:T(128)S(1)} %get-tuple-element.120) | copy-start | bytes 1540
  27.6 41.0 %copy-start.71 = (f32[128]{0:T(128)}, f32[128]{0:T(128)S(1)}, u32[]{:S(2)}) copy-start(f32[128]{0:T(128)S(1)} %get-tuple-element.121) | copy-start | bytes 1540
  27.6 41.0 %copy-start.73 = (f32[128]{0:T(128)}, f32[128]{0:T(128)S(1)}, u32[]{:S(2)}) copy-start(f32[128]{0:T(128)S(1)} %get-tuple-element.122) | copy-start | bytes 1540
  27.6 41.0 %copy-start.75 = (f32[128]{0:T(128)}, f32[128]{0:T(128)S(1)}, u32[]{:S(2)}) copy-start(f32[128]{0:T(128)S(1)} %get-tuple-element.123) | copy-start | bytes 1540
  27.6 41.0 %copy-start.77 = (f32[128]{0:T(128)}, f32[128]{0:T(128)S(1)}, u32[]{:S(2)}) copy-start(f32[128]{0:T(128)S(1)} %get-tuple-element.124) | copy-start | bytes 1540
  27.6 42.8 %copy-start.79 = (f32[128]{0:T(128)}, f32[128]{0:T(128)S(1)}, u32[]{:S(2)}) copy-start(f32[128]{0:T(128)S(1)} %get-tuple-element.125) | copy-start | bytes 1540
  27.6 42.8 %copy-start.81 = (f32[128]{0:T(128)}, f32[128]{0:T(128)S(1)}, u32[]{:S(2)}) copy-start(f32[128]{0:T(128)S(1)} %get-tuple-element.126) | copy-start | bytes 1540
  27.6 42.8 %copy-start.83 = (f32[128]{0:T(128)}, f32[128]{0:T(128)S(1)}, u32[]{:S(2)}) copy-start(f32[128]{0:T(128)S(1)} %get-tuple-element.127) | copy-start | bytes 1540
  27.7 18.3 %copy-start.60 = (pred[128,128]{0,1:T(8,128)(4,1)}, pred[128,128]{0,1:T(8,128)(4,1)S(1)}, u32[]{:S(2)}) copy-start(pred[128,128]{0,1:T(8,128)(4,1)S(1)} %broadcast_compare_fusion) | copy-start | bytes 49156
  44.1 16.3 %copy-start.13 = (bf16[128,768]{0,1:T(8,128)(2,1)}, bf16[128,768]{0,1:T(8,128)(2,1)S(1)}, u32[]{:S(2)}) copy-start(bf16[128,768]{0,1:T(8,128)(2,1)S(1)} %copy.59) | copy-start | bytes 589828
  44.3 16.1 %copy-start.9 = (bf16[128,768]{0,1:T(8,128)(2,1)}, bf16[128,768]{0,1:T(8,128)(2,1)S(1)}, u32[]{:S(2)}) copy-start(bf16[128,768]{0,1:T(8,128)(2,1)S(1)} %copy.58) | copy-start | bytes 589828
  47.2 13.4 %copy-start.8 = (bf16[128,1536]{1,0:T(8,128)(2,1)S(1)}, bf16[128,1536]{1,0:T(8,128)(2,1)}, u32[]{:S(2)}) copy-start(bf16[128,1536]{1,0:T(8,128)(2,1)} %param.12) | copy-start | bytes 1179652
  76.4 3.6 %copy-start.25 = (f32[1536]{0:T(1024)S(1)}, f32[1536]{0:T(1024)}, u32[]{:S(2)}) copy-start(f32[1536]{0:T(1024)} %copy-done.24) | copy-start | bytes 18436
  76.4 3.6 %copy-start.27 = (f32[1536]{0:T(1024)S(1)}, f32[1536]{0:T(1024)}, u32[]{:S(2)}) copy-start(f32[1536]{0:T(1024)} %copy-done.26) | copy-start | bytes 18436
  76.4 3.6 %copy-start.29 = (f32[1536]{0:T(1024)S(1)}, f32[1536]{0:T(1024)}, u32[]{:S(2)}) copy-start(f32[1536]{0:T(1024)} %copy-done.28) | copy-start | bytes 18436
  80.1 4.6 %copy-start.17 = (f32[1536]{0:T(1024)S(1)}, f32[1536]{0:T(1024)}, u32[]{:S(2)}) copy-start(f32[1536]{0:T(1024)} %copy-done.16) | copy-start | bytes 18436
  80.1 4.6 %copy-start.19 = (f32[1536]{0:T(1024)S(1)}, f32[1536]{0:T(1024)}, u32[]{:S(2)}) copy-start(f32[1536]{0:T(1024)} %copy-done.18) | copy-start | bytes 18436
  80.1 4.6 %copy-start.21 = (f32[1536]{0:T(1024)S(1)}, f32[1536]{0:T(1024)}, u32[]{:S(2)}) copy-start(f32[1536]{0:T(1024)} %copy-done.20) | copy-start | bytes 18436
  80.1 4.6 %copy-start.23 = (f32[1536]{0:T(1024)S(1)}, f32[1536]{0:T(1024)}, u32[]{:S(2)}) copy-start(f32[1536]{0:T(1024)} %copy-done.22) | copy-start | bytes 18436
  80.2 4.6 %copy-start.86 = (f32[128]{0:T(128)S(1)}, f32[128]{0:T(128)}, u32[]{:S(2)}) copy-start(f32[128]{0:T(128)} %copy-done.85) | copy-start | bytes 1540
  91.5 7.2 %copy-start.2 = (f32[128,1536]{1,0:T(8,128)S(1)}, f32[128,1536]{1,0:T(8,128)}, u32[]{:S(2)}) copy-start(f32[128,1536]{1,0:T(8,128)} %get-tuple-element.72) | copy-start | bytes 2359300
  91.5 7.2 %copy-start.3 = (f32[128,1536]{1,0:T(8,128)S(1)}, f32[128,1536]{1,0:T(8,128)}, u32[]{:S(2)}) copy-start(f32[128,1536]{1,0:T(8,128)} %get-tuple-element.73) | copy-start | bytes 2359300
  91.5 7.2 %copy-start.4 = (f32[128,1536]{1,0:T(8,128)S(1)}, f32[128,1536]{1,0:T(8,128)}, u32[]{:S(2)}) copy-start(f32[128,1536]{1,0:T(8,128)} %get-tuple-element.74) | copy-start | bytes 2359300
  91.5 7.2 %copy-start.5 = (f32[128,1536]{1,0:T(8,128)S(1)}, f32[128,1536]{1,0:T(8,128)}, u32[]{:S(2)}) copy-start(f32[128,1536]{1,0:T(8,128)} %get-tuple-element.75) | copy-start | bytes 2359300
  91.5 7.2 %copy-start.6 = (f32[128,1536]{1,0:T(8,128)S(1)}, f32[128,1536]{1,0:T(8,128)}, u32[]{:S(2)}) copy-start(f32[128,1536]{1,0:T(8,128)} %get-tuple-element.77) | copy-start | bytes 2359300
  91.5 7.3 %copy-start.7 = (f32[128,1536]{1,0:T(8,128)S(1)}, f32[128,1536]{1,0:T(8,128)}, u32[]{:S(2)}) copy-start(f32[128,1536]{1,0:T(8,128)} %get-tuple-element.71) | copy-start | bytes 2359300
  106.8 17.7 %all-to-all-start.3 = ((f32[16,2,1536]{2,1,0:T(2,128)}), f32[16,2,1536]{2,1,0:T(2,128)}, u32[]{:S(2)}, u32[]{:S(2)}) async-start(f32[16,2,1536]{2,1,0:T(2,128)} %reshape.318), calls=%async_computation.4 | async-start | bytes 393216 | tf_op jit(solution)/shard_map/all_to_all | solution.py:141
  111.5 3.7 %copy-start.1 = (bf16[768,1536]{1,0:T(8,128)(2,1)S(1)}, bf16[768,1536]{1,0:T(8,128)(2,1)}, u32[]{:S(2)}) copy-start(bf16[768,1536]{1,0:T(8,128)(2,1)} %all-gather.2.cloned.1.call-done) | copy-start | bytes 7077892
  111.5 42.5 %reduce-scatter.2.cloned.1.call-start = ((), (), s32[]{:S(2)}) async-start(), calls=%async_computation.10 | async-start | bytes 1327104 | tf_op jit(solution)/shard_map/reduce_scatter | solution.py:158
  124.5 28.0 %all-to-all-start.1 = ((bf16[32,4,2304]{2,1,0:T(4,128)(2,1)}), bf16[32,4,2304]{2,1,0:T(4,128)(2,1)S(1)}, u32[]{:S(2)}, u32[]{:S(2)}) async-start(bf16[32,4,2304]{2,1,0:T(4,128)(2,1)} %all_to_all.37), calls=%async_computation.1 | async-start | bytes 1179648 | tf_op jit(solution)/shard_map/all_to_all | solution.py:116
  184.6 14.1 %all-to-all-start.6 = ((f32[8,8,1536]{2,1,0:T(8,128)}), f32[8,8,1536]{2,1,0:T(8,128)S(1)}, u32[]{:S(2)}, u32[]{:S(2)}) async-start(f32[8,8,1536]{2,1,0:T(8,128)} %broadcast_in_dim.59), calls=%async_computation.7 | async-start | bytes 786432 | tf_op jit(solution)/shard_map/all_to_all | solution.py:148
  199.5 23.5 %all-to-all-start.7 = ((f32[16,2,1536]{2,1,0:T(2,128)}), f32[16,2,1536]{2,1,0:T(2,128)S(1)}, u32[]{:S(2)}, u32[]{:S(2)}) async-start(f32[16,2,1536]{2,1,0:T(2,128)} %broadcast_in_dim.60), calls=%async_computation.8 | async-start | bytes 393216 | tf_op jit(solution)/shard_map/all_to_all | solution.py:148
  (33 other events, 95.3 us)
Sparse Core Ops, SparseCore 0:
  10.1 48.0 all-gather.1
  115.3 38.6 reduce-scatter.1

commit v10 on v8

--- a/solution.py
+++ b/solution.py
@@ -123,14 +123,14 @@
     source_index = jnp.where(present, send_rows, row_count)
     projected_grad = jnp.zeros_like(projected).at[source_index].set(arrived, mode="drop")
     scale_factor = (row_count * lax.axis_size(DP) * lax.axis_size(FSDP)) ** (-0.5)
-    weight_share, arrived = lax.optimization_barrier((weight_share, arrived))
-    kernel_piece = sum_rows(kernel_part, FSDP)
+    kernel_rows = gather_rows(sum_rows(kernel_part, FSDP), FSDP)[: kernel.shape[0]]
+    weight_share, arrived, kernel_rows = lax.optimization_barrier((weight_share, arrived, kernel_rows))
     owned_rows = weight_share.shape[0]
-    both = jnp.concatenate([weight_share, kernel_piece], axis=0)
+    both = jnp.concatenate([weight_share, kernel_rows], axis=0)
     piece = sum_rows(both, DP)
     both = gather_rows(gather_rows(piece, "dx"), "dz")[: both.shape[0]]
     weight_total = both[:owned_rows]
-    kernel_total = gather_rows(both[owned_rows:], FSDP)[: kernel.shape[0]]
+    kernel_total = both[owned_rows:]
 
     return (
         result.astype(jnp.bfloat16),

time: 219 us -> 223 us (1.018)
  the two profiles are of different devices: /device:TPU:1 before, /device:TPU:25 now
where the time goes in v10:
time: 223 us; the launch traced here: 222 us
  waiting for transfers between devices  77.9 us (35%)
  blocking collectives  39 us (17%)
  starting transfers between devices  37.3 us (17%)
  other arithmetic  25.7 us (12%)
  between operations  15.8 us (7%)
  local copies, waits for them, and re-layouts  13.5 us (6%)
  matrix products  13.1 us (6%)
    all_to_all x1, blocking collectives, sum_rows(): lax.all_to_all(padded.reshape(count, per, x.shape[1]), axis, split_axis=0...  30.8 us
    all_to_all x2, waiting for transfers between devices, gather_rows(): got = lax.all_to_all(copies, axis, split_axis=0, concat_axis=0, tiled=True)  23.9 us
    all_to_all x1, waiting for transfers between devices, body(): lax.all_to_all(returning, DP, split_axis=0, concat_axis=0, tiled=True)  17.6 us
    all_to_all x1, waiting for transfers between devices, body(): lax.all_to_all(outgoing, DP, split_axis=0, concat_axis=0, tiled=True)  14.8 us
    reduce_sum x4, other arithmetic, finish(): kernel[offset] * padded[offset:offset + length] * matching[:, None]  14.8 us
    all_to_all x1, starting transfers between devices, body(): lax.all_to_all(outgoing, DP, split_axis=0, concat_axis=0, tiled=True)  12.9 us
    all_gather x1, waiting for transfers between devices, body(): lax.all_gather(out_weight, FSDP, axis=0, tiled=True)  11.9 us
    all_to_all x1, starting transfers between devices, body(): lax.all_to_all(returning, DP, split_axis=0, concat_axis=0, tiled=True)  10.2 us
  transfers between devices with their start and end apart: 7, of which 7 were waited for; matrix products, arithmetic and copies ran while one was open for 11% of the time, Pallas kernels for 0%

profile of v10, /device:TPU:25, one launch (start us, length us, event | category | flops | bytes accessed | tf_op | source)
XLA Modules:
  0.0 222.2 jit_solution(9095830994278058538)
XLA Ops:
  7.2 0.7 all-gather.2.cloned.1.call-update
  7.9 0.7 compare_select_fusion.1
  8.6 1.0 gather_fusion
  9.6 0.2 select_select_fusion.1
  9.8 1.0 all_to_all.31
  10.7 12.9 %all-to-all-start = ((bf16[32,4,2304]{2,1,0:T(4,128)(2,1)}), bf16[32,4,2304]{2,1,0:T(4,128)(2,1)S(1)}, u32[]{:S(2)}, u32[]{:S(2)}) async-start(bf16[32,4,2304]{2,1,0:T(4,128)(2,1)} %all_to_all.31), calls=%async_computation | async-start | bytes 1179648 | tf_op jit(solution)/shard_map/all_to_all | solution.py:87
  23.7 0.8 slice_reduce_fusion.29
  24.5 0.9 slice_reduce_fusion.30
  25.5 0.7 compare_convert_fusion.29
  26.3 14.8 %all-to-all-done = bf16[32,4,2304]{2,1,0:T(4,128)(2,1)S(1)} async-done(((bf16[32,4,2304]{2,1,0:T(4,128)(2,1)}), bf16[32,4,2304]{2,1,0:T(4,128)(2,1)S(1)}, u32[]{:S(2)}, u32[]{:S(2)}) %all-to-all-start) | async-done | bytes 589856 | tf_op jit(solution)/shard_map/all_to_all | solution.py:87
  41.1 0.1 all_to_all.33
  41.3 1.0 gather_fusion.1
  42.2 0.2 select_select_fusion
  42.5 0.2 copy.47
  42.6 0.2 copy.46
  42.8 0.2 copy.45
  43.0 1.2 fusion.39
  44.1 0.5 convolution_convert_fusion.6
  44.9 11.9 %all-gather.2.cloned.1.call-done = bf16[768,1536]{1,0:T(8,128)(2,1)} async-done(((bf16[48,1536]{1,0:T(8,128)(2,1)}), bf16[768,1536]{1,0:T(8,128)(2,1)}) %all-gather.2.cloned.1.call-update) | async-done | bytes 2359312 | tf_op jit(solution)/shard_map/all_gather | solution.py:95
  56.9 2.2 fusion.2
  59.5 7.8 %multiply_reduce_fusion.31 = (f32[1536]{0:T(1024)}, f32[1536]{0:T(1024)}, f32[1536]{0:T(1024)}, f32[1536]{0:T(1024)}, f32[1536]{0:T(1024)}, /*index=5*/f32[1536]...) fusion(f32[128,1536]{1,0:T(8,128)S(1)} %fusion.2, ...), kind=kLoop, calls=%fused_computation.99 | loop fusion | flops 25152000 | bytes 3013632 | tf_op jit(solution)/shard_map/transpose(jvp())/reduce_sum | solution.py:77
  67.3 2.4 %multiply_reduce_fusion.16 = (f32[1536]{0:T(1024)}, f32[1536]{0:T(1024)}, f32[1536]{0:T(1024)}, f32[1536]{0:T(1024)}, f32[1536]{0:T(1024)}, /*index=5*/f32[1536]...) fusion(f32[128,1536]{1,0:T(8,128)S(1)} %get-tuple-element.71, ...), kind=kLoop, calls=%fused_computation.84 | loop fusion | flops 5294592 | bytes 2424832 | tf_op jit(solution)/shard_map/transpose(jvp())/reduce_sum | solution.py:77
  69.6 0.5 multiply_multiply_fusion.27
  70.2 0.7 multiply_multiply_fusion.29
  70.9 0.7 multiply_multiply_fusion.28
  71.6 2.6 %multiply_reduce_fusion.4 = (f32[1536]{0:T(1024)}, f32[1536]{0:T(1024)}, f32[1536]{0:T(1024)}, f32[1536]{0:T(1024)S(1)}, f32[128,1536]{1,0:T(8,128)S(1)}, /*inde...) fusion(f32[128,1536]{1,0:T(8,128)S(1)} %get-tuple-element.71, ...), kind=kLoop, calls=%fused_computation.72 | loop fusion | flops 5105664 | bytes 7535616 | tf_op jit(solution)/shard_map/transpose(jvp())/reduce_sum | solution.py:77
  74.2 2.6 %pad_add_fusion = f32[158,1536]{1,0:T(8,128)S(1)} fusion(f32[128,1536]{1,0:T(8,128)S(1)} %get-tuple-element.80, f32[128,1536]{1,0:T(8,128)S(1)} %get-tuple-element.82, f32[128,1536]{1,0:T(8,128)S(1)} %get-tuple-element.83, f32[128,1536]{1,0:T(8,128)S(1)} %get-tuple-element.84, f32[128,1536]{1,0:T(8,128)S(1)} %get-tuple-element.85, ...), kind=kLoop, calls=%fused_computation.59 | loop fusion | flops 5824512 | bytes 20631552 | tf_op jit(solution)/shard_map/transpose(jvp())/add_any | solution.py:77
  76.8 0.7 fusion.16
  77.7 2.1 convolution_convert_fusion
  80.3 2.0 multiply_reduce_fusion.22
  82.7 0.3 pad_add_fusion.7
  83.1 0.8 reshape.310
  83.8 5.1 %all-to-all-start.2 = ((f32[16,2,1536]{2,1,0:T(2,128)}), f32[16,2,1536]{2,1,0:T(2,128)S(1)}, u32[]{:S(2)}, u32[]{:S(2)}) async-start(f32[16,2,1536]{2,1,0:T(2,128)} %reshape.310), calls=%async_computation.3 | async-start | bytes 393216 | tf_op jit(solution)/shard_map/all_to_all | solution.py:147
  88.9 2.5 %convolution_convert_fusion.5 = bf16[128,768]{1,0:T(8,128)(2,1)S(1)} fusion(bf16[128,1536]{1,0:T(8,128)(2,1)S(1)} %fusion.16, bf16[768,1536]{1,0:T(8,128)(2,1)} %all-gather.2.cloned.1.call-done), kind=kOutput, calls=%fused_computation.54 | convolution fusion | flops 302088192 | bytes 2949120 | tf_op jit(solution)/shard_map/rd,cd->rc/dot_general | solution.py:112
  91.4 0.2 copy.49
  91.6 1.3 convolution_convert_fusion.2
  92.9 0.1 copy.55
  93.1 0.3 fusion.40
  93.3 3.5 %all-to-all-done.2 = f32[16,2,1536]{2,1,0:T(2,128)S(1)} async-done(((f32[16,2,1536]{2,1,0:T(2,128)}), f32[16,2,1536]{2,1,0:T(2,128)S(1)}, u32[]{:S(2)}, u32[]{:S(2)}) %all-to-all-start.2) | async-done | bytes 196640 | tf_op jit(solution)/shard_map/all_to_all | solution.py:147
  96.9 0.7 broadcast_in_dim.57
  97.7 5.5 %all-to-all-start.3 = ((f32[16,2,1536]{2,1,0:T(2,128)}), f32[16,2,1536]{2,1,0:T(2,128)S(1)}, u32[]{:S(2)}, u32[]{:S(2)}) async-start(f32[16,2,1536]{2,1,0:T(2,128)} %broadcast_in_dim.57), calls=%async_computation.4 | async-start | bytes 393216 | tf_op jit(solution)/shard_map/all_to_all | solution.py:154
  103.1 1.5 convolution_convert_fusion.3
  104.7 0.1 copy.54
  104.8 1.5 convolution_convert_fusion.4
  106.3 0.1 copy.53
  106.5 1.6 scatter_custom_fusion
  108.1 1.0 all_to_all.34
  109.1 2.6 %all-to-all-done.3 = f32[16,2,1536]{2,1,0:T(2,128)S(1)} async-done(((f32[16,2,1536]{2,1,0:T(2,128)}), f32[16,2,1536]{2,1,0:T(2,128)S(1)}, u32[]{:S(2)}, u32[]{:S(2)}) %all-to-all-start.3) | async-done | bytes 196640 | tf_op jit(solution)/shard_map/all_to_all | solution.py:154
  111.7 10.2 %all-to-all-start.1 = ((bf16[32,4,2304]{2,1,0:T(4,128)(2,1)}), bf16[32,4,2304]{2,1,0:T(4,128)(2,1)S(1)}, u32[]{:S(2)}, u32[]{:S(2)}) async-start(bf16[32,4,2304]{2,1,0:T(4,128)(2,1)} %all_to_all.34), calls=%async_computation.1 | async-start | bytes 1179648 | tf_op jit(solution)/shard_map/all_to_all | solution.py:122
  121.9 0.1 reshape.311
  122.1 17.6 %all-to-all-done.1 = bf16[32,4,2304]{2,1,0:T(4,128)(2,1)S(1)} async-done(((bf16[32,4,2304]{2,1,0:T(4,128)(2,1)}), bf16[32,4,2304]{2,1,0:T(4,128)(2,1)S(1)}, u32[]{:S(2)}, u32[]{:S(2)}) %all-to-all-start.1) | async-done | bytes 589856 | tf_op jit(solution)/shard_map/all_to_all | solution.py:122
  139.7 0.1 reshape.342
  139.9 5.4 %reduce-scatter.2.cloned.1.call-done = bf16[48,1536]{1,0:T(8,128)(2,1)} async-done(((bf16[768,1536]{1,0:T(8,128)(2,1)}), bf16[48,1536]{1,0:T(8,128)(2,1)}) %reduce-scatter.2.cloned.1.call-update) | async-done | bytes 147472 | tf_op jit(solution)/shard_map/reduce_scatter | solution.py:104
  145.2 0.9 convert_element_type.216
  146.2 0.3 reshape.312
  146.5 30.8 %all_to_all.49 = f32[32,3,1536]{2,1,0:T(4,128)S(1)} all-to-all(f32[32,3,1536]{2,1,0:T(4,128)S(1)} %reshape.312), channel_id=1, replica_groups=mesh['dz'=8,'dx'=4,'fy'=8,'fc'=2] {'dz','dx'}, dimensions={0} | all-to-all | bytes 1179648 | tf_op jit(solution)/shard_map/all_to_all | solution.py:147
  177.3 0.1 reduce_sum.365
  177.4 8.2 %all_to_all.50 = f32[4,3,1536]{2,1,0:T(4,128)S(1)} all-to-all(f32[4,3,1536]{2,1,0:T(4,128)S(1)} %broadcast_in_dim.58), channel_id=1, replica_groups=mesh['dz'=8,'dx'=4,'fy'=8,'fc'=2] {'dx'}, dimensions={0} | all-to-all | bytes 147456 | tf_op jit(solution)/shard_map/all_to_all | solution.py:154
  185.7 1.0 broadcast_in_dim.60
  186.6 3.5 %all-to-all-start.6 = ((f32[8,12,1536]{2,1,0:T(8,128)}), f32[8,12,1536]{2,1,0:T(8,128)S(1)}, u32[]{:S(2)}, u32[]{:S(2)}) async-start(f32[8,12,1536]{2,1,0:T(8,128)} %broadcast_in_dim.60), calls=%async_computation.7 | async-start | bytes 1572864 | tf_op jit(solution)/shard_map/all_to_all | solution.py:154
  190.2 2.3 %scatter_custom_fusion.1 = bf16[128,2304]{1,0:T(8,128)(2,1)} fusion(s32[128]{0:T(128)S(1)} %get-tuple-element.110, bf16[128,2304]{1,0:T(8,128)(2,1)S(1)} %reshape.342, bf16[]{:T(256)} %constant.10.clone.1), kind=kCustom, calls=%fused_computation.145 | custom fusion | bytes 589826 | tf_op jit(solution)/shard_map/scatter | solution.py:124
  192.5 21.3 %all-to-all-done.6 = f32[8,12,1536]{2,1,0:T(8,128)S(1)} async-done(((f32[8,12,1536]{2,1,0:T(8,128)}), f32[8,12,1536]{2,1,0:T(8,128)S(1)}, u32[]{:S(2)}, u32[]{:S(2)}) %all-to-all-start.6) | async-done | bytes 589856 | tf_op jit(solution)/shard_map/all_to_all | solution.py:154
  213.9 0.7 slice_multiply_fusion.1
  214.6 0.7 mul.1323
  (209 shorter events, 1.2 us)
Async XLA Ops:
  7.2 49.6 %all-gather.2.cloned.1.call-start = ((), (), s32[]{:S(2)}) async-start(), calls=%async_computation.8 | async-start | bytes 2506752 | tf_op jit(solution)/shard_map/all_gather | solution.py:95
  9.6 14.1 %copy-start.4 = (f32[31,1536]{1,0:T(8,128)S(1)}, f32[31,1536]{1,0:T(8,128)}, u32[]{:S(2)}) copy-start(f32[31,1536]{1,0:T(8,128)} %param.11) | copy-start | bytes 571396
  9.6 14.9 %copy-start.77 = (s32[128]{0:T(128)S(1)}, s32[128]{0:T(128)}, u32[]{:S(2)}) copy-start(s32[128]{0:T(128)} %param.14) | copy-start | bytes 1540
  9.6 15.8 %copy-start.75 = (s32[128]{0:T(128)S(1)}, s32[128]{0:T(128)}, u32[]{:S(2)}) copy-start(s32[128]{0:T(128)} %param.15) | copy-start | bytes 1540
  10.7 30.4 %all-to-all-start = ((bf16[32,4,2304]{2,1,0:T(4,128)(2,1)}), bf16[32,4,2304]{2,1,0:T(4,128)(2,1)S(1)}, u32[]{:S(2)}, u32[]{:S(2)}) async-start(bf16[32,4,2304]{2,1,0:T(4,128)(2,1)} %all_to_all.31), calls=%async_computation | async-start | bytes 1179648 | tf_op jit(solution)/shard_map/all_to_all | solution.py:87
  23.6 121.6 %reduce-scatter.2.cloned.1.call-start = ((), (), s32[]{:S(2)}) async-start(), calls=%async_computation.9 | async-start | bytes 2506752 | tf_op jit(solution)/shard_map/reduce_scatter | solution.py:104
  26.3 17.8 %copy-start.55 = (pred[128,128]{0,1:T(8,128)(4,1)}, pred[128,128]{0,1:T(8,128)(4,1)S(1)}, u32[]{:S(2)}) copy-start(pred[128,128]{0,1:T(8,128)(4,1)S(1)} %broadcast_compare_fusion) | copy-start | bytes 49156
  42.8 14.0 %copy-start.2 = (bf16[128,768]{0,1:T(8,128)(2,1)}, bf16[128,768]{0,1:T(8,128)(2,1)S(1)}, u32[]{:S(2)}) copy-start(bf16[128,768]{0,1:T(8,128)(2,1)S(1)} %copy.46) | copy-start | bytes 589828
  44.1 15.0 %copy-start.78 = (f32[8,128]{1,0:T(8,128)}, f32[8,128]{1,0:T(8,128)S(1)}, u32[]{:S(2)}) copy-start(f32[8,128]{1,0:T(8,128)S(1)} %get-tuple-element.146) | copy-start | bytes 12292
  44.7 14.5 %copy-start.1 = (bf16[128,1536]{1,0:T(8,128)(2,1)S(1)}, bf16[128,1536]{1,0:T(8,128)(2,1)}, u32[]{:S(2)}) copy-start(bf16[128,1536]{1,0:T(8,128)(2,1)} %param.12) | copy-start | bytes 1179652
  44.7 14.5 %copy-start.5 = (f32[1536]{0:T(1024)S(1)}, f32[1536]{0:T(1024)}, u32[]{:S(2)}) copy-start(f32[1536]{0:T(1024)} %get-tuple-element.42) | copy-start | bytes 18436
  44.7 14.5 %copy-start.6 = (f32[1536]{0:T(1024)S(1)}, f32[1536]{0:T(1024)}, u32[]{:S(2)}) copy-start(f32[1536]{0:T(1024)} %get-tuple-element.43) | copy-start | bytes 18436
  44.7 14.5 %copy-start.7 = (f32[1536]{0:T(1024)S(1)}, f32[1536]{0:T(1024)}, u32[]{:S(2)}) copy-start(f32[1536]{0:T(1024)} %get-tuple-element.44) | copy-start | bytes 18436
  44.7 14.5 %copy-start.8 = (f32[1536]{0:T(1024)S(1)}, f32[1536]{0:T(1024)}, u32[]{:S(2)}) copy-start(f32[1536]{0:T(1024)} %get-tuple-element.45) | copy-start | bytes 18436
  44.7 14.5 %copy-start.9 = (f32[1536]{0:T(1024)S(1)}, f32[1536]{0:T(1024)}, u32[]{:S(2)}) copy-start(f32[1536]{0:T(1024)} %get-tuple-element.46) | copy-start | bytes 18436
  44.7 14.5 %copy-start.10 = (f32[1536]{0:T(1024)S(1)}, f32[1536]{0:T(1024)}, u32[]{:S(2)}) copy-start(f32[1536]{0:T(1024)} %get-tuple-element.59) | copy-start | bytes 18436
  44.7 14.4 %copy-start.11 = (f32[1536]{0:T(1024)S(1)}, f32[1536]{0:T(1024)}, u32[]{:S(2)}) copy-start(f32[1536]{0:T(1024)} %get-tuple-element.64) | copy-start | bytes 18436
  44.7 14.4 %copy-start.12 = (f32[1536]{0:T(1024)S(1)}, f32[1536]{0:T(1024)}, u32[]{:S(2)}) copy-start(f32[1536]{0:T(1024)} %get-tuple-element.65) | copy-start | bytes 18436
  44.7 14.4 %copy-start.13 = (f32[1536]{0:T(1024)S(1)}, f32[1536]{0:T(1024)}, u32[]{:S(2)}) copy-start(f32[1536]{0:T(1024)} %get-tuple-element.67) | copy-start | bytes 18436
  44.8 14.4 %copy-start.14 = (f32[1536]{0:T(1024)S(1)}, f32[1536]{0:T(1024)}, u32[]{:S(2)}) copy-start(f32[1536]{0:T(1024)} %get-tuple-element.68) | copy-start | bytes 18436
  44.8 14.4 %copy-start.15 = (f32[1536]{0:T(1024)S(1)}, f32[1536]{0:T(1024)}, u32[]{:S(2)}) copy-start(f32[1536]{0:T(1024)} %get-tuple-element.66) | copy-start | bytes 18436
  44.8 14.4 %copy-start.16 = (f32[1536]{0:T(1024)S(1)}, f32[1536]{0:T(1024)}, u32[]{:S(2)}) copy-start(f32[1536]{0:T(1024)} %get-tuple-element.47) | copy-start | bytes 18436
  44.8 14.4 %copy-start.17 = (f32[1536]{0:T(1024)S(1)}, f32[1536]{0:T(1024)}, u32[]{:S(2)}) copy-start(f32[1536]{0:T(1024)} %get-tuple-element.48) | copy-start | bytes 18436
  44.8 14.4 %copy-start.18 = (f32[1536]{0:T(1024)S(1)}, f32[1536]{0:T(1024)}, u32[]{:S(2)}) copy-start(f32[1536]{0:T(1024)} %get-tuple-element.49) | copy-start | bytes 18436
  44.8 14.4 %copy-start.19 = (f32[1536]{0:T(1024)S(1)}, f32[1536]{0:T(1024)}, u32[]{:S(2)}) copy-start(f32[1536]{0:T(1024)} %get-tuple-element.50) | copy-start | bytes 18436
  44.8 14.4 %copy-start.20 = (f32[1536]{0:T(1024)S(1)}, f32[1536]{0:T(1024)}, u32[]{:S(2)}) copy-start(f32[1536]{0:T(1024)} %get-tuple-element.51) | copy-start | bytes 18436
  44.8 14.4 %copy-start.21 = (f32[1536]{0:T(1024)S(1)}, f32[1536]{0:T(1024)}, u32[]{:S(2)}) copy-start(f32[1536]{0:T(1024)} %get-tuple-element.52) | copy-start | bytes 18436
  44.8 14.4 %copy-start.22 = (f32[1536]{0:T(1024)S(1)}, f32[1536]{0:T(1024)}, u32[]{:S(2)}) copy-start(f32[1536]{0:T(1024)} %get-tuple-element.53) | copy-start | bytes 18436
  44.8 14.4 %copy-start.23 = (f32[1536]{0:T(1024)S(1)}, f32[1536]{0:T(1024)}, u32[]{:S(2)}) copy-start(f32[1536]{0:T(1024)} %get-tuple-element.54) | copy-start | bytes 18436
  44.9 14.4 %copy-start.24 = (f32[1536]{0:T(1024)S(1)}, f32[1536]{0:T(1024)}, u32[]{:S(2)}) copy-start(f32[1536]{0:T(1024)} %get-tuple-element.55) | copy-start | bytes 18436
  44.9 14.4 %copy-start.25 = (f32[1536]{0:T(1024)S(1)}, f32[1536]{0:T(1024)}, u32[]{:S(2)}) copy-start(f32[1536]{0:T(1024)} %get-tuple-element.56) | copy-start | bytes 18436
  44.9 14.4 %copy-start.26 = (f32[1536]{0:T(1024)S(1)}, f32[1536]{0:T(1024)}, u32[]{:S(2)}) copy-start(f32[1536]{0:T(1024)} %get-tuple-element.57) | copy-start | bytes 18436
  44.9 14.4 %copy-start.27 = (f32[1536]{0:T(1024)S(1)}, f32[1536]{0:T(1024)}, u32[]{:S(2)}) copy-start(f32[1536]{0:T(1024)} %get-tuple-element.58) | copy-start | bytes 18436
  44.9 14.4 %copy-start.28 = (f32[1536]{0:T(1024)S(1)}, f32[1536]{0:T(1024)}, u32[]{:S(2)}) copy-start(f32[1536]{0:T(1024)} %get-tuple-element.70) | copy-start | bytes 18436
  56.8 2.6 %copy-start.32 = (f32[1536]{0:T(1024)S(1)}, f32[1536]{0:T(1024)}, u32[]{:S(2)}) copy-start(f32[1536]{0:T(1024)} %get-tuple-element.63) | copy-start | bytes 18436
  56.8 2.6 %copy-start.33 = (f32[1536]{0:T(1024)S(1)}, f32[1536]{0:T(1024)}, u32[]{:S(2)}) copy-start(f32[1536]{0:T(1024)} %get-tuple-element.69) | copy-start | bytes 18436
  56.8 2.6 %copy-start.56 = (f32[128]{0:T(128)S(1)}, f32[128]{0:T(128)}, u32[]{:S(2)}) copy-start(f32[128]{0:T(128)} %get-tuple-element.118) | copy-start | bytes 1540
  56.8 2.6 %copy-start.58 = (f32[128]{0:T(128)S(1)}, f32[128]{0:T(128)}, u32[]{:S(2)}) copy-start(f32[128]{0:T(128)} %get-tuple-element.119) | copy-start | bytes 1540
  56.9 2.6 %copy-start.60 = (f32[128]{0:T(128)S(1)}, f32[128]{0:T(128)}, u32[]{:S(2)}) copy-start(f32[128]{0:T(128)} %get-tuple-element.120) | copy-start | bytes 1540
  56.9 2.6 %copy-start.62 = (f32[128]{0:T(128)S(1)}, f32[128]{0:T(128)}, u32[]{:S(2)}) copy-start(f32[128]{0:T(128)} %get-tuple-element.121) | copy-start | bytes 1540
  56.9 2.6 %copy-start.64 = (f32[128]{0:T(128)S(1)}, f32[128]{0:T(128)}, u32[]{:S(2)}) copy-start(f32[128]{0:T(128)} %get-tuple-element.122) | copy-start | bytes 1540
  56.9 2.6 %copy-start.66 = (f32[128]{0:T(128)S(1)}, f32[128]{0:T(128)}, u32[]{:S(2)}) copy-start(f32[128]{0:T(128)} %get-tuple-element.123) | copy-start | bytes 1540
  56.9 2.6 %copy-start.68 = (f32[128]{0:T(128)S(1)}, f32[128]{0:T(128)}, u32[]{:S(2)}) copy-start(f32[128]{0:T(128)} %get-tuple-element.124) | copy-start | bytes 1540
  56.9 2.6 %copy-start.70 = (f32[128]{0:T(128)S(1)}, f32[128]{0:T(128)}, u32[]{:S(2)}) copy-start(f32[128]{0:T(128)} %get-tuple-element.125) | copy-start | bytes 1540
  56.9 2.6 %copy-start.72 = (f32[128]{0:T(128)S(1)}, f32[128]{0:T(128)}, u32[]{:S(2)}) copy-start(f32[128]{0:T(128)} %get-tuple-element.126) | copy-start | bytes 1540
  56.9 2.6 %copy-start.74 = (f32[128]{0:T(128)S(1)}, f32[128]{0:T(128)}, u32[]{:S(2)}) copy-start(f32[128]{0:T(128)} %get-tuple-element.127) | copy-start | bytes 1540
  77.6 2.6 %copy-start.57 = (f32[128]{0:T(128)S(1)}, f32[128]{0:T(128)}, u32[]{:S(2)}) copy-start(f32[128]{0:T(128)} %get-tuple-element.118) | copy-start | bytes 1540
  79.8 2.6 %copy-start.41 = (f32[1536]{0:T(1024)S(1)}, f32[1536]{0:T(1024)}, u32[]{:S(2)}) copy-start(f32[1536]{0:T(1024)} %get-tuple-element.28) | copy-start | bytes 18436
  79.8 2.6 %copy-start.40 = (f32[1536]{0:T(1024)S(1)}, f32[1536]{0:T(1024)}, u32[]{:S(2)}) copy-start(f32[1536]{0:T(1024)} %get-tuple-element.29) | copy-start | bytes 18436
  79.8 2.6 %copy-start.39 = (f32[1536]{0:T(1024)S(1)}, f32[1536]{0:T(1024)}, u32[]{:S(2)}) copy-start(f32[1536]{0:T(1024)} %get-tuple-element.30) | copy-start | bytes 18436
  79.8 2.6 %copy-start.38 = (f32[1536]{0:T(1024)S(1)}, f32[1536]{0:T(1024)}, u32[]{:S(2)}) copy-start(f32[1536]{0:T(1024)} %get-tuple-element.31) | copy-start | bytes 18436
  79.9 2.7 %copy-start.37 = (f32[1536]{0:T(1024)S(1)}, f32[1536]{0:T(1024)}, u32[]{:S(2)}) copy-start(f32[1536]{0:T(1024)} %get-tuple-element.32) | copy-start | bytes 18436
  79.9 2.7 %copy-start.36 = (f32[1536]{0:T(1024)S(1)}, f32[1536]{0:T(1024)}, u32[]{:S(2)}) copy-start(f32[1536]{0:T(1024)} %get-tuple-element.33) | copy-start | bytes 18436
  79.9 2.7 %copy-start.35 = (f32[1536]{0:T(1024)S(1)}, f32[1536]{0:T(1024)}, u32[]{:S(2)}) copy-start(f32[1536]{0:T(1024)} %get-tuple-element.34) | copy-start | bytes 18436
  79.9 2.7 %copy-start.34 = (f32[1536]{0:T(1024)S(1)}, f32[1536]{0:T(1024)}, u32[]{:S(2)}) copy-start(f32[1536]{0:T(1024)} %get-tuple-element.35) | copy-start | bytes 18436
  79.9 2.7 %copy-start.54 = (f32[1536]{0:T(1024)S(1)}, f32[1536]{0:T(1024)}, u32[]{:S(2)}) copy-start(f32[1536]{0:T(1024)} %get-tuple-element.36) | copy-start | bytes 18436
  79.9 2.7 %copy-start.53 = (f32[1536]{0:T(1024)S(1)}, f32[1536]{0:T(1024)}, u32[]{:S(2)}) copy-start(f32[1536]{0:T(1024)} %get-tuple-element.37) | copy-start | bytes 18436
  79.9 2.7 %copy-start.52 = (f32[1536]{0:T(1024)S(1)}, f32[1536]{0:T(1024)}, u32[]{:S(2)}) copy-start(f32[1536]{0:T(1024)} %get-tuple-element.38) | copy-start | bytes 18436
  82.7 8.9 %copy-start.3 = (bf16[128,768]{0,1:T(8,128)(2,1)S(1)}, bf16[128,768]{0,1:T(8,128)(2,1)}, u32[]{:S(2)}) copy-start(bf16[128,768]{0,1:T(8,128)(2,1)} %copy-done.2) | copy-start | bytes 589828
  82.7 8.9 %copy-start.79 = (f32[8,128]{1,0:T(8,128)S(1)}, f32[8,128]{1,0:T(8,128)}, u32[]{:S(2)}) copy-start(f32[8,128]{1,0:T(8,128)} %copy-done.78) | copy-start | bytes 12292
  83.8 13.0 %all-to-all-start.2 = ((f32[16,2,1536]{2,1,0:T(2,128)}), f32[16,2,1536]{2,1,0:T(2,128)S(1)}, u32[]{:S(2)}, u32[]{:S(2)}) async-start(f32[16,2,1536]{2,1,0:T(2,128)} %reshape.310), calls=%async_computation.3 | async-start | bytes 393216 | tf_op jit(solution)/shard_map/all_to_all | solution.py:147
  97.7 14.0 %all-to-all-start.3 = ((f32[16,2,1536]{2,1,0:T(2,128)}), f32[16,2,1536]{2,1,0:T(2,128)S(1)}, u32[]{:S(2)}, u32[]{:S(2)}) async-start(f32[16,2,1536]{2,1,0:T(2,128)} %broadcast_in_dim.57), calls=%async_computation.4 | async-start | bytes 393216 | tf_op jit(solution)/shard_map/all_to_all | solution.py:154
  111.7 28.0 %all-to-all-start.1 = ((bf16[32,4,2304]{2,1,0:T(4,128)(2,1)}), bf16[32,4,2304]{2,1,0:T(4,128)(2,1)S(1)}, u32[]{:S(2)}, u32[]{:S(2)}) async-start(bf16[32,4,2304]{2,1,0:T(4,128)(2,1)} %all_to_all.34), calls=%async_computation.1 | async-start | bytes 1179648 | tf_op jit(solution)/shard_map/all_to_all | solution.py:122
  186.6 27.1 %all-to-all-start.6 = ((f32[8,12,1536]{2,1,0:T(8,128)}), f32[8,12,1536]{2,1,0:T(8,128)S(1)}, u32[]{:S(2)}, u32[]{:S(2)}) async-start(f32[8,12,1536]{2,1,0:T(8,128)} %broadcast_in_dim.60), calls=%async_computation.7 | async-start | bytes 1572864 | tf_op jit(solution)/shard_map/all_to_all | solution.py:154
  (23 other events, 55.7 us)
Sparse Core Ops, SparseCore 0:
  10.1 46.6 all-gather.1
  80.1 65.1 reduce-scatter.1

commit v11 on v8

--- a/solution.py
+++ b/solution.py
@@ -128,7 +128,7 @@
     owned_rows = weight_share.shape[0]
     both = jnp.concatenate([weight_share, kernel_piece], axis=0)
     piece = sum_rows(both, DP)
-    both = gather_rows(gather_rows(piece, "dx"), "dz")[: both.shape[0]]
+    both = gather_rows(piece, DP)[: both.shape[0]]
     weight_total = both[:owned_rows]
     kernel_total = gather_rows(both[owned_rows:], FSDP)[: kernel.shape[0]]
 

time: 219 us -> 212 us (0.968)
  blocking collectives: 27.8 us -> 20.6 us
    all_to_all x1 -> x0, blocking collectives: 7.19 us -> none  [gather_rows(): got = lax.all_to_all(copies, axis, split_axis=0, concat_axis=0, tiled=True)]
where the time goes in v11:
time: 212 us; the launch traced here: 211 us
  waiting for transfers between devices  76.9 us (36%)
  starting transfers between devices  46.4 us (22%)
  other arithmetic  26.2 us (12%)
  blocking collectives  20.6 us (10%)
  between operations  15.3 us (7%)
  matrix products  13.3 us (6%)
  local copies, waits for them, and re-layouts  12.8 us (6%)
    all_to_all x1, blocking collectives, sum_rows(): lax.all_to_all(padded.reshape(count, per, x.shape[1]), axis, split_axis=0...  20.6 us
    all_to_all x2, waiting for transfers between devices, gather_rows(): got = lax.all_to_all(copies, axis, split_axis=0, concat_axis=0, tiled=True)  18.4 us
    all_to_all x2, starting transfers between devices, gather_rows(): got = lax.all_to_all(copies, axis, split_axis=0, concat_axis=0, tiled=True)  17.9 us
    all_to_all x1, waiting for transfers between devices, body(): lax.all_to_all(returning, DP, split_axis=0, concat_axis=0, tiled=True)  17.9 us
    all_to_all x1, waiting for transfers between devices, body(): lax.all_to_all(outgoing, DP, split_axis=0, concat_axis=0, tiled=True)  16 us
    reduce_sum x4, other arithmetic, finish(): kernel[offset] * padded[offset:offset + length] * matching[:, None]  14.6 us
    all_to_all x1, starting transfers between devices, body(): lax.all_to_all(outgoing, DP, split_axis=0, concat_axis=0, tiled=True)  13.7 us
    reduce_scatter x1, waiting for transfers between devices, body(): lax.psum_scatter(jnp.einsum('rc,rd->cd', columns, mixed_grad, preferred_e...  12.4 us
  transfers between devices with their start and end apart: 7, of which 6 were waited for; matrix products, arithmetic and copies ran while one was open for 11% of the time, Pallas kernels for 0%

profile of v11, /device:TPU:1, one launch (start us, length us, event | category | flops | bytes accessed | tf_op | source)
XLA Modules:
  0.0 211.4 jit_solution(173523416918727866)
XLA Ops:
  7.2 0.7 all-gather.2.cloned.1.call-update
  7.9 1.2 compare_select_fusion.1
  9.2 1.0 gather_fusion
  10.2 0.2 select_select_fusion.1
  10.4 1.0 all_to_all.28
  11.3 13.7 %all-to-all-start = ((bf16[32,4,2304]{2,1,0:T(4,128)(2,1)}), bf16[32,4,2304]{2,1,0:T(4,128)(2,1)S(1)}, u32[]{:S(2)}, u32[]{:S(2)}) async-start(bf16[32,4,2304]{2,1,0:T(4,128)(2,1)} %all_to_all.28), calls=%async_computation | async-start | bytes 1179648 | tf_op jit(solution)/shard_map/all_to_all | solution.py:87
  25.1 0.2 slice_reduce_fusion.29
  25.3 0.5 compare_select_fusion
  25.8 0.3 slice_reduce_fusion.30
  26.6 16.0 %all-to-all-done = bf16[32,4,2304]{2,1,0:T(4,128)(2,1)S(1)} async-done(((bf16[32,4,2304]{2,1,0:T(4,128)(2,1)}), bf16[32,4,2304]{2,1,0:T(4,128)(2,1)S(1)}, u32[]{:S(2)}, u32[]{:S(2)}) %all-to-all-start) | async-done | bytes 589856 | tf_op jit(solution)/shard_map/all_to_all | solution.py:87
  42.5 0.1 all_to_all.30
  42.7 1.0 gather_fusion.1
  43.6 0.2 select_select_fusion
  43.8 0.2 copy.47
  44.0 0.2 copy.46
  44.2 0.2 copy.45
  44.3 1.2 fusion.39
  45.5 0.6 copy-done.47
  46.1 0.5 convolution_convert_fusion.6
  46.6 11.6 %all-gather.2.cloned.1.call-done = bf16[768,1536]{1,0:T(8,128)(2,1)} async-done(((bf16[48,1536]{1,0:T(8,128)(2,1)}), bf16[768,1536]{1,0:T(8,128)(2,1)}) %all-gather.2.cloned.1.call-update) | async-done | bytes 2359312 | tf_op jit(solution)/shard_map/all_gather | solution.py:95
  58.2 2.2 %fusion.2 = f32[128,1536]{1,0:T(8,128)S(1)} fusion(bf16[128,768]{0,1:T(8,128)(2,1)S(1)} %bitcast.38, bf16[768,1536]{1,0:T(8,128)(2,1)} %all-gather.2.cloned.1.call-done), kind=kOutput, calls=%fused_computation.8 | convolution fusion | flops 302383104 | bytes 3342336 | tf_op jit(solution)/shard_map/dot_general | solution.py:93
  60.4 7.7 %multiply_reduce_fusion.31 = (f32[1536]{0:T(1024)}, f32[1536]{0:T(1024)}, f32[1536]{0:T(1024)}, f32[1536]{0:T(1024)}, f32[1536]{0:T(1024)}, /*index=5*/f32[1536]...) fusion(f32[128,1536]{1,0:T(8,128)S(1)} %fusion.2, ...), kind=kLoop, calls=%fused_computation.99 | loop fusion | flops 25152000 | bytes 3013632 | tf_op jit(solution)/shard_map/transpose(jvp())/reduce_sum | solution.py:77
  68.2 2.3 %multiply_reduce_fusion.16 = (f32[1536]{0:T(1024)}, f32[1536]{0:T(1024)}, f32[1536]{0:T(1024)}, f32[1536]{0:T(1024)}, f32[1536]{0:T(1024)}, /*index=5*/f32[1536]...) fusion(f32[128,1536]{1,0:T(8,128)S(1)} %get-tuple-element.69, ...), kind=kLoop, calls=%fused_computation.84 | loop fusion | flops 5294592 | bytes 2424832 | tf_op jit(solution)/shard_map/transpose(jvp())/reduce_sum | solution.py:77
  70.4 0.5 multiply_multiply_fusion.27
  71.0 0.7 multiply_multiply_fusion.29
  71.8 0.7 multiply_multiply_fusion.28
  72.5 2.6 %multiply_reduce_fusion.4 = (f32[1536]{0:T(1024)}, f32[1536]{0:T(1024)}, f32[1536]{0:T(1024)}, f32[1536]{0:T(1024)}, f32[128,1536]{1,0:T(8,128)S(1)}, /*index=5*...) fusion(f32[128,1536]{1,0:T(8,128)S(1)} %get-tuple-element.69, ...), kind=kLoop, calls=%fused_computation.72 | loop fusion | flops 5105664 | bytes 7535616 | tf_op jit(solution)/shard_map/transpose(jvp())/reduce_sum | solution.py:77
  75.1 2.6 %pad_add_fusion = f32[158,1536]{1,0:T(8,128)S(1)} fusion(f32[128,1536]{1,0:T(8,128)S(1)} %get-tuple-element.78, f32[128,1536]{1,0:T(8,128)S(1)} %get-tuple-element.80, f32[128,1536]{1,0:T(8,128)S(1)} %get-tuple-element.81, f32[128,1536]{1,0:T(8,128)S(1)} %get-tuple-element.82, f32[128,1536]{1,0:T(8,128)S(1)} %get-tuple-element.83, ...), kind=kLoop, calls=%fused_computation.59 | loop fusion | flops 5824512 | bytes 20631552 | tf_op jit(solution)/shard_map/transpose(jvp())/add_any | solution.py:77
  77.7 0.7 fusion.16
  78.6 2.2 %convolution_convert_fusion = bf16[768,1536]{1,0:T(8,128)(2,1)} fusion(bf16[128,768]{0,1:T(8,128)(2,1)S(1)} %bitcast.39, bf16[128,1536]{1,0:T(8,128)(2,1)S(1)} %fusion.16), kind=kOutput, calls=%fused_computation.6 | convolution fusion | flops 303169536 | bytes 2949120 | tf_op jit(solution)/shard_map/rc,rd->cd/dot_general | solution.py:105
  81.1 2.0 multiply_reduce_fusion.22
  83.6 0.3 pad_add_fusion.7
  83.9 0.8 reshape.309
  84.7 4.6 %all-to-all-start.2 = ((f32[16,2,1536]{2,1,0:T(2,128)}), f32[16,2,1536]{2,1,0:T(2,128)S(1)}, u32[]{:S(2)}, u32[]{:S(2)}) async-start(f32[16,2,1536]{2,1,0:T(2,128)} %reshape.309), calls=%async_computation.3 | async-start | bytes 393216 | tf_op jit(solution)/shard_map/all_to_all | solution.py:147
  89.3 2.5 %convolution_convert_fusion.5 = bf16[128,768]{1,0:T(8,128)(2,1)S(1)} fusion(bf16[128,1536]{1,0:T(8,128)(2,1)S(1)} %fusion.16, bf16[768,1536]{1,0:T(8,128)(2,1)} %all-gather.2.cloned.1.call-done), kind=kOutput, calls=%fused_computation.54 | convolution fusion | flops 302088192 | bytes 2949120 | tf_op jit(solution)/shard_map/rd,cd->rc/dot_general | solution.py:112
  91.9 0.2 copy.49
  92.0 1.3 convolution_convert_fusion.2
  93.3 0.1 copy.55
  93.5 0.3 fusion.40
  93.8 1.6 convolution_convert_fusion.3
  95.4 0.1 copy.54
  95.5 1.6 convolution_convert_fusion.4
  97.1 0.1 copy.53
  97.3 1.8 scatter_custom_fusion
  99.0 1.0 all_to_all.31
  100.0 10.0 %all-to-all-start.1 = ((bf16[32,4,2304]{2,1,0:T(4,128)(2,1)}), bf16[32,4,2304]{2,1,0:T(4,128)(2,1)S(1)}, u32[]{:S(2)}, u32[]{:S(2)}) async-start(bf16[32,4,2304]{2,1,0:T(4,128)(2,1)} %all_to_all.31), calls=%async_computation.1 | async-start | bytes 1179648 | tf_op jit(solution)/shard_map/all_to_all | solution.py:122
  110.1 17.9 %all-to-all-done.1 = bf16[32,4,2304]{2,1,0:T(4,128)(2,1)S(1)} async-done(((bf16[32,4,2304]{2,1,0:T(4,128)(2,1)}), bf16[32,4,2304]{2,1,0:T(4,128)(2,1)S(1)}, u32[]{:S(2)}, u32[]{:S(2)}) %all-to-all-start.1) | async-done | bytes 589856 | tf_op jit(solution)/shard_map/all_to_all | solution.py:122
  128.1 0.1 reshape.340
  128.2 12.4 %reduce-scatter.2.cloned.1.call-done = bf16[48,1536]{1,0:T(8,128)(2,1)} async-done(((bf16[768,1536]{1,0:T(8,128)(2,1)}), bf16[48,1536]{1,0:T(8,128)(2,1)}) %reduce-scatter.2.cloned.1.call-update) | async-done | bytes 147472 | tf_op jit(solution)/shard_map/reduce_scatter | solution.py:104
  140.6 0.9 convert_element_type.216
  141.5 0.2 reshape.310
  141.8 20.6 %all_to_all.44 = f32[32,2,1536]{2,1,0:T(2,128)S(1)} all-to-all(f32[32,2,1536]{2,1,0:T(2,128)S(1)} %reshape.310), channel_id=1, replica_groups=mesh['dz'=8,'dx'=4,'fy'=8,'fc'=2] {'dz','dx'}, dimensions={0} | all-to-all | bytes 786432 | tf_op jit(solution)/shard_map/all_to_all | solution.py:147
  162.3 0.1 reduce_sum.365
  162.5 0.8 broadcast_in_dim.55
  163.3 4.1 %all-to-all-start.4 = ((f32[32,2,1536]{2,1,0:T(2,128)}), f32[32,2,1536]{2,1,0:T(2,128)S(1)}, u32[]{:S(2)}, u32[]{:S(2)}) async-start(f32[32,2,1536]{2,1,0:T(2,128)} %broadcast_in_dim.55), calls=%async_computation.5 | async-start | bytes 786432 | tf_op jit(solution)/shard_map/all_to_all | solution.py:154
  167.4 2.4 %scatter_custom_fusion.1 = bf16[128,2304]{1,0:T(8,128)(2,1)} fusion(s32[128]{0:T(128)} %get-tuple-element.108, bf16[128,2304]{1,0:T(8,128)(2,1)S(1)} %reshape.340, bf16[]{:T(256)} %constant.10.clone.1), kind=kCustom, calls=%fused_computation.145 | custom fusion | bytes 590336 | tf_op jit(solution)/shard_map/scatter | solution.py:124
  169.8 9.1 %all-to-all-done.4 = f32[32,2,1536]{2,1,0:T(2,128)S(1)} async-done(((f32[32,2,1536]{2,1,0:T(2,128)}), f32[32,2,1536]{2,1,0:T(2,128)S(1)}, u32[]{:S(2)}, u32[]{:S(2)}) %all-to-all-start.4) | async-done | bytes 393248 | tf_op jit(solution)/shard_map/all_to_all | solution.py:154
  178.9 0.7 broadcast_in_dim.57
  179.6 13.8 %all-to-all-start.5 = ((f32[16,2,1536]{2,1,0:T(2,128)}), f32[16,2,1536]{2,1,0:T(2,128)S(1)}, u32[]{:S(2)}, u32[]{:S(2)}) async-start(f32[16,2,1536]{2,1,0:T(2,128)} %broadcast_in_dim.57), calls=%async_computation.6 | async-start | bytes 393216 | tf_op jit(solution)/shard_map/all_to_all | solution.py:154
  193.4 0.1 slice_multiply_fusion
  193.6 0.9 mul.1323
  194.5 9.3 %all-to-all-done.5 = f32[16,2,1536]{2,1,0:T(2,128)S(1)} async-done(((f32[16,2,1536]{2,1,0:T(2,128)}), f32[16,2,1536]{2,1,0:T(2,128)S(1)}, u32[]{:S(2)}, u32[]{:S(2)}) %all-to-all-start.5) | async-done | bytes 196640 | tf_op jit(solution)/shard_map/all_to_all | solution.py:154
  203.8 0.1 reshape.311
  203.9 0.7 slice_multiply_fusion.1
  (144 shorter events, 1.0 us)
Async XLA Ops:
  7.2 2.0 copy-start
  7.2 51.1 %all-gather.2.cloned.1.call-start = ((), (), s32[]{:S(2)}) async-start(), calls=%async_computation.7 | async-start | bytes 2506752 | tf_op jit(solution)/shard_map/all_gather | solution.py:95
  9.1 1.0 copy-start.45
  10.1 14.9 %copy-start.4 = (f32[31,1536]{1,0:T(8,128)S(1)}, f32[31,1536]{1,0:T(8,128)}, u32[]{:S(2)}) copy-start(f32[31,1536]{1,0:T(8,128)} %param.11) | copy-start | bytes 571396
  10.2 15.1 %copy-start.46 = (s32[128]{0:T(128)S(1)}, s32[128]{0:T(128)}, u32[]{:S(2)}) copy-start(s32[128]{0:T(128)} %param.14) | copy-start | bytes 1540
  10.2 16.0 %copy-start.44 = (s32[128]{0:T(128)S(1)}, s32[128]{0:T(128)}, u32[]{:S(2)}) copy-start(s32[128]{0:T(128)} %param.15) | copy-start | bytes 1540
  11.3 31.2 %all-to-all-start = ((bf16[32,4,2304]{2,1,0:T(4,128)(2,1)}), bf16[32,4,2304]{2,1,0:T(4,128)(2,1)S(1)}, u32[]{:S(2)}, u32[]{:S(2)}) async-start(bf16[32,4,2304]{2,1,0:T(4,128)(2,1)} %all_to_all.28), calls=%async_computation | async-start | bytes 1179648 | tf_op jit(solution)/shard_map/all_to_all | solution.py:87
  25.0 115.5 %reduce-scatter.2.cloned.1.call-start = ((), (), s32[]{:S(2)}) async-start(), calls=%async_computation.8 | async-start | bytes 2506752 | tf_op jit(solution)/shard_map/reduce_scatter | solution.py:104
  26.4 44.6 %copy-start.38 = (f32[128]{0:T(128)}, f32[128]{0:T(128)S(1)}, u32[]{:S(2)}) copy-start(f32[128]{0:T(128)S(1)} %get-tuple-element.122) | copy-start | bytes 1540
  26.4 44.6 %copy-start.40 = (f32[128]{0:T(128)}, f32[128]{0:T(128)S(1)}, u32[]{:S(2)}) copy-start(f32[128]{0:T(128)S(1)} %get-tuple-element.123) | copy-start | bytes 1540
  26.4 44.6 %copy-start.42 = (f32[128]{0:T(128)}, f32[128]{0:T(128)S(1)}, u32[]{:S(2)}) copy-start(f32[128]{0:T(128)S(1)} %get-tuple-element.124) | copy-start | bytes 1540
  26.4 45.3 %copy-start.26 = (f32[128]{0:T(128)}, f32[128]{0:T(128)S(1)}, u32[]{:S(2)}) copy-start(f32[128]{0:T(128)S(1)} %get-tuple-element.116) | copy-start | bytes 1540
  26.4 45.3 %copy-start.28 = (f32[128]{0:T(128)}, f32[128]{0:T(128)S(1)}, u32[]{:S(2)}) copy-start(f32[128]{0:T(128)S(1)} %get-tuple-element.117) | copy-start | bytes 1540
  26.4 45.3 %copy-start.30 = (f32[128]{0:T(128)}, f32[128]{0:T(128)S(1)}, u32[]{:S(2)}) copy-start(f32[128]{0:T(128)S(1)} %get-tuple-element.118) | copy-start | bytes 1540
  26.4 45.3 %copy-start.32 = (f32[128]{0:T(128)}, f32[128]{0:T(128)S(1)}, u32[]{:S(2)}) copy-start(f32[128]{0:T(128)S(1)} %get-tuple-element.119) | copy-start | bytes 1540
  26.4 45.3 %copy-start.34 = (f32[128]{0:T(128)}, f32[128]{0:T(128)S(1)}, u32[]{:S(2)}) copy-start(f32[128]{0:T(128)S(1)} %get-tuple-element.120) | copy-start | bytes 1540
  26.5 45.3 %copy-start.36 = (f32[128]{0:T(128)}, f32[128]{0:T(128)S(1)}, u32[]{:S(2)}) copy-start(f32[128]{0:T(128)S(1)} %get-tuple-element.121) | copy-start | bytes 1540
  26.6 19.0 %copy-start.25 = (pred[128,128]{0,1:T(8,128)(4,1)}, pred[128,128]{0,1:T(8,128)(4,1)S(1)}, u32[]{:S(2)}) copy-start(pred[128,128]{0,1:T(8,128)(4,1)S(1)} %broadcast_compare_fusion) | copy-start | bytes 49156
  44.2 14.1 %copy-start.2 = (bf16[128,768]{0,1:T(8,128)(2,1)}, bf16[128,768]{0,1:T(8,128)(2,1)S(1)}, u32[]{:S(2)}) copy-start(bf16[128,768]{0,1:T(8,128)(2,1)S(1)} %copy.46) | copy-start | bytes 589828
  45.5 0.6 copy-start.47
  46.6 13.8 %copy-start.1 = (bf16[128,1536]{1,0:T(8,128)(2,1)S(1)}, bf16[128,1536]{1,0:T(8,128)(2,1)}, u32[]{:S(2)}) copy-start(bf16[128,1536]{1,0:T(8,128)(2,1)} %param.12) | copy-start | bytes 1179652
  78.4 2.4 %copy-start.20 = (f32[1536]{0:T(1024)S(1)}, f32[1536]{0:T(1024)}, u32[]{:S(2)}) copy-start(f32[1536]{0:T(1024)} %get-tuple-element.7) | copy-start | bytes 18436
  78.4 2.5 %copy-start.19 = (f32[1536]{0:T(1024)S(1)}, f32[1536]{0:T(1024)}, u32[]{:S(2)}) copy-start(f32[1536]{0:T(1024)} %get-tuple-element.8) | copy-start | bytes 18436
  78.4 2.5 %copy-start.18 = (f32[1536]{0:T(1024)S(1)}, f32[1536]{0:T(1024)}, u32[]{:S(2)}) copy-start(f32[1536]{0:T(1024)} %get-tuple-element.9) | copy-start | bytes 18436
  78.4 2.5 %copy-start.17 = (f32[1536]{0:T(1024)S(1)}, f32[1536]{0:T(1024)}, u32[]{:S(2)}) copy-start(f32[1536]{0:T(1024)} %get-tuple-element.10) | copy-start | bytes 18436
  78.4 2.5 %copy-start.16 = (f32[1536]{0:T(1024)S(1)}, f32[1536]{0:T(1024)}, u32[]{:S(2)}) copy-start(f32[1536]{0:T(1024)} %get-tuple-element.11) | copy-start | bytes 18436
  78.5 2.5 %copy-start.15 = (f32[1536]{0:T(1024)S(1)}, f32[1536]{0:T(1024)}, u32[]{:S(2)}) copy-start(f32[1536]{0:T(1024)} %get-tuple-element.12) | copy-start | bytes 18436
  78.5 2.5 %copy-start.14 = (f32[1536]{0:T(1024)S(1)}, f32[1536]{0:T(1024)}, u32[]{:S(2)}) copy-start(f32[1536]{0:T(1024)} %get-tuple-element.13) | copy-start | bytes 18436
  78.5 2.5 %copy-start.13 = (f32[1536]{0:T(1024)S(1)}, f32[1536]{0:T(1024)}, u32[]{:S(2)}) copy-start(f32[1536]{0:T(1024)} %get-tuple-element.14) | copy-start | bytes 18436
  78.5 2.6 %copy-start.12 = (f32[1536]{0:T(1024)S(1)}, f32[1536]{0:T(1024)}, u32[]{:S(2)}) copy-start(f32[1536]{0:T(1024)} %get-tuple-element.15) | copy-start | bytes 18436
  78.5 2.6 %copy-start.27 = (f32[128]{0:T(128)S(1)}, f32[128]{0:T(128)}, u32[]{:S(2)}) copy-start(f32[128]{0:T(128)} %copy-done.26) | copy-start | bytes 1540
  78.5 2.6 %copy-start.29 = (f32[128]{0:T(128)S(1)}, f32[128]{0:T(128)}, u32[]{:S(2)}) copy-start(f32[128]{0:T(128)} %copy-done.28) | copy-start | bytes 1540
  78.5 2.6 %copy-start.31 = (f32[128]{0:T(128)S(1)}, f32[128]{0:T(128)}, u32[]{:S(2)}) copy-start(f32[128]{0:T(128)} %copy-done.30) | copy-start | bytes 1540
  78.5 2.6 %copy-start.33 = (f32[128]{0:T(128)S(1)}, f32[128]{0:T(128)}, u32[]{:S(2)}) copy-start(f32[128]{0:T(128)} %copy-done.32) | copy-start | bytes 1540
  78.5 2.6 %copy-start.35 = (f32[128]{0:T(128)S(1)}, f32[128]{0:T(128)}, u32[]{:S(2)}) copy-start(f32[128]{0:T(128)} %copy-done.34) | copy-start | bytes 1540
  78.5 2.6 %copy-start.37 = (f32[128]{0:T(128)S(1)}, f32[128]{0:T(128)}, u32[]{:S(2)}) copy-start(f32[128]{0:T(128)} %copy-done.36) | copy-start | bytes 1540
  78.6 2.6 %copy-start.39 = (f32[128]{0:T(128)S(1)}, f32[128]{0:T(128)}, u32[]{:S(2)}) copy-start(f32[128]{0:T(128)} %copy-done.38) | copy-start | bytes 1540
  78.6 2.6 %copy-start.41 = (f32[128]{0:T(128)S(1)}, f32[128]{0:T(128)}, u32[]{:S(2)}) copy-start(f32[128]{0:T(128)} %copy-done.40) | copy-start | bytes 1540
  78.6 2.6 %copy-start.43 = (f32[128]{0:T(128)S(1)}, f32[128]{0:T(128)}, u32[]{:S(2)}) copy-start(f32[128]{0:T(128)} %copy-done.42) | copy-start | bytes 1540
  80.7 2.5 %copy-start.11 = (f32[1536]{0:T(1024)S(1)}, f32[1536]{0:T(1024)}, u32[]{:S(2)}) copy-start(f32[1536]{0:T(1024)} %get-tuple-element.25) | copy-start | bytes 18436
  80.7 2.5 %copy-start.10 = (f32[1536]{0:T(1024)S(1)}, f32[1536]{0:T(1024)}, u32[]{:S(2)}) copy-start(f32[1536]{0:T(1024)} %get-tuple-element.26) | copy-start | bytes 18436
  80.7 2.6 %copy-start.9 = (f32[1536]{0:T(1024)S(1)}, f32[1536]{0:T(1024)}, u32[]{:S(2)}) copy-start(f32[1536]{0:T(1024)} %get-tuple-element.27) | copy-start | bytes 18436
  80.7 2.6 %copy-start.8 = (f32[1536]{0:T(1024)S(1)}, f32[1536]{0:T(1024)}, u32[]{:S(2)}) copy-start(f32[1536]{0:T(1024)} %get-tuple-element.28) | copy-start | bytes 18436
  80.7 2.6 %copy-start.7 = (f32[1536]{0:T(1024)S(1)}, f32[1536]{0:T(1024)}, u32[]{:S(2)}) copy-start(f32[1536]{0:T(1024)} %get-tuple-element.29) | copy-start | bytes 18436
  80.8 2.6 %copy-start.6 = (f32[1536]{0:T(1024)S(1)}, f32[1536]{0:T(1024)}, u32[]{:S(2)}) copy-start(f32[1536]{0:T(1024)} %get-tuple-element.30) | copy-start | bytes 18436
  80.8 2.6 %copy-start.5 = (f32[1536]{0:T(1024)S(1)}, f32[1536]{0:T(1024)}, u32[]{:S(2)}) copy-start(f32[1536]{0:T(1024)} %get-tuple-element.31) | copy-start | bytes 18436
  80.8 2.7 %copy-start.24 = (f32[1536]{0:T(1024)S(1)}, f32[1536]{0:T(1024)}, u32[]{:S(2)}) copy-start(f32[1536]{0:T(1024)} %get-tuple-element.34) | copy-start | bytes 18436
  80.8 2.7 %copy-start.23 = (f32[1536]{0:T(1024)S(1)}, f32[1536]{0:T(1024)}, u32[]{:S(2)}) copy-start(f32[1536]{0:T(1024)} %get-tuple-element.35) | copy-start | bytes 18436
  80.8 2.7 %copy-start.22 = (f32[1536]{0:T(1024)S(1)}, f32[1536]{0:T(1024)}, u32[]{:S(2)}) copy-start(f32[1536]{0:T(1024)} %get-tuple-element.36) | copy-start | bytes 18436
  80.8 2.7 %copy-start.21 = (f32[1536]{0:T(1024)S(1)}, f32[1536]{0:T(1024)}, u32[]{:S(2)}) copy-start(f32[1536]{0:T(1024)} %get-tuple-element.37) | copy-start | bytes 18436
  83.5 8.5 %copy-start.3 = (bf16[128,768]{0,1:T(8,128)(2,1)S(1)}, bf16[128,768]{0,1:T(8,128)(2,1)}, u32[]{:S(2)}) copy-start(bf16[128,768]{0,1:T(8,128)(2,1)} %copy-done.2) | copy-start | bytes 589828
  83.6 8.5 %copy-start.48 = (f32[8,128]{1,0:T(8,128)S(1)}, f32[8,128]{1,0:T(8,128)}, u32[]{:S(2)}) copy-start(f32[8,128]{1,0:T(8,128)} %copy-done.47) | copy-start | bytes 12292
  84.7 15.3 %all-to-all-start.2 = ((f32[16,2,1536]{2,1,0:T(2,128)}), f32[16,2,1536]{2,1,0:T(2,128)S(1)}, u32[]{:S(2)}, u32[]{:S(2)}) async-start(f32[16,2,1536]{2,1,0:T(2,128)} %reshape.309), calls=%async_computation.3 | async-start | bytes 393216 | tf_op jit(solution)/shard_map/all_to_all | solution.py:147
  100.0 28.1 %all-to-all-start.1 = ((bf16[32,4,2304]{2,1,0:T(4,128)(2,1)}), bf16[32,4,2304]{2,1,0:T(4,128)(2,1)S(1)}, u32[]{:S(2)}, u32[]{:S(2)}) async-start(bf16[32,4,2304]{2,1,0:T(4,128)(2,1)} %all_to_all.31), calls=%async_computation.1 | async-start | bytes 1179648 | tf_op jit(solution)/shard_map/all_to_all | solution.py:122
  163.3 15.6 %all-to-all-start.4 = ((f32[32,2,1536]{2,1,0:T(2,128)}), f32[32,2,1536]{2,1,0:T(2,128)S(1)}, u32[]{:S(2)}, u32[]{:S(2)}) async-start(f32[32,2,1536]{2,1,0:T(2,128)} %broadcast_in_dim.55), calls=%async_computation.5 | async-start | bytes 786432 | tf_op jit(solution)/shard_map/all_to_all | solution.py:154
  179.6 24.2 %all-to-all-start.5 = ((f32[16,2,1536]{2,1,0:T(2,128)}), f32[16,2,1536]{2,1,0:T(2,128)S(1)}, u32[]{:S(2)}, u32[]{:S(2)}) async-start(f32[16,2,1536]{2,1,0:T(2,128)} %broadcast_in_dim.57), calls=%async_computation.6 | async-start | bytes 393216 | tf_op jit(solution)/shard_map/all_to_all | solution.py:154
Sparse Core Ops, SparseCore 0:
  10.1 48.0 all-gather.1
  81.0 59.5 reduce-scatter.1

commit v12 on v11

--- a/solution.py
+++ b/solution.py
@@ -130,7 +130,7 @@
     piece = sum_rows(both, DP)
     both = gather_rows(piece, DP)[: both.shape[0]]
     weight_total = both[:owned_rows]
-    kernel_total = gather_rows(both[owned_rows:], FSDP)[: kernel.shape[0]]
+    kernel_total = gather_rows(gather_rows(both[owned_rows:], "fc"), "fy")[: kernel.shape[0]]
 
     return (
         result.astype(jnp.bfloat16),

time: 212 us -> 214 us (level)
  blocking collectives: 20.6 us -> 30.2 us
  starting transfers between devices: 46.4 us -> 39.9 us
    all_to_all x0 -> x1, blocking collectives: none -> 9.64 us  [gather_rows(): got = lax.all_to_all(copies, axis, split_axis=0, concat_axis=0, tiled=True)]
    all_to_all x2, starting transfers between devices: 17.9 us -> 11.4 us  [gather_rows(): got = lax.all_to_all(copies, axis, split_axis=0, concat_axis=0, tiled=True)]
where the time goes in v12:
time: 214 us
  waiting for transfers between devices  76.1 us (36%)
  starting transfers between devices  39.9 us (19%)
  blocking collectives  30.2 us (14%)
  other arithmetic  26.2 us (12%)
  between operations  15.3 us (7%)
  matrix products  13.3 us (6%)
  local copies, waits for them, and re-layouts  12.7 us (6%)
    all_to_all x1, blocking collectives, sum_rows(): lax.all_to_all(padded.reshape(count, per, x.shape[1]), axis, split_axis=0...  20.6 us
    all_to_all x1, waiting for transfers between devices, body(): lax.all_to_all(returning, DP, split_axis=0, concat_axis=0, tiled=True)  17.9 us
    all_to_all x2, waiting for transfers between devices, gather_rows(): got = lax.all_to_all(copies, axis, split_axis=0, concat_axis=0, tiled=True)  17.5 us
    all_to_all x1, waiting for transfers between devices, body(): lax.all_to_all(outgoing, DP, split_axis=0, concat_axis=0, tiled=True)  16 us
    reduce_sum x4, other arithmetic, finish(): kernel[offset] * padded[offset:offset + length] * matching[:, None]  14.6 us
    all_to_all x1, starting transfers between devices, body(): lax.all_to_all(outgoing, DP, split_axis=0, concat_axis=0, tiled=True)  13.7 us
    reduce_scatter x1, waiting for transfers between devices, body(): lax.psum_scatter(jnp.einsum('rc,rd->cd', columns, mixed_grad, preferred_e...  12.4 us
    all_gather x1, waiting for transfers between devices, body(): lax.all_gather(out_weight, FSDP, axis=0, tiled=True)  11.6 us
  transfers between devices with their start and end apart: 7, of which 6 were waited for; matrix products, arithmetic and copies ran while one was open for 11% of the time, Pallas kernels for 0%

profile of v12, /device:TPU:1, one launch (start us, length us, event | category | flops | bytes accessed | tf_op | source)
XLA Modules:
  0.0 213.6 jit_solution(7551023427433706175)
XLA Ops:
  7.2 0.7 all-gather.2.cloned.1.call-update
  7.9 1.2 compare_select_fusion.1
  9.2 1.0 gather_fusion
  10.2 0.2 select_select_fusion.1
  10.4 1.0 all_to_all.31
  11.3 13.7 %all-to-all-start = ((bf16[32,4,2304]{2,1,0:T(4,128)(2,1)}), bf16[32,4,2304]{2,1,0:T(4,128)(2,1)S(1)}, u32[]{:S(2)}, u32[]{:S(2)}) async-start(bf16[32,4,2304]{2,1,0:T(4,128)(2,1)} %all_to_all.31), calls=%async_computation | async-start | bytes 1179648 | tf_op jit(solution)/shard_map/all_to_all | solution.py:87
  25.1 0.2 slice_reduce_fusion.29
  25.3 0.5 compare_select_fusion
  25.8 0.3 slice_reduce_fusion.30
  26.6 16.0 %all-to-all-done = bf16[32,4,2304]{2,1,0:T(4,128)(2,1)S(1)} async-done(((bf16[32,4,2304]{2,1,0:T(4,128)(2,1)}), bf16[32,4,2304]{2,1,0:T(4,128)(2,1)S(1)}, u32[]{:S(2)}, u32[]{:S(2)}) %all-to-all-start) | async-done | bytes 589856 | tf_op jit(solution)/shard_map/all_to_all | solution.py:87
  42.5 0.1 all_to_all.33
  42.7 1.0 gather_fusion.1
  43.6 0.2 select_select_fusion
  43.8 0.2 copy.47
  44.0 0.2 copy.46
  44.2 0.2 copy.45
  44.3 1.2 fusion.39
  45.5 0.6 copy-done.47
  46.1 0.5 convolution_convert_fusion.6
  46.6 11.6 %all-gather.2.cloned.1.call-done = bf16[768,1536]{1,0:T(8,128)(2,1)} async-done(((bf16[48,1536]{1,0:T(8,128)(2,1)}), bf16[768,1536]{1,0:T(8,128)(2,1)}) %all-gather.2.cloned.1.call-update) | async-done | bytes 2359312 | tf_op jit(solution)/shard_map/all_gather | solution.py:95
  58.2 2.2 %fusion.2 = f32[128,1536]{1,0:T(8,128)S(1)} fusion(bf16[128,768]{0,1:T(8,128)(2,1)S(1)} %bitcast.38, bf16[768,1536]{1,0:T(8,128)(2,1)} %all-gather.2.cloned.1.call-done), kind=kOutput, calls=%fused_computation.8 | convolution fusion | flops 302383104 | bytes 3342336 | tf_op jit(solution)/shard_map/dot_general | solution.py:93
  60.4 7.7 %multiply_reduce_fusion.31 = (f32[1536]{0:T(1024)}, f32[1536]{0:T(1024)}, f32[1536]{0:T(1024)}, f32[1536]{0:T(1024)}, f32[1536]{0:T(1024)}, /*index=5*/f32[1536]...) fusion(f32[128,1536]{1,0:T(8,128)S(1)} %fusion.2, ...), kind=kLoop, calls=%fused_computation.99 | loop fusion | flops 25152000 | bytes 3013632 | tf_op jit(solution)/shard_map/transpose(jvp())/reduce_sum | solution.py:77
  68.2 2.3 %multiply_reduce_fusion.16 = (f32[1536]{0:T(1024)}, f32[1536]{0:T(1024)}, f32[1536]{0:T(1024)}, f32[1536]{0:T(1024)}, f32[1536]{0:T(1024)}, /*index=5*/f32[1536]...) fusion(f32[128,1536]{1,0:T(8,128)S(1)} %get-tuple-element.69, ...), kind=kLoop, calls=%fused_computation.84 | loop fusion | flops 5294592 | bytes 2424832 | tf_op jit(solution)/shard_map/transpose(jvp())/reduce_sum | solution.py:77
  70.4 0.5 multiply_multiply_fusion.27
  71.0 0.7 multiply_multiply_fusion.29
  71.8 0.7 multiply_multiply_fusion.28
  72.5 2.6 %multiply_reduce_fusion.4 = (f32[1536]{0:T(1024)}, f32[1536]{0:T(1024)}, f32[1536]{0:T(1024)}, f32[1536]{0:T(1024)}, f32[128,1536]{1,0:T(8,128)S(1)}, /*index=5*...) fusion(f32[128,1536]{1,0:T(8,128)S(1)} %get-tuple-element.69, ...), kind=kLoop, calls=%fused_computation.72 | loop fusion | flops 5105664 | bytes 7535616 | tf_op jit(solution)/shard_map/transpose(jvp())/reduce_sum | solution.py:77
  75.1 2.6 %pad_add_fusion = f32[158,1536]{1,0:T(8,128)S(1)} fusion(f32[128,1536]{1,0:T(8,128)S(1)} %get-tuple-element.78, f32[128,1536]{1,0:T(8,128)S(1)} %get-tuple-element.80, f32[128,1536]{1,0:T(8,128)S(1)} %get-tuple-element.81, f32[128,1536]{1,0:T(8,128)S(1)} %get-tuple-element.82, f32[128,1536]{1,0:T(8,128)S(1)} %get-tuple-element.83, ...), kind=kLoop, calls=%fused_computation.59 | loop fusion | flops 5824512 | bytes 20631552 | tf_op jit(solution)/shard_map/transpose(jvp())/add_any | solution.py:77
  77.7 0.7 fusion.16
  78.6 2.2 %convolution_convert_fusion = bf16[768,1536]{1,0:T(8,128)(2,1)} fusion(bf16[128,768]{0,1:T(8,128)(2,1)S(1)} %bitcast.39, bf16[128,1536]{1,0:T(8,128)(2,1)S(1)} %fusion.16), kind=kOutput, calls=%fused_computation.6 | convolution fusion | flops 303169536 | bytes 2949120 | tf_op jit(solution)/shard_map/rc,rd->cd/dot_general | solution.py:105
  81.1 2.0 multiply_reduce_fusion.22
  83.6 0.3 pad_add_fusion.7
  83.9 0.8 reshape.310
  84.7 4.6 %all-to-all-start.2 = ((f32[16,2,1536]{2,1,0:T(2,128)}), f32[16,2,1536]{2,1,0:T(2,128)S(1)}, u32[]{:S(2)}, u32[]{:S(2)}) async-start(f32[16,2,1536]{2,1,0:T(2,128)} %reshape.310), calls=%async_computation.3 | async-start | bytes 393216 | tf_op jit(solution)/shard_map/all_to_all | solution.py:147
  89.3 2.5 %convolution_convert_fusion.5 = bf16[128,768]{1,0:T(8,128)(2,1)S(1)} fusion(bf16[128,1536]{1,0:T(8,128)(2,1)S(1)} %fusion.16, bf16[768,1536]{1,0:T(8,128)(2,1)} %all-gather.2.cloned.1.call-done), kind=kOutput, calls=%fused_computation.54 | convolution fusion | flops 302088192 | bytes 2949120 | tf_op jit(solution)/shard_map/rd,cd->rc/dot_general | solution.py:112
  91.9 0.2 copy.49
  92.0 1.3 convolution_convert_fusion.2
  93.3 0.1 copy.55
  93.5 0.3 fusion.40
  93.8 1.6 convolution_convert_fusion.3
  95.4 0.1 copy.54
  95.5 1.6 convolution_convert_fusion.4
  97.1 0.1 copy.53
  97.3 1.8 scatter_custom_fusion
  99.0 1.0 all_to_all.34
  100.0 10.0 %all-to-all-start.1 = ((bf16[32,4,2304]{2,1,0:T(4,128)(2,1)}), bf16[32,4,2304]{2,1,0:T(4,128)(2,1)S(1)}, u32[]{:S(2)}, u32[]{:S(2)}) async-start(bf16[32,4,2304]{2,1,0:T(4,128)(2,1)} %all_to_all.34), calls=%async_computation.1 | async-start | bytes 1179648 | tf_op jit(solution)/shard_map/all_to_all | solution.py:122
  110.1 17.9 %all-to-all-done.1 = bf16[32,4,2304]{2,1,0:T(4,128)(2,1)S(1)} async-done(((bf16[32,4,2304]{2,1,0:T(4,128)(2,1)}), bf16[32,4,2304]{2,1,0:T(4,128)(2,1)S(1)}, u32[]{:S(2)}, u32[]{:S(2)}) %all-to-all-start.1) | async-done | bytes 589856 | tf_op jit(solution)/shard_map/all_to_all | solution.py:122
  128.1 0.1 reshape.341
  128.2 12.4 %reduce-scatter.2.cloned.1.call-done = bf16[48,1536]{1,0:T(8,128)(2,1)} async-done(((bf16[768,1536]{1,0:T(8,128)(2,1)}), bf16[48,1536]{1,0:T(8,128)(2,1)}) %reduce-scatter.2.cloned.1.call-update) | async-done | bytes 147472 | tf_op jit(solution)/shard_map/reduce_scatter | solution.py:104
  140.6 0.9 convert_element_type.216
  141.5 0.2 reshape.311
  141.8 20.6 %all_to_all.49 = f32[32,2,1536]{2,1,0:T(2,128)S(1)} all-to-all(f32[32,2,1536]{2,1,0:T(2,128)S(1)} %reshape.311), channel_id=1, replica_groups=mesh['dz'=8,'dx'=4,'fy'=8,'fc'=2] {'dz','dx'}, dimensions={0} | all-to-all | bytes 786432 | tf_op jit(solution)/shard_map/all_to_all | solution.py:147
  162.3 0.1 reduce_sum.365
  162.5 0.8 broadcast_in_dim.59
  163.3 4.1 %all-to-all-start.4 = ((f32[32,2,1536]{2,1,0:T(2,128)}), f32[32,2,1536]{2,1,0:T(2,128)S(1)}, u32[]{:S(2)}, u32[]{:S(2)}) async-start(f32[32,2,1536]{2,1,0:T(2,128)} %broadcast_in_dim.59), calls=%async_computation.5 | async-start | bytes 786432 | tf_op jit(solution)/shard_map/all_to_all | solution.py:154
  167.4 2.4 %scatter_custom_fusion.1 = bf16[128,2304]{1,0:T(8,128)(2,1)} fusion(s32[128]{0:T(128)} %get-tuple-element.108, bf16[128,2304]{1,0:T(8,128)(2,1)S(1)} %reshape.341, bf16[]{:T(256)} %constant.10.clone.1), kind=kCustom, calls=%fused_computation.145 | custom fusion | bytes 590336 | tf_op jit(solution)/shard_map/scatter | solution.py:124
  169.8 9.1 %all-to-all-done.4 = f32[32,2,1536]{2,1,0:T(2,128)S(1)} async-done(((f32[32,2,1536]{2,1,0:T(2,128)}), f32[32,2,1536]{2,1,0:T(2,128)S(1)}, u32[]{:S(2)}, u32[]{:S(2)}) %all-to-all-start.4) | async-done | bytes 393248 | tf_op jit(solution)/shard_map/all_to_all | solution.py:154
  178.9 9.6 %all_to_all.50 = f32[2,2,1536]{2,1,0:T(2,128)S(1)} all-to-all(f32[2,2,1536]{2,1,0:T(2,128)S(1)} %broadcast_in_dim.61), channel_id=1, replica_groups=mesh['dz'=8,'dx'=4,'fy'=8,'fc'=2] {'fc'}, dimensions={0} | all-to-all | bytes 49152 | tf_op jit(solution)/shard_map/all_to_all | solution.py:154
  188.5 0.7 broadcast_in_dim.63
  189.3 7.3 %all-to-all-start.6 = ((f32[8,4,1536]{2,1,0:T(4,128)}), f32[8,4,1536]{2,1,0:T(4,128)S(1)}, u32[]{:S(2)}, u32[]{:S(2)}) async-start(f32[8,4,1536]{2,1,0:T(4,128)} %broadcast_in_dim.63), calls=%async_computation.7 | async-start | bytes 393216 | tf_op jit(solution)/shard_map/all_to_all | solution.py:154
  196.5 0.1 slice_multiply_fusion
  196.7 0.9 mul.1323
  197.6 8.4 %all-to-all-done.6 = f32[8,4,1536]{2,1,0:T(4,128)S(1)} async-done(((f32[8,4,1536]{2,1,0:T(4,128)}), f32[8,4,1536]{2,1,0:T(4,128)S(1)}, u32[]{:S(2)}, u32[]{:S(2)}) %all-to-all-start.6) | async-done | bytes 196640 | tf_op jit(solution)/shard_map/all_to_all | solution.py:154
  206.1 0.7 slice_multiply_fusion.1
  (147 shorter events, 1.1 us)
Async XLA Ops:
  7.2 2.0 copy-start
  7.2 51.1 %all-gather.2.cloned.1.call-start = ((), (), s32[]{:S(2)}) async-start(), calls=%async_computation.8 | async-start | bytes 2506752 | tf_op jit(solution)/shard_map/all_gather | solution.py:95
  9.1 1.0 copy-start.45
  10.1 14.9 %copy-start.4 = (f32[31,1536]{1,0:T(8,128)S(1)}, f32[31,1536]{1,0:T(8,128)}, u32[]{:S(2)}) copy-start(f32[31,1536]{1,0:T(8,128)} %param.11) | copy-start | bytes 571396
  10.2 15.1 %copy-start.46 = (s32[128]{0:T(128)S(1)}, s32[128]{0:T(128)}, u32[]{:S(2)}) copy-start(s32[128]{0:T(128)} %param.14) | copy-start | bytes 1540
  10.2 16.0 %copy-start.44 = (s32[128]{0:T(128)S(1)}, s32[128]{0:T(128)}, u32[]{:S(2)}) copy-start(s32[128]{0:T(128)} %param.15) | copy-start | bytes 1540
  11.3 31.2 %all-to-all-start = ((bf16[32,4,2304]{2,1,0:T(4,128)(2,1)}), bf16[32,4,2304]{2,1,0:T(4,128)(2,1)S(1)}, u32[]{:S(2)}, u32[]{:S(2)}) async-start(bf16[32,4,2304]{2,1,0:T(4,128)(2,1)} %all_to_all.31), calls=%async_computation | async-start | bytes 1179648 | tf_op jit(solution)/shard_map/all_to_all | solution.py:87
  25.0 115.5 %reduce-scatter.2.cloned.1.call-start = ((), (), s32[]{:S(2)}) async-start(), calls=%async_computation.9 | async-start | bytes 2506752 | tf_op jit(solution)/shard_map/reduce_scatter | solution.py:104
  26.4 44.6 %copy-start.38 = (f32[128]{0:T(128)}, f32[128]{0:T(128)S(1)}, u32[]{:S(2)}) copy-start(f32[128]{0:T(128)S(1)} %get-tuple-element.122) | copy-start | bytes 1540
  26.4 44.6 %copy-start.40 = (f32[128]{0:T(128)}, f32[128]{0:T(128)S(1)}, u32[]{:S(2)}) copy-start(f32[128]{0:T(128)S(1)} %get-tuple-element.123) | copy-start | bytes 1540
  26.4 44.6 %copy-start.42 = (f32[128]{0:T(128)}, f32[128]{0:T(128)S(1)}, u32[]{:S(2)}) copy-start(f32[128]{0:T(128)S(1)} %get-tuple-element.124) | copy-start | bytes 1540
  26.4 45.3 %copy-start.26 = (f32[128]{0:T(128)}, f32[128]{0:T(128)S(1)}, u32[]{:S(2)}) copy-start(f32[128]{0:T(128)S(1)} %get-tuple-element.116) | copy-start | bytes 1540
  26.4 45.3 %copy-start.28 = (f32[128]{0:T(128)}, f32[128]{0:T(128)S(1)}, u32[]{:S(2)}) copy-start(f32[128]{0:T(128)S(1)} %get-tuple-element.117) | copy-start | bytes 1540
  26.4 45.3 %copy-start.30 = (f32[128]{0:T(128)}, f32[128]{0:T(128)S(1)}, u32[]{:S(2)}) copy-start(f32[128]{0:T(128)S(1)} %get-tuple-element.118) | copy-start | bytes 1540
  26.4 45.3 %copy-start.32 = (f32[128]{0:T(128)}, f32[128]{0:T(128)S(1)}, u32[]{:S(2)}) copy-start(f32[128]{0:T(128)S(1)} %get-tuple-element.119) | copy-start | bytes 1540
  26.4 45.3 %copy-start.34 = (f32[128]{0:T(128)}, f32[128]{0:T(128)S(1)}, u32[]{:S(2)}) copy-start(f32[128]{0:T(128)S(1)} %get-tuple-element.120) | copy-start | bytes 1540
  26.5 45.3 %copy-start.36 = (f32[128]{0:T(128)}, f32[128]{0:T(128)S(1)}, u32[]{:S(2)}) copy-start(f32[128]{0:T(128)S(1)} %get-tuple-element.121) | copy-start | bytes 1540
  26.6 19.0 %copy-start.25 = (pred[128,128]{0,1:T(8,128)(4,1)}, pred[128,128]{0,1:T(8,128)(4,1)S(1)}, u32[]{:S(2)}) copy-start(pred[128,128]{0,1:T(8,128)(4,1)S(1)} %broadcast_compare_fusion) | copy-start | bytes 49156
  44.2 14.1 %copy-start.2 = (bf16[128,768]{0,1:T(8,128)(2,1)}, bf16[128,768]{0,1:T(8,128)(2,1)S(1)}, u32[]{:S(2)}) copy-start(bf16[128,768]{0,1:T(8,128)(2,1)S(1)} %copy.46) | copy-start | bytes 589828
  45.5 0.6 copy-start.47
  46.6 13.8 %copy-start.1 = (bf16[128,1536]{1,0:T(8,128)(2,1)S(1)}, bf16[128,1536]{1,0:T(8,128)(2,1)}, u32[]{:S(2)}) copy-start(bf16[128,1536]{1,0:T(8,128)(2,1)} %param.12) | copy-start | bytes 1179652
  78.4 2.4 %copy-start.20 = (f32[1536]{0:T(1024)S(1)}, f32[1536]{0:T(1024)}, u32[]{:S(2)}) copy-start(f32[1536]{0:T(1024)} %get-tuple-element.7) | copy-start | bytes 18436
  78.4 2.5 %copy-start.19 = (f32[1536]{0:T(1024)S(1)}, f32[1536]{0:T(1024)}, u32[]{:S(2)}) copy-start(f32[1536]{0:T(1024)} %get-tuple-element.8) | copy-start | bytes 18436
  78.4 2.5 %copy-start.18 = (f32[1536]{0:T(1024)S(1)}, f32[1536]{0:T(1024)}, u32[]{:S(2)}) copy-start(f32[1536]{0:T(1024)} %get-tuple-element.9) | copy-start | bytes 18436
  78.4 2.5 %copy-start.17 = (f32[1536]{0:T(1024)S(1)}, f32[1536]{0:T(1024)}, u32[]{:S(2)}) copy-start(f32[1536]{0:T(1024)} %get-tuple-element.10) | copy-start | bytes 18436
  78.4 2.5 %copy-start.16 = (f32[1536]{0:T(1024)S(1)}, f32[1536]{0:T(1024)}, u32[]{:S(2)}) copy-start(f32[1536]{0:T(1024)} %get-tuple-element.11) | copy-start | bytes 18436
  78.5 2.5 %copy-start.15 = (f32[1536]{0:T(1024)S(1)}, f32[1536]{0:T(1024)}, u32[]{:S(2)}) copy-start(f32[1536]{0:T(1024)} %get-tuple-element.12) | copy-start | bytes 18436
  78.5 2.5 %copy-start.14 = (f32[1536]{0:T(1024)S(1)}, f32[1536]{0:T(1024)}, u32[]{:S(2)}) copy-start(f32[1536]{0:T(1024)} %get-tuple-element.13) | copy-start | bytes 18436
  78.5 2.5 %copy-start.13 = (f32[1536]{0:T(1024)S(1)}, f32[1536]{0:T(1024)}, u32[]{:S(2)}) copy-start(f32[1536]{0:T(1024)} %get-tuple-element.14) | copy-start | bytes 18436
  78.5 2.6 %copy-start.12 = (f32[1536]{0:T(1024)S(1)}, f32[1536]{0:T(1024)}, u32[]{:S(2)}) copy-start(f32[1536]{0:T(1024)} %get-tuple-element.15) | copy-start | bytes 18436
  78.5 2.6 %copy-start.27 = (f32[128]{0:T(128)S(1)}, f32[128]{0:T(128)}, u32[]{:S(2)}) copy-start(f32[128]{0:T(128)} %copy-done.26) | copy-start | bytes 1540
  78.5 2.6 %copy-start.29 = (f32[128]{0:T(128)S(1)}, f32[128]{0:T(128)}, u32[]{:S(2)}) copy-start(f32[128]{0:T(128)} %copy-done.28) | copy-start | bytes 1540
  78.5 2.6 %copy-start.31 = (f32[128]{0:T(128)S(1)}, f32[128]{0:T(128)}, u32[]{:S(2)}) copy-start(f32[128]{0:T(128)} %copy-done.30) | copy-start | bytes 1540
  78.5 2.6 %copy-start.33 = (f32[128]{0:T(128)S(1)}, f32[128]{0:T(128)}, u32[]{:S(2)}) copy-start(f32[128]{0:T(128)} %copy-done.32) | copy-start | bytes 1540
  78.5 2.6 %copy-start.35 = (f32[128]{0:T(128)S(1)}, f32[128]{0:T(128)}, u32[]{:S(2)}) copy-start(f32[128]{0:T(128)} %copy-done.34) | copy-start | bytes 1540
  78.5 2.6 %copy-start.37 = (f32[128]{0:T(128)S(1)}, f32[128]{0:T(128)}, u32[]{:S(2)}) copy-start(f32[128]{0:T(128)} %copy-done.36) | copy-start | bytes 1540
  78.6 2.6 %copy-start.39 = (f32[128]{0:T(128)S(1)}, f32[128]{0:T(128)}, u32[]{:S(2)}) copy-start(f32[128]{0:T(128)} %copy-done.38) | copy-start | bytes 1540
  78.6 2.6 %copy-start.41 = (f32[128]{0:T(128)S(1)}, f32[128]{0:T(128)}, u32[]{:S(2)}) copy-start(f32[128]{0:T(128)} %copy-done.40) | copy-start | bytes 1540
  78.6 2.6 %copy-start.43 = (f32[128]{0:T(128)S(1)}, f32[128]{0:T(128)}, u32[]{:S(2)}) copy-start(f32[128]{0:T(128)} %copy-done.42) | copy-start | bytes 1540
  80.7 2.5 %copy-start.11 = (f32[1536]{0:T(1024)S(1)}, f32[1536]{0:T(1024)}, u32[]{:S(2)}) copy-start(f32[1536]{0:T(1024)} %get-tuple-element.25) | copy-start | bytes 18436
  80.7 2.5 %copy-start.10 = (f32[1536]{0:T(1024)S(1)}, f32[1536]{0:T(1024)}, u32[]{:S(2)}) copy-start(f32[1536]{0:T(1024)} %get-tuple-element.26) | copy-start | bytes 18436
  80.7 2.6 %copy-start.9 = (f32[1536]{0:T(1024)S(1)}, f32[1536]{0:T(1024)}, u32[]{:S(2)}) copy-start(f32[1536]{0:T(1024)} %get-tuple-element.27) | copy-start | bytes 18436
  80.7 2.6 %copy-start.8 = (f32[1536]{0:T(1024)S(1)}, f32[1536]{0:T(1024)}, u32[]{:S(2)}) copy-start(f32[1536]{0:T(1024)} %get-tuple-element.28) | copy-start | bytes 18436
  80.7 2.6 %copy-start.7 = (f32[1536]{0:T(1024)S(1)}, f32[1536]{0:T(1024)}, u32[]{:S(2)}) copy-start(f32[1536]{0:T(1024)} %get-tuple-element.29) | copy-start | bytes 18436
  80.8 2.6 %copy-start.6 = (f32[1536]{0:T(1024)S(1)}, f32[1536]{0:T(1024)}, u32[]{:S(2)}) copy-start(f32[1536]{0:T(1024)} %get-tuple-element.30) | copy-start | bytes 18436
  80.8 2.6 %copy-start.5 = (f32[1536]{0:T(1024)S(1)}, f32[1536]{0:T(1024)}, u32[]{:S(2)}) copy-start(f32[1536]{0:T(1024)} %get-tuple-element.31) | copy-start | bytes 18436
  80.8 2.7 %copy-start.24 = (f32[1536]{0:T(1024)S(1)}, f32[1536]{0:T(1024)}, u32[]{:S(2)}) copy-start(f32[1536]{0:T(1024)} %get-tuple-element.34) | copy-start | bytes 18436
  80.8 2.7 %copy-start.23 = (f32[1536]{0:T(1024)S(1)}, f32[1536]{0:T(1024)}, u32[]{:S(2)}) copy-start(f32[1536]{0:T(1024)} %get-tuple-element.35) | copy-start | bytes 18436
  80.8 2.7 %copy-start.22 = (f32[1536]{0:T(1024)S(1)}, f32[1536]{0:T(1024)}, u32[]{:S(2)}) copy-start(f32[1536]{0:T(1024)} %get-tuple-element.36) | copy-start | bytes 18436
  80.8 2.7 %copy-start.21 = (f32[1536]{0:T(1024)S(1)}, f32[1536]{0:T(1024)}, u32[]{:S(2)}) copy-start(f32[1536]{0:T(1024)} %get-tuple-element.37) | copy-start | bytes 18436
  83.5 8.5 %copy-start.3 = (bf16[128,768]{0,1:T(8,128)(2,1)S(1)}, bf16[128,768]{0,1:T(8,128)(2,1)}, u32[]{:S(2)}) copy-start(bf16[128,768]{0,1:T(8,128)(2,1)} %copy-done.2) | copy-start | bytes 589828
  83.6 8.5 %copy-start.48 = (f32[8,128]{1,0:T(8,128)S(1)}, f32[8,128]{1,0:T(8,128)}, u32[]{:S(2)}) copy-start(f32[8,128]{1,0:T(8,128)} %copy-done.47) | copy-start | bytes 12292
  84.7 15.3 %all-to-all-start.2 = ((f32[16,2,1536]{2,1,0:T(2,128)}), f32[16,2,1536]{2,1,0:T(2,128)S(1)}, u32[]{:S(2)}, u32[]{:S(2)}) async-start(f32[16,2,1536]{2,1,0:T(2,128)} %reshape.310), calls=%async_computation.3 | async-start | bytes 393216 | tf_op jit(solution)/shard_map/all_to_all | solution.py:147
  100.0 28.1 %all-to-all-start.1 = ((bf16[32,4,2304]{2,1,0:T(4,128)(2,1)}), bf16[32,4,2304]{2,1,0:T(4,128)(2,1)S(1)}, u32[]{:S(2)}, u32[]{:S(2)}) async-start(bf16[32,4,2304]{2,1,0:T(4,128)(2,1)} %all_to_all.34), calls=%async_computation.1 | async-start | bytes 1179648 | tf_op jit(solution)/shard_map/all_to_all | solution.py:122
  163.3 15.6 %all-to-all-start.4 = ((f32[32,2,1536]{2,1,0:T(2,128)}), f32[32,2,1536]{2,1,0:T(2,128)S(1)}, u32[]{:S(2)}, u32[]{:S(2)}) async-start(f32[32,2,1536]{2,1,0:T(2,128)} %broadcast_in_dim.59), calls=%async_computation.5 | async-start | bytes 786432 | tf_op jit(solution)/shard_map/all_to_all | solution.py:154
  189.3 16.8 %all-to-all-start.6 = ((f32[8,4,1536]{2,1,0:T(4,128)}), f32[8,4,1536]{2,1,0:T(4,128)S(1)}, u32[]{:S(2)}, u32[]{:S(2)}) async-start(f32[8,4,1536]{2,1,0:T(4,128)} %broadcast_in_dim.63), calls=%async_computation.7 | async-start | bytes 393216 | tf_op jit(solution)/shard_map/all_to_all | solution.py:154
Sparse Core Ops, SparseCore 0:
  10.1 48.0 all-gather.1
  81.0 59.5 reduce-scatter.1
